TPU v7x, 128 devices: a whole 4x4x4 slice. The times are simulated.
128 devices in a mesh: row: 32 (over y, x, core), head: 4 (over z).
Axes of the slice: x: 4, y: 4, z: 4, core: 2. Of those that a mesh axis runs over, the one named last changes fastest.
Arguments:
- features: bfloat16 [16384, 1024], P('row'), may hold values from -6 to 6
- w_qkv: bfloat16 [3, 1024, 1024], P(None, None, 'head'), may hold values from -0.1875 to 0.1875
- w_out: bfloat16 [1024, 1024], P('head'), may hold values from -0.1875 to 0.1875
- bias_gain: float32 [16], P('head'), may hold values from 0.5 to 1.5
- edge_bias: bfloat16 [256, 64, 4096], P('row'), may hold values from -6 to 250
- neighbours: int32 [256, 64], P('row'), may hold values from 0 to 255, as said below
- counts: int32 [256], P('row'), may hold values from 1 to 64, as said below
Outputs:
- mixed: bfloat16 [16384, 1024], P('row', 'head')
Inputs may be any that keep to these rules, and one draw needn't show every extreme that they name: `neighbours`: key block b is owned by row device b // 8. Over all slots of the query blocks of one row device, at most 2 distinct key blocks of any one owner are named, and for every row device some owner has exactly 2. `counts`: the first query block of every row device has all 64 slots live.
All inputs are finite; a program needn't handle non-finite values.
Results may differ from a plain program's by a relative error of at most 0.011.
Values may be sent and summed in bfloat16 or wider, within the bound.
No kernel may reach another device: no remote copies, remote signals or barrier semaphores. Data moves between devices by JAX's collectives and lax.ppermute only.
A program may use at most 256 MiB of HBM per device.

v0:
```python
import jax
import jax.numpy as jnp
from jax import lax
from jax.sharding import PartitionSpec as P

HD = 64
BLK = 64
NB = 64


def body(features, w_qkv, w_out, bias_gain, edge_bias, neighbours, counts):
    rows = features.shape[0]
    width_heads = w_qkv.shape[2]
    heads_dev = width_heads // HD
    blocks_dev = rows // BLK
    row_devs = lax.axis_size("row")
    projected = jnp.einsum(
        "rd,tdc->trc", features, w_qkv, preferred_element_type=jnp.float32
    ).astype(jnp.bfloat16)
    queries = projected[0]
    kv_heads = projected[1:].reshape(2, rows, heads_dev, HD).transpose(0, 2, 1, 3)
    gathered = lax.all_gather(kv_heads, "row", axis=2, tiled=True)
    key_table = gathered.reshape(2, heads_dev, row_devs * blocks_dev, BLK, HD)
    group_size = min(8, blocks_dev)
    groups = blocks_dev // group_size
    scale = HD ** (-0.5)
    span = NB * BLK
    query_groups = queries.reshape(groups, group_size, BLK, heads_dev, HD).transpose(0, 3, 1, 2, 4)
    index_groups = neighbours.reshape(groups, group_size, NB)
    bias_groups = edge_bias.reshape(groups, group_size, BLK, span)
    count_groups = counts.reshape(groups, group_size)
    column_slot = jnp.arange(span, dtype=jnp.int32) // BLK

    def attend(inputs):
        query_tile, slot_ids, bias_tile, live_count = inputs
        near_keys = key_table[0][:, slot_ids].reshape(heads_dev, group_size, span, HD)
        near_values = key_table[1][:, slot_ids].reshape(heads_dev, group_size, span, HD)
        score = (
            jnp.einsum("hgqd,hgmd->hgqm", query_tile, near_keys, preferred_element_type=jnp.float32)
            * scale
        )
        score = score + bias_gain[:, None, None, None] * bias_tile.astype(jnp.float32)[None]
        live = column_slot[None, :] < live_count[:, None]
        score = jnp.where(live[None, :, None, :], score, jnp.float32(-1e30))
        top = jnp.max(score, axis=3, keepdims=True)
        expo = jnp.exp(score - top)
        total = jnp.sum(expo, axis=3, keepdims=True)
        weights = (expo / total).astype(jnp.bfloat16)
        result = jnp.einsum(
            "hgqm,hgmd->hgqd", weights, near_values, preferred_element_type=jnp.float32
        )
        return result.astype(jnp.bfloat16)

    attended = lax.map(attend, (query_groups, index_groups, bias_groups, count_groups))
    attended = attended.transpose(1, 0, 2, 3, 4).reshape(heads_dev, rows, HD)
    weight_heads = w_out.reshape(heads_dev, HD, w_out.shape[1])
    partial_out = jnp.einsum(
        "hrd,hdo->ro", attended, weight_heads, preferred_element_type=jnp.float32
    )
    return lax.psum_scatter(partial_out, "head", scatter_dimension=1, tiled=True).astype(
        jnp.bfloat16
    )


def solution(mesh):
    in_specs = (
        P("row", None),
        P(None, None, "head"),
        P("head", None),
        P("head"),
        P("row", None, None),
        P("row", None),
        P("row"),
    )
    out_specs = P("row", "head")
    return jax.shard_map(body, mesh=mesh, in_specs=in_specs, out_specs=out_specs, check_vma=False)
```

profile of v0, /device:TPU:2, one launch (start us, length us, event | category | flops | bytes accessed | tf_op | source)
XLA Modules:
  0.0 440.2 jit_solution(12831649080935923466)
XLA Ops:
  6.5 0.0 copy-start
  6.5 0.0 copy-start.4
  6.5 0.0 all-gather.2.cloned.1.call-start
  6.5 1.4 copy-done
  7.9 2.2 fusion.10
  10.2 0.8 slice.25
  11.0 0.0 all-gather.2.cloned.1.call-update
  11.0 0.0 reduce-scatter.2.cloned.1.call-start
  11.1 0.7 compare_select_fusion
  11.8 0.1 reshape.81
  11.9 6.6 %convert_element_type.25 = f32[8,64,4096]{2,1,0:T(8,128)} convert(bf16[8,64,4096]{2,1,0:T(8,128)(2,1)} %param.11) | non-fusion elementwise | flops 2097152 | bytes 12582912 | tf_op jit(solution)/shard_map/while/body/eval_jaxpr/convert_element_type | solution.py:42
  18.5 0.3 reshape_squeeze.3
  18.8 0.4 copy.19
  19.2 0.0 copy-done.4
  19.2 0.1 broadcast_compare_fusion
  19.3 73.8 %all-gather.2.cloned.1.call-done = bf16[2,4,16384,64]{2,3,1,0:T(8,128)(2,1)} async-done(((bf16[2,4,512,64]{2,3,1,0:T(8,128)(2,1)}), bf16[2,4,16384,64]{2,3,1,0:T(8,128)(2,1)}) %all-gather.2.cloned.1.call-update) | async-done | bytes 16777232 | tf_op jit(solution)/shard_map/all_gather | solution.py:22
  93.1 11.5 %fusion.25 = (bf16[1,4,16384,64]{2,3,1,0:T(8,128)(2,1)}, bf16[1,4,16384,64]{2,3,1,0:T(8,128)(2,1)}) fusion(bf16[2,4,16384,64]{2,3,1,0:T(8,128)(2,1)} %all-gather.2.cloned.1.call-done), kind=kLoop, calls=%fused_computation.34 | loop fusion | bytes 33554432 | tf_op jit(solution)/shard_map/while/body/eval_jaxpr/slice | solution.py:36
  104.6 15.5 %copy.32 = bf16[1,4,16384,64]{3,2,1,0:T(8,128)(2,1)} copy(bf16[1,4,16384,64]{2,3,1,0:T(8,128)(2,1)} %get-tuple-element.22) | data formatting | bytes 16777216 | tf_op jit(solution)/shard_map/while/body/eval_jaxpr/squeeze | solution.py:37
  120.1 21.9 %gather_fusion.1 = bf16[512,4,64,64]{3,2,1,0:T(8,128)(2,1)} fusion(bf16[4,256,64,64]{3,2,1,0:T(8,128)(2,1)} %bitcast.54, s32[1024]{0:T(1024)S(1)} %pad_clamp_fusion), kind=kCustom, calls=%fused_computation.1 | custom fusion | bytes 33556480 | tf_op jit(solution)/shard_map/while/body/eval_jaxpr/gather | solution.py:37
  142.0 44.5 %copy.25 = bf16[4,8,64,64,64]{3,2,4,1,0:T(8,128)(2,1)} copy(bf16[4,8,64,64,64]{4,3,0,2,1:T(8,128)(2,1)} %bitcast.56) | data formatting | bytes 33554432 | tf_op jit(solution)/shard_map/while/body/eval_jaxpr/gather | solution.py:37
  186.5 44.1 %reshape.77 = bf16[4,8,4096,64]{2,3,1,0:T(8,128)(2,1)} reshape(bf16[4,8,64,64,64]{3,2,4,1,0:T(8,128)(2,1)} %copy.25) | data formatting | bytes 33554432 | tf_op jit(solution)/shard_map/while/body/eval_jaxpr/reshape | solution.py:37
  230.5 15.5 %copy.29 = bf16[1,4,16384,64]{3,2,1,0:T(8,128)(2,1)} copy(bf16[1,4,16384,64]{2,3,1,0:T(8,128)(2,1)} %get-tuple-element.21) | data formatting | bytes 16777216 | tf_op jit(solution)/shard_map/while/body/eval_jaxpr/squeeze | solution.py:36
  246.1 21.9 %gather_fusion = bf16[512,4,64,64]{3,2,1,0:T(8,128)(2,1)} fusion(bf16[4,256,64,64]{3,2,1,0:T(8,128)(2,1)} %bitcast.53, s32[1024]{0:T(1024)S(1)} %pad_clamp_fusion), kind=kCustom, calls=%fused_computation | custom fusion | bytes 33556480 | tf_op jit(solution)/shard_map/while/body/eval_jaxpr/gather | solution.py:36
  268.0 44.5 %copy.22 = bf16[4,8,64,64,64]{3,2,4,1,0:T(8,128)(2,1)} copy(bf16[4,8,64,64,64]{4,3,0,2,1:T(8,128)(2,1)} %bitcast.55) | data formatting | bytes 33554432 | tf_op jit(solution)/shard_map/while/body/eval_jaxpr/gather | solution.py:36
  312.4 0.0 copy-start.3
  312.4 44.1 %reshape.76 = bf16[4,8,4096,64]{2,3,1,0:T(8,128)(2,1)} reshape(bf16[4,8,64,64,64]{3,2,4,1,0:T(8,128)(2,1)} %copy.22) | data formatting | bytes 33554432 | tf_op jit(solution)/shard_map/while/body/eval_jaxpr/reshape | solution.py:36
  356.5 0.0 copy-done.3
  356.5 24.4 %fusion.26 = (f32[4,8,64]{2,1,0:T(8,128)S(1)}, f32[4,8,64,4096]{3,2,1,0:T(8,128)}) fusion(f32[8,64,4096]{2,1,0:T(8,128)} %convert_element_type.25, f32[4]{0:T(128)S(1)} %copy-done.3, pred[8,4096]{1,0:T(8,128)(4,1)S(1)} %broadcast_compare_fusion, bf16[4,8,4096,64]{2,3,1,0:T(8,128)(2,1)} %reshape.76, bf16[1,8,64,4,64]{4,2,1,3,0:T(8,128)(2,1)S(1)} %copy.19), kind=kOutput, calls=%fused_computation.35 | convolution fusion | flops 1124077568 | bytes 59023376 | tf_op jit(solution)/shard_map/while/body/eval_jaxpr/sub | solution.py:46
  380.9 0.0 copy-start.2
  380.9 0.0 copy-start.1
  380.9 18.2 %fusion.11 = bf16[4,8,64,64]{3,2,1,0:T(8,128)(2,1)S(1)} fusion(bf16[4,8,4096,64]{2,3,1,0:T(8,128)(2,1)} %reshape.77, f32[4,8,64,4096]{3,2,1,0:T(8,128)} %get-tuple-element.24, f32[4,8,64]{2,1,0:T(8,128)S(1)} %get-tuple-element.23), kind=kOutput, calls=%fused_computation.17 | convolution fusion | flops 1090650112 | bytes 50601984 | tf_op jit(solution)/shard_map/while/body/eval_jaxpr/hgqm,hgmd->hgqd/dot_general | solution.py:49
  399.2 0.0 copy-done.2
  399.2 1.8 convolution_bitcast_fusion
  401.0 0.0 reduce-scatter.2.cloned.1.call-update
  401.0 30.6 %reduce-scatter.2.cloned.1.call-done = f32[512,256]{1,0:T(8,128)} async-done(((f32[512,1024]{1,0:T(8,128)}), f32[512,256]{1,0:T(8,128)}) %reduce-scatter.2.cloned.1.call-update) | async-done | bytes 524304 | tf_op jit(solution)/shard_map/reduce_scatter | solution.py:60
  431.6 1.8 convert_element_type.28
  433.4 0.0 copy-done.1
  (3 shorter events, 0.0 us)
Async XLA Ops:
  6.5 1.4 copy-start
  6.5 12.6 %copy-start.4 = (s32[8]{0:T(128)S(1)}, s32[8]{0:T(128)}, u32[]{:S(2)}) copy-start(s32[8]{0:T(128)} %param.13) | copy-start | bytes 100
  6.5 86.5 %all-gather.2.cloned.1.call-start = ((), (), s32[]{:S(2)}) async-start(), calls=%async_computation.1 | async-start | bytes 17301504 | tf_op jit(solution)/shard_map/all_gather | solution.py:22
  11.0 420.6 %reduce-scatter.2.cloned.1.call-start = ((), (), s32[]{:S(2)}) async-start(), calls=%async_computation.2 | async-start | bytes 2621440 | tf_op jit(solution)/shard_map/reduce_scatter | solution.py:60
  312.4 44.1 %copy-start.3 = (f32[4]{0:T(128)S(1)}, f32[4]{0:T(128)}, u32[]{:S(2)}) copy-start(f32[4]{0:T(128)} %param.10) | copy-start | bytes 52
  380.9 18.2 %copy-start.2 = (bf16[256,1024]{1,0:T(8,128)(2,1)S(1)}, bf16[256,1024]{1,0:T(8,128)(2,1)}, u32[]{:S(2)}) copy-start(bf16[256,1024]{1,0:T(8,128)(2,1)} %param.9) | copy-start | bytes 1572868
  380.9 52.4 %copy-start.1 = (bf16[3,1024,256]{2,1,0:T(8,128)(2,1)S(1)}, bf16[3,1024,256]{2,1,0:T(8,128)(2,1)}, u32[]{:S(2)}) copy-start(bf16[3,1024,256]{2,1,0:T(8,128)(2,1)} %param.8) | copy-start | bytes 4718596
Sparse Core Ops, SparseCore 0:
  11.2 81.8 all-gather.1
  401.1 30.4 reduce-scatter.1
where the time goes:
time: 446 us; the launch traced here: 440 us
  local copies, waits for them, and re-layouts  266 us (60%)
  waiting for transfers between devices  104 us (23%)
  matrix products  46.7 us (10%)
  between operations  13.5 us (3%)
  other arithmetic  9.14 us (2%)
    all_gather x1, waiting for transfers between devices, body(): gathered = lax.all_gather(kv_heads, 'row', axis=2, tiled=True)  73.8 us
    gather x2, local copies, waits for them, and re-layouts, attend(): key_table[1][:, slot_ids].reshape(heads_dev, group_size, span, HD)  66.4 us
    gather x2, local copies, waits for them, and re-layouts, attend(): key_table[0][:, slot_ids].reshape(heads_dev, group_size, span, HD)  66.4 us
    reshape x1, local copies, waits for them, and re-layouts, attend(): key_table[1][:, slot_ids].reshape(heads_dev, group_size, span, HD)  44.1 us
    reshape x1, local copies, waits for them, and re-layouts, attend(): key_table[0][:, slot_ids].reshape(heads_dev, group_size, span, HD)  44.1 us
    reduce_scatter x1, waiting for transfers between devices, body(): lax.psum_scatter(partial_out, 'head', scatter_dimension=1, tiled=True)  30.6 us
    sub x1, matrix products, attend(): expo = jnp.exp(score - top)  24.4 us
    dot_general x1, matrix products, attend(): jnp.einsum('hgqm,hgmd->hgqd', weights, near_values, preferred_element_typ...  18.2 us
  transfers between devices with their start and end apart: 2, of which 2 were waited for; matrix products, arithmetic and copies ran while one was open for 2% of the time, Pallas kernels for 0%

commit v1 on v0

v1 whole, which is shorter than its diff:
```python
import jax
import jax.numpy as jnp
from jax import lax
from jax.experimental import pallas as pl
from jax.experimental.pallas import tpu as pltpu
from jax.sharding import PartitionSpec as P

HD = 64
BLK = 64
NB = 64


def _attend_kernel(nbr_ref, cnt_ref, gain_ref, q_ref, bias_ref, kv_hbm, o_ref, kv_buf, sem):
    g = pl.program_id(0)
    steps = pl.num_programs(0)
    width = kv_buf.shape[-1]
    half_w = width // 2
    pairs = half_w // 128

    def start(gi, slot):
        def issue(j, carry):
            pltpu.make_async_copy(
                kv_hbm.at[nbr_ref[gi, j]], kv_buf.at[slot, j], sem.at[slot]
            ).start()
            return carry

        lax.fori_loop(0, NB, issue, 0)

    @pl.when(g == 0)
    def _():
        start(0, 0)

    @pl.when(g + 1 < steps)
    def _():
        start(g + 1, (g + 1) % 2)

    slot = g % 2
    pltpu.make_async_copy(kv_hbm.at[pl.ds(0, NB)], kv_buf.at[slot], sem.at[slot]).wait()

    span = NB * BLK
    live_cols = cnt_ref[g] * BLK
    col = lax.broadcasted_iota(jnp.int32, (BLK, span), 1)
    live = col < live_cols
    bias = bias_ref[0].astype(jnp.float32)
    q = q_ref[0]
    lane = lax.broadcasted_iota(jnp.int32, (BLK, 128), 1)
    scale = HD ** (-0.5)
    outs = []
    for pair in range(pairs):
        kp = kv_buf[slot, :, :, pair * 128:(pair + 1) * 128].reshape(span, 128)
        vp = kv_buf[slot, :, :, half_w + pair * 128:half_w + (pair + 1) * 128].reshape(span, 128)
        qp = q[:, pair * 128:(pair + 1) * 128]
        res = None
        for half in range(2):
            h = pair * 2 + half
            in_head = (lane >= half * HD) & (lane < (half + 1) * HD)
            qm = jnp.where(in_head, qp, jnp.zeros_like(qp))
            s = lax.dot_general(
                qm, kp, (((1,), (1,)), ((), ())), preferred_element_type=jnp.float32
            )
            s = s * scale + gain_ref[h] * bias
            s = jnp.where(live, s, jnp.float32(-1e30))
            top = jnp.max(s, axis=1, keepdims=True)
            expo = jnp.exp(s - top)
            total = jnp.sum(expo, axis=1, keepdims=True)
            w = (expo * (1.0 / total)).astype(jnp.bfloat16)
            o = jnp.dot(w, vp, preferred_element_type=jnp.float32)
            res = o if res is None else jnp.where(lane < HD, res, o)
        outs.append(res.astype(jnp.bfloat16))
    o_ref[0] = jnp.concatenate(outs, axis=1)


def attend(nbr, cnt, gain, q_blocks, bias, kv_table):
    blocks, _, width_q = q_blocks.shape
    width = kv_table.shape[-1]
    span = NB * BLK
    grid_spec = pltpu.PrefetchScalarGridSpec(
        num_scalar_prefetch=2,
        grid=(blocks,),
        in_specs=[
            pl.BlockSpec(memory_space=pltpu.SMEM),
            pl.BlockSpec((1, BLK, width_q), lambda g, n, c: (g, 0, 0)),
            pl.BlockSpec((1, BLK, span), lambda g, n, c: (g, 0, 0)),
            pl.BlockSpec(memory_space=pl.ANY),
        ],
        out_specs=pl.BlockSpec((1, BLK, width_q), lambda g, n, c: (g, 0, 0)),
        scratch_shapes=[
            pltpu.VMEM((2, NB, BLK, width), jnp.bfloat16),
            pltpu.SemaphoreType.DMA((2,)),
        ],
    )
    return pl.pallas_call(
        _attend_kernel,
        grid_spec=grid_spec,
        out_shape=jax.ShapeDtypeStruct((blocks, BLK, width_q), jnp.bfloat16),
        compiler_params=pltpu.CompilerParams(
            dimension_semantics=("arbitrary",), vmem_limit_bytes=48 * 1024 * 1024
        ),
    )(nbr, cnt, gain, q_blocks, bias, kv_table)


def body(features, w_qkv, w_out, bias_gain, edge_bias, neighbours, counts):
    rows = features.shape[0]
    width_heads = w_qkv.shape[2]
    blocks_dev = rows // BLK
    queries = jnp.dot(features, w_qkv[0], preferred_element_type=jnp.float32).astype(jnp.bfloat16)
    keys = jnp.dot(features, w_qkv[1], preferred_element_type=jnp.float32).astype(jnp.bfloat16)
    values = jnp.dot(features, w_qkv[2], preferred_element_type=jnp.float32).astype(jnp.bfloat16)
    kv = jnp.concatenate([keys, values], axis=1)
    gathered = lax.all_gather(kv, "row", axis=0, tiled=True)
    kv_table = gathered.reshape(-1, BLK, 2 * width_heads)
    w_cols = lax.all_to_all(w_out, "head", 1, 0, tiled=True)
    attended = attend(
        neighbours,
        counts,
        bias_gain,
        queries.reshape(blocks_dev, BLK, width_heads),
        edge_bias,
        kv_table,
    ).reshape(rows, width_heads)
    attended_all = lax.all_gather(attended, "head", axis=1, tiled=True)
    return jnp.dot(attended_all, w_cols, preferred_element_type=jnp.float32).astype(jnp.bfloat16)


def solution(mesh):
    in_specs = (
        P("row", None),
        P(None, None, "head"),
        P("head", None),
        P("head"),
        P("row", None, None),
        P("row", None),
        P("row"),
    )
    out_specs = P("row", "head")
    return jax.shard_map(body, mesh=mesh, in_specs=in_specs, out_specs=out_specs, check_vma=False)
```

time: 446 us -> 195 us (0.44); the launches traced: 440 us -> 194 us
  local copies, waits for them, and re-layouts: 266 us -> 26.2 us
  matrix products: 46.7 us -> 4.81 us
  Pallas kernels: 0 us -> 41 us
  blocking collectives: 0 us -> 14 us
  waiting for transfers between devices: 104 us -> 93.3 us
  other arithmetic: 9.14 us -> 0.85 us
    gather x4 -> x0, local copies, waits for them, and re-layouts: 133 us -> none  [the longest x2 66.4 us: attend(): key_table[1][:, slot_ids].reshape(heads_dev, group_size, span, HD)]
    reshape x2 -> x0, local copies, waits for them, and re-layouts: 88.2 us -> none  [the longest x1 44.1 us: attend(): key_table[1][:, slot_ids].reshape(heads_dev, group_size, span, HD)]
    pallas_call x0 -> x1, Pallas kernels: none -> 41 us  [attend(): pl.pallas_call(_attend_kernel, grid_spec=grid_spec, out_shape=jax.ShapeDt...]
    squeeze x2 -> x0, local copies, waits for them, and re-layouts: 31.1 us -> none  [the longest x1 15.5 us: attend(): key_table[1][:, slot_ids].reshape(heads_dev, group_size, span, HD)]
    reduce_scatter x1 -> x0, waiting for transfers between devices: 30.6 us -> none  [body(): lax.psum_scatter(partial_out, 'head', scatter_dimension=1, tiled=True)]
    sub x1 -> x0, matrix products: 24.4 us -> none  [attend(): expo = jnp.exp(score - top)]
    all_gather x0 -> x1, local copies, waits for them, and re-layouts: none -> 22.3 us  [body(): gathered = lax.all_gather(kv, 'row', axis=0, tiled=True)]
    all_gather x1 -> x2, waiting for transfers between devices: 73.8 us -> 93.3 us  [the longest x1 81.5 us: body(): gathered = lax.all_gather(kv, 'row', axis=0, tiled=True)]
  transfers between devices with their start and end apart: 2 -> 2, of which waited for: 2 -> 2; matrix products, arithmetic and copies ran while one was open for 2% -> 0% of each run, Pallas kernels for 0% -> 0%
where the time goes in v1:
time: 195 us; the launch traced here: 194 us
  waiting for transfers between devices  93.3 us (48%)
  Pallas kernels  41 us (21%)
  local copies, waits for them, and re-layouts  26.2 us (13%)
  blocking collectives  14 us (7%)
  between operations  13.5 us (7%)
  matrix products  4.81 us (2%)
    all_gather x1, waiting for transfers between devices, body(): gathered = lax.all_gather(kv, 'row', axis=0, tiled=True)  81.5 us
    pallas_call x1, Pallas kernels, attend(): pl.pallas_call(_attend_kernel, grid_spec=grid_spec, out_shape=jax.ShapeDt...  41 us
    all_gather x1, local copies, waits for them, and re-layouts, body(): gathered = lax.all_gather(kv, 'row', axis=0, tiled=True)  22.3 us
    all_to_all x1, blocking collectives, body(): w_cols = lax.all_to_all(w_out, 'head', 1, 0, tiled=True)  14 us
    all_gather x1, waiting for transfers between devices, body(): attended_all = lax.all_gather(attended, 'head', axis=1, tiled=True)  11.8 us
  transfers between devices with their start and end apart: 2, of which 2 were waited for; matrix products, arithmetic and copies ran while one was open for 0% of the time, Pallas kernels for 0%

profile of v1, /device:TPU:2, one launch (start us, length us, event | category | flops | bytes accessed | tf_op | source)
XLA Modules:
  0.0 193.7 jit_solution(7268673585084861438)
XLA Ops:
  6.5 0.0 copy-start
  6.5 0.0 copy-start.6
  6.5 0.0 all-gather.3.cloned.1.call-start
  6.5 1.2 copy-done
  7.8 1.5 convolution_convert_fusion.1
  9.3 0.0 copy-done.6
  9.3 0.5 convolution_convert_fusion.2
  9.8 0.8 pad_maximum_fusion
  10.6 0.0 all-gather.3.cloned.1.call-update
  10.7 0.0 all-gather.5.cloned.1.call-start
  10.7 0.4 convolution_convert_fusion.3
  11.2 0.0 copy-start.2
  11.2 0.0 copy-start.3
  11.2 0.0 copy-start.4
  11.2 81.5 %all-gather.3.cloned.1.call-done = bf16[16384,512]{0,1:T(8,128)(2,1)} async-done(((bf16[512,512]{0,1:T(8,128)(2,1)}), bf16[16384,512]{0,1:T(8,128)(2,1)}) %all-gather.3.cloned.1.call-update) | async-done | bytes 16777232 | tf_op jit(solution)/shard_map/all_gather | solution.py:110
  92.7 22.3 %copy.10 = bf16[16384,512]{1,0:T(8,128)(2,1)} copy(bf16[16384,512]{0,1:T(8,128)(2,1)} %all-gather.3.cloned.1.call-done) | data formatting | bytes 33554432 | tf_op jit(solution)/shard_map/all_gather | solution.py:110
  115.0 0.0 copy-done.2
  115.0 0.0 copy-done.3
  115.0 0.0 copy-done.4
  115.0 0.0 copy-start.1
  115.0 2.2 %copy-done.1 = bf16[8,64,4096]{2,1,0:T(8,128)(2,1)S(1)} copy-done((bf16[8,64,4096]{2,1,0:T(8,128)(2,1)S(1)}, bf16[8,64,4096]{2,1,0:T(8,128)(2,1)}, u32[]{:S(2)}) %copy-start.1) | copy-done | bytes 4194328
  117.2 0.0 copy-start.5
  117.2 41.0 %shard_map.73 = bf16[8,64,256]{2,1,0:T(8,128)(2,1)} custom-call(s32[8,64]{1,0:T(8,128)S(1)} %copy-done.2, s32[8]{0:T(128)S(1)} %copy-done.3, f32[4]{0:T(128)S(1)} %copy-done.4, bf16[8,64,256]{2,1,0:T(8,128)(2,1)S(1)} %bitcast.20, bf16[8,64,4096]{2,1,0:T(8,128)(2,1)S(1)} %copy-done.1, bf16[256,64,512]{2,1,0:T(8,128)(2,1)} %bitcast.21), custom_call_target="tpu_custom_call" | custom-call | tf_op jit(solution)/shard_map/pallas_call | solution.py:92
  158.3 0.0 all-gather.5.cloned.1.call-update
  158.3 0.0 copy-done.5
  158.3 0.2 copy.11
  158.5 14.0 %all_to_all.19 = bf16[256,4,256]{0,2,1:T(8,128)(2,1)S(1)} all-to-all(bf16[256,4,256]{0,2,1:T(8,128)(2,1)S(1)} %bitcast.23), channel_id=1, replica_groups=mesh['row'=32,'head'=4] {'head'}, dimensions={1} | all-to-all | bytes 1048576 | tf_op jit(solution)/shard_map/all_to_all | solution.py:112
  172.5 0.2 copy.12
  172.7 11.8 %all-gather.5.cloned.1.call-done = bf16[512,1024]{1,0:T(8,128)(2,1)} async-done(((bf16[512,256]{1,0:T(8,128)(2,1)}), bf16[512,1024]{1,0:T(8,128)(2,1)}) %all-gather.5.cloned.1.call-update) | async-done | bytes 1048592 | tf_op jit(solution)/shard_map/all_gather | solution.py:121
  184.5 2.4 %convolution_convert_fusion = bf16[512,256]{1,0:T(8,128)(2,1)} fusion(bf16[512,1024]{1,0:T(8,128)(2,1)} %all-gather.5.cloned.1.call-done, bf16[1024,256]{1,0:T(8,128)(2,1)S(1)} %bitcast.24), kind=kOutput, calls=%fused_computation | convolution fusion | flops 268566528 | bytes 1835008 | tf_op jit(solution)/shard_map/dot_general | solution.py:122
Async XLA Ops:
  6.5 1.2 copy-start
  6.5 2.8 %copy-start.6 = (bf16[3,1024,256]{2,1,0:T(8,128)(2,1)S(1)}, bf16[3,1024,256]{2,1,0:T(8,128)(2,1)}, u32[]{:S(2)}) copy-start(bf16[3,1024,256]{2,1,0:T(8,128)(2,1)} %param.8) | copy-start | bytes 4718596
  6.5 86.1 %all-gather.3.cloned.1.call-start = ((), (), s32[]{:S(2)}) async-start(), calls=%async_computation.1 | async-start | bytes 17301504 | tf_op jit(solution)/shard_map/all_gather | solution.py:110
  10.7 173.9 %all-gather.5.cloned.1.call-start = ((), (), s32[]{:S(2)}) async-start(), calls=%async_computation.2 | async-start | bytes 1310720 | tf_op jit(solution)/shard_map/all_gather | solution.py:121
  11.2 103.9 %copy-start.2 = (s32[8,64]{1,0:T(8,128)S(1)}, s32[8,64]{1,0:T(8,128)}, u32[]{:S(2)}) copy-start(s32[8,64]{1,0:T(8,128)} %nbr_ref.1) | copy-start | bytes 6148
  11.2 103.8 %copy-start.3 = (s32[8]{0:T(128)S(1)}, s32[8]{0:T(128)}, u32[]{:S(2)}) copy-start(s32[8]{0:T(128)} %cnt_ref.1) | copy-start | bytes 100
  11.2 103.8 %copy-start.4 = (f32[4]{0:T(128)S(1)}, f32[4]{0:T(128)}, u32[]{:S(2)}) copy-start(f32[4]{0:T(128)} %gain_ref.1) | copy-start | bytes 52
  115.0 2.2 %copy-start.1 = (bf16[8,64,4096]{2,1,0:T(8,128)(2,1)S(1)}, bf16[8,64,4096]{2,1,0:T(8,128)(2,1)}, u32[]{:S(2)}) copy-start(bf16[8,64,4096]{2,1,0:T(8,128)(2,1)} %bias_ref.1) | copy-start | bytes 12582916
  117.2 41.1 %copy-start.5 = (bf16[256,1024]{1,0:T(8,128)(2,1)S(1)}, bf16[256,1024]{1,0:T(8,128)(2,1)}, u32[]{:S(2)}) copy-start(bf16[256,1024]{1,0:T(8,128)(2,1)} %param.9) | copy-start | bytes 1572868
Sparse Core Ops, SparseCore 0:
  10.8 81.8 all-gather.2
  158.4 26.0 all-gather.4

commit v2 on v1

--- a/solution.py
+++ b/solution.py
@@ -103,23 +103,43 @@
     rows = features.shape[0]
     width_heads = w_qkv.shape[2]
     blocks_dev = rows // BLK
+    head_devs = lax.axis_size("head")
+    me = lax.axis_index("head")
+    chunk = 128
+    chunks = width_heads // chunk
     queries = jnp.dot(features, w_qkv[0], preferred_element_type=jnp.float32).astype(jnp.bfloat16)
     keys = jnp.dot(features, w_qkv[1], preferred_element_type=jnp.float32).astype(jnp.bfloat16)
     values = jnp.dot(features, w_qkv[2], preferred_element_type=jnp.float32).astype(jnp.bfloat16)
-    kv = jnp.concatenate([keys, values], axis=1)
-    gathered = lax.all_gather(kv, "row", axis=0, tiled=True)
-    kv_table = gathered.reshape(-1, BLK, 2 * width_heads)
-    w_cols = lax.all_to_all(w_out, "head", 1, 0, tiled=True)
-    attended = attend(
-        neighbours,
-        counts,
-        bias_gain,
-        queries.reshape(blocks_dev, BLK, width_heads),
-        edge_bias,
-        kv_table,
-    ).reshape(rows, width_heads)
-    attended_all = lax.all_gather(attended, "head", axis=1, tiled=True)
-    return jnp.dot(attended_all, w_cols, preferred_element_type=jnp.float32).astype(jnp.bfloat16)
+    w_parts = []
+    for s in range(1, head_devs):
+        target = (me + s) % head_devs
+        piece = lax.dynamic_slice_in_dim(w_out, target * width_heads, width_heads, axis=1)
+        perm = [(i, (i + s) % head_devs) for i in range(head_devs)]
+        w_parts.append(lax.ppermute(piece, "head", perm))
+    w_own = lax.dynamic_slice_in_dim(w_out, me * width_heads, width_heads, axis=1)
+    outs = []
+    for c in range(chunks):
+        cols = slice(c * chunk, (c + 1) * chunk)
+        kv = jnp.concatenate([keys[:, cols], values[:, cols]], axis=1)
+        kv = kv.reshape(blocks_dev, BLK, 2 * chunk)
+        kv_table = lax.all_gather(kv, "row", axis=0, tiled=True)
+        outs.append(
+            attend(
+                neighbours,
+                counts,
+                bias_gain[c * 2:(c + 1) * 2],
+                queries[:, cols].reshape(blocks_dev, BLK, chunk),
+                edge_bias,
+                kv_table,
+            ).reshape(rows, chunk)
+        )
+    attended = jnp.concatenate(outs, axis=1)
+    total = jnp.dot(attended, w_own, preferred_element_type=jnp.float32)
+    for s in range(1, head_devs):
+        perm = [(i, (i + s) % head_devs) for i in range(head_devs)]
+        att_s = lax.ppermute(attended, "head", perm)
+        total = total + jnp.dot(att_s, w_parts[s - 1], preferred_element_type=jnp.float32)
+    return total.astype(jnp.bfloat16)
 
 
 def solution(mesh):

time: 195 us -> 177 us (0.908)
  local copies, waits for them, and re-layouts: 26.2 us -> 7.5 us
  blocking collectives: 14 us -> 0 us
  starting transfers between devices: 0.04 us -> 10.4 us
  Pallas kernels: 41 us -> 46.5 us
    all_gather x1 -> x0, local copies, waits for them, and re-layouts: 22.3 us -> none  [body(): gathered = lax.all_gather(kv, 'row', axis=0, tiled=True)]
    all_to_all x1 -> x0, blocking collectives: 14 us -> none  [body(): w_cols = lax.all_to_all(w_out, 'head', 1, 0, tiled=True)]
    ppermute x0 -> x6, waiting for transfers between devices: none -> 11.3 us  [the longest x3 6.73 us: body(): att_s = lax.ppermute(attended, 'head', perm)]
    all_gather x2, waiting for transfers between devices: 93.3 us -> 82.8 us  [body(): kv_table = lax.all_gather(kv, 'row', axis=0, tiled=True)]
    ppermute x0 -> x6, starting transfers between devices: none -> 10.3 us  [the longest x3 5.38 us: body(): att_s = lax.ppermute(attended, 'head', perm)]
    pallas_call x1 -> x2, Pallas kernels: 41 us -> 46.5 us  [attend(): pl.pallas_call(_attend_kernel, grid_spec=grid_spec, out_shape=jax.ShapeDt...]
    unnamed x15 -> x16, local copies, waits for them, and re-layouts: 3.63 us -> 5.62 us
  transfers between devices with their start and end apart: 2 -> 8, of which waited for: 2 -> 5; matrix products, arithmetic and copies ran while one was open for 0% -> 1% of each run, Pallas kernels for 0% -> 13%
where the time goes in v2:
time: 177 us; the launch traced here: 176 us
  waiting for transfers between devices  94.1 us (53%)
  Pallas kernels  46.5 us (26%)
  between operations  13.6 us (8%)
  starting transfers between devices  10.4 us (6%)
  local copies, waits for them, and re-layouts  7.5 us (4%)
  matrix products  4.06 us (2%)
    all_gather x2, waiting for transfers between devices, body(): kv_table = lax.all_gather(kv, 'row', axis=0, tiled=True)  82.8 us
    pallas_call x2, Pallas kernels, attend(): pl.pallas_call(_attend_kernel, grid_spec=grid_spec, out_shape=jax.ShapeDt...  46.5 us
    ppermute x3, waiting for transfers between devices, body(): att_s = lax.ppermute(attended, 'head', perm)  6.73 us
    unnamed x16, local copies, waits for them, and re-layouts  5.62 us
    ppermute x3, starting transfers between devices, body(): att_s = lax.ppermute(attended, 'head', perm)  5.38 us
    ppermute x3, starting transfers between devices, body(): w_parts.append(lax.ppermute(piece, 'head', perm))  4.95 us
    ppermute x3, waiting for transfers between devices, body(): w_parts.append(lax.ppermute(piece, 'head', perm))  4.6 us
  transfers between devices with their start and end apart: 8, of which 5 were waited for; matrix products, arithmetic and copies ran while one was open for 1% of the time, Pallas kernels for 13%

profile of v2, /device:TPU:2, one launch (start us, length us, event | category | flops | bytes accessed | tf_op | source)
XLA Modules:
  0.0 176.2 jit_solution(1951870381740197443)
XLA Ops:
  6.5 0.0 copy-start
  6.5 0.0 copy-start.7
  6.5 0.0 all-gather.5.cloned.1.call-start
  6.5 1.2 copy-done
  7.8 1.5 convolution_convert_fusion
  9.3 0.0 copy-done.7
  9.3 0.5 convolution_convert_fusion.1
  9.8 0.0 copy-start.6
  9.9 0.8 copy.13
  10.7 0.0 all-gather.5.cloned.1.call-update
  10.8 0.0 all-gather.3.cloned.1.call-start
  10.8 0.9 copy.12
  11.7 0.0 copy-start.3
  11.7 0.0 copy-start.4
  11.7 0.0 all-gather.3.cloned.1.call-update
  11.7 0.0 copy-done.6
  11.7 0.1 fusion.14
  11.8 0.4 convolution_convert_fusion.2
  12.3 53.7 %all-gather.5.cloned.1.call-done.kv_hbm = bf16[256,64,256]{2,1,0:T(8,128)(2,1)} async-done(((bf16[8,64,256]{2,1,0:T(8,128)(2,1)}), bf16[256,64,256]{2,1,0:T(8,128)(2,1)}) %all-gather.5.cloned.1.call-update) | async-done | bytes 8388624 | tf_op jit(solution)/shard_map/all_gather | solution.py:125
  65.9 0.0 copy-done.3
  65.9 0.0 copy-done.4
  65.9 0.0 copy-start.1
  65.9 2.2 %copy-done.1 = bf16[8,64,4096]{2,1,0:T(8,128)(2,1)S(1)} copy-done((bf16[8,64,4096]{2,1,0:T(8,128)(2,1)S(1)}, bf16[8,64,4096]{2,1,0:T(8,128)(2,1)}, u32[]{:S(2)}) %copy-start.1) | copy-done | bytes 4194328
  68.1 23.3 %shard_map.74 = bf16[8,64,128]{2,1,0:T(8,128)(2,1)S(1)} custom-call(s32[8,64]{1,0:T(8,128)S(1)} %copy-done.3, s32[8]{0:T(128)S(1)} %copy-done.4, f32[2]{0:T(128)S(1)} %get-tuple-element.15.gain_ref, bf16[8,64,128]{2,1,0:T(8,128)(2,1)S(1)} %bitcast.29, bf16[8,64,4096]{2,1,0:T(8,128)(2,1)S(1)} %copy-done.1, ...), custom_call_target="tpu_custom_call" | custom-call | tf_op jit(solution)/shard_map/pallas_call | solution.py:92
  91.5 29.1 %all-gather.3.cloned.1.call-done.kv_hbm = bf16[256,64,256]{2,1,0:T(8,128)(2,1)} async-done(((bf16[8,64,256]{2,1,0:T(8,128)(2,1)}), bf16[256,64,256]{2,1,0:T(8,128)(2,1)}) %all-gather.3.cloned.1.call-update) | async-done | bytes 8388624 | tf_op jit(solution)/shard_map/all_gather | solution.py:125
  120.6 0.0 copy-start.2
  120.6 2.2 %copy-done.2 = bf16[8,64,4096]{2,1,0:T(8,128)(2,1)S(1)} copy-done((bf16[8,64,4096]{2,1,0:T(8,128)(2,1)S(1)}, bf16[8,64,4096]{2,1,0:T(8,128)(2,1)}, u32[]{:S(2)}) %copy-start.2) | copy-done | bytes 4194328
  122.7 0.0 copy-start.5
  122.8 23.2 %shard_map.73 = bf16[8,64,128]{2,1,0:T(8,128)(2,1)S(1)} custom-call(s32[8,64]{1,0:T(8,128)S(1)} %copy-done.3, s32[8]{0:T(128)S(1)} %copy-done.4, f32[2]{0:T(128)S(1)} %get-tuple-element.14.gain_ref, bf16[8,64,128]{2,1,0:T(8,128)(2,1)S(1)} %bitcast.28, bf16[8,64,4096]{2,1,0:T(8,128)(2,1)S(1)} %copy-done.2, ...), custom_call_target="tpu_custom_call" | custom-call | tf_op jit(solution)/shard_map/pallas_call | solution.py:92
  146.0 1.6 collective-permute-start
  147.6 0.0 copy-done.5
  147.6 0.1 constant_dynamic-slice_fusion.1
  147.7 1.6 collective-permute-start.1
  149.3 1.7 collective-permute-start.5
  151.0 1.6 collective-permute-start.3
  152.6 1.4 collective-permute-start.4
  154.0 0.2 fusion.8
  154.2 4.6 %collective-permute-done.1 = bf16[256,256]{1,0:T(8,128)(2,1)S(1)} collective-permute-done((bf16[256,256]{1,0:T(8,128)(2,1)S(1)}, bf16[256,256]{1,0:T(8,128)(2,1)S(1)}, u32[]{:S(2)}, u32[]{:S(2)}) %collective-permute-start.1) | collective-permute-done | bytes 131104 | tf_op jit(solution)/shard_map/ppermute | solution.py:118
  158.8 2.4 %collective-permute-start.2 = (bf16[512,256]{1,0:T(8,128)(2,1)S(1)}, bf16[512,256]{1,0:T(8,128)(2,1)S(1)}, u32[]{:S(2)}, u32[]{:S(2)}) collective-permute-start(bf16[512,256]{1,0:T(8,128)(2,1)S(1)} %pad_maximum_fusion.2), channel_id=1, source_target_pairs={{0,2},{1,3},{2,0},{3,1},{4,6},{5,7},{6,4},{7,5},{8,10},{9,11},{10,... | collective-permute-start | bytes 786440 | tf_op jit(solution)/shard_map/ppermute | solution.py:140
  161.2 0.0 collective-permute-done
  161.2 0.2 convolution_add_fusion.1
  161.5 0.0 collective-permute-done.5
  161.5 2.6 %collective-permute-done.4 = bf16[512,256]{1,0:T(8,128)(2,1)S(1)} collective-permute-done((bf16[512,256]{1,0:T(8,128)(2,1)S(1)}, bf16[512,256]{1,0:T(8,128)(2,1)S(1)}, u32[]{:S(2)}, u32[]{:S(2)}) %collective-permute-start.4) | collective-permute-done | bytes 262176 | tf_op jit(solution)/shard_map/ppermute | solution.py:140
  164.1 0.2 fusion.15
  164.3 0.0 collective-permute-done.3
  164.3 4.1 %collective-permute-done.2 = bf16[512,256]{1,0:T(8,128)(2,1)S(1)} collective-permute-done((bf16[512,256]{1,0:T(8,128)(2,1)S(1)}, bf16[512,256]{1,0:T(8,128)(2,1)S(1)}, u32[]{:S(2)}, u32[]{:S(2)}) %collective-permute-start.2) | collective-permute-done | bytes 262176 | tf_op jit(solution)/shard_map/ppermute | solution.py:140
  168.4 0.9 fusion.1
  (5 shorter events, 0.1 us)
Async XLA Ops:
  6.5 1.2 copy-start
  6.5 2.8 %copy-start.7 = (bf16[3,1024,256]{2,1,0:T(8,128)(2,1)S(1)}, bf16[3,1024,256]{2,1,0:T(8,128)(2,1)}, u32[]{:S(2)}) copy-start(bf16[3,1024,256]{2,1,0:T(8,128)(2,1)} %param.8) | copy-start | bytes 4718596
  6.5 59.4 %all-gather.5.cloned.1.call-start = ((), (), s32[]{:S(2)}) async-start(), calls=%async_computation.1 | async-start | bytes 8650752 | tf_op jit(solution)/shard_map/all_gather | solution.py:125
  9.8 1.9 %copy-start.6 = (f32[4]{0:T(128)S(1)}, f32[4]{0:T(128)}, u32[]{:S(2)}) copy-start(f32[4]{0:T(128)} %param.10) | copy-start | bytes 52
  10.8 109.8 %all-gather.3.cloned.1.call-start = ((), (), s32[]{:S(2)}) async-start(), calls=%async_computation | async-start | bytes 8650752 | tf_op jit(solution)/shard_map/all_gather | solution.py:125
  11.7 54.2 %copy-start.3 = (s32[8,64]{1,0:T(8,128)S(1)}, s32[8,64]{1,0:T(8,128)}, u32[]{:S(2)}) copy-start(s32[8,64]{1,0:T(8,128)} %nbr_ref.3) | copy-start | bytes 6148
  11.7 54.2 %copy-start.4 = (s32[8]{0:T(128)S(1)}, s32[8]{0:T(128)}, u32[]{:S(2)}) copy-start(s32[8]{0:T(128)} %cnt_ref.3) | copy-start | bytes 100
  65.9 2.2 %copy-start.1 = (bf16[8,64,4096]{2,1,0:T(8,128)(2,1)S(1)}, bf16[8,64,4096]{2,1,0:T(8,128)(2,1)}, u32[]{:S(2)}) copy-start(bf16[8,64,4096]{2,1,0:T(8,128)(2,1)} %bias_ref.3) | copy-start | bytes 12582916
  120.6 2.2 %copy-start.2 = (bf16[8,64,4096]{2,1,0:T(8,128)(2,1)S(1)}, bf16[8,64,4096]{2,1,0:T(8,128)(2,1)}, u32[]{:S(2)}) copy-start(bf16[8,64,4096]{2,1,0:T(8,128)(2,1)} %bias_ref.3) | copy-start | bytes 12582916
  122.7 24.9 %copy-start.5 = (bf16[256,1024]{1,0:T(8,128)(2,1)S(1)}, bf16[256,1024]{1,0:T(8,128)(2,1)}, u32[]{:S(2)}) copy-start(bf16[256,1024]{1,0:T(8,128)(2,1)} %param.9) | copy-start | bytes 1572868
  146.0 15.2 %collective-permute-start = (bf16[512,256]{1,0:T(8,128)(2,1)S(1)}, bf16[512,256]{1,0:T(8,128)(2,1)S(1)}, u32[]{:S(2)}, u32[]{:S(2)}) collective-permute-start(bf16[512,256]{1,0:T(8,128)(2,1)S(1)} %pad_maximum_fusion.2), channel_id=1, source_target_pairs={{0,1},{1,2},{2,3},{3,0},{4,5},{5,6},{6,7},{7,4},{8,9},{9,10},{10,1... | collective-permute-start | bytes 786440 | tf_op jit(solution)/shard_map/ppermute | solution.py:140
  147.7 11.1 %collective-permute-start.1 = (bf16[256,256]{1,0:T(8,128)(2,1)S(1)}, bf16[256,256]{1,0:T(8,128)(2,1)S(1)}, u32[]{:S(2)}, u32[]{:S(2)}) collective-permute-start(bf16[256,256]{1,0:T(8,128)(2,1)S(1)} %get-tuple-element.6), channel_id=1, source_target_pairs={{0,1},{1,2},{2,3},{3,0},{4,5},{5,6},{6,7},{7,4},{8,9},{9,10},{10,1... | collective-permute-start | bytes 393224 | tf_op jit(solution)/shard_map/ppermute | solution.py:118
  149.3 12.2 %collective-permute-start.5 = (bf16[256,256]{1,0:T(8,128)(2,1)S(1)}, bf16[256,256]{1,0:T(8,128)(2,1)S(1)}, u32[]{:S(2)}, u32[]{:S(2)}) collective-permute-start(bf16[256,256]{1,0:T(8,128)(2,1)S(1)} %get-tuple-element.7), channel_id=1, source_target_pairs={{0,3},{1,0},{2,1},{3,2},{4,7},{5,4},{6,5},{7,6},{8,11},{9,8},{10,9... | collective-permute-start | bytes 393224 | tf_op jit(solution)/shard_map/ppermute | solution.py:118
  151.0 13.3 %collective-permute-start.3 = (bf16[256,256]{1,0:T(8,128)(2,1)S(1)}, bf16[256,256]{1,0:T(8,128)(2,1)S(1)}, u32[]{:S(2)}, u32[]{:S(2)}) collective-permute-start(bf16[256,256]{1,0:T(8,128)(2,1)S(1)} %get-tuple-element.5), channel_id=1, source_target_pairs={{0,2},{1,3},{2,0},{3,1},{4,6},{5,7},{6,4},{7,5},{8,10},{9,11},{10,... | collective-permute-start | bytes 393224 | tf_op jit(solution)/shard_map/ppermute | solution.py:118
  152.6 11.5 %collective-permute-start.4 = (bf16[512,256]{1,0:T(8,128)(2,1)S(1)}, bf16[512,256]{1,0:T(8,128)(2,1)S(1)}, u32[]{:S(2)}, u32[]{:S(2)}) collective-permute-start(bf16[512,256]{1,0:T(8,128)(2,1)S(1)} %pad_maximum_fusion.2), channel_id=1, source_target_pairs={{0,3},{1,0},{2,1},{3,2},{4,7},{5,4},{6,5},{7,6},{8,11},{9,8},{10,9... | collective-permute-start | bytes 786440 | tf_op jit(solution)/shard_map/ppermute | solution.py:140
  158.8 9.6 %collective-permute-start.2 = (bf16[512,256]{1,0:T(8,128)(2,1)S(1)}, bf16[512,256]{1,0:T(8,128)(2,1)S(1)}, u32[]{:S(2)}, u32[]{:S(2)}) collective-permute-start(bf16[512,256]{1,0:T(8,128)(2,1)S(1)} %pad_maximum_fusion.2), channel_id=1, source_target_pairs={{0,2},{1,3},{2,0},{3,1},{4,6},{5,7},{6,4},{7,5},{8,10},{9,11},{10,... | collective-permute-start | bytes 786440 | tf_op jit(solution)/shard_map/ppermute | solution.py:140
Sparse Core Ops, SparseCore 0:
  10.9 54.9 all-gather.4
  68.2 52.3 all-gather.2

commit v3 on v1

--- a/solution.py
+++ b/solution.py
@@ -99,27 +99,58 @@
     )(nbr, cnt, gain, q_blocks, bias, kv_table)
 
 
+def plan_requests(neighbours, per_owner, owners):
+    owner = neighbours // per_owner
+    local = neighbours % per_owner
+    flat = neighbours.reshape(-1)
+    ids = jnp.arange(owners * per_owner, dtype=jnp.int32)
+    present = jnp.any(flat[:, None] == ids[None, :], axis=0).reshape(owners, per_owner)
+    lidx = jnp.arange(per_owner, dtype=jnp.int32)[None, :]
+    first = jnp.min(jnp.where(present, lidx, per_owner), axis=1)
+    first = jnp.where(first == per_owner, 0, first)
+    second = jnp.max(jnp.where(present, lidx, -1), axis=1)
+    second = jnp.where(second < 0, first, second)
+    req = jnp.stack([first, second], axis=1).astype(jnp.int32)
+    pos = owner * 2 + (local != first[owner]).astype(jnp.int32)
+    return req, pos.astype(jnp.int32)
+
+
 def body(features, w_qkv, w_out, bias_gain, edge_bias, neighbours, counts):
     rows = features.shape[0]
     width_heads = w_qkv.shape[2]
     blocks_dev = rows // BLK
+    head_devs = lax.axis_size("head")
+    row_devs = lax.axis_size("row")
+    me = lax.axis_index("head")
+    req, pos = plan_requests(neighbours, blocks_dev, row_devs)
+    wanted = lax.all_to_all(req, "row", 0, 0, tiled=True)
     queries = jnp.dot(features, w_qkv[0], preferred_element_type=jnp.float32).astype(jnp.bfloat16)
     keys = jnp.dot(features, w_qkv[1], preferred_element_type=jnp.float32).astype(jnp.bfloat16)
     values = jnp.dot(features, w_qkv[2], preferred_element_type=jnp.float32).astype(jnp.bfloat16)
-    kv = jnp.concatenate([keys, values], axis=1)
-    gathered = lax.all_gather(kv, "row", axis=0, tiled=True)
-    kv_table = gathered.reshape(-1, BLK, 2 * width_heads)
-    w_cols = lax.all_to_all(w_out, "head", 1, 0, tiled=True)
+    kv = jnp.concatenate([keys, values], axis=1).reshape(blocks_dev, BLK, 2 * width_heads)
+    outgoing = jnp.take(kv, wanted.reshape(-1), axis=0)
+    kv_table = lax.all_to_all(outgoing, "row", 0, 0, tiled=True)
+    w_parts = []
+    for s in range(1, head_devs):
+        target = (me + s) % head_devs
+        piece = lax.dynamic_slice_in_dim(w_out, target * width_heads, width_heads, axis=1)
+        perm = [(i, (i + s) % head_devs) for i in range(head_devs)]
+        w_parts.append(lax.ppermute(piece, "head", perm))
+    w_own = lax.dynamic_slice_in_dim(w_out, me * width_heads, width_heads, axis=1)
     attended = attend(
-        neighbours,
+        pos,
         counts,
         bias_gain,
         queries.reshape(blocks_dev, BLK, width_heads),
         edge_bias,
         kv_table,
     ).reshape(rows, width_heads)
-    attended_all = lax.all_gather(attended, "head", axis=1, tiled=True)
-    return jnp.dot(attended_all, w_cols, preferred_element_type=jnp.float32).astype(jnp.bfloat16)
+    total = jnp.dot(attended, w_own, preferred_element_type=jnp.float32)
+    for s in range(1, head_devs):
+        perm = [(i, (i + s) % head_devs) for i in range(head_devs)]
+        att_s = lax.ppermute(attended, "head", perm)
+        total = total + jnp.dot(att_s, w_parts[s - 1], preferred_element_type=jnp.float32)
+    return total.astype(jnp.bfloat16)
 
 
 def solution(mesh):

time: 195 us -> 152 us (0.78)
  waiting for transfers between devices: 93.3 us -> 58.1 us
  starting transfers between devices: 0.04 us -> 26.4 us
  local copies, waits for them, and re-layouts: 26.2 us -> 11.1 us
  blocking collectives: 14 us -> 0 us
  between operations: 13.5 us -> 0.26 us
  other arithmetic: 0.85 us -> 5.68 us
    all_gather x2 -> x0, waiting for transfers between devices: 93.3 us -> none  [the longest x1 81.5 us: body(): gathered = lax.all_gather(kv, 'row', axis=0, tiled=True)]
    all_to_all x0 -> x2, waiting for transfers between devices: none -> 49.2 us  [the longest x1 46.4 us: body(): kv_table = lax.all_to_all(outgoing, 'row', 0, 0, tiled=True)]
    all_gather x1 -> x0, local copies, waits for them, and re-layouts: 22.3 us -> none  [body(): gathered = lax.all_gather(kv, 'row', axis=0, tiled=True)]
    all_to_all x1 -> x0, blocking collectives: 14 us -> none  [body(): w_cols = lax.all_to_all(w_out, 'head', 1, 0, tiled=True)]
    all_to_all x0 -> x2, starting transfers between devices: none -> 13.6 us  [the longest x1 7.62 us: body(): wanted = lax.all_to_all(req, 'row', 0, 0, tiled=True)]
    ppermute x0 -> x6, starting transfers between devices: none -> 12.8 us  [the longest x3 7.11 us: body(): att_s = lax.ppermute(attended, 'head', perm)]
    ppermute x0 -> x6, waiting for transfers between devices: none -> 8.95 us  [the longest x3 4.74 us: body(): att_s = lax.ppermute(attended, 'head', perm)]
    gather x0 -> x3, local copies, waits for them, and re-layouts: none -> 6.23 us  [the longest x2 3.42 us: plan_requests(): pos = owner * 2 + (local != first[owner]).astype(jnp.int32)]
  transfers between devices with their start and end apart: 2 -> 8, of which waited for: 2 -> 5; matrix products, arithmetic and copies ran while one was open for 0% -> 6% of each run, Pallas kernels for 0% -> 0%
where the time goes in v3:
time: 152 us; the launch traced here: 149 us
  waiting for transfers between devices  58.1 us (38%)
  Pallas kernels  41.7 us (27%)
  starting transfers between devices  26.4 us (17%)
  local copies, waits for them, and re-layouts  11.1 us (7%)
  matrix products  6.14 us (4%)
  other arithmetic  5.68 us (4%)
    all_to_all x1, waiting for transfers between devices, body(): kv_table = lax.all_to_all(outgoing, 'row', 0, 0, tiled=True)  46.4 us
    pallas_call x1, Pallas kernels, attend(): pl.pallas_call(_attend_kernel, grid_spec=grid_spec, out_shape=jax.ShapeDt...  41.7 us
    all_to_all x1, starting transfers between devices, body(): wanted = lax.all_to_all(req, 'row', 0, 0, tiled=True)  7.62 us
    ppermute x3, starting transfers between devices, body(): att_s = lax.ppermute(attended, 'head', perm)  7.11 us
    all_to_all x1, starting transfers between devices, body(): kv_table = lax.all_to_all(outgoing, 'row', 0, 0, tiled=True)  6.02 us
    ppermute x3, starting transfers between devices, body(): w_parts.append(lax.ppermute(piece, 'head', perm))  5.67 us
    ppermute x3, waiting for transfers between devices, body(): att_s = lax.ppermute(attended, 'head', perm)  4.74 us
    select_n x2, other arithmetic, body(): outgoing = jnp.take(kv, wanted.reshape(-1), axis=0)  4.62 us
  transfers between devices with their start and end apart: 8, of which 5 were waited for; matrix products, arithmetic and copies ran while one was open for 6% of the time, Pallas kernels for 0%

profile of v3, /device:TPU:2, one launch (start us, length us, event | category | flops | bytes accessed | tf_op | source)
XLA Modules:
  0.0 149.5 jit_solution(17583923476763662899)
XLA Ops:
  0.0 0.0 copy-start
  0.0 0.8 eq.42
  0.9 0.2 fusion.8
  1.0 0.1 reshape.80
  1.1 0.1 select_reduce_fusion
  1.3 0.7 copy.15
  2.0 7.6 %all-to-all-start = ((s32[32,1,2]{2,1,0:T(1,128)}), s32[32,1,2]{2,1,0:T(1,128)S(1)}, u32[]{:S(2)}, u32[]{:S(2)}) async-start(s32[32,1,2]{2,1,0:T(1,128)} %copy.15), calls=%async_computation | async-start | bytes 32768 | tf_op jit(solution)/shard_map/all_to_all | solution.py:126
  9.6 0.0 copy-done
  9.6 1.5 %convolution_convert_fusion = bf16[512,256]{0,1:T(8,128)(2,1)S(1)} fusion(bf16[512,1024]{1,0:T(8,128)(2,1)S(1)} %copy-done, bf16[3,1024,256]{2,1,0:T(8,128)(2,1)} %param.8), kind=kOutput, calls=%fused_computation.7 | convolution fusion | flops 268566528 | bytes 1835008 | tf_op jit(solution)/shard_map/dot_general | solution.py:129
  11.1 1.5 %convolution_convert_fusion.1 = bf16[512,256]{0,1:T(8,128)(2,1)S(1)} fusion(bf16[512,1024]{1,0:T(8,128)(2,1)S(1)} %copy-done, bf16[3,1024,256]{2,1,0:T(8,128)(2,1)} %param.8), kind=kOutput, calls=%fused_computation.8 | convolution fusion | flops 268566528 | bytes 1835008 | tf_op jit(solution)/shard_map/dot_general | solution.py:128
  12.7 0.2 copy.16
  12.9 2.8 %all-to-all-done = s32[32,1,2]{2,1,0:T(1,128)S(1)} async-done(((s32[32,1,2]{2,1,0:T(1,128)}), s32[32,1,2]{2,1,0:T(1,128)S(1)}, u32[]{:S(2)}, u32[]{:S(2)}) %all-to-all-start) | async-done | bytes 288 | tf_op jit(solution)/shard_map/all_to_all | solution.py:126
  15.7 0.1 reshape.84
  15.8 0.5 broadcast.96
  16.3 0.7 reduce.5
  17.0 0.1 reshape.82
  17.1 2.8 %gather_fusion.1 = bf16[64,64,512]{2,1,0:T(8,128)(2,1)} fusion(bf16[8,64,512]{2,1,0:T(8,128)(2,1)S(1)} %bitcast.38, s32[1024]{0:T(1024)S(1)} %pad_clamp_fusion), kind=kCustom, calls=%fused_computation.1 | custom fusion | bytes 8388864 | tf_op jit(solution)/shard_map/jit(_take)/gather | solution.py:131
  19.9 4.6 %broadcast_select_fusion = bf16[64,64,512]{2,1,0:T(8,128)(2,1)} fusion(bf16[64,64,512]{2,1,0:T(8,128)(2,1)} %gather_fusion.1, pred[64]{0:T(512)(128)(4,1)S(1)} %compare_and_fusion), kind=kLoop, calls=%fused_computation.2 | loop fusion | flops 2097152 | bytes 8388672 | tf_op jit(solution)/shard_map/jit(_take)/select_n | solution.py:131
  24.5 0.0 copy-start.5
  24.5 6.0 %all-to-all-start.1 = ((bf16[64,64,512]{2,1,0:T(8,128)(2,1)}), bf16[64,64,512]{2,1,0:T(8,128)(2,1)}, u32[]{:S(2)}, u32[]{:S(2)}) async-start(bf16[64,64,512]{2,1,0:T(8,128)(2,1)} %broadcast_select_fusion), calls=%async_computation.1 | async-start | bytes 8388608 | tf_op jit(solution)/shard_map/all_to_all | solution.py:132
  30.6 0.0 copy-start.2
  30.6 0.0 copy-start.3
  30.6 0.0 copy-done.5
  30.7 0.1 reshape.88
  30.8 3.3 %gather_fusion = s32[512]{0:T(512)S(1)} fusion(s32[32]{0:T(128)S(1)} %compare_select_fusion.5, s32[1024]{0:T(1024)S(1)} %pad_clamp_fusion.1), kind=kCustom, calls=%fused_computation | custom fusion | bytes 6144 | tf_op jit(solution)/shard_map/gather | solution.py:114
  34.1 0.1 reshape.87
  34.2 1.5 convolution_convert_fusion.2
  35.7 46.4 %all-to-all-done.1.kv_hbm = bf16[64,64,512]{2,1,0:T(8,128)(2,1)} async-done(((bf16[64,64,512]{2,1,0:T(8,128)(2,1)}), bf16[64,64,512]{2,1,0:T(8,128)(2,1)}, u32[]{:S(2)}, u32[]{:S(2)}) %all-to-all-start.1) | async-done | bytes 4194336 | tf_op jit(solution)/shard_map/all_to_all | solution.py:132
  82.1 0.0 copy-done.2
  82.1 0.0 copy-done.3
  82.1 0.0 copy-start.1
  82.1 2.2 %copy-done.1 = bf16[8,64,4096]{2,1,0:T(8,128)(2,1)S(1)} copy-done((bf16[8,64,4096]{2,1,0:T(8,128)(2,1)S(1)}, bf16[8,64,4096]{2,1,0:T(8,128)(2,1)}, u32[]{:S(2)}) %copy-start.1) | copy-done | bytes 4194328
  84.3 0.0 copy-start.4
  84.3 41.7 %shard_map.73 = bf16[8,64,256]{2,1,0:T(8,128)(2,1)S(1)} custom-call(s32[8,64]{1,0:T(8,128)S(1)} %convert_add_fusion.nbr_ref, s32[8]{0:T(128)S(1)} %copy-done.2, f32[4]{0:T(128)S(1)} %copy-done.3, bf16[8,64,256]{2,1,0:T(8,128)(2,1)S(1)} %bitcast.37, bf16[8,64,4096]{2,1,0:T(8,128)(2,1)S(1)} %copy-done.1, bf16[64,64,512]{2,1,0:T(8,128)(2,1)} %all-to-all-done.1.kv_hbm), custom_call_target="tpu_custom_call" | custom-call | tf_op jit(solution)/shard_map/pallas_call | solution.py:92
  126.0 2.0 %collective-permute-start = (bf16[512,256]{1,0:T(8,128)(2,1)S(1)}, bf16[512,256]{1,0:T(8,128)(2,1)S(1)}, u32[]{:S(2)}, u32[]{:S(2)}) collective-permute-start(bf16[512,256]{1,0:T(8,128)(2,1)S(1)} %bitcast.33), channel_id=1, source_target_pairs={{0,1},{1,2},{2,3},{3,0},{4,5},{5,6},{6,7},{7,4},{8,9},{9,10},{10,1... | collective-permute-start | bytes 786440 | tf_op jit(solution)/shard_map/ppermute | solution.py:151
  128.0 0.0 copy-done.4
  128.0 0.1 constant_dynamic-slice_fusion.1
  128.1 2.2 %collective-permute-start.5 = (bf16[256,256]{1,0:T(8,128)(2,1)S(1)}, bf16[256,256]{1,0:T(8,128)(2,1)S(1)}, u32[]{:S(2)}, u32[]{:S(2)}) collective-permute-start(bf16[256,256]{1,0:T(8,128)(2,1)S(1)} %get-tuple-element.9), channel_id=1, source_target_pairs={{0,3},{1,0},{2,1},{3,2},{4,7},{5,4},{6,5},{7,6},{8,11},{9,8},{10,9... | collective-permute-start | bytes 393224 | tf_op jit(solution)/shard_map/ppermute | solution.py:138
  130.3 0.0 collective-permute-start.1
  130.3 3.5 %collective-permute-start.3 = (bf16[256,256]{1,0:T(8,128)(2,1)S(1)}, bf16[256,256]{1,0:T(8,128)(2,1)S(1)}, u32[]{:S(2)}, u32[]{:S(2)}) collective-permute-start(bf16[256,256]{1,0:T(8,128)(2,1)S(1)} %get-tuple-element.7), channel_id=1, source_target_pairs={{0,2},{1,3},{2,0},{3,1},{4,6},{5,7},{6,4},{7,5},{8,10},{9,11},{10,... | collective-permute-start | bytes 393224 | tf_op jit(solution)/shard_map/ppermute | solution.py:138
  133.8 1.0 collective-permute-start.4
  134.8 0.2 fusion.9
  135.0 4.2 %collective-permute-done.1 = bf16[256,256]{1,0:T(8,128)(2,1)S(1)} collective-permute-done((bf16[256,256]{1,0:T(8,128)(2,1)S(1)}, bf16[256,256]{1,0:T(8,128)(2,1)S(1)}, u32[]{:S(2)}, u32[]{:S(2)}) %collective-permute-start.1) | collective-permute-done | bytes 131104 | tf_op jit(solution)/shard_map/ppermute | solution.py:138
  139.2 4.1 %collective-permute-start.2 = (bf16[512,256]{1,0:T(8,128)(2,1)S(1)}, bf16[512,256]{1,0:T(8,128)(2,1)S(1)}, u32[]{:S(2)}, u32[]{:S(2)}) collective-permute-start(bf16[512,256]{1,0:T(8,128)(2,1)S(1)} %bitcast.36), channel_id=1, source_target_pairs={{0,2},{1,3},{2,0},{3,1},{4,6},{5,7},{6,4},{7,5},{8,10},{9,11},{10,... | collective-permute-start | bytes 786440 | tf_op jit(solution)/shard_map/ppermute | solution.py:151
  143.3 0.0 collective-permute-done
  143.3 0.2 convolution_add_fusion.1
  143.5 0.0 collective-permute-done.5
  143.6 0.4 collective-permute-done.4
  143.9 0.2 fusion.16
  144.2 0.0 collective-permute-done.3
  144.2 4.4 %collective-permute-done.2 = bf16[512,256]{1,0:T(8,128)(2,1)S(1)} collective-permute-done((bf16[512,256]{1,0:T(8,128)(2,1)S(1)}, bf16[512,256]{1,0:T(8,128)(2,1)S(1)}, u32[]{:S(2)}, u32[]{:S(2)}) %collective-permute-start.2) | collective-permute-done | bytes 262176 | tf_op jit(solution)/shard_map/ppermute | solution.py:151
  148.5 0.9 fusion.1
  (10 shorter events, 0.1 us)
Async XLA Ops:
  0.0 9.6 %copy-start = (bf16[512,1024]{1,0:T(8,128)(2,1)S(1)}, bf16[512,1024]{1,0:T(8,128)(2,1)}, u32[]{:S(2)}) copy-start(bf16[512,1024]{1,0:T(8,128)(2,1)} %param.7) | copy-start | bytes 3145732
  2.0 13.7 %all-to-all-start = ((s32[32,1,2]{2,1,0:T(1,128)}), s32[32,1,2]{2,1,0:T(1,128)S(1)}, u32[]{:S(2)}, u32[]{:S(2)}) async-start(s32[32,1,2]{2,1,0:T(1,128)} %copy.15), calls=%async_computation | async-start | bytes 32768 | tf_op jit(solution)/shard_map/all_to_all | solution.py:126
  24.5 6.1 %copy-start.5 = (s32[8,64]{1,0:T(8,128)S(1)}, s32[8,64]{1,0:T(8,128)}, u32[]{:S(2)}) copy-start(s32[8,64]{1,0:T(8,128)} %param.12) | copy-start | bytes 6148
  24.5 57.6 %all-to-all-start.1 = ((bf16[64,64,512]{2,1,0:T(8,128)(2,1)}), bf16[64,64,512]{2,1,0:T(8,128)(2,1)}, u32[]{:S(2)}, u32[]{:S(2)}) async-start(bf16[64,64,512]{2,1,0:T(8,128)(2,1)} %broadcast_select_fusion), calls=%async_computation.1 | async-start | bytes 8388608 | tf_op jit(solution)/shard_map/all_to_all | solution.py:132
  30.6 51.5 %copy-start.2 = (s32[8]{0:T(128)S(1)}, s32[8]{0:T(128)}, u32[]{:S(2)}) copy-start(s32[8]{0:T(128)} %cnt_ref.1) | copy-start | bytes 100
  30.6 51.5 %copy-start.3 = (f32[4]{0:T(128)S(1)}, f32[4]{0:T(128)}, u32[]{:S(2)}) copy-start(f32[4]{0:T(128)} %gain_ref.1) | copy-start | bytes 52
  82.1 2.2 %copy-start.1 = (bf16[8,64,4096]{2,1,0:T(8,128)(2,1)S(1)}, bf16[8,64,4096]{2,1,0:T(8,128)(2,1)}, u32[]{:S(2)}) copy-start(bf16[8,64,4096]{2,1,0:T(8,128)(2,1)} %bias_ref.1) | copy-start | bytes 12582916
  84.3 43.7 %copy-start.4 = (bf16[256,1024]{1,0:T(8,128)(2,1)S(1)}, bf16[256,1024]{1,0:T(8,128)(2,1)}, u32[]{:S(2)}) copy-start(bf16[256,1024]{1,0:T(8,128)(2,1)} %param.9) | copy-start | bytes 1572868
  126.0 17.3 %collective-permute-start = (bf16[512,256]{1,0:T(8,128)(2,1)S(1)}, bf16[512,256]{1,0:T(8,128)(2,1)S(1)}, u32[]{:S(2)}, u32[]{:S(2)}) collective-permute-start(bf16[512,256]{1,0:T(8,128)(2,1)S(1)} %bitcast.33), channel_id=1, source_target_pairs={{0,1},{1,2},{2,3},{3,0},{4,5},{5,6},{6,7},{7,4},{8,9},{9,10},{10,1... | collective-permute-start | bytes 786440 | tf_op jit(solution)/shard_map/ppermute | solution.py:151
  128.1 15.5 %collective-permute-start.5 = (bf16[256,256]{1,0:T(8,128)(2,1)S(1)}, bf16[256,256]{1,0:T(8,128)(2,1)S(1)}, u32[]{:S(2)}, u32[]{:S(2)}) collective-permute-start(bf16[256,256]{1,0:T(8,128)(2,1)S(1)} %get-tuple-element.9), channel_id=1, source_target_pairs={{0,3},{1,0},{2,1},{3,2},{4,7},{5,4},{6,5},{7,6},{8,11},{9,8},{10,9... | collective-permute-start | bytes 393224 | tf_op jit(solution)/shard_map/ppermute | solution.py:138
  130.3 8.9 %collective-permute-start.1 = (bf16[256,256]{1,0:T(8,128)(2,1)S(1)}, bf16[256,256]{1,0:T(8,128)(2,1)S(1)}, u32[]{:S(2)}, u32[]{:S(2)}) collective-permute-start(bf16[256,256]{1,0:T(8,128)(2,1)S(1)} %get-tuple-element.8), channel_id=1, source_target_pairs={{0,1},{1,2},{2,3},{3,0},{4,5},{5,6},{6,7},{7,4},{8,9},{9,10},{10,1... | collective-permute-start | bytes 393224 | tf_op jit(solution)/shard_map/ppermute | solution.py:138
  130.3 13.9 %collective-permute-start.3 = (bf16[256,256]{1,0:T(8,128)(2,1)S(1)}, bf16[256,256]{1,0:T(8,128)(2,1)S(1)}, u32[]{:S(2)}, u32[]{:S(2)}) collective-permute-start(bf16[256,256]{1,0:T(8,128)(2,1)S(1)} %get-tuple-element.7), channel_id=1, source_target_pairs={{0,2},{1,3},{2,0},{3,1},{4,6},{5,7},{6,4},{7,5},{8,10},{9,11},{10,... | collective-permute-start | bytes 393224 | tf_op jit(solution)/shard_map/ppermute | solution.py:138
  133.8 10.2 %collective-permute-start.4 = (bf16[512,256]{1,0:T(8,128)(2,1)S(1)}, bf16[512,256]{1,0:T(8,128)(2,1)S(1)}, u32[]{:S(2)}, u32[]{:S(2)}) collective-permute-start(bf16[512,256]{1,0:T(8,128)(2,1)S(1)} %bitcast.34), channel_id=1, source_target_pairs={{0,3},{1,0},{2,1},{3,2},{4,7},{5,4},{6,5},{7,6},{8,11},{9,8},{10,9... | collective-permute-start | bytes 786440 | tf_op jit(solution)/shard_map/ppermute | solution.py:151
  139.2 9.3 %collective-permute-start.2 = (bf16[512,256]{1,0:T(8,128)(2,1)S(1)}, bf16[512,256]{1,0:T(8,128)(2,1)S(1)}, u32[]{:S(2)}, u32[]{:S(2)}) collective-permute-start(bf16[512,256]{1,0:T(8,128)(2,1)S(1)} %bitcast.36), channel_id=1, source_target_pairs={{0,2},{1,3},{2,0},{3,1},{4,6},{5,7},{6,4},{7,5},{8,10},{9,11},{10,... | collective-permute-start | bytes 786440 | tf_op jit(solution)/shard_map/ppermute | solution.py:151

commit v4 on v3

--- a/solution.py
+++ b/solution.py
@@ -122,14 +122,13 @@
     head_devs = lax.axis_size("head")
     row_devs = lax.axis_size("row")
     me = lax.axis_index("head")
+    chunk = 128
+    chunks = width_heads // chunk
     req, pos = plan_requests(neighbours, blocks_dev, row_devs)
-    wanted = lax.all_to_all(req, "row", 0, 0, tiled=True)
+    wanted = lax.all_to_all(req, "row", 0, 0, tiled=True).reshape(-1)
     queries = jnp.dot(features, w_qkv[0], preferred_element_type=jnp.float32).astype(jnp.bfloat16)
     keys = jnp.dot(features, w_qkv[1], preferred_element_type=jnp.float32).astype(jnp.bfloat16)
     values = jnp.dot(features, w_qkv[2], preferred_element_type=jnp.float32).astype(jnp.bfloat16)
-    kv = jnp.concatenate([keys, values], axis=1).reshape(blocks_dev, BLK, 2 * width_heads)
-    outgoing = jnp.take(kv, wanted.reshape(-1), axis=0)
-    kv_table = lax.all_to_all(outgoing, "row", 0, 0, tiled=True)
     w_parts = []
     for s in range(1, head_devs):
         target = (me + s) % head_devs
@@ -137,19 +136,34 @@
         perm = [(i, (i + s) % head_devs) for i in range(head_devs)]
         w_parts.append(lax.ppermute(piece, "head", perm))
     w_own = lax.dynamic_slice_in_dim(w_out, me * width_heads, width_heads, axis=1)
-    attended = attend(
-        pos,
-        counts,
-        bias_gain,
-        queries.reshape(blocks_dev, BLK, width_heads),
-        edge_bias,
-        kv_table,
-    ).reshape(rows, width_heads)
-    total = jnp.dot(attended, w_own, preferred_element_type=jnp.float32)
-    for s in range(1, head_devs):
-        perm = [(i, (i + s) % head_devs) for i in range(head_devs)]
-        att_s = lax.ppermute(attended, "head", perm)
-        total = total + jnp.dot(att_s, w_parts[s - 1], preferred_element_type=jnp.float32)
+    outgoing = []
+    for c in range(chunks):
+        cols = slice(c * chunk, (c + 1) * chunk)
+        kv = jnp.concatenate([keys[:, cols], values[:, cols]], axis=1)
+        kv = kv.reshape(blocks_dev, BLK, 2 * chunk)
+        outgoing.append(jnp.take(kv, wanted, axis=0, mode="clip"))
+    total = None
+    table = None
+    for c in range(chunks):
+        cols = slice(c * chunk, (c + 1) * chunk)
+        send = outgoing[c]
+        if table is not None:
+            table, send = lax.optimization_barrier((table, send))
+        table = lax.all_to_all(send, "row", 0, 0, tiled=True)
+        att = attend(
+            pos,
+            counts,
+            bias_gain[c * 2:(c + 1) * 2],
+            queries[:, cols].reshape(blocks_dev, BLK, chunk),
+            edge_bias,
+            table,
+        ).reshape(rows, chunk)
+        part = jnp.dot(att, w_own[cols], preferred_element_type=jnp.float32)
+        total = part if total is None else total + part
+        for s in range(1, head_devs):
+            perm = [(i, (i + s) % head_devs) for i in range(head_devs)]
+            att_s = lax.ppermute(att, "head", perm)
+            total = total + jnp.dot(att_s, w_parts[s - 1][cols], preferred_element_type=jnp.float32)
     return total.astype(jnp.bfloat16)
 
 

time: 152 us -> 155 us (1.020); the launches traced: 149 us -> 154 us
  waiting for transfers between devices: 58.1 us -> 19.7 us
  Pallas kernels: 41.7 us -> 69.3 us
  starting transfers between devices: 26.4 us -> 38.2 us
  matrix products: 6.14 us -> 12 us
  other arithmetic: 5.68 us -> 1.73 us
  local copies, waits for them, and re-layouts: 11.1 us -> 13 us
    all_to_all x2 -> x3, waiting for transfers between devices: 49.2 us -> 19.2 us  [the longest x2 17.1 us: body(): table = lax.all_to_all(send, 'row', 0, 0, tiled=True)]
    pallas_call x1 -> x2, Pallas kernels: 41.7 us -> 69.3 us  [attend(): pl.pallas_call(_attend_kernel, grid_spec=grid_spec, out_shape=jax.ShapeDt...]
    all_to_all x2 -> x3, starting transfers between devices: 13.6 us -> 19.6 us  [the longest x2 11.9 us: body(): table = lax.all_to_all(send, 'row', 0, 0, tiled=True)]
    dot_general x4 -> x8, matrix products: 1.6 us -> 7.42 us  [the longest x6 5.34 us: body(): jnp.dot(att_s, w_parts[s - 1][cols], preferred_element_type=jnp.float32)]
    ppermute x3 -> x6, starting transfers between devices: 7.11 us -> 12.7 us  [body(): att_s = lax.ppermute(att, 'head', perm)]
    select_n x2 -> x0, other arithmetic: 4.62 us -> none  [body(): outgoing = jnp.take(kv, wanted.reshape(-1), axis=0)]
    ppermute x3 -> x6, waiting for transfers between devices: 4.74 us -> 0.47 us  [body(): att_s = lax.ppermute(att, 'head', perm)]
    ppermute x3, waiting for transfers between devices: 4.21 us -> 0.01 us  [body(): w_parts.append(lax.ppermute(piece, 'head', perm))]
  transfers between devices with their start and end apart: 8 -> 12, of which waited for: 5 -> 4; matrix products, arithmetic and copies ran while one was open for 6% -> 13% of each run, Pallas kernels for 0% -> 45%
where the time goes in v4:
time: 155 us; the launch traced here: 154 us
  Pallas kernels  69.3 us (45%)
  starting transfers between devices  38.2 us (25%)
  waiting for transfers between devices  19.7 us (13%)
  local copies, waits for them, and re-layouts  13 us (8%)
  matrix products  12 us (8%)
  other arithmetic  1.73 us (1%)
    pallas_call x2, Pallas kernels, attend(): pl.pallas_call(_attend_kernel, grid_spec=grid_spec, out_shape=jax.ShapeDt...  69.3 us
    all_to_all x2, waiting for transfers between devices, body(): table = lax.all_to_all(send, 'row', 0, 0, tiled=True)  17.1 us
    ppermute x6, starting transfers between devices, body(): att_s = lax.ppermute(att, 'head', perm)  12.7 us
    all_to_all x2, starting transfers between devices, body(): table = lax.all_to_all(send, 'row', 0, 0, tiled=True)  11.9 us
    all_to_all x1, starting transfers between devices, body(): wanted = lax.all_to_all(req, 'row', 0, 0, tiled=True).reshape(-1)  7.62 us
    ppermute x3, starting transfers between devices, body(): w_parts.append(lax.ppermute(piece, 'head', perm))  5.9 us
    dot_general x6, matrix products, body(): jnp.dot(att_s, w_parts[s - 1][cols], preferred_element_type=jnp.float32)  5.34 us
    gather x2, local copies, waits for them, and re-layouts, body(): outgoing.append(jnp.take(kv, wanted, axis=0, mode='clip'))  4.01 us
  transfers between devices with their start and end apart: 12, of which 4 were waited for; matrix products, arithmetic and copies ran while one was open for 13% of the time, Pallas kernels for 45%

profile of v4, /device:TPU:2, one launch (start us, length us, event | category | flops | bytes accessed | tf_op | source)
XLA Modules:
  0.0 154.2 jit_solution(13704185387541878864)
XLA Ops:
  0.0 0.0 copy-start
  0.0 0.8 eq.42
  0.9 0.2 fusion.11
  1.0 0.1 reshape.51
  1.1 0.1 select_reduce_fusion
  1.3 0.7 copy.16
  1.9 7.6 %all-to-all-start = ((s32[32,1,2]{2,1,0:T(1,128)}), s32[32,1,2]{2,1,0:T(1,128)S(1)}, u32[]{:S(2)}, u32[]{:S(2)}) async-start(s32[32,1,2]{2,1,0:T(1,128)} %copy.16), calls=%async_computation | async-start | bytes 32768 | tf_op jit(solution)/shard_map/all_to_all | solution.py:128
  9.6 0.0 copy-done
  9.6 1.5 convolution_convert_fusion.1
  11.1 1.5 convolution_convert_fusion
  12.7 0.7 pad_maximum_fusion
  13.4 0.1 copy.15
  13.6 2.2 %all-to-all-done = s32[32,1,2]{2,1,0:T(1,128)S(1)} async-done(((s32[32,1,2]{2,1,0:T(1,128)}), s32[32,1,2]{2,1,0:T(1,128)S(1)}, u32[]{:S(2)}, u32[]{:S(2)}) %all-to-all-start) | async-done | bytes 288 | tf_op jit(solution)/shard_map/all_to_all | solution.py:128
  15.7 0.6 broadcast.72
  16.3 0.7 reduce.3
  17.0 0.1 reshape.68
  17.1 2.0 %gather_fusion.1 = bf16[64,64,256]{2,1,0:T(8,128)(2,1)} fusion(bf16[8,64,256]{2,1,0:T(8,128)(2,1)S(1)} %bitcast.44, s32[1024]{0:T(1024)S(1)} %pad_clamp_fusion), kind=kCustom, calls=%fused_computation.1 | custom fusion | bytes 4194560 | tf_op jit(solution)/shard_map/jit(_take)/gather | solution.py:144
  19.1 5.2 %all-to-all-start.1 = ((bf16[64,64,256]{2,1,0:T(8,128)(2,1)}), bf16[64,64,256]{2,1,0:T(8,128)(2,1)S(1)}, u32[]{:S(2)}, u32[]{:S(2)}) async-start(bf16[64,64,256]{2,1,0:T(8,128)(2,1)} %gather_fusion.1), calls=%async_computation.1 | async-start | bytes 4194304 | tf_op jit(solution)/shard_map/all_to_all | solution.py:152
  24.4 1.8 %constant_dynamic-slice_fusion.2 = (bf16[256,256]{1,0:T(8,128)(2,1)}, bf16[256,256]{1,0:T(8,128)(2,1)}, bf16[256,256]{1,0:T(8,128)(2,1)}) fusion(bf16[256,1024]{1,0:T(8,128)(2,1)} %param.9, s32[]{:T(128)S(6)} %select_n.86, s32[]{:T(128)S(6)} %select_n.90, s32[]{:T(128)S(6)} %select_n.88), kind=kLoop, calls=%fused_computation.59 | loop fusion | bytes 786444 | tf_op jit(solution)/shard_map/dynamic_slice | solution.py:135
  26.2 1.9 %collective-permute-start.1 = (bf16[256,256]{1,0:T(8,128)(2,1)}, bf16[256,256]{1,0:T(8,128)(2,1)S(1)}, u32[]{:S(2)}, u32[]{:S(2)}) collective-permute-start(bf16[256,256]{1,0:T(8,128)(2,1)} %get-tuple-element.9), channel_id=1, source_target_pairs={{0,1},{1,2},{2,3},{3,0},{4,5},{5,6},{6,7},{7,4},{8,9},{9,10},{10,1... | collective-permute-start | bytes 393224 | tf_op jit(solution)/shard_map/ppermute | solution.py:137
  28.1 2.1 %collective-permute-start.5 = (bf16[256,256]{1,0:T(8,128)(2,1)}, bf16[256,256]{1,0:T(8,128)(2,1)}, u32[]{:S(2)}, u32[]{:S(2)}) collective-permute-start(bf16[256,256]{1,0:T(8,128)(2,1)} %get-tuple-element.10), channel_id=1, source_target_pairs={{0,3},{1,0},{2,1},{3,2},{4,7},{5,4},{6,5},{7,6},{8,11},{9,8},{10,9... | collective-permute-start | bytes 393224 | tf_op jit(solution)/shard_map/ppermute | solution.py:137
  30.2 1.9 %collective-permute-start.3 = (bf16[256,256]{1,0:T(8,128)(2,1)}, bf16[256,256]{1,0:T(8,128)(2,1)}, u32[]{:S(2)}, u32[]{:S(2)}) collective-permute-start(bf16[256,256]{1,0:T(8,128)(2,1)} %get-tuple-element.11), channel_id=1, source_target_pairs={{0,2},{1,3},{2,0},{3,1},{4,6},{5,7},{6,4},{7,5},{8,10},{9,11},{10,... | collective-permute-start | bytes 393224 | tf_op jit(solution)/shard_map/ppermute | solution.py:137
  32.1 1.1 copy.17
  33.2 2.0 %gather_fusion.2 = bf16[64,64,256]{2,1,0:T(8,128)(2,1)} fusion(bf16[8,64,256]{2,1,0:T(8,128)(2,1)S(1)} %bitcast.45, s32[1024]{0:T(1024)S(1)} %pad_clamp_fusion), kind=kCustom, calls=%fused_computation.2 | custom fusion | bytes 4194560 | tf_op jit(solution)/shard_map/jit(_take)/gather | solution.py:144
  35.2 0.0 copy-start.2
  35.2 17.1 %all-to-all-done.1.kv_hbm = bf16[64,64,256]{2,1,0:T(8,128)(2,1)S(1)} async-done(((bf16[64,64,256]{2,1,0:T(8,128)(2,1)}), bf16[64,64,256]{2,1,0:T(8,128)(2,1)S(1)}, u32[]{:S(2)}, u32[]{:S(2)}) %all-to-all-start.1) | async-done | bytes 2097184 | tf_op jit(solution)/shard_map/all_to_all | solution.py:152
  52.3 6.7 %all-to-all-start.2 = ((bf16[64,64,256]{2,1,0:T(8,128)(2,1)}), bf16[64,64,256]{2,1,0:T(8,128)(2,1)}, u32[]{:S(2)}, u32[]{:S(2)}) async-start(bf16[64,64,256]{2,1,0:T(8,128)(2,1)} %gather_fusion.2), calls=%async_computation.2 | async-start | bytes 4194304 | tf_op jit(solution)/shard_map/all_to_all | solution.py:152
  59.0 0.0 copy-done.2
  59.0 0.1 reshape.60
  59.1 0.0 copy-start.3
  59.1 3.3 %gather_fusion = s32[512]{0:T(512)S(1)} fusion(s32[32]{0:T(128)S(1)} %compare_select_fusion.3, s32[1024]{0:T(1024)S(1)} %pad_clamp_fusion.1), kind=kCustom, calls=%fused_computation | custom fusion | bytes 6144 | tf_op jit(solution)/shard_map/gather | solution.py:114
  62.5 0.0 copy-start.1
  62.5 0.1 reshape.59
  62.6 0.0 copy-done.3
  62.6 0.1 fusion.32
  62.7 1.5 convolution_convert_fusion.2
  64.2 0.0 copy-done.1
  64.2 45.5 %shard_map.73 = bf16[8,64,128]{2,1,0:T(8,128)(2,1)S(1)} custom-call(s32[8,64]{1,0:T(8,128)S(1)} %convert_add_fusion.nbr_ref, s32[8]{0:T(128)S(1)} %copy-done.1, f32[2]{0:T(128)S(1)} %get-tuple-element.18.gain_ref, bf16[8,64,128]{2,1,0:T(8,128)(2,1)S(1)} %bitcast.43, bf16[8,64,4096]{2,1,0:T(8,128)(2,1)} %bias_ref.3, ...), custom_call_target="tpu_custom_call" | custom-call | tf_op jit(solution)/shard_map/pallas_call | solution.py:92
  109.7 2.0 %collective-permute-start = (bf16[512,128]{1,0:T(8,128)(2,1)S(1)}, bf16[512,128]{1,0:T(8,128)(2,1)S(1)}, u32[]{:S(2)}, u32[]{:S(2)}) collective-permute-start(bf16[512,128]{1,0:T(8,128)(2,1)S(1)} %bitcast.34), channel_id=1, source_target_pairs={{0,1},{1,2},{2,3},{3,0},{4,5},{5,6},{6,7},{7,4},{8,9},{9,10},{10,1... | collective-permute-start | bytes 393224 | tf_op jit(solution)/shard_map/ppermute | solution.py:165
  111.7 2.2 %collective-permute-start.4 = (bf16[512,128]{1,0:T(8,128)(2,1)S(1)}, bf16[512,128]{1,0:T(8,128)(2,1)S(1)}, u32[]{:S(2)}, u32[]{:S(2)}) collective-permute-start(bf16[512,128]{1,0:T(8,128)(2,1)S(1)} %bitcast.35), channel_id=1, source_target_pairs={{0,3},{1,0},{2,1},{3,2},{4,7},{5,4},{6,5},{7,6},{8,11},{9,8},{10,9... | collective-permute-start | bytes 393224 | tf_op jit(solution)/shard_map/ppermute | solution.py:165
  113.9 1.0 fusion.23
  115.0 0.0 collective-permute-done.5
  115.0 1.9 %collective-permute-start.2 = (bf16[512,128]{1,0:T(8,128)(2,1)S(1)}, bf16[512,128]{1,0:T(8,128)(2,1)S(1)}, u32[]{:S(2)}, u32[]{:S(2)}) collective-permute-start(bf16[512,128]{1,0:T(8,128)(2,1)S(1)} %bitcast.37), channel_id=1, source_target_pairs={{0,2},{1,3},{2,0},{3,1},{4,6},{5,7},{6,4},{7,5},{8,10},{9,11},{10,... | collective-permute-start | bytes 393224 | tf_op jit(solution)/shard_map/ppermute | solution.py:165
  116.8 0.3 collective-permute-done.4
  117.1 1.0 fusion.19
  118.2 0.0 collective-permute-done.1
  118.2 0.0 collective-permute-done
  118.2 0.2 convolution_add_fusion.2
  118.4 0.0 all-to-all-done.2.kv_hbm
  118.4 23.7 %shard_map.74 = bf16[8,64,128]{2,1,0:T(8,128)(2,1)S(1)} custom-call(s32[8,64]{1,0:T(8,128)S(1)} %convert_add_fusion.nbr_ref, s32[8]{0:T(128)S(1)} %copy-done.1, f32[2]{0:T(128)S(1)} %get-tuple-element.19.gain_ref, bf16[8,64,128]{2,1,0:T(8,128)(2,1)S(1)} %bitcast.38, bf16[8,64,4096]{2,1,0:T(8,128)(2,1)} %bias_ref.3, bf16[64,64,256]{2,1,0:T(8,128)(2,1)} %all-to-all-done.2.kv_hbm), custom_call_target="tpu_custom_call" | custom-call | tf_op jit(solution)/shard_map/pallas_call | solution.py:92
  142.2 4.6 %collective-permute-start.7 = (bf16[512,128]{1,0:T(8,128)(2,1)S(1)}, bf16[512,128]{1,0:T(8,128)(2,1)S(1)}, u32[]{:S(2)}, u32[]{:S(2)}) collective-permute-start(bf16[512,128]{1,0:T(8,128)(2,1)S(1)} %bitcast.39), channel_id=1, source_target_pairs={{0,2},{1,3},{2,0},{3,1},{4,6},{5,7},{6,4},{7,5},{8,10},{9,11},{10,... | collective-permute-start | bytes 393224 | tf_op jit(solution)/shard_map/ppermute | solution.py:165
  146.8 0.0 collective-permute-start.8
  146.8 2.0 %collective-permute-start.6 = (bf16[512,128]{1,0:T(8,128)(2,1)S(1)}, bf16[512,128]{1,0:T(8,128)(2,1)S(1)}, u32[]{:S(2)}, u32[]{:S(2)}) collective-permute-start(bf16[512,128]{1,0:T(8,128)(2,1)S(1)} %bitcast.41), channel_id=1, source_target_pairs={{0,1},{1,2},{2,3},{3,0},{4,5},{5,6},{6,7},{7,4},{8,9},{9,10},{10,1... | collective-permute-start | bytes 393224 | tf_op jit(solution)/shard_map/ppermute | solution.py:165
  148.8 1.0 fusion.17
  149.9 0.0 collective-permute-done.3
  149.9 0.0 collective-permute-done.2
  149.9 1.1 fusion.1
  151.0 0.2 collective-permute-done.7
  151.1 1.0 fusion.14
  152.2 0.0 collective-permute-done.8
  152.2 1.0 fusion.12
  153.2 0.0 collective-permute-done.6
  153.3 0.9 fusion.4
  (10 shorter events, 0.1 us)
Async XLA Ops:
  0.0 9.6 %copy-start = (bf16[512,1024]{1,0:T(8,128)(2,1)S(1)}, bf16[512,1024]{1,0:T(8,128)(2,1)}, u32[]{:S(2)}) copy-start(bf16[512,1024]{1,0:T(8,128)(2,1)} %param.7) | copy-start | bytes 3145732
  1.9 13.8 %all-to-all-start = ((s32[32,1,2]{2,1,0:T(1,128)}), s32[32,1,2]{2,1,0:T(1,128)S(1)}, u32[]{:S(2)}, u32[]{:S(2)}) async-start(s32[32,1,2]{2,1,0:T(1,128)} %copy.16), calls=%async_computation | async-start | bytes 32768 | tf_op jit(solution)/shard_map/all_to_all | solution.py:128
  19.1 33.2 %all-to-all-start.1 = ((bf16[64,64,256]{2,1,0:T(8,128)(2,1)}), bf16[64,64,256]{2,1,0:T(8,128)(2,1)S(1)}, u32[]{:S(2)}, u32[]{:S(2)}) async-start(bf16[64,64,256]{2,1,0:T(8,128)(2,1)} %gather_fusion.1), calls=%async_computation.1 | async-start | bytes 4194304 | tf_op jit(solution)/shard_map/all_to_all | solution.py:152
  26.2 92.0 %collective-permute-start.1 = (bf16[256,256]{1,0:T(8,128)(2,1)}, bf16[256,256]{1,0:T(8,128)(2,1)S(1)}, u32[]{:S(2)}, u32[]{:S(2)}) collective-permute-start(bf16[256,256]{1,0:T(8,128)(2,1)} %get-tuple-element.9), channel_id=1, source_target_pairs={{0,1},{1,2},{2,3},{3,0},{4,5},{5,6},{6,7},{7,4},{8,9},{9,10},{10,1... | collective-permute-start | bytes 393224 | tf_op jit(solution)/shard_map/ppermute | solution.py:137
  28.1 86.8 %collective-permute-start.5 = (bf16[256,256]{1,0:T(8,128)(2,1)}, bf16[256,256]{1,0:T(8,128)(2,1)}, u32[]{:S(2)}, u32[]{:S(2)}) collective-permute-start(bf16[256,256]{1,0:T(8,128)(2,1)} %get-tuple-element.10), channel_id=1, source_target_pairs={{0,3},{1,0},{2,1},{3,2},{4,7},{5,4},{6,5},{7,6},{8,11},{9,8},{10,9... | collective-permute-start | bytes 393224 | tf_op jit(solution)/shard_map/ppermute | solution.py:137
  30.2 119.6 %collective-permute-start.3 = (bf16[256,256]{1,0:T(8,128)(2,1)}, bf16[256,256]{1,0:T(8,128)(2,1)}, u32[]{:S(2)}, u32[]{:S(2)}) collective-permute-start(bf16[256,256]{1,0:T(8,128)(2,1)} %get-tuple-element.11), channel_id=1, source_target_pairs={{0,2},{1,3},{2,0},{3,1},{4,6},{5,7},{6,4},{7,5},{8,10},{9,11},{10,... | collective-permute-start | bytes 393224 | tf_op jit(solution)/shard_map/ppermute | solution.py:137
  35.2 23.8 %copy-start.2 = (s32[8,64]{1,0:T(8,128)S(1)}, s32[8,64]{1,0:T(8,128)}, u32[]{:S(2)}) copy-start(s32[8,64]{1,0:T(8,128)} %param.12) | copy-start | bytes 6148
  52.3 66.2 %all-to-all-start.2 = ((bf16[64,64,256]{2,1,0:T(8,128)(2,1)}), bf16[64,64,256]{2,1,0:T(8,128)(2,1)}, u32[]{:S(2)}, u32[]{:S(2)}) async-start(bf16[64,64,256]{2,1,0:T(8,128)(2,1)} %gather_fusion.2), calls=%async_computation.2 | async-start | bytes 4194304 | tf_op jit(solution)/shard_map/all_to_all | solution.py:152
  59.1 3.5 %copy-start.3 = (f32[4]{0:T(128)S(1)}, f32[4]{0:T(128)}, u32[]{:S(2)}) copy-start(f32[4]{0:T(128)} %param.10) | copy-start | bytes 52
  62.5 1.7 %copy-start.1 = (s32[8]{0:T(128)S(1)}, s32[8]{0:T(128)}, u32[]{:S(2)}) copy-start(s32[8]{0:T(128)} %cnt_ref.3) | copy-start | bytes 100
  109.7 8.5 %collective-permute-start = (bf16[512,128]{1,0:T(8,128)(2,1)S(1)}, bf16[512,128]{1,0:T(8,128)(2,1)S(1)}, u32[]{:S(2)}, u32[]{:S(2)}) collective-permute-start(bf16[512,128]{1,0:T(8,128)(2,1)S(1)} %bitcast.34), channel_id=1, source_target_pairs={{0,1},{1,2},{2,3},{3,0},{4,5},{5,6},{6,7},{7,4},{8,9},{9,10},{10,1... | collective-permute-start | bytes 393224 | tf_op jit(solution)/shard_map/ppermute | solution.py:165
  111.7 5.4 %collective-permute-start.4 = (bf16[512,128]{1,0:T(8,128)(2,1)S(1)}, bf16[512,128]{1,0:T(8,128)(2,1)S(1)}, u32[]{:S(2)}, u32[]{:S(2)}) collective-permute-start(bf16[512,128]{1,0:T(8,128)(2,1)S(1)} %bitcast.35), channel_id=1, source_target_pairs={{0,3},{1,0},{2,1},{3,2},{4,7},{5,4},{6,5},{7,6},{8,11},{9,8},{10,9... | collective-permute-start | bytes 393224 | tf_op jit(solution)/shard_map/ppermute | solution.py:165
  115.0 34.9 %collective-permute-start.2 = (bf16[512,128]{1,0:T(8,128)(2,1)S(1)}, bf16[512,128]{1,0:T(8,128)(2,1)S(1)}, u32[]{:S(2)}, u32[]{:S(2)}) collective-permute-start(bf16[512,128]{1,0:T(8,128)(2,1)S(1)} %bitcast.37), channel_id=1, source_target_pairs={{0,2},{1,3},{2,0},{3,1},{4,6},{5,7},{6,4},{7,5},{8,10},{9,11},{10,... | collective-permute-start | bytes 393224 | tf_op jit(solution)/shard_map/ppermute | solution.py:165
  142.2 8.9 %collective-permute-start.7 = (bf16[512,128]{1,0:T(8,128)(2,1)S(1)}, bf16[512,128]{1,0:T(8,128)(2,1)S(1)}, u32[]{:S(2)}, u32[]{:S(2)}) collective-permute-start(bf16[512,128]{1,0:T(8,128)(2,1)S(1)} %bitcast.39), channel_id=1, source_target_pairs={{0,2},{1,3},{2,0},{3,1},{4,6},{5,7},{6,4},{7,5},{8,10},{9,11},{10,... | collective-permute-start | bytes 393224 | tf_op jit(solution)/shard_map/ppermute | solution.py:165
  146.8 5.4 %collective-permute-start.8 = (bf16[512,128]{1,0:T(8,128)(2,1)S(1)}, bf16[512,128]{1,0:T(8,128)(2,1)S(1)}, u32[]{:S(2)}, u32[]{:S(2)}) collective-permute-start(bf16[512,128]{1,0:T(8,128)(2,1)S(1)} %bitcast.40), channel_id=1, source_target_pairs={{0,3},{1,0},{2,1},{3,2},{4,7},{5,4},{6,5},{7,6},{8,11},{9,8},{10,9... | collective-permute-start | bytes 393224 | tf_op jit(solution)/shard_map/ppermute | solution.py:165
  146.8 6.4 %collective-permute-start.6 = (bf16[512,128]{1,0:T(8,128)(2,1)S(1)}, bf16[512,128]{1,0:T(8,128)(2,1)S(1)}, u32[]{:S(2)}, u32[]{:S(2)}) collective-permute-start(bf16[512,128]{1,0:T(8,128)(2,1)S(1)} %bitcast.41), channel_id=1, source_target_pairs={{0,1},{1,2},{2,3},{3,0},{4,5},{5,6},{6,7},{7,4},{8,9},{9,10},{10,1... | collective-permute-start | bytes 393224 | tf_op jit(solution)/shard_map/ppermute | solution.py:165

commit v5 on v3

v5 whole, which is shorter than its diff:
```python
import functools

import jax
import jax.numpy as jnp
from jax import lax
from jax.experimental import pallas as pl
from jax.experimental.pallas import tpu as pltpu
from jax.sharding import PartitionSpec as P

HD = 64
BLK = 64
NB = 64


CH = 8


def _attend_kernel(g0, nbr_ref, cnt_ref, gain_ref, q_ref, bias_ref, kv_hbm, o_ref,
                   kv_buf, s_scr, bm_scr, sem):
    g = pl.program_id(0)
    steps = pl.num_programs(0)
    width = kv_buf.shape[-1]
    half_w = width // 2
    pairs = half_w // 128
    span = NB * BLK
    cw = CH * BLK
    nchunks = NB // CH

    def live_chunks(gi):
        return (cnt_ref[g0 + gi] + (CH - 1)) // CH

    def start(gi, slot):
        def issue(c, carry):
            for i in range(CH):
                j = c * CH + i
                pltpu.make_async_copy(
                    kv_hbm.at[nbr_ref[g0 + gi, j]], kv_buf.at[slot, j], sem.at[slot, c]
                ).start()
            return carry

        lax.fori_loop(0, live_chunks(gi), issue, 0)

    @pl.when(g == 0)
    def _():
        start(0, 0)

    @pl.when(g + 1 < steps)
    def _():
        start(g + 1, (g + 1) % 2)

    slot = g % 2
    nc = live_chunks(g)

    def wait(c, carry):
        pltpu.make_async_copy(
            kv_hbm.at[pl.ds(0, CH)], kv_buf.at[slot, pl.ds(c * CH, CH)], sem.at[slot, c]
        ).wait()
        return carry

    lax.fori_loop(0, nc, wait, 0)

    live_cols = cnt_ref[g0 + g] * BLK
    col = lax.broadcasted_iota(jnp.int32, (BLK, cw), 1)
    for c in range(nchunks):
        @pl.when(c < nc)
        def _():
            b = bias_ref[0, :, c * cw:(c + 1) * cw].astype(jnp.float32)
            bm_scr[c] = jnp.where(col + c * cw < live_cols, b, -jnp.inf)

    q = q_ref[0]
    lane = lax.broadcasted_iota(jnp.int32, (BLK, 128), 1)
    scale = HD ** (-0.5)
    outs = []
    for pair in range(pairs):
        qp = (q[:, pair * 128:(pair + 1) * 128].astype(jnp.float32) * scale).astype(jnp.bfloat16)
        k_lo = pair * 128
        v_lo = half_w + pair * 128
        res = None
        for half in range(2):
            h = pair * 2 + half
            in_head = (lane >= half * HD) & (lane < (half + 1) * HD)
            qm = jnp.where(in_head, qp, jnp.zeros_like(qp))
            gain = gain_ref[h]

            def score(c, top):
                kc = kv_buf[slot, pl.ds(c * CH, CH), :, k_lo:k_lo + 128].reshape(cw, 128)
                s = lax.dot_general(
                    qm, kc, (((1,), (1,)), ((), ())), preferred_element_type=jnp.float32
                )
                s = s + gain * bm_scr[c]
                s_scr[c] = s
                return jnp.maximum(top, jnp.max(s, axis=1, keepdims=True))

            top = lax.fori_loop(0, nc, score, jnp.full((BLK, 1), -jnp.inf, jnp.float32))

            def accumulate(c, carry):
                total, acc = carry
                expo = jnp.exp(s_scr[c] - top)
                total = total + jnp.sum(expo, axis=1, keepdims=True)
                vc = kv_buf[slot, pl.ds(c * CH, CH), :, v_lo:v_lo + 128].reshape(cw, 128)
                acc = acc + jnp.dot(expo.astype(jnp.bfloat16), vc, preferred_element_type=jnp.float32)
                return total, acc

            total, acc = lax.fori_loop(
                0, nc, accumulate,
                (jnp.zeros((BLK, 1), jnp.float32), jnp.zeros((BLK, 128), jnp.float32)),
            )
            o = acc * (1.0 / total)
            res = o if res is None else jnp.where(lane < HD, res, o)
        outs.append(res.astype(jnp.bfloat16))
    o_ref[0] = jnp.concatenate(outs, axis=1)


def attend(nbr, cnt, gain, q_blocks, bias, kv_table, g0, steps):
    width_q = q_blocks.shape[-1]
    width = kv_table.shape[-1]
    span = NB * BLK
    grid_spec = pltpu.PrefetchScalarGridSpec(
        num_scalar_prefetch=2,
        grid=(steps,),
        in_specs=[
            pl.BlockSpec(memory_space=pltpu.SMEM),
            pl.BlockSpec((1, BLK, width_q), lambda g, n, c: (g + g0, 0, 0)),
            pl.BlockSpec((1, BLK, span), lambda g, n, c: (g + g0, 0, 0)),
            pl.BlockSpec(memory_space=pl.ANY),
        ],
        out_specs=pl.BlockSpec((1, BLK, width_q), lambda g, n, c: (g, 0, 0)),
        scratch_shapes=[
            pltpu.VMEM((2, NB, BLK, width), jnp.bfloat16),
            pltpu.VMEM((NB // CH, BLK, CH * BLK), jnp.float32),
            pltpu.VMEM((NB // CH, BLK, CH * BLK), jnp.float32),
            pltpu.SemaphoreType.DMA((2, NB // CH)),
        ],
    )
    return pl.pallas_call(
        functools.partial(_attend_kernel, g0),
        grid_spec=grid_spec,
        out_shape=jax.ShapeDtypeStruct((steps, BLK, width_q), jnp.bfloat16),
        compiler_params=pltpu.CompilerParams(
            dimension_semantics=("arbitrary",), vmem_limit_bytes=48 * 1024 * 1024
        ),
    )(nbr, cnt, gain, q_blocks, bias, kv_table)


def plan_requests(neighbours, per_owner, owners):
    owner = neighbours // per_owner
    local = neighbours % per_owner
    flat = neighbours.reshape(-1)
    ids = jnp.arange(owners * per_owner, dtype=jnp.int32)
    present = jnp.any(flat[:, None] == ids[None, :], axis=0).reshape(owners, per_owner)
    lidx = jnp.arange(per_owner, dtype=jnp.int32)[None, :]
    first = jnp.min(jnp.where(present, lidx, per_owner), axis=1)
    first = jnp.where(first == per_owner, 0, first)
    second = jnp.max(jnp.where(present, lidx, -1), axis=1)
    second = jnp.where(second < 0, first, second)
    req = jnp.stack([first, second], axis=1).astype(jnp.int32)
    pos = owner * 2 + (local != first[owner]).astype(jnp.int32)
    return req, pos.astype(jnp.int32)


def body(features, w_qkv, w_out, bias_gain, edge_bias, neighbours, counts):
    rows = features.shape[0]
    width_heads = w_qkv.shape[2]
    blocks_dev = rows // BLK
    head_devs = lax.axis_size("head")
    row_devs = lax.axis_size("row")
    me = lax.axis_index("head")
    req, pos = plan_requests(neighbours, blocks_dev, row_devs)
    wanted = lax.all_to_all(req, "row", 0, 0, tiled=True).reshape(-1)
    queries = jnp.dot(features, w_qkv[0], preferred_element_type=jnp.float32).astype(jnp.bfloat16)
    keys = jnp.dot(features, w_qkv[1], preferred_element_type=jnp.float32).astype(jnp.bfloat16)
    values = jnp.dot(features, w_qkv[2], preferred_element_type=jnp.float32).astype(jnp.bfloat16)
    kv = jnp.concatenate([keys, values], axis=1).reshape(blocks_dev, BLK, 2 * width_heads)
    outgoing = jnp.take(kv, wanted, axis=0, mode="clip")
    kv_table = lax.all_to_all(outgoing, "row", 0, 0, tiled=True)
    w_parts = []
    for s in range(1, head_devs):
        target = (me + s) % head_devs
        piece = lax.dynamic_slice_in_dim(w_out, target * width_heads, width_heads, axis=1)
        perm = [(i, (i + s) % head_devs) for i in range(head_devs)]
        w_parts.append(lax.ppermute(piece, "head", perm))
    w_own = lax.dynamic_slice_in_dim(w_out, me * width_heads, width_heads, axis=1)
    q_blocks = queries.reshape(blocks_dev, BLK, width_heads)
    halves = 2
    steps = blocks_dev // halves
    results = []
    for part in range(halves):
        att = attend(pos, counts, bias_gain, q_blocks, edge_bias, kv_table, part * steps, steps)
        att = att.reshape(steps * BLK, width_heads)
        total = jnp.dot(att, w_own, preferred_element_type=jnp.float32)
        for s in range(1, head_devs):
            perm = [(i, (i + s) % head_devs) for i in range(head_devs)]
            att_s = lax.ppermute(att, "head", perm)
            total = total + jnp.dot(att_s, w_parts[s - 1], preferred_element_type=jnp.float32)
        results.append(total.astype(jnp.bfloat16))
    return jnp.concatenate(results, axis=0)


def solution(mesh):
    in_specs = (
        P("row", None),
        P(None, None, "head"),
        P("head", None),
        P("head"),
        P("row", None, None),
        P("row", None),
        P("row"),
    )
    out_specs = P("row", "head")
    return jax.shard_map(body, mesh=mesh, in_specs=in_specs, out_specs=out_specs, check_vma=False)
```

time: 152 us -> 217 us (1.43); the launches traced: 149 us -> 217 us
  Pallas kernels: 41.7 us -> 120 us
  waiting for transfers between devices: 58.1 us -> 47.4 us
  other arithmetic: 5.68 us -> 1.78 us
  starting transfers between devices: 26.4 us -> 30.1 us
    pallas_call x1 -> x2, Pallas kernels: 41.7 us -> 120 us  [attend(): pl.pallas_call(functools.partial(_attend_kernel, g0), grid_spec=grid_spec...]
    all_to_all x1, waiting for transfers between devices: 46.4 us -> 40.4 us  [body(): kv_table = lax.all_to_all(outgoing, 'row', 0, 0, tiled=True)]
    select_n x2 -> x0, other arithmetic: 4.62 us -> none  [body(): outgoing = jnp.take(kv, wanted.reshape(-1), axis=0)]
    ppermute x3, waiting for transfers between devices: 4.21 us -> 0.01 us  [body(): w_parts.append(lax.ppermute(piece, 'head', perm))]
    ppermute x3 -> x6, starting transfers between devices: 7.11 us -> 10.5 us  [body(): att_s = lax.ppermute(att, 'head', perm)]
    ppermute x3 -> x6, waiting for transfers between devices: 4.74 us -> 4.25 us  [body(): att_s = lax.ppermute(att, 'head', perm)]
  transfers between devices with their start and end apart: 8 -> 11, of which waited for: 5 -> 3; matrix products, arithmetic and copies ran while one was open for 6% -> 4% of each run, Pallas kernels for 0% -> 55%
where the time goes in v5:
time: 217 us
  Pallas kernels  120 us (55%)
  waiting for transfers between devices  47.4 us (22%)
  starting transfers between devices  30.1 us (14%)
  local copies, waits for them, and re-layouts  11 us (5%)
  matrix products  6.03 us (3%)
    pallas_call x2, Pallas kernels, attend(): pl.pallas_call(functools.partial(_attend_kernel, g0), grid_spec=grid_spec...  120 us
    all_to_all x1, waiting for transfers between devices, body(): kv_table = lax.all_to_all(outgoing, 'row', 0, 0, tiled=True)  40.4 us
    ppermute x6, starting transfers between devices, body(): att_s = lax.ppermute(att, 'head', perm)  10.5 us
    all_to_all x1, starting transfers between devices, body(): wanted = lax.all_to_all(req, 'row', 0, 0, tiled=True).reshape(-1)  7.62 us
    all_to_all x1, starting transfers between devices, body(): kv_table = lax.all_to_all(outgoing, 'row', 0, 0, tiled=True)  6.02 us
    ppermute x3, starting transfers between devices, body(): w_parts.append(lax.ppermute(piece, 'head', perm))  5.97 us
  transfers between devices with their start and end apart: 11, of which 3 were waited for; matrix products, arithmetic and copies ran while one was open for 4% of the time, Pallas kernels for 55%

profile of v5, /device:TPU:2, one launch (start us, length us, event | category | flops | bytes accessed | tf_op | source)
XLA Modules:
  0.0 217.0 jit_solution(5380150233719251746)
XLA Ops:
  0.0 0.0 copy-start
  0.0 0.8 eq.42
  0.9 0.2 fusion.10
  1.0 0.1 reshape.45
  1.1 0.1 select_reduce_fusion
  1.3 0.7 copy.14
  2.0 7.6 %all-to-all-start = ((s32[32,1,2]{2,1,0:T(1,128)}), s32[32,1,2]{2,1,0:T(1,128)S(1)}, u32[]{:S(2)}, u32[]{:S(2)}) async-start(s32[32,1,2]{2,1,0:T(1,128)} %copy.14), calls=%async_computation | async-start | bytes 32768 | tf_op jit(solution)/shard_map/all_to_all | solution.py:169
  9.6 0.0 copy-done
  9.6 1.5 convolution_convert_fusion
  11.1 1.5 convolution_convert_fusion.1
  12.7 0.2 copy.13
  12.9 2.8 %all-to-all-done = s32[32,1,2]{2,1,0:T(1,128)S(1)} async-done(((s32[32,1,2]{2,1,0:T(1,128)}), s32[32,1,2]{2,1,0:T(1,128)S(1)}, u32[]{:S(2)}, u32[]{:S(2)}) %all-to-all-start) | async-done | bytes 288 | tf_op jit(solution)/shard_map/all_to_all | solution.py:169
  15.7 0.5 broadcast.70
  16.2 0.7 reduce.3
  16.9 0.1 reshape.60
  17.0 2.8 %gather_fusion.1 = bf16[64,64,512]{2,1,0:T(8,128)(2,1)} fusion(bf16[8,64,512]{2,1,0:T(8,128)(2,1)S(1)} %bitcast.48, s32[1024]{0:T(1024)S(1)} %pad_clamp_fusion), kind=kCustom, calls=%fused_computation.1 | custom fusion | bytes 8388864 | tf_op jit(solution)/shard_map/jit(_take)/gather | solution.py:174
  19.8 0.0 copy-start.4
  19.8 0.0 copy-start.5
  19.8 6.0 %all-to-all-start.1 = ((bf16[64,64,512]{2,1,0:T(8,128)(2,1)}), bf16[64,64,512]{2,1,0:T(8,128)(2,1)}, u32[]{:S(2)}, u32[]{:S(2)}) async-start(bf16[64,64,512]{2,1,0:T(8,128)(2,1)} %gather_fusion.1), calls=%async_computation.1 | async-start | bytes 8388608 | tf_op jit(solution)/shard_map/all_to_all | solution.py:175
  25.9 0.0 copy-done.4
  25.9 0.1 constant_dynamic-slice_fusion.1
  25.9 4.1 %collective-permute-start.5 = (bf16[256,256]{1,0:T(8,128)(2,1)S(1)}, bf16[256,256]{1,0:T(8,128)(2,1)S(1)}, u32[]{:S(2)}, u32[]{:S(2)}) collective-permute-start(bf16[256,256]{1,0:T(8,128)(2,1)S(1)} %get-tuple-element.9), channel_id=1, source_target_pairs={{0,3},{1,0},{2,1},{3,2},{4,7},{5,4},{6,5},{7,6},{8,11},{9,8},{10,9... | collective-permute-start | bytes 393224 | tf_op jit(solution)/shard_map/ppermute | solution.py:181
  30.0 0.0 collective-permute-start.1
  30.0 1.9 collective-permute-start.3
  31.9 0.0 copy-done.5
  31.9 0.1 reshape.52
  32.0 3.3 %gather_fusion = s32[512]{0:T(512)S(1)} fusion(s32[32]{0:T(128)S(1)} %compare_select_fusion.3, s32[1024]{0:T(1024)S(1)} %pad_clamp_fusion.1), kind=kCustom, calls=%fused_computation | custom fusion | bytes 6144 | tf_op jit(solution)/shard_map/gather | solution.py:157
  35.4 0.0 copy-start.2
  35.4 0.0 copy-start.3
  35.4 0.1 reshape.51
  35.5 1.5 convolution_convert_fusion.2
  37.0 40.4 %all-to-all-done.1.kv_hbm = bf16[64,64,512]{2,1,0:T(8,128)(2,1)} async-done(((bf16[64,64,512]{2,1,0:T(8,128)(2,1)}), bf16[64,64,512]{2,1,0:T(8,128)(2,1)}, u32[]{:S(2)}, u32[]{:S(2)}) %all-to-all-start.1) | async-done | bytes 4194336 | tf_op jit(solution)/shard_map/all_to_all | solution.py:175
  77.3 0.0 copy-done.2
  77.3 0.0 copy-done.3
  77.3 0.0 copy-start.1
  77.3 2.2 %copy-done.1 = bf16[8,64,4096]{2,1,0:T(8,128)(2,1)S(1)} copy-done((bf16[8,64,4096]{2,1,0:T(8,128)(2,1)S(1)}, bf16[8,64,4096]{2,1,0:T(8,128)(2,1)}, u32[]{:S(2)}) %copy-start.1) | copy-done | bytes 4194328
  79.5 60.2 %shard_map.74 = bf16[4,64,256]{2,1,0:T(8,128)(2,1)S(1)} custom-call(s32[8,64]{1,0:T(8,128)S(1)} %convert_add_fusion.nbr_ref, s32[8]{0:T(128)S(1)} %copy-done.2, f32[4]{0:T(128)S(1)} %copy-done.3, bf16[8,64,256]{2,1,0:T(8,128)(2,1)S(1)} %bitcast.38, bf16[8,64,4096]{2,1,0:T(8,128)(2,1)S(1)} %copy-done.1, bf16[64,64,512]{2,1,0:T(8,128)(2,1)} %all-to-all-done.1.kv_hbm), custom_call_target="tpu_custom_call" | custom-call | tf_op jit(solution)/shard_map/pallas_call | solution.py:135
  139.8 4.1 %collective-permute-start.8 = (bf16[256,256]{1,0:T(8,128)(2,1)S(1)}, bf16[256,256]{1,0:T(8,128)(2,1)S(1)}, u32[]{:S(2)}, u32[]{:S(2)}) collective-permute-start(bf16[256,256]{1,0:T(8,128)(2,1)S(1)} %bitcast.44), channel_id=1, source_target_pairs={{0,3},{1,0},{2,1},{3,2},{4,7},{5,4},{6,5},{7,6},{8,11},{9,8},{10,9... | collective-permute-start | bytes 393224 | tf_op jit(solution)/shard_map/ppermute | solution.py:193
  143.9 0.0 collective-permute-start.6
  143.9 0.2 fusion.11
  144.1 60.1 %shard_map.73 = bf16[4,64,256]{2,1,0:T(8,128)(2,1)S(1)} custom-call(s32[8,64]{1,0:T(8,128)S(1)} %convert_add_fusion.nbr_ref, s32[8]{0:T(128)S(1)} %copy-done.2, f32[4]{0:T(128)S(1)} %copy-done.3, bf16[8,64,256]{2,1,0:T(8,128)(2,1)S(1)} %bitcast.39, bf16[8,64,4096]{2,1,0:T(8,128)(2,1)S(1)} %copy-done.1, bf16[64,64,512]{2,1,0:T(8,128)(2,1)} %all-to-all-done.1.kv_hbm), custom_call_target="tpu_custom_call" | custom-call | tf_op jit(solution)/shard_map/pallas_call | solution.py:135
  204.2 0.2 fusion.13
  204.4 0.0 collective-permute-done.1
  204.4 2.0 collective-permute-start.7
  206.3 0.0 collective-permute-done.6
  206.3 1.5 collective-permute-start.4
  207.8 0.2 convolution_add_fusion.1
  208.0 0.0 collective-permute-done.5
  208.0 0.8 collective-permute-start
  208.8 0.0 collective-permute-done.8
  208.8 2.2 collective-permute-start.2
  211.0 0.2 fusion.21
  211.2 0.0 collective-permute-done.3
  211.2 0.0 collective-permute-done.7
  211.2 0.2 fusion.3
  211.4 4.2 %collective-permute-done = bf16[256,256]{1,0:T(8,128)(2,1)S(1)} collective-permute-done((bf16[256,256]{1,0:T(8,128)(2,1)S(1)}, bf16[256,256]{1,0:T(8,128)(2,1)S(1)}, u32[]{:S(2)}, u32[]{:S(2)}) %collective-permute-start) | collective-permute-done | bytes 131104 | tf_op jit(solution)/shard_map/ppermute | solution.py:193
  215.6 0.2 convolution_add_fusion.3
  215.8 0.0 collective-permute-done.4
  215.9 0.2 fusion.20
  216.0 0.0 collective-permute-done.2
  216.1 0.2 fusion.2
  216.3 0.7 pad_maximum_fusion.1
  (8 shorter events, 0.1 us)
Async XLA Ops:
  0.0 9.6 %copy-start = (bf16[512,1024]{1,0:T(8,128)(2,1)S(1)}, bf16[512,1024]{1,0:T(8,128)(2,1)}, u32[]{:S(2)}) copy-start(bf16[512,1024]{1,0:T(8,128)(2,1)} %param.7) | copy-start | bytes 3145732
  2.0 13.7 %all-to-all-start = ((s32[32,1,2]{2,1,0:T(1,128)}), s32[32,1,2]{2,1,0:T(1,128)S(1)}, u32[]{:S(2)}, u32[]{:S(2)}) async-start(s32[32,1,2]{2,1,0:T(1,128)} %copy.14), calls=%async_computation | async-start | bytes 32768 | tf_op jit(solution)/shard_map/all_to_all | solution.py:169
  19.8 6.1 %copy-start.4 = (bf16[256,1024]{1,0:T(8,128)(2,1)S(1)}, bf16[256,1024]{1,0:T(8,128)(2,1)}, u32[]{:S(2)}) copy-start(bf16[256,1024]{1,0:T(8,128)(2,1)} %param.9) | copy-start | bytes 1572868
  19.8 12.1 %copy-start.5 = (s32[8,64]{1,0:T(8,128)S(1)}, s32[8,64]{1,0:T(8,128)}, u32[]{:S(2)}) copy-start(s32[8,64]{1,0:T(8,128)} %param.12) | copy-start | bytes 6148
  19.8 57.5 %all-to-all-start.1 = ((bf16[64,64,512]{2,1,0:T(8,128)(2,1)}), bf16[64,64,512]{2,1,0:T(8,128)(2,1)}, u32[]{:S(2)}, u32[]{:S(2)}) async-start(bf16[64,64,512]{2,1,0:T(8,128)(2,1)} %gather_fusion.1), calls=%async_computation.1 | async-start | bytes 8388608 | tf_op jit(solution)/shard_map/all_to_all | solution.py:175
  25.9 182.0 %collective-permute-start.5 = (bf16[256,256]{1,0:T(8,128)(2,1)S(1)}, bf16[256,256]{1,0:T(8,128)(2,1)S(1)}, u32[]{:S(2)}, u32[]{:S(2)}) collective-permute-start(bf16[256,256]{1,0:T(8,128)(2,1)S(1)} %get-tuple-element.9), channel_id=1, source_target_pairs={{0,3},{1,0},{2,1},{3,2},{4,7},{5,4},{6,5},{7,6},{8,11},{9,8},{10,9... | collective-permute-start | bytes 393224 | tf_op jit(solution)/shard_map/ppermute | solution.py:181
  30.0 174.3 %collective-permute-start.1 = (bf16[256,256]{1,0:T(8,128)(2,1)S(1)}, bf16[256,256]{1,0:T(8,128)(2,1)S(1)}, u32[]{:S(2)}, u32[]{:S(2)}) collective-permute-start(bf16[256,256]{1,0:T(8,128)(2,1)S(1)} %get-tuple-element.8), channel_id=1, source_target_pairs={{0,1},{1,2},{2,3},{3,0},{4,5},{5,6},{6,7},{7,4},{8,9},{9,10},{10,1... | collective-permute-start | bytes 393224 | tf_op jit(solution)/shard_map/ppermute | solution.py:181
  30.0 181.1 %collective-permute-start.3 = (bf16[256,256]{1,0:T(8,128)(2,1)S(1)}, bf16[256,256]{1,0:T(8,128)(2,1)S(1)}, u32[]{:S(2)}, u32[]{:S(2)}) collective-permute-start(bf16[256,256]{1,0:T(8,128)(2,1)S(1)} %get-tuple-element.7), channel_id=1, source_target_pairs={{0,2},{1,3},{2,0},{3,1},{4,6},{5,7},{6,4},{7,5},{8,10},{9,11},{10,... | collective-permute-start | bytes 393224 | tf_op jit(solution)/shard_map/ppermute | solution.py:181
  35.4 42.0 %copy-start.2 = (s32[8]{0:T(128)S(1)}, s32[8]{0:T(128)}, u32[]{:S(2)}) copy-start(s32[8]{0:T(128)} %cnt_ref.3) | copy-start | bytes 100
  35.4 42.0 %copy-start.3 = (f32[4]{0:T(128)S(1)}, f32[4]{0:T(128)}, u32[]{:S(2)}) copy-start(f32[4]{0:T(128)} %gain_ref.3) | copy-start | bytes 52
  77.3 2.2 %copy-start.1 = (bf16[8,64,4096]{2,1,0:T(8,128)(2,1)S(1)}, bf16[8,64,4096]{2,1,0:T(8,128)(2,1)}, u32[]{:S(2)}) copy-start(bf16[8,64,4096]{2,1,0:T(8,128)(2,1)} %bias_ref.3) | copy-start | bytes 12582916
  139.8 69.0 %collective-permute-start.8 = (bf16[256,256]{1,0:T(8,128)(2,1)S(1)}, bf16[256,256]{1,0:T(8,128)(2,1)S(1)}, u32[]{:S(2)}, u32[]{:S(2)}) collective-permute-start(bf16[256,256]{1,0:T(8,128)(2,1)S(1)} %bitcast.44), channel_id=1, source_target_pairs={{0,3},{1,0},{2,1},{3,2},{4,7},{5,4},{6,5},{7,6},{8,11},{9,8},{10,9... | collective-permute-start | bytes 393224 | tf_op jit(solution)/shard_map/ppermute | solution.py:193
  143.9 62.4 %collective-permute-start.6 = (bf16[256,256]{1,0:T(8,128)(2,1)S(1)}, bf16[256,256]{1,0:T(8,128)(2,1)S(1)}, u32[]{:S(2)}, u32[]{:S(2)}) collective-permute-start(bf16[256,256]{1,0:T(8,128)(2,1)S(1)} %bitcast.45), channel_id=1, source_target_pairs={{0,1},{1,2},{2,3},{3,0},{4,5},{5,6},{6,7},{7,4},{8,9},{9,10},{10,1... | collective-permute-start | bytes 393224 | tf_op jit(solution)/shard_map/ppermute | solution.py:193
  204.4 6.8 %collective-permute-start.7 = (bf16[256,256]{1,0:T(8,128)(2,1)S(1)}, bf16[256,256]{1,0:T(8,128)(2,1)S(1)}, u32[]{:S(2)}, u32[]{:S(2)}) collective-permute-start(bf16[256,256]{1,0:T(8,128)(2,1)S(1)} %bitcast.47), channel_id=1, source_target_pairs={{0,2},{1,3},{2,0},{3,1},{4,6},{5,7},{6,4},{7,5},{8,10},{9,11},{10,... | collective-permute-start | bytes 393224 | tf_op jit(solution)/shard_map/ppermute | solution.py:193
  206.3 9.5 %collective-permute-start.4 = (bf16[256,256]{1,0:T(8,128)(2,1)S(1)}, bf16[256,256]{1,0:T(8,128)(2,1)S(1)}, u32[]{:S(2)}, u32[]{:S(2)}) collective-permute-start(bf16[256,256]{1,0:T(8,128)(2,1)S(1)} %bitcast.41), channel_id=1, source_target_pairs={{0,3},{1,0},{2,1},{3,2},{4,7},{5,4},{6,5},{7,6},{8,11},{9,8},{10,9... | collective-permute-start | bytes 393224 | tf_op jit(solution)/shard_map/ppermute | solution.py:193
  208.0 7.7 %collective-permute-start = (bf16[256,256]{1,0:T(8,128)(2,1)S(1)}, bf16[256,256]{1,0:T(8,128)(2,1)S(1)}, u32[]{:S(2)}, u32[]{:S(2)}) collective-permute-start(bf16[256,256]{1,0:T(8,128)(2,1)S(1)} %bitcast.42), channel_id=1, source_target_pairs={{0,1},{1,2},{2,3},{3,0},{4,5},{5,6},{6,7},{7,4},{8,9},{9,10},{10,1... | collective-permute-start | bytes 393224 | tf_op jit(solution)/shard_map/ppermute | solution.py:193
  208.8 7.2 %collective-permute-start.2 = (bf16[256,256]{1,0:T(8,128)(2,1)S(1)}, bf16[256,256]{1,0:T(8,128)(2,1)S(1)}, u32[]{:S(2)}, u32[]{:S(2)}) collective-permute-start(bf16[256,256]{1,0:T(8,128)(2,1)S(1)} %bitcast.43), channel_id=1, source_target_pairs={{0,2},{1,3},{2,0},{3,1},{4,6},{5,7},{6,4},{7,5},{8,10},{9,11},{10,... | collective-permute-start | bytes 393224 | tf_op jit(solution)/shard_map/ppermute | solution.py:193

commit v6 on v3

v6 whole, which is shorter than its diff:
```python
import functools

import jax
import jax.numpy as jnp
from jax import lax
from jax.experimental import pallas as pl
from jax.experimental.pallas import tpu as pltpu
from jax.sharding import PartitionSpec as P

HD = 64
BLK = 64
NB = 64


def _attend_kernel(g0, nbr_ref, cnt_ref, gain_ref, q_ref, bias_ref, kv_ref, o_ref):
    gi = g0 + pl.program_id(0)
    width = kv_ref.shape[-1]
    half_w = width // 2
    pairs = half_w // 128
    span = NB * BLK
    live_cols = cnt_ref[gi] * BLK
    col = lax.broadcasted_iota(jnp.int32, (BLK, span), 1)
    live = col < live_cols
    bias = bias_ref[0].astype(jnp.float32)
    q = q_ref[0]
    lane = lax.broadcasted_iota(jnp.int32, (BLK, 128), 1)
    scale = HD ** (-0.5)
    slots = [nbr_ref[gi, j] for j in range(NB)]
    outs = []
    for pair in range(pairs):
        k_lo = pair * 128
        v_lo = half_w + pair * 128
        kp = jnp.concatenate([kv_ref[b, :, k_lo:k_lo + 128] for b in slots], axis=0)
        vp = jnp.concatenate([kv_ref[b, :, v_lo:v_lo + 128] for b in slots], axis=0)
        qp = q[:, pair * 128:(pair + 1) * 128]
        res = None
        for half in range(2):
            h = pair * 2 + half
            in_head = (lane >= half * HD) & (lane < (half + 1) * HD)
            qm = jnp.where(in_head, qp, jnp.zeros_like(qp))
            s = lax.dot_general(
                qm, kp, (((1,), (1,)), ((), ())), preferred_element_type=jnp.float32
            )
            s = s * scale + gain_ref[h] * bias
            s = jnp.where(live, s, jnp.float32(-1e30))
            top = jnp.max(s, axis=1, keepdims=True)
            expo = jnp.exp(s - top)
            total = jnp.sum(expo, axis=1, keepdims=True)
            w = (expo * (1.0 / total)).astype(jnp.bfloat16)
            o = jnp.dot(w, vp, preferred_element_type=jnp.float32)
            res = o if res is None else jnp.where(lane < HD, res, o)
        outs.append(res.astype(jnp.bfloat16))
    o_ref[0] = jnp.concatenate(outs, axis=1)


def attend(nbr, cnt, gain, q_blocks, bias, kv_table, g0, steps):
    width_q = q_blocks.shape[-1]
    span = NB * BLK
    grid_spec = pltpu.PrefetchScalarGridSpec(
        num_scalar_prefetch=2,
        grid=(steps,),
        in_specs=[
            pl.BlockSpec(memory_space=pltpu.SMEM),
            pl.BlockSpec((1, BLK, width_q), lambda g, n, c: (g + g0, 0, 0)),
            pl.BlockSpec((1, BLK, span), lambda g, n, c: (g + g0, 0, 0)),
            pl.BlockSpec(kv_table.shape, lambda g, n, c: (0, 0, 0)),
        ],
        out_specs=pl.BlockSpec((1, BLK, width_q), lambda g, n, c: (g, 0, 0)),
    )
    return pl.pallas_call(
        functools.partial(_attend_kernel, g0),
        grid_spec=grid_spec,
        out_shape=jax.ShapeDtypeStruct((steps, BLK, width_q), jnp.bfloat16),
        compiler_params=pltpu.CompilerParams(
            dimension_semantics=("arbitrary",), vmem_limit_bytes=48 * 1024 * 1024
        ),
    )(nbr, cnt, gain, q_blocks, bias, kv_table)


def plan_requests(neighbours, per_owner, owners):
    owner = neighbours // per_owner
    local = neighbours % per_owner
    flat = neighbours.reshape(-1)
    ids = jnp.arange(owners * per_owner, dtype=jnp.int32)
    present = jnp.any(flat[:, None] == ids[None, :], axis=0).reshape(owners, per_owner)
    lidx = jnp.arange(per_owner, dtype=jnp.int32)[None, :]
    first = jnp.min(jnp.where(present, lidx, per_owner), axis=1)
    first = jnp.where(first == per_owner, 0, first)
    second = jnp.max(jnp.where(present, lidx, -1), axis=1)
    second = jnp.where(second < 0, first, second)
    req = jnp.stack([first, second], axis=1).astype(jnp.int32)
    pos = owner * 2 + (local != first[owner]).astype(jnp.int32)
    return req, pos.astype(jnp.int32)


def body(features, w_qkv, w_out, bias_gain, edge_bias, neighbours, counts):
    rows = features.shape[0]
    width_heads = w_qkv.shape[2]
    blocks_dev = rows // BLK
    head_devs = lax.axis_size("head")
    row_devs = lax.axis_size("row")
    me = lax.axis_index("head")
    req, pos = plan_requests(neighbours, blocks_dev, row_devs)
    wanted = lax.all_to_all(req, "row", 0, 0, tiled=True).reshape(-1)
    queries = jnp.dot(features, w_qkv[0], preferred_element_type=jnp.float32).astype(jnp.bfloat16)
    keys = jnp.dot(features, w_qkv[1], preferred_element_type=jnp.float32).astype(jnp.bfloat16)
    values = jnp.dot(features, w_qkv[2], preferred_element_type=jnp.float32).astype(jnp.bfloat16)
    kv = jnp.concatenate([keys, values], axis=1).reshape(blocks_dev, BLK, 2 * width_heads)
    outgoing = jnp.take(kv, wanted, axis=0, mode="clip")
    kv_table = lax.all_to_all(outgoing, "row", 0, 0, tiled=True)
    w_parts = []
    for s in range(1, head_devs):
        target = (me + s) % head_devs
        piece = lax.dynamic_slice_in_dim(w_out, target * width_heads, width_heads, axis=1)
        perm = [(i, (i + s) % head_devs) for i in range(head_devs)]
        w_parts.append(lax.ppermute(piece, "head", perm))
    w_own = lax.dynamic_slice_in_dim(w_out, me * width_heads, width_heads, axis=1)
    q_blocks = queries.reshape(blocks_dev, BLK, width_heads)
    halves = 2
    steps = blocks_dev // halves
    results = []
    for part in range(halves):
        att = attend(pos, counts, bias_gain, q_blocks, edge_bias, kv_table, part * steps, steps)
        att = att.reshape(steps * BLK, width_heads)
        total = jnp.dot(att, w_own, preferred_element_type=jnp.float32)
        for s in range(1, head_devs):
            perm = [(i, (i + s) % head_devs) for i in range(head_devs)]
            att_s = lax.ppermute(att, "head", perm)
            total = total + jnp.dot(att_s, w_parts[s - 1], preferred_element_type=jnp.float32)
        results.append(total.astype(jnp.bfloat16))
    return jnp.concatenate(results, axis=0)


def solution(mesh):
    in_specs = (
        P("row", None),
        P(None, None, "head"),
        P("head", None),
        P("head"),
        P("row", None, None),
        P("row", None),
        P("row"),
    )
    out_specs = P("row", "head")
    return jax.shard_map(body, mesh=mesh, in_specs=in_specs, out_specs=out_specs, check_vma=False)
```

time: 152 us -> 139 us (0.914)
  waiting for transfers between devices: 58.1 us -> 48.5 us
  other arithmetic: 5.68 us -> 1.78 us
  starting transfers between devices: 26.4 us -> 30.1 us
  Pallas kernels: 41.7 us -> 39.8 us
    all_to_all x1, waiting for transfers between devices: 46.4 us -> 40.4 us  [body(): kv_table = lax.all_to_all(outgoing, 'row', 0, 0, tiled=True)]
    select_n x2 -> x0, other arithmetic: 4.62 us -> none  [body(): outgoing = jnp.take(kv, wanted.reshape(-1), axis=0)]
    ppermute x3, waiting for transfers between devices: 4.21 us -> 0.01 us  [body(): w_parts.append(lax.ppermute(piece, 'head', perm))]
    ppermute x3 -> x6, starting transfers between devices: 7.11 us -> 10.5 us  [body(): att_s = lax.ppermute(att, 'head', perm)]
    pallas_call x1 -> x2, Pallas kernels: 41.7 us -> 39.8 us  [attend(): pl.pallas_call(functools.partial(_attend_kernel, g0), grid_spec=grid_spec...]
    ppermute x3 -> x6, waiting for transfers between devices: 4.74 us -> 5.36 us  [body(): att_s = lax.ppermute(att, 'head', perm)]
  transfers between devices with their start and end apart: 8 -> 11, of which waited for: 5 -> 4; matrix products, arithmetic and copies ran while one was open for 6% -> 7% of each run, Pallas kernels for 0% -> 29%
where the time goes in v6:
time: 139 us; the launch traced here: 138 us
  waiting for transfers between devices  48.5 us (35%)
  Pallas kernels  39.8 us (29%)
  starting transfers between devices  30.1 us (22%)
  local copies, waits for them, and re-layouts  11 us (8%)
  matrix products  6.02 us (4%)
  other arithmetic  1.78 us (1%)
    all_to_all x1, waiting for transfers between devices, body(): kv_table = lax.all_to_all(outgoing, 'row', 0, 0, tiled=True)  40.4 us
    pallas_call x2, Pallas kernels, attend(): pl.pallas_call(functools.partial(_attend_kernel, g0), grid_spec=grid_spec...  39.8 us
    ppermute x6, starting transfers between devices, body(): att_s = lax.ppermute(att, 'head', perm)  10.5 us
    all_to_all x1, starting transfers between devices, body(): wanted = lax.all_to_all(req, 'row', 0, 0, tiled=True).reshape(-1)  7.62 us
    all_to_all x1, starting transfers between devices, body(): kv_table = lax.all_to_all(outgoing, 'row', 0, 0, tiled=True)  6.02 us
    ppermute x3, starting transfers between devices, body(): w_parts.append(lax.ppermute(piece, 'head', perm))  5.97 us
    ppermute x6, waiting for transfers between devices, body(): att_s = lax.ppermute(att, 'head', perm)  5.36 us
    gather x2, local copies, waits for them, and re-layouts, plan_requests(): pos = owner * 2 + (local != first[owner]).astype(jnp.int32)  3.42 us
  transfers between devices with their start and end apart: 11, of which 4 were waited for; matrix products, arithmetic and copies ran while one was open for 7% of the time, Pallas kernels for 29%

profile of v6, /device:TPU:2, one launch (start us, length us, event | category | flops | bytes accessed | tf_op | source)
XLA Modules:
  0.0 137.6 jit_solution(17228925120213351728)
XLA Ops:
  0.0 0.0 copy-start
  0.0 0.8 eq.42
  0.9 0.2 fusion.10
  1.0 0.1 reshape.45
  1.1 0.1 select_reduce_fusion
  1.3 0.7 copy.14
  2.0 7.6 %all-to-all-start = ((s32[32,1,2]{2,1,0:T(1,128)}), s32[32,1,2]{2,1,0:T(1,128)S(1)}, u32[]{:S(2)}, u32[]{:S(2)}) async-start(s32[32,1,2]{2,1,0:T(1,128)} %copy.14), calls=%async_computation | async-start | bytes 32768 | tf_op jit(solution)/shard_map/all_to_all | solution.py:104
  9.6 0.0 copy-done
  9.6 1.5 %convolution_convert_fusion = bf16[512,256]{0,1:T(8,128)(2,1)S(1)} fusion(bf16[512,1024]{1,0:T(8,128)(2,1)S(1)} %copy-done, bf16[3,1024,256]{2,1,0:T(8,128)(2,1)} %param.8), kind=kOutput, calls=%fused_computation.2 | convolution fusion | flops 268566528 | bytes 1835008 | tf_op jit(solution)/shard_map/dot_general | solution.py:107
  11.1 1.5 %convolution_convert_fusion.1 = bf16[512,256]{0,1:T(8,128)(2,1)S(1)} fusion(bf16[512,1024]{1,0:T(8,128)(2,1)S(1)} %copy-done, bf16[3,1024,256]{2,1,0:T(8,128)(2,1)} %param.8), kind=kOutput, calls=%fused_computation.3 | convolution fusion | flops 268566528 | bytes 1835008 | tf_op jit(solution)/shard_map/dot_general | solution.py:106
  12.7 0.2 copy.13
  12.9 2.8 %all-to-all-done = s32[32,1,2]{2,1,0:T(1,128)S(1)} async-done(((s32[32,1,2]{2,1,0:T(1,128)}), s32[32,1,2]{2,1,0:T(1,128)S(1)}, u32[]{:S(2)}, u32[]{:S(2)}) %all-to-all-start) | async-done | bytes 288 | tf_op jit(solution)/shard_map/all_to_all | solution.py:104
  15.7 0.5 broadcast.70
  16.2 0.7 reduce.3
  16.9 0.1 reshape.60
  17.0 2.8 %gather_fusion.1 = bf16[64,64,512]{2,1,0:T(8,128)(2,1)} fusion(bf16[8,64,512]{2,1,0:T(8,128)(2,1)S(1)} %bitcast.48, s32[1024]{0:T(1024)S(1)} %pad_clamp_fusion), kind=kCustom, calls=%fused_computation.1 | custom fusion | bytes 8388864 | tf_op jit(solution)/shard_map/jit(_take)/gather | solution.py:109
  19.8 0.0 copy-start.4
  19.8 0.0 copy-start.5
  19.8 6.0 %all-to-all-start.1 = ((bf16[64,64,512]{2,1,0:T(8,128)(2,1)}), bf16[64,64,512]{2,1,0:T(8,128)(2,1)}, u32[]{:S(2)}, u32[]{:S(2)}) async-start(bf16[64,64,512]{2,1,0:T(8,128)(2,1)} %gather_fusion.1), calls=%async_computation.1 | async-start | bytes 8388608 | tf_op jit(solution)/shard_map/all_to_all | solution.py:110
  25.9 0.0 copy-done.4
  25.9 0.1 constant_dynamic-slice_fusion.1
  25.9 4.1 %collective-permute-start.5 = (bf16[256,256]{1,0:T(8,128)(2,1)S(1)}, bf16[256,256]{1,0:T(8,128)(2,1)S(1)}, u32[]{:S(2)}, u32[]{:S(2)}) collective-permute-start(bf16[256,256]{1,0:T(8,128)(2,1)S(1)} %get-tuple-element.9), channel_id=1, source_target_pairs={{0,3},{1,0},{2,1},{3,2},{4,7},{5,4},{6,5},{7,6},{8,11},{9,8},{10,9... | collective-permute-start | bytes 393224 | tf_op jit(solution)/shard_map/ppermute | solution.py:116
  30.0 0.0 collective-permute-start.1
  30.0 1.9 %collective-permute-start.3 = (bf16[256,256]{1,0:T(8,128)(2,1)S(1)}, bf16[256,256]{1,0:T(8,128)(2,1)S(1)}, u32[]{:S(2)}, u32[]{:S(2)}) collective-permute-start(bf16[256,256]{1,0:T(8,128)(2,1)S(1)} %get-tuple-element.7), channel_id=1, source_target_pairs={{0,2},{1,3},{2,0},{3,1},{4,6},{5,7},{6,4},{7,5},{8,10},{9,11},{10,... | collective-permute-start | bytes 393224 | tf_op jit(solution)/shard_map/ppermute | solution.py:116
  31.9 0.0 copy-done.5
  31.9 0.1 reshape.52
  32.0 3.3 %gather_fusion = s32[512]{0:T(512)S(1)} fusion(s32[32]{0:T(128)S(1)} %compare_select_fusion.3, s32[1024]{0:T(1024)S(1)} %pad_clamp_fusion.1), kind=kCustom, calls=%fused_computation | custom fusion | bytes 6144 | tf_op jit(solution)/shard_map/gather | solution.py:92
  35.4 0.0 copy-start.2
  35.4 0.0 copy-start.3
  35.4 0.1 reshape.51
  35.5 1.5 %convolution_convert_fusion.2 = bf16[512,256]{1,0:T(8,128)(2,1)S(1)} fusion(bf16[512,1024]{1,0:T(8,128)(2,1)S(1)} %copy-done, bf16[3,1024,256]{2,1,0:T(8,128)(2,1)} %param.8), kind=kOutput, calls=%fused_computation.4 | convolution fusion | flops 268566528 | bytes 1835008 | tf_op jit(solution)/shard_map/dot_general | solution.py:105
  37.0 40.4 %all-to-all-done.1.kv_ref = bf16[64,64,512]{2,1,0:T(8,128)(2,1)} async-done(((bf16[64,64,512]{2,1,0:T(8,128)(2,1)}), bf16[64,64,512]{2,1,0:T(8,128)(2,1)}, u32[]{:S(2)}, u32[]{:S(2)}) %all-to-all-start.1) | async-done | bytes 4194336 | tf_op jit(solution)/shard_map/all_to_all | solution.py:110
  77.3 0.0 copy-done.2
  77.3 0.0 copy-done.3
  77.3 0.0 copy-start.1
  77.3 2.2 %copy-done.1 = bf16[8,64,4096]{2,1,0:T(8,128)(2,1)S(1)} copy-done((bf16[8,64,4096]{2,1,0:T(8,128)(2,1)S(1)}, bf16[8,64,4096]{2,1,0:T(8,128)(2,1)}, u32[]{:S(2)}) %copy-start.1) | copy-done | bytes 4194328
  79.5 19.9 %shard_map.74 = bf16[4,64,256]{2,1,0:T(8,128)(2,1)S(1)} custom-call(s32[8,64]{1,0:T(8,128)S(1)} %convert_add_fusion.nbr_ref, s32[8]{0:T(128)S(1)} %copy-done.2, f32[4]{0:T(128)S(1)} %copy-done.3, bf16[8,64,256]{2,1,0:T(8,128)(2,1)S(1)} %bitcast.38, bf16[8,64,4096]{2,1,0:T(8,128)(2,1)S(1)} %copy-done.1, bf16[64,64,512]{2,1,0:T(8,128)(2,1)} %all-to-all-done.1.kv_ref), custom_call_target="tpu_custom_call" | custom-call | tf_op jit(solution)/shard_map/pallas_call | solution.py:70
  99.5 4.1 %collective-permute-start.8 = (bf16[256,256]{1,0:T(8,128)(2,1)S(1)}, bf16[256,256]{1,0:T(8,128)(2,1)S(1)}, u32[]{:S(2)}, u32[]{:S(2)}) collective-permute-start(bf16[256,256]{1,0:T(8,128)(2,1)S(1)} %bitcast.44), channel_id=1, source_target_pairs={{0,3},{1,0},{2,1},{3,2},{4,7},{5,4},{6,5},{7,6},{8,11},{9,8},{10,9... | collective-permute-start | bytes 393224 | tf_op jit(solution)/shard_map/ppermute | solution.py:128
  103.6 0.0 collective-permute-start.6
  103.6 0.2 fusion.11
  103.8 19.9 %shard_map.73 = bf16[4,64,256]{2,1,0:T(8,128)(2,1)S(1)} custom-call(s32[8,64]{1,0:T(8,128)S(1)} %convert_add_fusion.nbr_ref, s32[8]{0:T(128)S(1)} %copy-done.2, f32[4]{0:T(128)S(1)} %copy-done.3, bf16[8,64,256]{2,1,0:T(8,128)(2,1)S(1)} %bitcast.39, bf16[8,64,4096]{2,1,0:T(8,128)(2,1)S(1)} %copy-done.1, bf16[64,64,512]{2,1,0:T(8,128)(2,1)} %all-to-all-done.1.kv_ref), custom_call_target="tpu_custom_call" | custom-call | tf_op jit(solution)/shard_map/pallas_call | solution.py:70
  123.7 0.2 fusion.13
  123.9 0.0 collective-permute-done.1
  123.9 2.0 %collective-permute-start.7 = (bf16[256,256]{1,0:T(8,128)(2,1)S(1)}, bf16[256,256]{1,0:T(8,128)(2,1)S(1)}, u32[]{:S(2)}, u32[]{:S(2)}) collective-permute-start(bf16[256,256]{1,0:T(8,128)(2,1)S(1)} %bitcast.47), channel_id=1, source_target_pairs={{0,2},{1,3},{2,0},{3,1},{4,6},{5,7},{6,4},{7,5},{8,10},{9,11},{10,... | collective-permute-start | bytes 393224 | tf_op jit(solution)/shard_map/ppermute | solution.py:128
  125.8 0.0 collective-permute-done.6
  125.8 1.5 %collective-permute-start.4 = (bf16[256,256]{1,0:T(8,128)(2,1)S(1)}, bf16[256,256]{1,0:T(8,128)(2,1)S(1)}, u32[]{:S(2)}, u32[]{:S(2)}) collective-permute-start(bf16[256,256]{1,0:T(8,128)(2,1)S(1)} %bitcast.41), channel_id=1, source_target_pairs={{0,3},{1,0},{2,1},{3,2},{4,7},{5,4},{6,5},{7,6},{8,11},{9,8},{10,9... | collective-permute-start | bytes 393224 | tf_op jit(solution)/shard_map/ppermute | solution.py:128
  127.3 0.2 convolution_add_fusion.1
  127.5 0.0 collective-permute-done.5
  127.5 0.8 collective-permute-start
  128.3 0.0 collective-permute-done.8
  128.3 2.2 %collective-permute-start.2 = (bf16[256,256]{1,0:T(8,128)(2,1)S(1)}, bf16[256,256]{1,0:T(8,128)(2,1)S(1)}, u32[]{:S(2)}, u32[]{:S(2)}) collective-permute-start(bf16[256,256]{1,0:T(8,128)(2,1)S(1)} %bitcast.43), channel_id=1, source_target_pairs={{0,2},{1,3},{2,0},{3,1},{4,6},{5,7},{6,4},{7,5},{8,10},{9,11},{10,... | collective-permute-start | bytes 393224 | tf_op jit(solution)/shard_map/ppermute | solution.py:128
  130.5 0.2 fusion.21
  130.7 0.0 collective-permute-done.3
  130.7 0.4 collective-permute-done.7
  131.1 0.2 fusion.3
  131.3 4.9 %collective-permute-done = bf16[256,256]{1,0:T(8,128)(2,1)S(1)} collective-permute-done((bf16[256,256]{1,0:T(8,128)(2,1)S(1)}, bf16[256,256]{1,0:T(8,128)(2,1)S(1)}, u32[]{:S(2)}, u32[]{:S(2)}) %collective-permute-start) | collective-permute-done | bytes 131104 | tf_op jit(solution)/shard_map/ppermute | solution.py:128
  136.3 0.2 convolution_add_fusion.3
  136.4 0.0 collective-permute-done.4
  136.5 0.2 fusion.20
  136.6 0.0 collective-permute-done.2
  136.7 0.2 fusion.2
  136.9 0.7 pad_maximum_fusion.1
  (8 shorter events, 0.1 us)
Async XLA Ops:
  0.0 9.6 %copy-start = (bf16[512,1024]{1,0:T(8,128)(2,1)S(1)}, bf16[512,1024]{1,0:T(8,128)(2,1)}, u32[]{:S(2)}) copy-start(bf16[512,1024]{1,0:T(8,128)(2,1)} %param.7) | copy-start | bytes 3145732
  2.0 13.7 %all-to-all-start = ((s32[32,1,2]{2,1,0:T(1,128)}), s32[32,1,2]{2,1,0:T(1,128)S(1)}, u32[]{:S(2)}, u32[]{:S(2)}) async-start(s32[32,1,2]{2,1,0:T(1,128)} %copy.14), calls=%async_computation | async-start | bytes 32768 | tf_op jit(solution)/shard_map/all_to_all | solution.py:104
  19.8 6.1 %copy-start.4 = (bf16[256,1024]{1,0:T(8,128)(2,1)S(1)}, bf16[256,1024]{1,0:T(8,128)(2,1)}, u32[]{:S(2)}) copy-start(bf16[256,1024]{1,0:T(8,128)(2,1)} %param.9) | copy-start | bytes 1572868
  19.8 12.1 %copy-start.5 = (s32[8,64]{1,0:T(8,128)S(1)}, s32[8,64]{1,0:T(8,128)}, u32[]{:S(2)}) copy-start(s32[8,64]{1,0:T(8,128)} %param.12) | copy-start | bytes 6148
  19.8 57.5 %all-to-all-start.1 = ((bf16[64,64,512]{2,1,0:T(8,128)(2,1)}), bf16[64,64,512]{2,1,0:T(8,128)(2,1)}, u32[]{:S(2)}, u32[]{:S(2)}) async-start(bf16[64,64,512]{2,1,0:T(8,128)(2,1)} %gather_fusion.1), calls=%async_computation.1 | async-start | bytes 8388608 | tf_op jit(solution)/shard_map/all_to_all | solution.py:110
  25.9 101.6 %collective-permute-start.5 = (bf16[256,256]{1,0:T(8,128)(2,1)S(1)}, bf16[256,256]{1,0:T(8,128)(2,1)S(1)}, u32[]{:S(2)}, u32[]{:S(2)}) collective-permute-start(bf16[256,256]{1,0:T(8,128)(2,1)S(1)} %get-tuple-element.9), channel_id=1, source_target_pairs={{0,3},{1,0},{2,1},{3,2},{4,7},{5,4},{6,5},{7,6},{8,11},{9,8},{10,9... | collective-permute-start | bytes 393224 | tf_op jit(solution)/shard_map/ppermute | solution.py:116
  30.0 93.8 %collective-permute-start.1 = (bf16[256,256]{1,0:T(8,128)(2,1)S(1)}, bf16[256,256]{1,0:T(8,128)(2,1)S(1)}, u32[]{:S(2)}, u32[]{:S(2)}) collective-permute-start(bf16[256,256]{1,0:T(8,128)(2,1)S(1)} %get-tuple-element.8), channel_id=1, source_target_pairs={{0,1},{1,2},{2,3},{3,0},{4,5},{5,6},{6,7},{7,4},{8,9},{9,10},{10,1... | collective-permute-start | bytes 393224 | tf_op jit(solution)/shard_map/ppermute | solution.py:116
  30.0 100.7 %collective-permute-start.3 = (bf16[256,256]{1,0:T(8,128)(2,1)S(1)}, bf16[256,256]{1,0:T(8,128)(2,1)S(1)}, u32[]{:S(2)}, u32[]{:S(2)}) collective-permute-start(bf16[256,256]{1,0:T(8,128)(2,1)S(1)} %get-tuple-element.7), channel_id=1, source_target_pairs={{0,2},{1,3},{2,0},{3,1},{4,6},{5,7},{6,4},{7,5},{8,10},{9,11},{10,... | collective-permute-start | bytes 393224 | tf_op jit(solution)/shard_map/ppermute | solution.py:116
  35.4 42.0 %copy-start.2 = (s32[8]{0:T(128)S(1)}, s32[8]{0:T(128)}, u32[]{:S(2)}) copy-start(s32[8]{0:T(128)} %cnt_ref.3) | copy-start | bytes 100
  35.4 42.0 %copy-start.3 = (f32[4]{0:T(128)S(1)}, f32[4]{0:T(128)}, u32[]{:S(2)}) copy-start(f32[4]{0:T(128)} %gain_ref.3) | copy-start | bytes 52
  77.3 2.2 %copy-start.1 = (bf16[8,64,4096]{2,1,0:T(8,128)(2,1)S(1)}, bf16[8,64,4096]{2,1,0:T(8,128)(2,1)}, u32[]{:S(2)}) copy-start(bf16[8,64,4096]{2,1,0:T(8,128)(2,1)} %bias_ref.3) | copy-start | bytes 12582916
  99.5 28.9 %collective-permute-start.8 = (bf16[256,256]{1,0:T(8,128)(2,1)S(1)}, bf16[256,256]{1,0:T(8,128)(2,1)S(1)}, u32[]{:S(2)}, u32[]{:S(2)}) collective-permute-start(bf16[256,256]{1,0:T(8,128)(2,1)S(1)} %bitcast.44), channel_id=1, source_target_pairs={{0,3},{1,0},{2,1},{3,2},{4,7},{5,4},{6,5},{7,6},{8,11},{9,8},{10,9... | collective-permute-start | bytes 393224 | tf_op jit(solution)/shard_map/ppermute | solution.py:128
  103.6 22.3 %collective-permute-start.6 = (bf16[256,256]{1,0:T(8,128)(2,1)S(1)}, bf16[256,256]{1,0:T(8,128)(2,1)S(1)}, u32[]{:S(2)}, u32[]{:S(2)}) collective-permute-start(bf16[256,256]{1,0:T(8,128)(2,1)S(1)} %bitcast.45), channel_id=1, source_target_pairs={{0,1},{1,2},{2,3},{3,0},{4,5},{5,6},{6,7},{7,4},{8,9},{9,10},{10,1... | collective-permute-start | bytes 393224 | tf_op jit(solution)/shard_map/ppermute | solution.py:128
  123.9 7.2 %collective-permute-start.7 = (bf16[256,256]{1,0:T(8,128)(2,1)S(1)}, bf16[256,256]{1,0:T(8,128)(2,1)S(1)}, u32[]{:S(2)}, u32[]{:S(2)}) collective-permute-start(bf16[256,256]{1,0:T(8,128)(2,1)S(1)} %bitcast.47), channel_id=1, source_target_pairs={{0,2},{1,3},{2,0},{3,1},{4,6},{5,7},{6,4},{7,5},{8,10},{9,11},{10,... | collective-permute-start | bytes 393224 | tf_op jit(solution)/shard_map/ppermute | solution.py:128
  125.8 10.6 %collective-permute-start.4 = (bf16[256,256]{1,0:T(8,128)(2,1)S(1)}, bf16[256,256]{1,0:T(8,128)(2,1)S(1)}, u32[]{:S(2)}, u32[]{:S(2)}) collective-permute-start(bf16[256,256]{1,0:T(8,128)(2,1)S(1)} %bitcast.41), channel_id=1, source_target_pairs={{0,3},{1,0},{2,1},{3,2},{4,7},{5,4},{6,5},{7,6},{8,11},{9,8},{10,9... | collective-permute-start | bytes 393224 | tf_op jit(solution)/shard_map/ppermute | solution.py:128
  127.5 8.8 %collective-permute-start = (bf16[256,256]{1,0:T(8,128)(2,1)S(1)}, bf16[256,256]{1,0:T(8,128)(2,1)S(1)}, u32[]{:S(2)}, u32[]{:S(2)}) collective-permute-start(bf16[256,256]{1,0:T(8,128)(2,1)S(1)} %bitcast.42), channel_id=1, source_target_pairs={{0,1},{1,2},{2,3},{3,0},{4,5},{5,6},{6,7},{7,4},{8,9},{9,10},{10,1... | collective-permute-start | bytes 393224 | tf_op jit(solution)/shard_map/ppermute | solution.py:128
  128.3 8.3 %collective-permute-start.2 = (bf16[256,256]{1,0:T(8,128)(2,1)S(1)}, bf16[256,256]{1,0:T(8,128)(2,1)S(1)}, u32[]{:S(2)}, u32[]{:S(2)}) collective-permute-start(bf16[256,256]{1,0:T(8,128)(2,1)S(1)} %bitcast.43), channel_id=1, source_target_pairs={{0,2},{1,3},{2,0},{3,1},{4,6},{5,7},{6,4},{7,5},{8,10},{9,11},{10,... | collective-permute-start | bytes 393224 | tf_op jit(solution)/shard_map/ppermute | solution.py:128

commit v7 on v6

--- a/solution.py
+++ b/solution.py
@@ -12,37 +12,35 @@
 NB = 64
 
 
-def _attend_kernel(g0, nbr_ref, cnt_ref, gain_ref, q_ref, bias_ref, kv_ref, o_ref):
-    gi = g0 + pl.program_id(0)
+def _attend_kernel(p0, nbr_ref, cnt_ref, gain_ref, q_ref, bias_ref, kv_ref, o_ref):
+    g = pl.program_id(0)
     width = kv_ref.shape[-1]
     half_w = width // 2
     pairs = half_w // 128
     span = NB * BLK
-    live_cols = cnt_ref[gi] * BLK
+    live_cols = cnt_ref[g] * BLK
     col = lax.broadcasted_iota(jnp.int32, (BLK, span), 1)
-    live = col < live_cols
-    bias = bias_ref[0].astype(jnp.float32)
+    bias = jnp.where(col < live_cols, bias_ref[0].astype(jnp.float32), -jnp.inf)
     q = q_ref[0]
     lane = lax.broadcasted_iota(jnp.int32, (BLK, 128), 1)
     scale = HD ** (-0.5)
-    slots = [nbr_ref[gi, j] for j in range(NB)]
+    slots = [nbr_ref[g, j] for j in range(NB)]
     outs = []
     for pair in range(pairs):
         k_lo = pair * 128
         v_lo = half_w + pair * 128
         kp = jnp.concatenate([kv_ref[b, :, k_lo:k_lo + 128] for b in slots], axis=0)
         vp = jnp.concatenate([kv_ref[b, :, v_lo:v_lo + 128] for b in slots], axis=0)
-        qp = q[:, pair * 128:(pair + 1) * 128]
+        qp = (q[:, pair * 128:(pair + 1) * 128].astype(jnp.float32) * scale).astype(jnp.bfloat16)
         res = None
         for half in range(2):
-            h = pair * 2 + half
+            h = (p0 + pair) * 2 + half
             in_head = (lane >= half * HD) & (lane < (half + 1) * HD)
             qm = jnp.where(in_head, qp, jnp.zeros_like(qp))
             s = lax.dot_general(
                 qm, kp, (((1,), (1,)), ((), ())), preferred_element_type=jnp.float32
             )
-            s = s * scale + gain_ref[h] * bias
-            s = jnp.where(live, s, jnp.float32(-1e30))
+            s = s + gain_ref[h] * bias
             top = jnp.max(s, axis=1, keepdims=True)
             expo = jnp.exp(s - top)
             total = jnp.sum(expo, axis=1, keepdims=True)
@@ -50,25 +48,25 @@
             o = jnp.dot(w, vp, preferred_element_type=jnp.float32)
             res = o if res is None else jnp.where(lane < HD, res, o)
         outs.append(res.astype(jnp.bfloat16))
-    o_ref[0] = jnp.concatenate(outs, axis=1)
+    o_ref[0] = outs[0] if len(outs) == 1 else jnp.concatenate(outs, axis=1)
 
 
-def attend(nbr, cnt, gain, q_blocks, bias, kv_table, g0, steps):
-    width_q = q_blocks.shape[-1]
+def attend(nbr, cnt, gain, q_blocks, bias, kv_table, p0, width_q):
+    steps = q_blocks.shape[0]
     span = NB * BLK
     grid_spec = pltpu.PrefetchScalarGridSpec(
         num_scalar_prefetch=2,
         grid=(steps,),
         in_specs=[
             pl.BlockSpec(memory_space=pltpu.SMEM),
-            pl.BlockSpec((1, BLK, width_q), lambda g, n, c: (g + g0, 0, 0)),
-            pl.BlockSpec((1, BLK, span), lambda g, n, c: (g + g0, 0, 0)),
+            pl.BlockSpec((1, BLK, width_q), lambda g, n, c: (g, 0, p0)),
+            pl.BlockSpec((1, BLK, span), lambda g, n, c: (g, 0, 0)),
             pl.BlockSpec(kv_table.shape, lambda g, n, c: (0, 0, 0)),
         ],
         out_specs=pl.BlockSpec((1, BLK, width_q), lambda g, n, c: (g, 0, 0)),
     )
     return pl.pallas_call(
-        functools.partial(_attend_kernel, g0),
+        functools.partial(_attend_kernel, p0),
         grid_spec=grid_spec,
         out_shape=jax.ShapeDtypeStruct((steps, BLK, width_q), jnp.bfloat16),
         compiler_params=pltpu.CompilerParams(
@@ -100,14 +98,13 @@
     head_devs = lax.axis_size("head")
     row_devs = lax.axis_size("row")
     me = lax.axis_index("head")
+    chunk = 128
+    chunks = width_heads // chunk
     req, pos = plan_requests(neighbours, blocks_dev, row_devs)
     wanted = lax.all_to_all(req, "row", 0, 0, tiled=True).reshape(-1)
     queries = jnp.dot(features, w_qkv[0], preferred_element_type=jnp.float32).astype(jnp.bfloat16)
     keys = jnp.dot(features, w_qkv[1], preferred_element_type=jnp.float32).astype(jnp.bfloat16)
     values = jnp.dot(features, w_qkv[2], preferred_element_type=jnp.float32).astype(jnp.bfloat16)
-    kv = jnp.concatenate([keys, values], axis=1).reshape(blocks_dev, BLK, 2 * width_heads)
-    outgoing = jnp.take(kv, wanted, axis=0, mode="clip")
-    kv_table = lax.all_to_all(outgoing, "row", 0, 0, tiled=True)
     w_parts = []
     for s in range(1, head_devs):
         target = (me + s) % head_devs
@@ -116,19 +113,29 @@
         w_parts.append(lax.ppermute(piece, "head", perm))
     w_own = lax.dynamic_slice_in_dim(w_out, me * width_heads, width_heads, axis=1)
     q_blocks = queries.reshape(blocks_dev, BLK, width_heads)
-    halves = 2
-    steps = blocks_dev // halves
-    results = []
-    for part in range(halves):
-        att = attend(pos, counts, bias_gain, q_blocks, edge_bias, kv_table, part * steps, steps)
-        att = att.reshape(steps * BLK, width_heads)
-        total = jnp.dot(att, w_own, preferred_element_type=jnp.float32)
+    outgoing = []
+    for c in range(chunks):
+        cols = slice(c * chunk, (c + 1) * chunk)
+        kv = jnp.concatenate([keys[:, cols], values[:, cols]], axis=1)
+        kv = kv.reshape(blocks_dev, BLK, 2 * chunk)
+        outgoing.append(jnp.take(kv, wanted, axis=0, mode="clip"))
+    total = None
+    table = None
+    for c in range(chunks):
+        cols = slice(c * chunk, (c + 1) * chunk)
+        send = outgoing[c]
+        if table is not None:
+            table, send = lax.optimization_barrier((table, send))
+        table = lax.all_to_all(send, "row", 0, 0, tiled=True)
+        att = attend(pos, counts, bias_gain, q_blocks, edge_bias, table, c, chunk)
+        att = att.reshape(rows, chunk)
+        part = jnp.dot(att, w_own[cols], preferred_element_type=jnp.float32)
+        total = part if total is None else total + part
         for s in range(1, head_devs):
             perm = [(i, (i + s) % head_devs) for i in range(head_devs)]
             att_s = lax.ppermute(att, "head", perm)
-            total = total + jnp.dot(att_s, w_parts[s - 1], preferred_element_type=jnp.float32)
-        results.append(total.astype(jnp.bfloat16))
-    return jnp.concatenate(results, axis=0)
+            total = total + jnp.dot(att_s, w_parts[s - 1][cols], preferred_element_type=jnp.float32)
+    return total.astype(jnp.bfloat16)
 
 
 def solution(mesh):

time: 139 us -> 134 us (0.964)
  waiting for transfers between devices: 48.5 us -> 31.5 us
  matrix products: 6.02 us -> 15.5 us
  local copies, waits for them, and re-layouts: 11 us -> 14.2 us
  starting transfers between devices: 30.1 us -> 33.3 us
  Pallas kernels: 39.8 us -> 37 us
    all_to_all x1 -> x2, waiting for transfers between devices: 40.4 us -> 24.8 us  [body(): table = lax.all_to_all(send, 'row', 0, 0, tiled=True)]
    dot_general x8, matrix products: 1.49 us -> 10.8 us  [the longest x6 8.69 us: body(): jnp.dot(att_s, w_parts[s - 1][cols], preferred_element_type=jnp.float32)]
    all_to_all x1 -> x2, starting transfers between devices: 6.02 us -> 11.3 us  [body(): table = lax.all_to_all(send, 'row', 0, 0, tiled=True)]
    pallas_call x2, Pallas kernels: 39.8 us -> 37 us  [attend(): pl.pallas_call(functools.partial(_attend_kernel, p0), grid_spec=grid_spec...]
    ppermute x6, starting transfers between devices: 10.5 us -> 8.46 us  [body(): att_s = lax.ppermute(att, 'head', perm)]
    dynamic_slice x1, local copies, waits for them, and re-layouts: 0.06 us -> 1.79 us  [body(): lax.dynamic_slice_in_dim(w_out, target * width_heads, width_heads, axis=1)]
    gather x1 -> x2, local copies, waits for them, and re-layouts: 2.79 us -> 4.03 us  [body(): outgoing.append(jnp.take(kv, wanted, axis=0, mode='clip'))]
  transfers between devices with their start and end apart: 11 -> 12, of which waited for: 4 -> 4; matrix products, arithmetic and copies ran while one was open for 7% -> 17% of each run, Pallas kernels for 29% -> 28%
where the time goes in v7:
time: 134 us; the launch traced here: 133 us
  Pallas kernels  37 us (28%)
  starting transfers between devices  33.3 us (25%)
  waiting for transfers between devices  31.5 us (24%)
  matrix products  15.5 us (12%)
  local copies, waits for them, and re-layouts  14.2 us (11%)
  other arithmetic  1.65 us (1%)
    pallas_call x2, Pallas kernels, attend(): pl.pallas_call(functools.partial(_attend_kernel, p0), grid_spec=grid_spec...  37 us
    all_to_all x2, waiting for transfers between devices, body(): table = lax.all_to_all(send, 'row', 0, 0, tiled=True)  24.8 us
    all_to_all x2, starting transfers between devices, body(): table = lax.all_to_all(send, 'row', 0, 0, tiled=True)  11.3 us
    dot_general x6, matrix products, body(): jnp.dot(att_s, w_parts[s - 1][cols], preferred_element_type=jnp.float32)  8.69 us
    ppermute x6, starting transfers between devices, body(): att_s = lax.ppermute(att, 'head', perm)  8.46 us
    all_to_all x1, starting transfers between devices, body(): wanted = lax.all_to_all(req, 'row', 0, 0, tiled=True).reshape(-1)  7.62 us
    ppermute x3, starting transfers between devices, body(): w_parts.append(lax.ppermute(piece, 'head', perm))  5.9 us
    ppermute x6, waiting for transfers between devices, body(): att_s = lax.ppermute(att, 'head', perm)  4.56 us
  transfers between devices with their start and end apart: 12, of which 4 were waited for; matrix products, arithmetic and copies ran while one was open for 17% of the time, Pallas kernels for 28%

profile of v7, /device:TPU:2, one launch (start us, length us, event | category | flops | bytes accessed | tf_op | source)
XLA Modules:
  0.0 133.5 jit_solution(14348323873420576152)
XLA Ops:
  0.0 0.0 copy-start
  0.0 0.8 eq.42
  0.9 0.2 fusion.11
  1.0 0.1 reshape.48
  1.1 0.1 select_reduce_fusion
  1.3 0.7 copy.16
  2.0 7.6 %all-to-all-start = ((s32[32,1,2]{2,1,0:T(1,128)}), s32[32,1,2]{2,1,0:T(1,128)S(1)}, u32[]{:S(2)}, u32[]{:S(2)}) async-start(s32[32,1,2]{2,1,0:T(1,128)} %copy.16), calls=%async_computation | async-start | bytes 32768 | tf_op jit(solution)/shard_map/all_to_all | solution.py:104
  9.6 0.0 copy-done
  9.6 1.5 %convolution_convert_fusion.1 = bf16[512,256]{0,1:T(8,128)(2,1)S(1)} fusion(bf16[512,1024]{1,0:T(8,128)(2,1)S(1)} %copy-done, bf16[3,1024,256]{2,1,0:T(8,128)(2,1)} %param.8), kind=kOutput, calls=%fused_computation.12 | convolution fusion | flops 268566528 | bytes 1835008 | tf_op jit(solution)/shard_map/dot_general | solution.py:106
  11.1 1.5 %convolution_convert_fusion = bf16[512,256]{0,1:T(8,128)(2,1)S(1)} fusion(bf16[512,1024]{1,0:T(8,128)(2,1)S(1)} %copy-done, bf16[3,1024,256]{2,1,0:T(8,128)(2,1)} %param.8), kind=kOutput, calls=%fused_computation.11 | convolution fusion | flops 268566528 | bytes 1835008 | tf_op jit(solution)/shard_map/dot_general | solution.py:107
  12.7 0.7 pad_maximum_fusion
  13.5 0.1 copy.15
  13.6 2.1 %all-to-all-done = s32[32,1,2]{2,1,0:T(1,128)S(1)} async-done(((s32[32,1,2]{2,1,0:T(1,128)}), s32[32,1,2]{2,1,0:T(1,128)S(1)}, u32[]{:S(2)}, u32[]{:S(2)}) %all-to-all-start) | async-done | bytes 288 | tf_op jit(solution)/shard_map/all_to_all | solution.py:104
  15.7 0.5 broadcast.72
  16.2 0.6 reduce.3
  16.8 0.1 reshape.64
  16.9 2.0 %gather_fusion.1 = bf16[64,64,256]{2,1,0:T(8,128)(2,1)} fusion(bf16[8,64,256]{2,1,0:T(8,128)(2,1)S(1)} %bitcast.43, s32[1024]{0:T(1024)S(1)} %pad_clamp_fusion), kind=kCustom, calls=%fused_computation.1 | custom fusion | bytes 4194560 | tf_op jit(solution)/shard_map/jit(_take)/gather | solution.py:121
  18.9 5.2 %all-to-all-start.1 = ((bf16[64,64,256]{2,1,0:T(8,128)(2,1)}), bf16[64,64,256]{2,1,0:T(8,128)(2,1)S(1)}, u32[]{:S(2)}, u32[]{:S(2)}) async-start(bf16[64,64,256]{2,1,0:T(8,128)(2,1)} %gather_fusion.1), calls=%async_computation.1 | async-start | bytes 4194304 | tf_op jit(solution)/shard_map/all_to_all | solution.py:129
  24.2 1.1 copy.17
  25.3 2.0 %gather_fusion.2 = bf16[64,64,256]{2,1,0:T(8,128)(2,1)} fusion(bf16[8,64,256]{2,1,0:T(8,128)(2,1)S(1)} %bitcast.44, s32[1024]{0:T(1024)S(1)} %pad_clamp_fusion), kind=kCustom, calls=%fused_computation.2 | custom fusion | bytes 4194560 | tf_op jit(solution)/shard_map/jit(_take)/gather | solution.py:121
  27.3 24.8 %all-to-all-done.1.kv_ref = bf16[64,64,256]{2,1,0:T(8,128)(2,1)S(1)} async-done(((bf16[64,64,256]{2,1,0:T(8,128)(2,1)}), bf16[64,64,256]{2,1,0:T(8,128)(2,1)S(1)}, u32[]{:S(2)}, u32[]{:S(2)}) %all-to-all-start.1) | async-done | bytes 2097184 | tf_op jit(solution)/shard_map/all_to_all | solution.py:129
  52.1 1.3 copy-done.1
  53.4 6.0 %all-to-all-start.2 = ((bf16[64,64,256]{2,1,0:T(8,128)(2,1)}), bf16[64,64,256]{2,1,0:T(8,128)(2,1)S(1)}, u32[]{:S(2)}, u32[]{:S(2)}) async-start(bf16[64,64,256]{2,1,0:T(8,128)(2,1)} %gather_fusion.2), calls=%async_computation.2 | async-start | bytes 4194304 | tf_op jit(solution)/shard_map/all_to_all | solution.py:129
  59.5 1.8 %constant_dynamic-slice_fusion.2 = (bf16[256,256]{1,0:T(8,128)(2,1)}, bf16[256,256]{1,0:T(8,128)(2,1)}, bf16[256,256]{1,0:T(8,128)(2,1)}) fusion(bf16[256,1024]{1,0:T(8,128)(2,1)} %param.9, s32[]{:T(128)S(6)} %select_n.86, s32[]{:T(128)S(6)} %select_n.90, s32[]{:T(128)S(6)} %select_n.88), kind=kLoop, calls=%fused_computation.59 | loop fusion | bytes 786444 | tf_op jit(solution)/shard_map/dynamic_slice | solution.py:111
  61.3 1.9 %collective-permute-start.1 = (bf16[256,256]{1,0:T(8,128)(2,1)}, bf16[256,256]{1,0:T(8,128)(2,1)}, u32[]{:S(2)}, u32[]{:S(2)}) collective-permute-start(bf16[256,256]{1,0:T(8,128)(2,1)} %get-tuple-element.9), channel_id=1, source_target_pairs={{0,1},{1,2},{2,3},{3,0},{4,5},{5,6},{6,7},{7,4},{8,9},{9,10},{10,1... | collective-permute-start | bytes 393224 | tf_op jit(solution)/shard_map/ppermute | solution.py:113
  63.2 2.1 %collective-permute-start.5 = (bf16[256,256]{1,0:T(8,128)(2,1)}, bf16[256,256]{1,0:T(8,128)(2,1)}, u32[]{:S(2)}, u32[]{:S(2)}) collective-permute-start(bf16[256,256]{1,0:T(8,128)(2,1)} %get-tuple-element.10), channel_id=1, source_target_pairs={{0,3},{1,0},{2,1},{3,2},{4,7},{5,4},{6,5},{7,6},{8,11},{9,8},{10,9... | collective-permute-start | bytes 393224 | tf_op jit(solution)/shard_map/ppermute | solution.py:113
  65.4 1.9 %collective-permute-start.3 = (bf16[256,256]{1,0:T(8,128)(2,1)}, bf16[256,256]{1,0:T(8,128)(2,1)}, u32[]{:S(2)}, u32[]{:S(2)}) collective-permute-start(bf16[256,256]{1,0:T(8,128)(2,1)} %get-tuple-element.11), channel_id=1, source_target_pairs={{0,2},{1,3},{2,0},{3,1},{4,6},{5,7},{6,4},{7,5},{8,10},{9,11},{10,... | collective-permute-start | bytes 393224 | tf_op jit(solution)/shard_map/ppermute | solution.py:113
  67.2 0.0 copy-done.7
  67.2 0.1 reshape.56
  67.3 3.3 %gather_fusion = s32[512]{0:T(512)S(1)} fusion(s32[32]{0:T(128)S(1)} %compare_select_fusion.3, s32[1024]{0:T(1024)S(1)} %pad_clamp_fusion.1), kind=kCustom, calls=%fused_computation | custom fusion | bytes 6144 | tf_op jit(solution)/shard_map/gather | solution.py:90
  70.7 0.0 copy-start.3
  70.7 0.0 copy-start.4
  70.7 0.1 reshape.55
  70.8 1.6 %convolution_convert_fusion.2 = bf16[512,256]{1,0:T(8,128)(2,1)S(1)} fusion(bf16[512,1024]{1,0:T(8,128)(2,1)S(1)} %copy-done, bf16[3,1024,256]{2,1,0:T(8,128)(2,1)} %param.8), kind=kOutput, calls=%fused_computation.13 | convolution fusion | flops 268566528 | bytes 1835008 | tf_op jit(solution)/shard_map/dot_general | solution.py:105
  72.4 0.0 copy-done.3
  72.4 0.0 copy-done.4
  72.5 0.1 copy-done.2
  72.5 18.5 %shard_map.73 = bf16[8,64,128]{2,1,0:T(8,128)(2,1)S(1)} custom-call(s32[8,64]{1,0:T(8,128)S(1)} %convert_add_fusion.nbr_ref, s32[8]{0:T(128)S(1)} %copy-done.3, f32[4]{0:T(128)S(1)} %copy-done.4, bf16[8,64,256]{2,1,0:T(8,128)(2,1)S(1)} %bitcast.33, bf16[8,64,4096]{2,1,0:T(8,128)(2,1)} %bias_ref.3, bf16[64,64,256]{2,1,0:T(8,128)(2,1)S(1)} %copy-done.2), custom_call_target="tpu_custom_call" | custom-call | tf_op jit(solution)/shard_map/pallas_call | solution.py:68
  91.0 1.1 collective-permute-start
  92.1 2.2 %collective-permute-start.4 = (bf16[512,128]{1,0:T(8,128)(2,1)S(1)}, bf16[512,128]{1,0:T(8,128)(2,1)S(1)}, u32[]{:S(2)}, u32[]{:S(2)}) collective-permute-start(bf16[512,128]{1,0:T(8,128)(2,1)S(1)} %bitcast.36), channel_id=1, source_target_pairs={{0,3},{1,0},{2,1},{3,2},{4,7},{5,4},{6,5},{7,6},{8,11},{9,8},{10,9... | collective-permute-start | bytes 393224 | tf_op jit(solution)/shard_map/ppermute | solution.py:136
  94.3 1.0 fusion.23
  95.4 0.0 collective-permute-done.5
  95.4 0.5 collective-permute-start.2
  95.9 3.5 %collective-permute-done.4 = bf16[512,128]{1,0:T(8,128)(2,1)S(1)} collective-permute-done((bf16[512,128]{1,0:T(8,128)(2,1)S(1)}, bf16[512,128]{1,0:T(8,128)(2,1)S(1)}, u32[]{:S(2)}, u32[]{:S(2)}) %collective-permute-start.4) | collective-permute-done | bytes 131104 | tf_op jit(solution)/shard_map/ppermute | solution.py:136
  99.4 1.9 %fusion.19 = f32[512,256]{1,0:T(8,128)} fusion(bf16[512,128]{1,0:T(8,128)(2,1)S(1)} %collective-permute-done.4, bf16[256,256]{1,0:T(8,128)(2,1)} %collective-permute-done.5), kind=kOutput, calls=%fused_computation.31 | convolution fusion | flops 33554432 | bytes 720896 | tf_op jit(solution)/shard_map/dot_general | solution.py:137
  101.3 0.0 collective-permute-done.1
  101.3 0.0 collective-permute-done
  101.3 1.9 %convolution_add_fusion.2 = f32[512,256]{1,0:T(8,128)} fusion(f32[512,256]{1,0:T(8,128)S(1)} %fusion.23, bf16[512,128]{1,0:T(8,128)(2,1)S(1)} %collective-permute-done, bf16[256,256]{1,0:T(8,128)(2,1)} %collective-permute-done.1), kind=kOutput, calls=%fused_computation.5 | convolution fusion | flops 33685504 | bytes 1245184 | tf_op jit(solution)/shard_map/dot_general | solution.py:137
  103.1 0.0 all-to-all-done.2.kv_ref
  103.1 18.5 %shard_map.74 = bf16[8,64,128]{2,1,0:T(8,128)(2,1)S(1)} custom-call(s32[8,64]{1,0:T(8,128)S(1)} %convert_add_fusion.nbr_ref, s32[8]{0:T(128)S(1)} %copy-done.3, f32[4]{0:T(128)S(1)} %copy-done.4, bf16[8,64,256]{2,1,0:T(8,128)(2,1)S(1)} %bitcast.34, bf16[8,64,4096]{2,1,0:T(8,128)(2,1)} %bias_ref.3, bf16[64,64,256]{2,1,0:T(8,128)(2,1)S(1)} %all-to-all-done.2.kv_ref), custom_call_target="tpu_custom_call" | custom-call | tf_op jit(solution)/shard_map/pallas_call | solution.py:68
  121.6 0.1 collective-permute-start.7
  121.7 3.7 %collective-permute-start.8 = (bf16[512,128]{1,0:T(8,128)(2,1)S(1)}, bf16[512,128]{1,0:T(8,128)(2,1)S(1)}, u32[]{:S(2)}, u32[]{:S(2)}) collective-permute-start(bf16[512,128]{1,0:T(8,128)(2,1)S(1)} %bitcast.40), channel_id=1, source_target_pairs={{0,3},{1,0},{2,1},{3,2},{4,7},{5,4},{6,5},{7,6},{8,11},{9,8},{10,9... | collective-permute-start | bytes 393224 | tf_op jit(solution)/shard_map/ppermute | solution.py:136
  125.5 0.8 collective-permute-start.6
  126.3 1.0 fusion.17
  127.3 0.0 collective-permute-done.3
  127.3 0.0 collective-permute-done.2
  127.3 0.0 copy-done.5
  127.3 1.1 fusion.1
  128.5 0.0 collective-permute-done.7
  128.5 1.0 fusion.14
  129.5 1.1 collective-permute-done.8
  130.6 1.0 fusion.12
  131.7 0.0 collective-permute-done.6
  131.7 1.8 %fusion.4 = bf16[512,256]{1,0:T(8,128)(2,1)} fusion(f32[512,256]{1,0:T(8,128)S(1)} %fusion.12, f32[512,256]{1,0:T(8,128)S(1)} %fusion.14, f32[512,256]{1,0:T(8,128)S(1)} %fusion.1, bf16[512,128]{1,0:T(8,128)(2,1)S(1)} %collective-permute-done.6, bf16[256,256]{1,0:T(8,128)(2,1)} %collective-permute-done.1), kind=kOutput, calls=%fused_computation.10 | convolution fusion | flops 34078720 | bytes 2031616 | tf_op jit(solution)/shard_map/dot_general | solution.py:137
  (15 shorter events, 0.1 us)
Async XLA Ops:
  0.0 9.6 %copy-start = (bf16[512,1024]{1,0:T(8,128)(2,1)S(1)}, bf16[512,1024]{1,0:T(8,128)(2,1)}, u32[]{:S(2)}) copy-start(bf16[512,1024]{1,0:T(8,128)(2,1)} %param.7) | copy-start | bytes 3145732
  2.0 13.8 %all-to-all-start = ((s32[32,1,2]{2,1,0:T(1,128)}), s32[32,1,2]{2,1,0:T(1,128)S(1)}, u32[]{:S(2)}, u32[]{:S(2)}) async-start(s32[32,1,2]{2,1,0:T(1,128)} %copy.16), calls=%async_computation | async-start | bytes 32768 | tf_op jit(solution)/shard_map/all_to_all | solution.py:104
  18.9 33.2 %all-to-all-start.1 = ((bf16[64,64,256]{2,1,0:T(8,128)(2,1)}), bf16[64,64,256]{2,1,0:T(8,128)(2,1)S(1)}, u32[]{:S(2)}, u32[]{:S(2)}) async-start(bf16[64,64,256]{2,1,0:T(8,128)(2,1)} %gather_fusion.1), calls=%async_computation.1 | async-start | bytes 4194304 | tf_op jit(solution)/shard_map/all_to_all | solution.py:129
  27.3 39.9 %copy-start.7 = (s32[8,64]{1,0:T(8,128)S(1)}, s32[8,64]{1,0:T(8,128)}, u32[]{:S(2)}) copy-start(s32[8,64]{1,0:T(8,128)} %param.12) | copy-start | bytes 6148
  52.1 1.3 copy-start.1
  53.4 49.7 %all-to-all-start.2 = ((bf16[64,64,256]{2,1,0:T(8,128)(2,1)}), bf16[64,64,256]{2,1,0:T(8,128)(2,1)S(1)}, u32[]{:S(2)}, u32[]{:S(2)}) async-start(bf16[64,64,256]{2,1,0:T(8,128)(2,1)} %gather_fusion.2), calls=%async_computation.2 | async-start | bytes 4194304 | tf_op jit(solution)/shard_map/all_to_all | solution.py:129
  61.3 39.9 %collective-permute-start.1 = (bf16[256,256]{1,0:T(8,128)(2,1)}, bf16[256,256]{1,0:T(8,128)(2,1)}, u32[]{:S(2)}, u32[]{:S(2)}) collective-permute-start(bf16[256,256]{1,0:T(8,128)(2,1)} %get-tuple-element.9), channel_id=1, source_target_pairs={{0,1},{1,2},{2,3},{3,0},{4,5},{5,6},{6,7},{7,4},{8,9},{9,10},{10,1... | collective-permute-start | bytes 393224 | tf_op jit(solution)/shard_map/ppermute | solution.py:113
  63.2 32.2 %collective-permute-start.5 = (bf16[256,256]{1,0:T(8,128)(2,1)}, bf16[256,256]{1,0:T(8,128)(2,1)}, u32[]{:S(2)}, u32[]{:S(2)}) collective-permute-start(bf16[256,256]{1,0:T(8,128)(2,1)} %get-tuple-element.10), channel_id=1, source_target_pairs={{0,3},{1,0},{2,1},{3,2},{4,7},{5,4},{6,5},{7,6},{8,11},{9,8},{10,9... | collective-permute-start | bytes 393224 | tf_op jit(solution)/shard_map/ppermute | solution.py:113
  65.4 61.9 %collective-permute-start.3 = (bf16[256,256]{1,0:T(8,128)(2,1)}, bf16[256,256]{1,0:T(8,128)(2,1)}, u32[]{:S(2)}, u32[]{:S(2)}) collective-permute-start(bf16[256,256]{1,0:T(8,128)(2,1)} %get-tuple-element.11), channel_id=1, source_target_pairs={{0,2},{1,3},{2,0},{3,1},{4,6},{5,7},{6,4},{7,5},{8,10},{9,11},{10,... | collective-permute-start | bytes 393224 | tf_op jit(solution)/shard_map/ppermute | solution.py:113
  70.7 1.8 %copy-start.3 = (s32[8]{0:T(128)S(1)}, s32[8]{0:T(128)}, u32[]{:S(2)}) copy-start(s32[8]{0:T(128)} %cnt_ref.3) | copy-start | bytes 100
  70.7 1.8 %copy-start.4 = (f32[4]{0:T(128)S(1)}, f32[4]{0:T(128)}, u32[]{:S(2)}) copy-start(f32[4]{0:T(128)} %gain_ref.3) | copy-start | bytes 52
  70.8 1.7 %copy-start.2 = (bf16[64,64,256]{2,1,0:T(8,128)(2,1)S(1)}, bf16[64,64,256]{2,1,0:T(8,128)(2,1)}, u32[]{:S(2)}) copy-start(bf16[64,64,256]{2,1,0:T(8,128)(2,1)} %copy-done.1) | copy-start | bytes 6291460
  91.0 10.2 %collective-permute-start = (bf16[512,128]{1,0:T(8,128)(2,1)S(1)}, bf16[512,128]{1,0:T(8,128)(2,1)S(1)}, u32[]{:S(2)}, u32[]{:S(2)}) collective-permute-start(bf16[512,128]{1,0:T(8,128)(2,1)S(1)} %bitcast.35), channel_id=1, source_target_pairs={{0,1},{1,2},{2,3},{3,0},{4,5},{5,6},{6,7},{7,4},{8,9},{9,10},{10,1... | collective-permute-start | bytes 393224 | tf_op jit(solution)/shard_map/ppermute | solution.py:136
  92.1 7.3 %collective-permute-start.4 = (bf16[512,128]{1,0:T(8,128)(2,1)S(1)}, bf16[512,128]{1,0:T(8,128)(2,1)S(1)}, u32[]{:S(2)}, u32[]{:S(2)}) collective-permute-start(bf16[512,128]{1,0:T(8,128)(2,1)S(1)} %bitcast.36), channel_id=1, source_target_pairs={{0,3},{1,0},{2,1},{3,2},{4,7},{5,4},{6,5},{7,6},{8,11},{9,8},{10,9... | collective-permute-start | bytes 393224 | tf_op jit(solution)/shard_map/ppermute | solution.py:136
  95.4 31.9 %collective-permute-start.2 = (bf16[512,128]{1,0:T(8,128)(2,1)S(1)}, bf16[512,128]{1,0:T(8,128)(2,1)}, u32[]{:S(2)}, u32[]{:S(2)}) collective-permute-start(bf16[512,128]{1,0:T(8,128)(2,1)S(1)} %bitcast.38), channel_id=1, source_target_pairs={{0,2},{1,3},{2,0},{3,1},{4,6},{5,7},{6,4},{7,5},{8,10},{9,11},{10,... | collective-permute-start | bytes 393224 | tf_op jit(solution)/shard_map/ppermute | solution.py:136
  103.1 24.2 %copy-start.5 = (f32[512,256]{1,0:T(8,128)S(1)}, f32[512,256]{1,0:T(8,128)}, u32[]{:S(2)}) copy-start(f32[512,256]{1,0:T(8,128)} %fusion.19) | copy-start | bytes 1572868
  103.1 24.2 %copy-start.6 = (f32[512,256]{1,0:T(8,128)S(1)}, f32[512,256]{1,0:T(8,128)}, u32[]{:S(2)}) copy-start(f32[512,256]{1,0:T(8,128)} %convolution_add_fusion.2) | copy-start | bytes 1572868
  121.6 6.8 %collective-permute-start.7 = (bf16[512,128]{1,0:T(8,128)(2,1)S(1)}, bf16[512,128]{1,0:T(8,128)(2,1)S(1)}, u32[]{:S(2)}, u32[]{:S(2)}) collective-permute-start(bf16[512,128]{1,0:T(8,128)(2,1)S(1)} %bitcast.39), channel_id=1, source_target_pairs={{0,2},{1,3},{2,0},{3,1},{4,6},{5,7},{6,4},{7,5},{8,10},{9,11},{10,... | collective-permute-start | bytes 393224 | tf_op jit(solution)/shard_map/ppermute | solution.py:136
  121.7 8.9 %collective-permute-start.8 = (bf16[512,128]{1,0:T(8,128)(2,1)S(1)}, bf16[512,128]{1,0:T(8,128)(2,1)S(1)}, u32[]{:S(2)}, u32[]{:S(2)}) collective-permute-start(bf16[512,128]{1,0:T(8,128)(2,1)S(1)} %bitcast.40), channel_id=1, source_target_pairs={{0,3},{1,0},{2,1},{3,2},{4,7},{5,4},{6,5},{7,6},{8,11},{9,8},{10,9... | collective-permute-start | bytes 393224 | tf_op jit(solution)/shard_map/ppermute | solution.py:136
  125.5 6.2 %collective-permute-start.6 = (bf16[512,128]{1,0:T(8,128)(2,1)S(1)}, bf16[512,128]{1,0:T(8,128)(2,1)S(1)}, u32[]{:S(2)}, u32[]{:S(2)}) collective-permute-start(bf16[512,128]{1,0:T(8,128)(2,1)S(1)} %bitcast.41), channel_id=1, source_target_pairs={{0,1},{1,2},{2,3},{3,0},{4,5},{5,6},{6,7},{7,4},{8,9},{9,10},{10,1... | collective-permute-start | bytes 393224 | tf_op jit(solution)/shard_map/ppermute | solution.py:136

commit v8 on v7

--- a/solution.py
+++ b/solution.py
@@ -105,13 +105,8 @@
     queries = jnp.dot(features, w_qkv[0], preferred_element_type=jnp.float32).astype(jnp.bfloat16)
     keys = jnp.dot(features, w_qkv[1], preferred_element_type=jnp.float32).astype(jnp.bfloat16)
     values = jnp.dot(features, w_qkv[2], preferred_element_type=jnp.float32).astype(jnp.bfloat16)
-    w_parts = []
-    for s in range(1, head_devs):
-        target = (me + s) % head_devs
-        piece = lax.dynamic_slice_in_dim(w_out, target * width_heads, width_heads, axis=1)
-        perm = [(i, (i + s) % head_devs) for i in range(head_devs)]
-        w_parts.append(lax.ppermute(piece, "head", perm))
-    w_own = lax.dynamic_slice_in_dim(w_out, me * width_heads, width_heads, axis=1)
+    w_full = lax.all_gather(w_out, "head", axis=0, tiled=True)
+    w_cols = lax.dynamic_slice_in_dim(w_full, me * width_heads, width_heads, axis=1)
     q_blocks = queries.reshape(blocks_dev, BLK, width_heads)
     outgoing = []
     for c in range(chunks):
@@ -119,23 +114,29 @@
         kv = jnp.concatenate([keys[:, cols], values[:, cols]], axis=1)
         kv = kv.reshape(blocks_dev, BLK, 2 * chunk)
         outgoing.append(jnp.take(kv, wanted, axis=0, mode="clip"))
-    total = None
+    pieces = []
+    w_pieces = []
     table = None
     for c in range(chunks):
-        cols = slice(c * chunk, (c + 1) * chunk)
         send = outgoing[c]
         if table is not None:
             table, send = lax.optimization_barrier((table, send))
         table = lax.all_to_all(send, "row", 0, 0, tiled=True)
         att = attend(pos, counts, bias_gain, q_blocks, edge_bias, table, c, chunk)
         att = att.reshape(rows, chunk)
-        part = jnp.dot(att, w_own[cols], preferred_element_type=jnp.float32)
-        total = part if total is None else total + part
-        for s in range(1, head_devs):
-            perm = [(i, (i + s) % head_devs) for i in range(head_devs)]
-            att_s = lax.ppermute(att, "head", perm)
-            total = total + jnp.dot(att_s, w_parts[s - 1][cols], preferred_element_type=jnp.float32)
-    return total.astype(jnp.bfloat16)
+        for s in range(head_devs):
+            if s == 0:
+                pieces.append(att)
+            else:
+                perm = [(i, (i + s) % head_devs) for i in range(head_devs)]
+                pieces.append(lax.ppermute(att, "head", perm))
+            src = (me - s) % head_devs
+            w_pieces.append(
+                lax.dynamic_slice_in_dim(w_cols, src * width_heads + c * chunk, chunk, axis=0)
+            )
+    att_all = jnp.concatenate(pieces, axis=1)
+    w_all = jnp.concatenate(w_pieces, axis=0)
+    return jnp.dot(att_all, w_all, preferred_element_type=jnp.float32).astype(jnp.bfloat16)
 
 
 def solution(mesh):

time: 134 us -> 157 us (1.17)
  local copies, waits for them, and re-layouts: 14.2 us -> 33.3 us
  between operations: 0.35 us -> 13.6 us
  matrix products: 15.5 us -> 7.03 us
  starting transfers between devices: 33.3 us -> 30.5 us
    unnamed x16 -> x26, local copies, waits for them, and re-layouts: 1.43 us -> 19.9 us
    dot_general x8 -> x1, matrix products: 10.8 us -> 2.5 us  [body(): jnp.dot(att_all, w_all, preferred_element_type=jnp.float32)]
    ppermute x9 -> x6, starting transfers between devices: 14.4 us -> 10.8 us  [body(): pieces.append(lax.ppermute(att, 'head', perm))]
    concatenate x0 -> x2, local copies, waits for them, and re-layouts: none -> 2.3 us  [the longest x1 1.61 us: body(): w_all = jnp.concatenate(w_pieces, axis=0)]
    dynamic_slice x1 -> x0, local copies, waits for them, and re-layouts: 1.79 us -> none  [body(): lax.dynamic_slice_in_dim(w_out, target * width_heads, width_heads, axis=1)]
    ppermute x9 -> x6, waiting for transfers between devices: 4.57 us -> 6.08 us  [body(): pieces.append(lax.ppermute(att, 'head', perm))]
  transfers between devices with their start and end apart: 12 -> 10, of which waited for: 4 -> 6; matrix products, arithmetic and copies ran while one was open for 17% -> 20% of each run, Pallas kernels for 28% -> 12%
where the time goes in v8:
time: 157 us; the launch traced here: 156 us
  Pallas kernels  37.4 us (24%)
  local copies, waits for them, and re-layouts  33.3 us (21%)
  waiting for transfers between devices  32.2 us (21%)
  starting transfers between devices  30.5 us (19%)
  between operations  13.6 us (9%)
  matrix products  7.03 us (4%)
  other arithmetic  2.41 us (2%)
    pallas_call x2, Pallas kernels, attend(): pl.pallas_call(functools.partial(_attend_kernel, p0), grid_spec=grid_spec...  37.4 us
    all_to_all x2, waiting for transfers between devices, body(): table = lax.all_to_all(send, 'row', 0, 0, tiled=True)  24.1 us
    unnamed x26, local copies, waits for them, and re-layouts  19.9 us
    all_to_all x2, starting transfers between devices, body(): table = lax.all_to_all(send, 'row', 0, 0, tiled=True)  12 us
    ppermute x6, starting transfers between devices, body(): pieces.append(lax.ppermute(att, 'head', perm))  10.8 us
    all_to_all x1, starting transfers between devices, body(): wanted = lax.all_to_all(req, 'row', 0, 0, tiled=True).reshape(-1)  7.62 us
    ppermute x6, waiting for transfers between devices, body(): pieces.append(lax.ppermute(att, 'head', perm))  6.08 us
    gather x2, local copies, waits for them, and re-layouts, body(): outgoing.append(jnp.take(kv, wanted, axis=0, mode='clip'))  4.02 us
  transfers between devices with their start and end apart: 10, of which 6 were waited for; matrix products, arithmetic and copies ran while one was open for 20% of the time, Pallas kernels for 12%

profile of v8, /device:TPU:2, one launch (start us, length us, event | category | flops | bytes accessed | tf_op | source)
XLA Modules:
  0.0 156.5 jit_solution(11535369152470582591)
XLA Ops:
  6.5 0.8 eq.47
  7.4 0.2 fusion.6
  7.5 0.1 reshape.48
  7.6 0.1 select_reduce_fusion
  7.8 0.7 copy.16
  8.5 7.6 %all-to-all-start = ((s32[32,1,2]{2,1,0:T(1,128)}), s32[32,1,2]{2,1,0:T(1,128)S(1)}, u32[]{:S(2)}, u32[]{:S(2)}) async-start(s32[32,1,2]{2,1,0:T(1,128)} %copy.16), calls=%async_computation | async-start | bytes 32768 | tf_op jit(solution)/shard_map/all_to_all | solution.py:104
  16.1 0.7 compare_select_fusion
  16.8 1.5 convolution_convert_fusion.2
  18.3 1.5 convolution_convert_fusion.1
  19.9 0.7 pad_maximum_fusion
  20.7 0.1 reshape.56
  20.8 0.1 copy.15
  20.9 1.4 all-to-all-done
  22.3 0.6 broadcast.73
  22.9 0.7 reduce.3
  23.5 0.1 reshape.64
  23.6 2.0 %gather_fusion.1 = bf16[64,64,256]{2,1,0:T(8,128)(2,1)} fusion(bf16[8,64,256]{2,1,0:T(8,128)(2,1)S(1)} %bitcast.37, s32[1024]{0:T(1024)S(1)} %get-tuple-element.15), kind=kCustom, calls=%fused_computation.1 | custom fusion | bytes 4194560 | tf_op jit(solution)/shard_map/jit(_take)/gather | solution.py:116
  25.7 6.0 %all-to-all-start.1 = ((bf16[64,64,256]{2,1,0:T(8,128)(2,1)}), bf16[64,64,256]{2,1,0:T(8,128)(2,1)S(1)}, u32[]{:S(2)}, u32[]{:S(2)}) async-start(bf16[64,64,256]{2,1,0:T(8,128)(2,1)} %gather_fusion.1), calls=%async_computation.1 | async-start | bytes 4194304 | tf_op jit(solution)/shard_map/all_to_all | solution.py:124
  31.7 0.0 all-gather.2.cloned.1.call-start
  31.7 0.7 all-gather.2.cloned.1.call-update
  32.4 1.1 copy.17
  33.5 2.0 %gather_fusion.2 = bf16[64,64,256]{2,1,0:T(8,128)(2,1)} fusion(bf16[8,64,256]{2,1,0:T(8,128)(2,1)S(1)} %bitcast.38, s32[1024]{0:T(1024)S(1)} %get-tuple-element.15), kind=kCustom, calls=%fused_computation.2 | custom fusion | bytes 4194560 | tf_op jit(solution)/shard_map/jit(_take)/gather | solution.py:116
  35.5 24.1 %all-to-all-done.1.kv_ref = bf16[64,64,256]{2,1,0:T(8,128)(2,1)S(1)} async-done(((bf16[64,64,256]{2,1,0:T(8,128)(2,1)}), bf16[64,64,256]{2,1,0:T(8,128)(2,1)S(1)}, u32[]{:S(2)}, u32[]{:S(2)}) %all-to-all-start.1) | async-done | bytes 2097184 | tf_op jit(solution)/shard_map/all_to_all | solution.py:124
  59.6 1.3 copy-done.1
  60.9 6.0 %all-to-all-start.2 = ((bf16[64,64,256]{2,1,0:T(8,128)(2,1)}), bf16[64,64,256]{2,1,0:T(8,128)(2,1)S(1)}, u32[]{:S(2)}, u32[]{:S(2)}) async-start(bf16[64,64,256]{2,1,0:T(8,128)(2,1)} %gather_fusion.2), calls=%async_computation.2 | async-start | bytes 4194304 | tf_op jit(solution)/shard_map/all_to_all | solution.py:124
  67.0 1.5 convolution_convert_fusion.3
  68.5 0.0 copy-start.5
  68.5 0.0 copy-start.3
  68.5 0.0 copy-start.4
  68.5 3.3 %gather_fusion = s32[512]{0:T(512)S(1)} fusion(s32[32]{0:T(128)S(1)} %compare_select_fusion.3, s32[1024]{0:T(1024)S(1)} %get-tuple-element.16), kind=kCustom, calls=%fused_computation | custom fusion | bytes 6144 | tf_op jit(solution)/shard_map/gather | solution.py:90
  71.9 0.1 reshape.55
  72.0 1.6 %copy-done.2 = bf16[64,64,256]{2,1,0:T(8,128)(2,1)S(1)} copy-done((bf16[64,64,256]{2,1,0:T(8,128)(2,1)S(1)}, bf16[64,64,256]{2,1,0:T(8,128)(2,1)}, u32[]{:S(2)}) %copy-start.2) | copy-done | bytes 2097176
  73.6 18.8 %shard_map.73 = bf16[8,64,128]{2,1,0:T(8,128)(2,1)S(1)} custom-call(s32[8,64]{1,0:T(8,128)S(1)} %convert_add_fusion.nbr_ref, s32[8]{0:T(128)S(1)} %copy-done.3, f32[4]{0:T(128)S(1)} %copy-done.4, bf16[8,64,256]{2,1,0:T(8,128)(2,1)S(1)} %bitcast.27, bf16[8,64,4096]{2,1,0:T(8,128)(2,1)} %bias_ref.3, bf16[64,64,256]{2,1,0:T(8,128)(2,1)S(1)} %copy-done.2), custom_call_target="tpu_custom_call" | custom-call | tf_op jit(solution)/shard_map/pallas_call | solution.py:68
  92.4 2.0 %collective-permute-start = (bf16[512,128]{1,0:T(8,128)(2,1)S(1)}, bf16[512,128]{1,0:T(8,128)(2,1)}, u32[]{:S(2)}, u32[]{:S(2)}) collective-permute-start(bf16[512,128]{1,0:T(8,128)(2,1)S(1)} %bitcast.29), channel_id=1, source_target_pairs={{0,1},{1,2},{2,3},{3,0},{4,5},{5,6},{6,7},{7,4},{8,9},{9,10},{10,1... | collective-permute-start | bytes 393224 | tf_op jit(solution)/shard_map/ppermute | solution.py:132
  94.4 3.6 %collective-permute-start.1 = (bf16[512,128]{1,0:T(8,128)(2,1)S(1)}, bf16[512,128]{1,0:T(8,128)(2,1)S(1)}, u32[]{:S(2)}, u32[]{:S(2)}) collective-permute-start(bf16[512,128]{1,0:T(8,128)(2,1)S(1)} %bitcast.30), channel_id=1, source_target_pairs={{0,2},{1,3},{2,0},{3,1},{4,6},{5,7},{6,4},{7,5},{8,10},{9,11},{10,... | collective-permute-start | bytes 393224 | tf_op jit(solution)/shard_map/ppermute | solution.py:132
  98.0 0.7 constant_dynamic-update-slice_fusion.7
  98.7 1.0 collective-permute-start.2
  99.7 0.7 collective-permute-done
  100.4 1.6 %constant_dynamic-update-slice_fusion.6 = bf16[512,1024]{1,0:T(8,128)(2,1)} fusion(bf16[512,1024]{1,0:T(8,128)(2,1)} %constant_dynamic-update-slice_fusion.7, bf16[512,128]{1,0:T(8,128)(2,1)} %collective-permute-done), kind=kLoop, calls=%fused_computation.31 | loop fusion | bytes 262144
  102.0 2.3 %collective-permute-done.1 = bf16[512,128]{1,0:T(8,128)(2,1)S(1)} collective-permute-done((bf16[512,128]{1,0:T(8,128)(2,1)S(1)}, bf16[512,128]{1,0:T(8,128)(2,1)S(1)}, u32[]{:S(2)}, u32[]{:S(2)}) %collective-permute-start.1) | collective-permute-done | bytes 131104 | tf_op jit(solution)/shard_map/ppermute | solution.py:132
  104.3 0.7 constant_dynamic-update-slice_fusion.5
  105.0 0.0 collective-permute-done.2
  105.0 0.7 constant_dynamic-update-slice_fusion.4
  105.7 1.6 %dynamic-slice_dynamic-update-slice_fusion.7 = bf16[1024,256]{1,0:T(8,128)(2,1)} fusion(bf16[1024,1024]{1,0:T(8,128)(2,1)} %all-gather.2.cloned.1.call-done, s32[]{:T(128)S(6)} %select_n.131, s32[]{:T(128)S(6)} %select_n.133), kind=kLoop, calls=%fused_computation.24 | loop fusion | bytes 131080
  107.3 1.6 %dynamic-slice_dynamic-update-slice_fusion.6 = bf16[1024,256]{1,0:T(8,128)(2,1)} fusion(bf16[1024,256]{1,0:T(8,128)(2,1)} %dynamic-slice_dynamic-update-slice_fusion.7, bf16[1024,1024]{1,0:T(8,128)(2,1)} %all-gather.2.cloned.1.call-done, s32[]{:T(128)S(6)} %select_n.136, s32[]{:T(128)S(6)} %select_n.133), kind=kLoop, calls=%fused_computation.23 | loop fusion | bytes 131080
  108.9 1.6 %dynamic-slice_dynamic-update-slice_fusion.5 = bf16[1024,256]{1,0:T(8,128)(2,1)} fusion(bf16[1024,256]{1,0:T(8,128)(2,1)} %dynamic-slice_dynamic-update-slice_fusion.6, bf16[1024,1024]{1,0:T(8,128)(2,1)} %all-gather.2.cloned.1.call-done, s32[]{:T(128)S(6)} %select_n.139, s32[]{:T(128)S(6)} %select_n.133), kind=kLoop, calls=%fused_computation.22 | loop fusion | bytes 131080
  110.5 1.6 %dynamic-slice_dynamic-update-slice_fusion.4 = bf16[1024,256]{1,0:T(8,128)(2,1)} fusion(bf16[1024,256]{1,0:T(8,128)(2,1)} %dynamic-slice_dynamic-update-slice_fusion.5, bf16[1024,1024]{1,0:T(8,128)(2,1)} %all-gather.2.cloned.1.call-done, s32[]{:T(128)S(6)} %select_n.142, s32[]{:T(128)S(6)} %select_n.133), kind=kLoop, calls=%fused_computation.21 | loop fusion | bytes 131080
  112.1 1.6 %dynamic-slice_dynamic-update-slice_fusion.3 = bf16[1024,256]{1,0:T(8,128)(2,1)} fusion(bf16[1024,256]{1,0:T(8,128)(2,1)} %dynamic-slice_dynamic-update-slice_fusion.4, bf16[1024,1024]{1,0:T(8,128)(2,1)} %all-gather.2.cloned.1.call-done, s32[]{:T(128)S(6)} %select_n.144, s32[]{:T(128)S(6)} %select_n.133), kind=kLoop, calls=%fused_computation.20 | loop fusion | bytes 131080
  113.7 1.6 %dynamic-slice_dynamic-update-slice_fusion.2 = bf16[1024,256]{1,0:T(8,128)(2,1)} fusion(bf16[1024,256]{1,0:T(8,128)(2,1)} %dynamic-slice_dynamic-update-slice_fusion.3, bf16[1024,1024]{1,0:T(8,128)(2,1)} %all-gather.2.cloned.1.call-done, s32[]{:T(128)S(6)} %select_n.146, s32[]{:T(128)S(6)} %select_n.133), kind=kLoop, calls=%fused_computation.19 | loop fusion | bytes 131080
  115.3 1.6 %dynamic-slice_dynamic-update-slice_fusion.1 = bf16[1024,256]{1,0:T(8,128)(2,1)} fusion(bf16[1024,256]{1,0:T(8,128)(2,1)} %dynamic-slice_dynamic-update-slice_fusion.2, bf16[1024,1024]{1,0:T(8,128)(2,1)} %all-gather.2.cloned.1.call-done, s32[]{:T(128)S(6)} %select_n.148, s32[]{:T(128)S(6)} %select_n.133), kind=kLoop, calls=%fused_computation.18 | loop fusion | bytes 131080
  117.0 0.0 all-to-all-done.2.kv_ref
  117.0 18.6 %shard_map.74 = bf16[8,64,128]{2,1,0:T(8,128)(2,1)S(1)} custom-call(s32[8,64]{1,0:T(8,128)S(1)} %convert_add_fusion.nbr_ref, s32[8]{0:T(128)S(1)} %copy-done.3, f32[4]{0:T(128)S(1)} %copy-done.4, bf16[8,64,256]{2,1,0:T(8,128)(2,1)S(1)} %bitcast.28, bf16[8,64,4096]{2,1,0:T(8,128)(2,1)} %bias_ref.3, bf16[64,64,256]{2,1,0:T(8,128)(2,1)S(1)} %all-to-all-done.2.kv_ref), custom_call_target="tpu_custom_call" | custom-call | tf_op jit(solution)/shard_map/pallas_call | solution.py:68
  135.5 1.0 collective-permute-start.3
  136.5 1.6 %dynamic-slice_dynamic-update-slice_fusion = bf16[1024,256]{1,0:T(8,128)(2,1)} fusion(bf16[1024,256]{1,0:T(8,128)(2,1)} %dynamic-slice_dynamic-update-slice_fusion.1, bf16[1024,1024]{1,0:T(8,128)(2,1)} %all-gather.2.cloned.1.call-done, s32[]{:T(128)S(6)} %select_n.150, s32[]{:T(128)S(6)} %select_n.133), kind=kLoop, calls=%fused_computation.17 | loop fusion | bytes 131080 | tf_op jit(solution)/shard_map/concatenate | solution.py:138
  138.1 2.0 %collective-permute-start.4 = (bf16[512,128]{1,0:T(8,128)(2,1)S(1)}, bf16[512,128]{1,0:T(8,128)(2,1)S(1)}, u32[]{:S(2)}, u32[]{:S(2)}) collective-permute-start(bf16[512,128]{1,0:T(8,128)(2,1)S(1)} %bitcast.34), channel_id=1, source_target_pairs={{0,2},{1,3},{2,0},{3,1},{4,6},{5,7},{6,4},{7,5},{8,10},{9,11},{10,... | collective-permute-start | bytes 393224 | tf_op jit(solution)/shard_map/ppermute | solution.py:132
  140.1 1.2 collective-permute-start.5
  141.3 0.7 constant_dynamic-update-slice_fusion.3
  142.0 0.0 collective-permute-done.3
  142.0 0.7 constant_dynamic-update-slice_fusion.2
  142.7 2.0 %collective-permute-done.4 = bf16[512,128]{1,0:T(8,128)(2,1)S(1)} collective-permute-done((bf16[512,128]{1,0:T(8,128)(2,1)S(1)}, bf16[512,128]{1,0:T(8,128)(2,1)S(1)}, u32[]{:S(2)}, u32[]{:S(2)}) %collective-permute-start.4) | collective-permute-done | bytes 131104 | tf_op jit(solution)/shard_map/ppermute | solution.py:132
  144.7 0.7 constant_dynamic-update-slice_fusion.1
  145.4 1.0 collective-permute-done.5
  146.5 0.7 constant_dynamic-update-slice_fusion
  147.1 2.5 %convolution_convert_fusion = bf16[512,256]{1,0:T(8,128)(2,1)} fusion(bf16[512,1024]{1,0:T(8,128)(2,1)} %constant_dynamic-update-slice_fusion, bf16[1024,256]{1,0:T(8,128)(2,1)} %dynamic-slice_dynamic-update-slice_fusion), kind=kOutput, calls=%fused_computation.3 | convolution fusion | flops 268566528 | bytes 1835008 | tf_op jit(solution)/shard_map/dot_general | solution.py:139
  (15 shorter events, 0.1 us)
Async XLA Ops:
  6.5 10.3 %copy-start = (bf16[512,1024]{1,0:T(8,128)(2,1)S(1)}, bf16[512,1024]{1,0:T(8,128)(2,1)}, u32[]{:S(2)}) copy-start(bf16[512,1024]{1,0:T(8,128)(2,1)} %param.7) | copy-start | bytes 3145732
  8.5 13.8 %all-to-all-start = ((s32[32,1,2]{2,1,0:T(1,128)}), s32[32,1,2]{2,1,0:T(1,128)S(1)}, u32[]{:S(2)}, u32[]{:S(2)}) async-start(s32[32,1,2]{2,1,0:T(1,128)} %copy.16), calls=%async_computation | async-start | bytes 32768 | tf_op jit(solution)/shard_map/all_to_all | solution.py:104
  25.7 33.9 %all-to-all-start.1 = ((bf16[64,64,256]{2,1,0:T(8,128)(2,1)}), bf16[64,64,256]{2,1,0:T(8,128)(2,1)S(1)}, u32[]{:S(2)}, u32[]{:S(2)}) async-start(bf16[64,64,256]{2,1,0:T(8,128)(2,1)} %gather_fusion.1), calls=%async_computation.1 | async-start | bytes 4194304 | tf_op jit(solution)/shard_map/all_to_all | solution.py:124
  31.7 74.0 %all-gather.2.cloned.1.call-start = ((), (), s32[]{:S(2)}) async-start(), calls=%async_computation.3 | async-start | bytes 2621440 | tf_op jit(solution)/shard_map/all_gather | solution.py:108
  59.6 1.3 copy-start.1
  60.9 56.0 %all-to-all-start.2 = ((bf16[64,64,256]{2,1,0:T(8,128)(2,1)}), bf16[64,64,256]{2,1,0:T(8,128)(2,1)S(1)}, u32[]{:S(2)}, u32[]{:S(2)}) async-start(bf16[64,64,256]{2,1,0:T(8,128)(2,1)} %gather_fusion.2), calls=%async_computation.2 | async-start | bytes 4194304 | tf_op jit(solution)/shard_map/all_to_all | solution.py:124
  68.5 3.5 %copy-start.5 = (s32[8,64]{1,0:T(8,128)S(1)}, s32[8,64]{1,0:T(8,128)}, u32[]{:S(2)}) copy-start(s32[8,64]{1,0:T(8,128)} %param.12) | copy-start | bytes 6148
  68.5 3.5 %copy-start.3 = (s32[8]{0:T(128)S(1)}, s32[8]{0:T(128)}, u32[]{:S(2)}) copy-start(s32[8]{0:T(128)} %cnt_ref.3) | copy-start | bytes 100
  68.5 3.5 %copy-start.4 = (f32[4]{0:T(128)S(1)}, f32[4]{0:T(128)}, u32[]{:S(2)}) copy-start(f32[4]{0:T(128)} %gain_ref.3) | copy-start | bytes 52
  72.0 1.6 %copy-start.2 = (bf16[64,64,256]{2,1,0:T(8,128)(2,1)S(1)}, bf16[64,64,256]{2,1,0:T(8,128)(2,1)}, u32[]{:S(2)}) copy-start(bf16[64,64,256]{2,1,0:T(8,128)(2,1)} %copy-done.1) | copy-start | bytes 6291460
  92.4 8.0 %collective-permute-start = (bf16[512,128]{1,0:T(8,128)(2,1)S(1)}, bf16[512,128]{1,0:T(8,128)(2,1)}, u32[]{:S(2)}, u32[]{:S(2)}) collective-permute-start(bf16[512,128]{1,0:T(8,128)(2,1)S(1)} %bitcast.29), channel_id=1, source_target_pairs={{0,1},{1,2},{2,3},{3,0},{4,5},{5,6},{6,7},{7,4},{8,9},{9,10},{10,1... | collective-permute-start | bytes 393224 | tf_op jit(solution)/shard_map/ppermute | solution.py:132
  94.4 9.9 %collective-permute-start.1 = (bf16[512,128]{1,0:T(8,128)(2,1)S(1)}, bf16[512,128]{1,0:T(8,128)(2,1)S(1)}, u32[]{:S(2)}, u32[]{:S(2)}) collective-permute-start(bf16[512,128]{1,0:T(8,128)(2,1)S(1)} %bitcast.30), channel_id=1, source_target_pairs={{0,2},{1,3},{2,0},{3,1},{4,6},{5,7},{6,4},{7,5},{8,10},{9,11},{10,... | collective-permute-start | bytes 393224 | tf_op jit(solution)/shard_map/ppermute | solution.py:132
  98.7 6.3 %collective-permute-start.2 = (bf16[512,128]{1,0:T(8,128)(2,1)S(1)}, bf16[512,128]{1,0:T(8,128)(2,1)S(1)}, u32[]{:S(2)}, u32[]{:S(2)}) collective-permute-start(bf16[512,128]{1,0:T(8,128)(2,1)S(1)} %bitcast.32), channel_id=1, source_target_pairs={{0,3},{1,0},{2,1},{3,2},{4,7},{5,4},{6,5},{7,6},{8,11},{9,8},{10,9... | collective-permute-start | bytes 393224 | tf_op jit(solution)/shard_map/ppermute | solution.py:132
  135.5 6.5 %collective-permute-start.3 = (bf16[512,128]{1,0:T(8,128)(2,1)S(1)}, bf16[512,128]{1,0:T(8,128)(2,1)S(1)}, u32[]{:S(2)}, u32[]{:S(2)}) collective-permute-start(bf16[512,128]{1,0:T(8,128)(2,1)S(1)} %bitcast.33), channel_id=1, source_target_pairs={{0,1},{1,2},{2,3},{3,0},{4,5},{5,6},{6,7},{7,4},{8,9},{9,10},{10,1... | collective-permute-start | bytes 393224 | tf_op jit(solution)/shard_map/ppermute | solution.py:132
  138.1 6.6 %collective-permute-start.4 = (bf16[512,128]{1,0:T(8,128)(2,1)S(1)}, bf16[512,128]{1,0:T(8,128)(2,1)S(1)}, u32[]{:S(2)}, u32[]{:S(2)}) collective-permute-start(bf16[512,128]{1,0:T(8,128)(2,1)S(1)} %bitcast.34), channel_id=1, source_target_pairs={{0,2},{1,3},{2,0},{3,1},{4,6},{5,7},{6,4},{7,5},{8,10},{9,11},{10,... | collective-permute-start | bytes 393224 | tf_op jit(solution)/shard_map/ppermute | solution.py:132
  140.1 6.3 %collective-permute-start.5 = (bf16[512,128]{1,0:T(8,128)(2,1)S(1)}, bf16[512,128]{1,0:T(8,128)(2,1)S(1)}, u32[]{:S(2)}, u32[]{:S(2)}) collective-permute-start(bf16[512,128]{1,0:T(8,128)(2,1)S(1)} %bitcast.35), channel_id=1, source_target_pairs={{0,3},{1,0},{2,1},{3,2},{4,7},{5,4},{6,5},{7,6},{8,11},{9,8},{10,9... | collective-permute-start | bytes 393224 | tf_op jit(solution)/shard_map/ppermute | solution.py:132
Sparse Core Ops, SparseCore 0:
  34.1 33.1 all-gather.1

commit v9 on v7

--- a/solution.py
+++ b/solution.py
@@ -32,21 +32,23 @@
         kp = jnp.concatenate([kv_ref[b, :, k_lo:k_lo + 128] for b in slots], axis=0)
         vp = jnp.concatenate([kv_ref[b, :, v_lo:v_lo + 128] for b in slots], axis=0)
         qp = (q[:, pair * 128:(pair + 1) * 128].astype(jnp.float32) * scale).astype(jnp.bfloat16)
-        res = None
+        zeros = jnp.zeros_like(qp)
+        q2 = jnp.concatenate(
+            [jnp.where(lane < HD, qp, zeros), jnp.where(lane >= HD, qp, zeros)], axis=0
+        )
+        s2 = lax.dot_general(
+            q2, kp, (((1,), (1,)), ((), ())), preferred_element_type=jnp.float32
+        )
+        ws = []
         for half in range(2):
             h = (p0 + pair) * 2 + half
-            in_head = (lane >= half * HD) & (lane < (half + 1) * HD)
-            qm = jnp.where(in_head, qp, jnp.zeros_like(qp))
-            s = lax.dot_general(
-                qm, kp, (((1,), (1,)), ((), ())), preferred_element_type=jnp.float32
-            )
-            s = s + gain_ref[h] * bias
+            s = s2[half * BLK:(half + 1) * BLK] + gain_ref[h] * bias
             top = jnp.max(s, axis=1, keepdims=True)
             expo = jnp.exp(s - top)
             total = jnp.sum(expo, axis=1, keepdims=True)
-            w = (expo * (1.0 / total)).astype(jnp.bfloat16)
-            o = jnp.dot(w, vp, preferred_element_type=jnp.float32)
-            res = o if res is None else jnp.where(lane < HD, res, o)
+            ws.append((expo * (1.0 / total)).astype(jnp.bfloat16))
+        o2 = jnp.dot(jnp.concatenate(ws, axis=0), vp, preferred_element_type=jnp.float32)
+        res = jnp.where(lane < HD, o2[:BLK], o2[BLK:])
         outs.append(res.astype(jnp.bfloat16))
     o_ref[0] = outs[0] if len(outs) == 1 else jnp.concatenate(outs, axis=1)
 

time: 134 us -> 124 us (0.925)
  Pallas kernels: 37 us -> 26.6 us
    pallas_call x2, Pallas kernels: 37 us -> 26.6 us  [attend(): pl.pallas_call(functools.partial(_attend_kernel, p0), grid_spec=grid_spec...]
  transfers between devices with their start and end apart: 12 -> 12, of which waited for: 4 -> 4; matrix products, arithmetic and copies ran while one was open for 17% -> 19% of each run, Pallas kernels for 28% -> 22%
where the time goes in v9:
time: 124 us; the launch traced here: 123 us
  starting transfers between devices  33.3 us (27%)
  waiting for transfers between devices  31.5 us (25%)
  Pallas kernels  26.6 us (21%)
  matrix products  15.4 us (12%)
  local copies, waits for them, and re-layouts  14.2 us (11%)
  other arithmetic  1.65 us (1%)
    pallas_call x2, Pallas kernels, attend(): pl.pallas_call(functools.partial(_attend_kernel, p0), grid_spec=grid_spec...  26.6 us
    all_to_all x2, waiting for transfers between devices, body(): table = lax.all_to_all(send, 'row', 0, 0, tiled=True)  24.8 us
    all_to_all x2, starting transfers between devices, body(): table = lax.all_to_all(send, 'row', 0, 0, tiled=True)  11.3 us
    dot_general x6, matrix products, body(): jnp.dot(att_s, w_parts[s - 1][cols], preferred_element_type=jnp.float32)  8.67 us
    ppermute x6, starting transfers between devices, body(): att_s = lax.ppermute(att, 'head', perm)  8.45 us
    all_to_all x1, starting transfers between devices, body(): wanted = lax.all_to_all(req, 'row', 0, 0, tiled=True).reshape(-1)  7.62 us
    ppermute x3, starting transfers between devices, body(): w_parts.append(lax.ppermute(piece, 'head', perm))  5.9 us
    ppermute x6, waiting for transfers between devices, body(): att_s = lax.ppermute(att, 'head', perm)  4.58 us
  transfers between devices with their start and end apart: 12, of which 4 were waited for; matrix products, arithmetic and copies ran while one was open for 19% of the time, Pallas kernels for 22%

profile of v9, /device:TPU:2, one launch (start us, length us, event | category | flops | bytes accessed | tf_op | source)
XLA Modules:
  0.0 123.0 jit_solution(15074050422244316087)
XLA Ops:
  0.0 0.0 copy-start
  0.0 0.8 eq.42
  0.9 0.2 fusion.11
  1.0 0.1 reshape.48
  1.1 0.1 select_reduce_fusion
  1.3 0.7 copy.16
  2.0 7.6 %all-to-all-start = ((s32[32,1,2]{2,1,0:T(1,128)}), s32[32,1,2]{2,1,0:T(1,128)S(1)}, u32[]{:S(2)}, u32[]{:S(2)}) async-start(s32[32,1,2]{2,1,0:T(1,128)} %copy.16), calls=%async_computation | async-start | bytes 32768 | tf_op jit(solution)/shard_map/all_to_all | solution.py:106
  9.6 0.0 copy-done
  9.6 1.5 %convolution_convert_fusion.1 = bf16[512,256]{0,1:T(8,128)(2,1)S(1)} fusion(bf16[512,1024]{1,0:T(8,128)(2,1)S(1)} %copy-done, bf16[3,1024,256]{2,1,0:T(8,128)(2,1)} %param.8), kind=kOutput, calls=%fused_computation.12 | convolution fusion | flops 268566528 | bytes 1835008 | tf_op jit(solution)/shard_map/dot_general | solution.py:108
  11.1 1.5 %convolution_convert_fusion = bf16[512,256]{0,1:T(8,128)(2,1)S(1)} fusion(bf16[512,1024]{1,0:T(8,128)(2,1)S(1)} %copy-done, bf16[3,1024,256]{2,1,0:T(8,128)(2,1)} %param.8), kind=kOutput, calls=%fused_computation.11 | convolution fusion | flops 268566528 | bytes 1835008 | tf_op jit(solution)/shard_map/dot_general | solution.py:109
  12.7 0.7 pad_maximum_fusion
  13.5 0.1 copy.15
  13.6 2.1 %all-to-all-done = s32[32,1,2]{2,1,0:T(1,128)S(1)} async-done(((s32[32,1,2]{2,1,0:T(1,128)}), s32[32,1,2]{2,1,0:T(1,128)S(1)}, u32[]{:S(2)}, u32[]{:S(2)}) %all-to-all-start) | async-done | bytes 288 | tf_op jit(solution)/shard_map/all_to_all | solution.py:106
  15.7 0.5 broadcast.72
  16.2 0.6 reduce.3
  16.8 0.1 reshape.64
  16.9 2.0 %gather_fusion.1 = bf16[64,64,256]{2,1,0:T(8,128)(2,1)} fusion(bf16[8,64,256]{2,1,0:T(8,128)(2,1)S(1)} %bitcast.43, s32[1024]{0:T(1024)S(1)} %pad_clamp_fusion), kind=kCustom, calls=%fused_computation.1 | custom fusion | bytes 4194560 | tf_op jit(solution)/shard_map/jit(_take)/gather | solution.py:123
  18.9 5.2 %all-to-all-start.1 = ((bf16[64,64,256]{2,1,0:T(8,128)(2,1)}), bf16[64,64,256]{2,1,0:T(8,128)(2,1)S(1)}, u32[]{:S(2)}, u32[]{:S(2)}) async-start(bf16[64,64,256]{2,1,0:T(8,128)(2,1)} %gather_fusion.1), calls=%async_computation.1 | async-start | bytes 4194304 | tf_op jit(solution)/shard_map/all_to_all | solution.py:131
  24.2 1.1 copy.17
  25.3 2.0 %gather_fusion.2 = bf16[64,64,256]{2,1,0:T(8,128)(2,1)} fusion(bf16[8,64,256]{2,1,0:T(8,128)(2,1)S(1)} %bitcast.44, s32[1024]{0:T(1024)S(1)} %pad_clamp_fusion), kind=kCustom, calls=%fused_computation.2 | custom fusion | bytes 4194560 | tf_op jit(solution)/shard_map/jit(_take)/gather | solution.py:123
  27.3 24.8 %all-to-all-done.1.kv_ref = bf16[64,64,256]{2,1,0:T(8,128)(2,1)S(1)} async-done(((bf16[64,64,256]{2,1,0:T(8,128)(2,1)}), bf16[64,64,256]{2,1,0:T(8,128)(2,1)S(1)}, u32[]{:S(2)}, u32[]{:S(2)}) %all-to-all-start.1) | async-done | bytes 2097184 | tf_op jit(solution)/shard_map/all_to_all | solution.py:131
  52.1 1.3 %copy-done.1 = bf16[64,64,256]{2,1,0:T(8,128)(2,1)} copy-done((bf16[64,64,256]{2,1,0:T(8,128)(2,1)}, bf16[64,64,256]{2,1,0:T(8,128)(2,1)S(1)}, u32[]{:S(2)}) %copy-start.1) | copy-done | bytes 2097176
  53.4 6.0 %all-to-all-start.2 = ((bf16[64,64,256]{2,1,0:T(8,128)(2,1)}), bf16[64,64,256]{2,1,0:T(8,128)(2,1)S(1)}, u32[]{:S(2)}, u32[]{:S(2)}) async-start(bf16[64,64,256]{2,1,0:T(8,128)(2,1)} %gather_fusion.2), calls=%async_computation.2 | async-start | bytes 4194304 | tf_op jit(solution)/shard_map/all_to_all | solution.py:131
  59.5 1.8 %constant_dynamic-slice_fusion.2 = (bf16[256,256]{1,0:T(8,128)(2,1)}, bf16[256,256]{1,0:T(8,128)(2,1)}, bf16[256,256]{1,0:T(8,128)(2,1)}) fusion(bf16[256,1024]{1,0:T(8,128)(2,1)} %param.9, s32[]{:T(128)S(6)} %select_n.86, s32[]{:T(128)S(6)} %select_n.90, s32[]{:T(128)S(6)} %select_n.88), kind=kLoop, calls=%fused_computation.59 | loop fusion | bytes 786444 | tf_op jit(solution)/shard_map/dynamic_slice | solution.py:113
  61.3 1.9 %collective-permute-start.1 = (bf16[256,256]{1,0:T(8,128)(2,1)}, bf16[256,256]{1,0:T(8,128)(2,1)}, u32[]{:S(2)}, u32[]{:S(2)}) collective-permute-start(bf16[256,256]{1,0:T(8,128)(2,1)} %get-tuple-element.9), channel_id=1, source_target_pairs={{0,1},{1,2},{2,3},{3,0},{4,5},{5,6},{6,7},{7,4},{8,9},{9,10},{10,1... | collective-permute-start | bytes 393224 | tf_op jit(solution)/shard_map/ppermute | solution.py:115
  63.2 2.1 %collective-permute-start.5 = (bf16[256,256]{1,0:T(8,128)(2,1)}, bf16[256,256]{1,0:T(8,128)(2,1)}, u32[]{:S(2)}, u32[]{:S(2)}) collective-permute-start(bf16[256,256]{1,0:T(8,128)(2,1)} %get-tuple-element.10), channel_id=1, source_target_pairs={{0,3},{1,0},{2,1},{3,2},{4,7},{5,4},{6,5},{7,6},{8,11},{9,8},{10,9... | collective-permute-start | bytes 393224 | tf_op jit(solution)/shard_map/ppermute | solution.py:115
  65.4 1.9 %collective-permute-start.3 = (bf16[256,256]{1,0:T(8,128)(2,1)}, bf16[256,256]{1,0:T(8,128)(2,1)}, u32[]{:S(2)}, u32[]{:S(2)}) collective-permute-start(bf16[256,256]{1,0:T(8,128)(2,1)} %get-tuple-element.11), channel_id=1, source_target_pairs={{0,2},{1,3},{2,0},{3,1},{4,6},{5,7},{6,4},{7,5},{8,10},{9,11},{10,... | collective-permute-start | bytes 393224 | tf_op jit(solution)/shard_map/ppermute | solution.py:115
  67.2 0.0 copy-done.7
  67.2 0.1 reshape.56
  67.3 3.3 %gather_fusion = s32[512]{0:T(512)S(1)} fusion(s32[32]{0:T(128)S(1)} %compare_select_fusion.3, s32[1024]{0:T(1024)S(1)} %pad_clamp_fusion.1), kind=kCustom, calls=%fused_computation | custom fusion | bytes 6144 | tf_op jit(solution)/shard_map/gather | solution.py:92
  70.7 0.0 copy-start.3
  70.7 0.0 copy-start.4
  70.7 0.1 reshape.55
  70.8 1.6 %convolution_convert_fusion.2 = bf16[512,256]{1,0:T(8,128)(2,1)S(1)} fusion(bf16[512,1024]{1,0:T(8,128)(2,1)S(1)} %copy-done, bf16[3,1024,256]{2,1,0:T(8,128)(2,1)} %param.8), kind=kOutput, calls=%fused_computation.13 | convolution fusion | flops 268566528 | bytes 1835008 | tf_op jit(solution)/shard_map/dot_general | solution.py:107
  72.4 0.0 copy-done.3
  72.4 0.0 copy-done.4
  72.5 0.1 copy-done.2
  72.5 13.3 %shard_map.73 = bf16[8,64,128]{2,1,0:T(8,128)(2,1)S(1)} custom-call(s32[8,64]{1,0:T(8,128)S(1)} %convert_add_fusion.nbr_ref, s32[8]{0:T(128)S(1)} %copy-done.3, f32[4]{0:T(128)S(1)} %copy-done.4, bf16[8,64,256]{2,1,0:T(8,128)(2,1)S(1)} %bitcast.33, bf16[8,64,4096]{2,1,0:T(8,128)(2,1)} %bias_ref.3, bf16[64,64,256]{2,1,0:T(8,128)(2,1)S(1)} %copy-done.2), custom_call_target="tpu_custom_call" | custom-call | tf_op jit(solution)/shard_map/pallas_call | solution.py:70
  85.8 1.1 collective-permute-start
  86.9 2.2 %collective-permute-start.4 = (bf16[512,128]{1,0:T(8,128)(2,1)S(1)}, bf16[512,128]{1,0:T(8,128)(2,1)S(1)}, u32[]{:S(2)}, u32[]{:S(2)}) collective-permute-start(bf16[512,128]{1,0:T(8,128)(2,1)S(1)} %bitcast.36), channel_id=1, source_target_pairs={{0,3},{1,0},{2,1},{3,2},{4,7},{5,4},{6,5},{7,6},{8,11},{9,8},{10,9... | collective-permute-start | bytes 393224 | tf_op jit(solution)/shard_map/ppermute | solution.py:138
  89.1 1.0 fusion.23
  90.2 0.0 collective-permute-done.5
  90.2 0.5 collective-permute-start.2
  90.7 3.5 %collective-permute-done.4 = bf16[512,128]{1,0:T(8,128)(2,1)S(1)} collective-permute-done((bf16[512,128]{1,0:T(8,128)(2,1)S(1)}, bf16[512,128]{1,0:T(8,128)(2,1)S(1)}, u32[]{:S(2)}, u32[]{:S(2)}) %collective-permute-start.4) | collective-permute-done | bytes 131104 | tf_op jit(solution)/shard_map/ppermute | solution.py:138
  94.2 1.9 %fusion.19 = f32[512,256]{1,0:T(8,128)} fusion(bf16[512,128]{1,0:T(8,128)(2,1)S(1)} %collective-permute-done.4, bf16[256,256]{1,0:T(8,128)(2,1)} %collective-permute-done.5), kind=kOutput, calls=%fused_computation.31 | convolution fusion | flops 33554432 | bytes 720896 | tf_op jit(solution)/shard_map/dot_general | solution.py:139
  96.1 0.0 collective-permute-done.1
  96.1 0.0 collective-permute-done
  96.1 1.9 %convolution_add_fusion.2 = f32[512,256]{1,0:T(8,128)} fusion(f32[512,256]{1,0:T(8,128)S(1)} %fusion.23, bf16[512,128]{1,0:T(8,128)(2,1)S(1)} %collective-permute-done, bf16[256,256]{1,0:T(8,128)(2,1)} %collective-permute-done.1), kind=kOutput, calls=%fused_computation.5 | convolution fusion | flops 33685504 | bytes 1245184 | tf_op jit(solution)/shard_map/dot_general | solution.py:139
  97.9 0.0 all-to-all-done.2.kv_ref
  97.9 13.3 %shard_map.74 = bf16[8,64,128]{2,1,0:T(8,128)(2,1)S(1)} custom-call(s32[8,64]{1,0:T(8,128)S(1)} %convert_add_fusion.nbr_ref, s32[8]{0:T(128)S(1)} %copy-done.3, f32[4]{0:T(128)S(1)} %copy-done.4, bf16[8,64,256]{2,1,0:T(8,128)(2,1)S(1)} %bitcast.34, bf16[8,64,4096]{2,1,0:T(8,128)(2,1)} %bias_ref.3, bf16[64,64,256]{2,1,0:T(8,128)(2,1)S(1)} %all-to-all-done.2.kv_ref), custom_call_target="tpu_custom_call" | custom-call | tf_op jit(solution)/shard_map/pallas_call | solution.py:70
  111.2 0.1 collective-permute-start.7
  111.3 3.7 %collective-permute-start.8 = (bf16[512,128]{1,0:T(8,128)(2,1)S(1)}, bf16[512,128]{1,0:T(8,128)(2,1)S(1)}, u32[]{:S(2)}, u32[]{:S(2)}) collective-permute-start(bf16[512,128]{1,0:T(8,128)(2,1)S(1)} %bitcast.40), channel_id=1, source_target_pairs={{0,3},{1,0},{2,1},{3,2},{4,7},{5,4},{6,5},{7,6},{8,11},{9,8},{10,9... | collective-permute-start | bytes 393224 | tf_op jit(solution)/shard_map/ppermute | solution.py:138
  115.1 0.8 collective-permute-start.6
  115.8 1.0 fusion.17
  116.9 0.0 collective-permute-done.3
  116.9 0.0 collective-permute-done.2
  116.9 0.0 copy-done.5
  116.9 1.1 fusion.1
  118.1 0.0 collective-permute-done.7
  118.1 1.0 fusion.14
  119.1 1.1 collective-permute-done.8
  120.2 1.0 fusion.12
  121.3 0.0 collective-permute-done.6
  121.3 1.8 %fusion.4 = bf16[512,256]{1,0:T(8,128)(2,1)} fusion(f32[512,256]{1,0:T(8,128)S(1)} %fusion.12, f32[512,256]{1,0:T(8,128)S(1)} %fusion.14, f32[512,256]{1,0:T(8,128)S(1)} %fusion.1, bf16[512,128]{1,0:T(8,128)(2,1)S(1)} %collective-permute-done.6, bf16[256,256]{1,0:T(8,128)(2,1)} %collective-permute-done.1), kind=kOutput, calls=%fused_computation.10 | convolution fusion | flops 34078720 | bytes 2031616 | tf_op jit(solution)/shard_map/dot_general | solution.py:139
  (15 shorter events, 0.1 us)
Async XLA Ops:
  0.0 9.6 %copy-start = (bf16[512,1024]{1,0:T(8,128)(2,1)S(1)}, bf16[512,1024]{1,0:T(8,128)(2,1)}, u32[]{:S(2)}) copy-start(bf16[512,1024]{1,0:T(8,128)(2,1)} %param.7) | copy-start | bytes 3145732
  2.0 13.8 %all-to-all-start = ((s32[32,1,2]{2,1,0:T(1,128)}), s32[32,1,2]{2,1,0:T(1,128)S(1)}, u32[]{:S(2)}, u32[]{:S(2)}) async-start(s32[32,1,2]{2,1,0:T(1,128)} %copy.16), calls=%async_computation | async-start | bytes 32768 | tf_op jit(solution)/shard_map/all_to_all | solution.py:106
  18.9 33.2 %all-to-all-start.1 = ((bf16[64,64,256]{2,1,0:T(8,128)(2,1)}), bf16[64,64,256]{2,1,0:T(8,128)(2,1)S(1)}, u32[]{:S(2)}, u32[]{:S(2)}) async-start(bf16[64,64,256]{2,1,0:T(8,128)(2,1)} %gather_fusion.1), calls=%async_computation.1 | async-start | bytes 4194304 | tf_op jit(solution)/shard_map/all_to_all | solution.py:131
  27.3 39.9 %copy-start.7 = (s32[8,64]{1,0:T(8,128)S(1)}, s32[8,64]{1,0:T(8,128)}, u32[]{:S(2)}) copy-start(s32[8,64]{1,0:T(8,128)} %param.12) | copy-start | bytes 6148
  52.1 1.3 %copy-start.1 = (bf16[64,64,256]{2,1,0:T(8,128)(2,1)}, bf16[64,64,256]{2,1,0:T(8,128)(2,1)S(1)}, u32[]{:S(2)}) copy-start(bf16[64,64,256]{2,1,0:T(8,128)(2,1)S(1)} %all-to-all-done.1.kv_ref) | copy-start | bytes 6291460
  53.4 44.5 %all-to-all-start.2 = ((bf16[64,64,256]{2,1,0:T(8,128)(2,1)}), bf16[64,64,256]{2,1,0:T(8,128)(2,1)S(1)}, u32[]{:S(2)}, u32[]{:S(2)}) async-start(bf16[64,64,256]{2,1,0:T(8,128)(2,1)} %gather_fusion.2), calls=%async_computation.2 | async-start | bytes 4194304 | tf_op jit(solution)/shard_map/all_to_all | solution.py:131
  61.3 34.7 %collective-permute-start.1 = (bf16[256,256]{1,0:T(8,128)(2,1)}, bf16[256,256]{1,0:T(8,128)(2,1)}, u32[]{:S(2)}, u32[]{:S(2)}) collective-permute-start(bf16[256,256]{1,0:T(8,128)(2,1)} %get-tuple-element.9), channel_id=1, source_target_pairs={{0,1},{1,2},{2,3},{3,0},{4,5},{5,6},{6,7},{7,4},{8,9},{9,10},{10,1... | collective-permute-start | bytes 393224 | tf_op jit(solution)/shard_map/ppermute | solution.py:115
  63.2 26.9 %collective-permute-start.5 = (bf16[256,256]{1,0:T(8,128)(2,1)}, bf16[256,256]{1,0:T(8,128)(2,1)}, u32[]{:S(2)}, u32[]{:S(2)}) collective-permute-start(bf16[256,256]{1,0:T(8,128)(2,1)} %get-tuple-element.10), channel_id=1, source_target_pairs={{0,3},{1,0},{2,1},{3,2},{4,7},{5,4},{6,5},{7,6},{8,11},{9,8},{10,9... | collective-permute-start | bytes 393224 | tf_op jit(solution)/shard_map/ppermute | solution.py:115
  65.4 51.5 %collective-permute-start.3 = (bf16[256,256]{1,0:T(8,128)(2,1)}, bf16[256,256]{1,0:T(8,128)(2,1)}, u32[]{:S(2)}, u32[]{:S(2)}) collective-permute-start(bf16[256,256]{1,0:T(8,128)(2,1)} %get-tuple-element.11), channel_id=1, source_target_pairs={{0,2},{1,3},{2,0},{3,1},{4,6},{5,7},{6,4},{7,5},{8,10},{9,11},{10,... | collective-permute-start | bytes 393224 | tf_op jit(solution)/shard_map/ppermute | solution.py:115
  70.7 1.8 %copy-start.3 = (s32[8]{0:T(128)S(1)}, s32[8]{0:T(128)}, u32[]{:S(2)}) copy-start(s32[8]{0:T(128)} %cnt_ref.3) | copy-start | bytes 100
  70.7 1.8 %copy-start.4 = (f32[4]{0:T(128)S(1)}, f32[4]{0:T(128)}, u32[]{:S(2)}) copy-start(f32[4]{0:T(128)} %gain_ref.3) | copy-start | bytes 52
  70.8 1.7 %copy-start.2 = (bf16[64,64,256]{2,1,0:T(8,128)(2,1)S(1)}, bf16[64,64,256]{2,1,0:T(8,128)(2,1)}, u32[]{:S(2)}) copy-start(bf16[64,64,256]{2,1,0:T(8,128)(2,1)} %copy-done.1) | copy-start | bytes 6291460
  85.8 10.2 %collective-permute-start = (bf16[512,128]{1,0:T(8,128)(2,1)S(1)}, bf16[512,128]{1,0:T(8,128)(2,1)S(1)}, u32[]{:S(2)}, u32[]{:S(2)}) collective-permute-start(bf16[512,128]{1,0:T(8,128)(2,1)S(1)} %bitcast.35), channel_id=1, source_target_pairs={{0,1},{1,2},{2,3},{3,0},{4,5},{5,6},{6,7},{7,4},{8,9},{9,10},{10,1... | collective-permute-start | bytes 393224 | tf_op jit(solution)/shard_map/ppermute | solution.py:138
  86.9 7.3 %collective-permute-start.4 = (bf16[512,128]{1,0:T(8,128)(2,1)S(1)}, bf16[512,128]{1,0:T(8,128)(2,1)S(1)}, u32[]{:S(2)}, u32[]{:S(2)}) collective-permute-start(bf16[512,128]{1,0:T(8,128)(2,1)S(1)} %bitcast.36), channel_id=1, source_target_pairs={{0,3},{1,0},{2,1},{3,2},{4,7},{5,4},{6,5},{7,6},{8,11},{9,8},{10,9... | collective-permute-start | bytes 393224 | tf_op jit(solution)/shard_map/ppermute | solution.py:138
  90.2 26.7 %collective-permute-start.2 = (bf16[512,128]{1,0:T(8,128)(2,1)S(1)}, bf16[512,128]{1,0:T(8,128)(2,1)}, u32[]{:S(2)}, u32[]{:S(2)}) collective-permute-start(bf16[512,128]{1,0:T(8,128)(2,1)S(1)} %bitcast.38), channel_id=1, source_target_pairs={{0,2},{1,3},{2,0},{3,1},{4,6},{5,7},{6,4},{7,5},{8,10},{9,11},{10,... | collective-permute-start | bytes 393224 | tf_op jit(solution)/shard_map/ppermute | solution.py:138
  97.9 19.0 %copy-start.5 = (f32[512,256]{1,0:T(8,128)S(1)}, f32[512,256]{1,0:T(8,128)}, u32[]{:S(2)}) copy-start(f32[512,256]{1,0:T(8,128)} %fusion.19) | copy-start | bytes 1572868
  97.9 19.0 %copy-start.6 = (f32[512,256]{1,0:T(8,128)S(1)}, f32[512,256]{1,0:T(8,128)}, u32[]{:S(2)}) copy-start(f32[512,256]{1,0:T(8,128)} %convolution_add_fusion.2) | copy-start | bytes 1572868
  111.2 6.8 %collective-permute-start.7 = (bf16[512,128]{1,0:T(8,128)(2,1)S(1)}, bf16[512,128]{1,0:T(8,128)(2,1)S(1)}, u32[]{:S(2)}, u32[]{:S(2)}) collective-permute-start(bf16[512,128]{1,0:T(8,128)(2,1)S(1)} %bitcast.39), channel_id=1, source_target_pairs={{0,2},{1,3},{2,0},{3,1},{4,6},{5,7},{6,4},{7,5},{8,10},{9,11},{10,... | collective-permute-start | bytes 393224 | tf_op jit(solution)/shard_map/ppermute | solution.py:138
  111.3 8.9 %collective-permute-start.8 = (bf16[512,128]{1,0:T(8,128)(2,1)S(1)}, bf16[512,128]{1,0:T(8,128)(2,1)S(1)}, u32[]{:S(2)}, u32[]{:S(2)}) collective-permute-start(bf16[512,128]{1,0:T(8,128)(2,1)S(1)} %bitcast.40), channel_id=1, source_target_pairs={{0,3},{1,0},{2,1},{3,2},{4,7},{5,4},{6,5},{7,6},{8,11},{9,8},{10,9... | collective-permute-start | bytes 393224 | tf_op jit(solution)/shard_map/ppermute | solution.py:138
  115.1 6.2 %collective-permute-start.6 = (bf16[512,128]{1,0:T(8,128)(2,1)S(1)}, bf16[512,128]{1,0:T(8,128)(2,1)S(1)}, u32[]{:S(2)}, u32[]{:S(2)}) collective-permute-start(bf16[512,128]{1,0:T(8,128)(2,1)S(1)} %bitcast.41), channel_id=1, source_target_pairs={{0,1},{1,2},{2,3},{3,0},{4,5},{5,6},{6,7},{7,4},{8,9},{9,10},{10,1... | collective-permute-start | bytes 393224 | tf_op jit(solution)/shard_map/ppermute | solution.py:138

commit v10 on v9

--- a/solution.py
+++ b/solution.py
@@ -89,7 +89,9 @@
     second = jnp.max(jnp.where(present, lidx, -1), axis=1)
     second = jnp.where(second < 0, first, second)
     req = jnp.stack([first, second], axis=1).astype(jnp.int32)
-    pos = owner * 2 + (local != first[owner]).astype(jnp.int32)
+    hit = owner.reshape(-1)[:, None] == jnp.arange(owners, dtype=jnp.int32)[None, :]
+    first_of = jnp.sum(jnp.where(hit, first[None, :], 0), axis=1).reshape(owner.shape)
+    pos = owner * 2 + (local != first_of).astype(jnp.int32)
     return req, pos.astype(jnp.int32)
 
 
@@ -131,12 +133,18 @@
         table = lax.all_to_all(send, "row", 0, 0, tiled=True)
         att = attend(pos, counts, bias_gain, q_blocks, edge_bias, table, c, chunk)
         att = att.reshape(rows, chunk)
-        part = jnp.dot(att, w_own[cols], preferred_element_type=jnp.float32)
-        total = part if total is None else total + part
+        att_all = [att]
+        w_all = [w_own[cols]]
         for s in range(1, head_devs):
             perm = [(i, (i + s) % head_devs) for i in range(head_devs)]
-            att_s = lax.ppermute(att, "head", perm)
-            total = total + jnp.dot(att_s, w_parts[s - 1][cols], preferred_element_type=jnp.float32)
+            att_all.append(lax.ppermute(att, "head", perm))
+            w_all.append(w_parts[s - 1][cols])
+        part = jnp.dot(
+            jnp.concatenate(att_all, axis=1),
+            jnp.concatenate(w_all, axis=0),
+            preferred_element_type=jnp.float32,
+        )
+        total = part if total is None else total + part
     return total.astype(jnp.bfloat16)
 
 

time: 124 us -> 138 us (1.11); the launches traced: 123 us -> 136 us
  waiting for transfers between devices: 31.5 us -> 51 us
  matrix products: 15.4 us -> 5.82 us
  starting transfers between devices: 33.3 us -> 35.2 us
    all_to_all x2, waiting for transfers between devices: 24.8 us -> 39.3 us  [body(): table = lax.all_to_all(send, 'row', 0, 0, tiled=True)]
    dot_general x8 -> x2, matrix products: 10.7 us -> 1.29 us  [body(): jnp.dot(jnp.concatenate(att_all, axis=1), jnp.concatenate(w_all, axis=0),...]
    slice x0 -> x4, local copies, waits for them, and re-layouts: none -> 3.95 us  [the longest x3 2.42 us: body(): w_all.append(w_parts[s - 1][cols])]
    ppermute x6, waiting for transfers between devices: 4.58 us -> 8.5 us  [body(): att_all.append(lax.ppermute(att, 'head', perm))]
    gather x2 -> x0, local copies, waits for them, and re-layouts: 3.42 us -> none  [plan_requests(): pos = owner * 2 + (local != first[owner]).astype(jnp.int32)]
    ppermute x6, starting transfers between devices: 8.45 us -> 10.3 us  [body(): att_all.append(lax.ppermute(att, 'head', perm))]
    unnamed x16 -> x18, local copies, waits for them, and re-layouts: 1.43 us -> 0.04 us
  transfers between devices with their start and end apart: 12 -> 12, of which waited for: 4 -> 6; matrix products, arithmetic and copies ran while one was open for 19% -> 11% of each run, Pallas kernels for 22% -> 20%
where the time goes in v10:
time: 138 us; the launch traced here: 136 us
  waiting for transfers between devices  51 us (37%)
  starting transfers between devices  35.2 us (26%)
  Pallas kernels  27.3 us (20%)
  local copies, waits for them, and re-layouts  14.1 us (10%)
  matrix products  5.82 us (4%)
  other arithmetic  1.88 us (1%)
    all_to_all x2, waiting for transfers between devices, body(): table = lax.all_to_all(send, 'row', 0, 0, tiled=True)  39.3 us
    pallas_call x2, Pallas kernels, attend(): pl.pallas_call(functools.partial(_attend_kernel, p0), grid_spec=grid_spec...  27.3 us
    all_to_all x2, starting transfers between devices, body(): table = lax.all_to_all(send, 'row', 0, 0, tiled=True)  12 us
    ppermute x6, starting transfers between devices, body(): att_all.append(lax.ppermute(att, 'head', perm))  10.3 us
    ppermute x6, waiting for transfers between devices, body(): att_all.append(lax.ppermute(att, 'head', perm))  8.5 us
    all_to_all x1, starting transfers between devices, body(): wanted = lax.all_to_all(req, 'row', 0, 0, tiled=True).reshape(-1)  7.62 us
    ppermute x3, starting transfers between devices, body(): w_parts.append(lax.ppermute(piece, 'head', perm))  5.3 us
    gather x2, local copies, waits for them, and re-layouts, body(): outgoing.append(jnp.take(kv, wanted, axis=0, mode='clip'))  4.02 us
  transfers between devices with their start and end apart: 12, of which 6 were waited for; matrix products, arithmetic and copies ran while one was open for 11% of the time, Pallas kernels for 20%

profile of v10, /device:TPU:2, one launch (start us, length us, event | category | flops | bytes accessed | tf_op | source)
XLA Modules:
  0.0 135.7 jit_solution(18417107013822742847)
XLA Ops:
  0.0 0.0 copy-start
  0.0 0.8 eq.65
  0.9 0.2 fusion.22
  1.0 0.1 reshape.56
  1.1 0.1 select_reduce_fusion.1
  1.3 0.7 copy.16
  1.9 7.6 %all-to-all-start = ((s32[32,1,2]{2,1,0:T(1,128)}), s32[32,1,2]{2,1,0:T(1,128)S(1)}, u32[]{:S(2)}, u32[]{:S(2)}) async-start(s32[32,1,2]{2,1,0:T(1,128)} %copy.16), calls=%async_computation | async-start | bytes 32768 | tf_op jit(solution)/shard_map/all_to_all | solution.py:108
  9.6 0.0 copy-done
  9.6 1.5 %convolution_convert_fusion = bf16[512,256]{0,1:T(8,128)(2,1)S(1)} fusion(bf16[512,1024]{1,0:T(8,128)(2,1)S(1)} %copy-done, bf16[3,1024,256]{2,1,0:T(8,128)(2,1)} %param.8), kind=kOutput, calls=%fused_computation.4 | convolution fusion | flops 268566528 | bytes 1835008 | tf_op jit(solution)/shard_map/dot_general | solution.py:111
  11.1 1.5 %convolution_convert_fusion.1 = bf16[512,256]{0,1:T(8,128)(2,1)S(1)} fusion(bf16[512,1024]{1,0:T(8,128)(2,1)S(1)} %copy-done, bf16[3,1024,256]{2,1,0:T(8,128)(2,1)} %param.8), kind=kOutput, calls=%fused_computation.5 | convolution fusion | flops 268566528 | bytes 1835008 | tf_op jit(solution)/shard_map/dot_general | solution.py:110
  12.7 0.7 pad_maximum_fusion
  13.4 0.1 copy.15
  13.6 2.2 %all-to-all-done = s32[32,1,2]{2,1,0:T(1,128)S(1)} async-done(((s32[32,1,2]{2,1,0:T(1,128)}), s32[32,1,2]{2,1,0:T(1,128)S(1)}, u32[]{:S(2)}, u32[]{:S(2)}) %all-to-all-start) | async-done | bytes 288 | tf_op jit(solution)/shard_map/all_to_all | solution.py:108
  15.7 0.6 broadcast.71
  16.3 0.7 reduce.3
  17.1 0.1 reshape.65
  17.2 2.0 %gather_fusion = bf16[64,64,256]{2,1,0:T(8,128)(2,1)} fusion(bf16[8,64,256]{2,1,0:T(8,128)(2,1)S(1)} %bitcast.35, s32[1024]{0:T(1024)S(1)} %pad_clamp_fusion), kind=kCustom, calls=%fused_computation | custom fusion | bytes 4194560 | tf_op jit(solution)/shard_map/jit(_take)/gather | solution.py:125
  19.2 5.2 %all-to-all-start.1 = ((bf16[64,64,256]{2,1,0:T(8,128)(2,1)}), bf16[64,64,256]{2,1,0:T(8,128)(2,1)S(1)}, u32[]{:S(2)}, u32[]{:S(2)}) async-start(bf16[64,64,256]{2,1,0:T(8,128)(2,1)} %gather_fusion), calls=%async_computation.1 | async-start | bytes 4194304 | tf_op jit(solution)/shard_map/all_to_all | solution.py:133
  24.4 1.1 copy.17
  25.5 2.0 %gather_fusion.1 = bf16[64,64,256]{2,1,0:T(8,128)(2,1)} fusion(bf16[8,64,256]{2,1,0:T(8,128)(2,1)S(1)} %bitcast.36, s32[1024]{0:T(1024)S(1)} %pad_clamp_fusion), kind=kCustom, calls=%fused_computation.1 | custom fusion | bytes 4194560 | tf_op jit(solution)/shard_map/jit(_take)/gather | solution.py:125
  27.5 24.8 %all-to-all-done.1.kv_ref = bf16[64,64,256]{2,1,0:T(8,128)(2,1)S(1)} async-done(((bf16[64,64,256]{2,1,0:T(8,128)(2,1)}), bf16[64,64,256]{2,1,0:T(8,128)(2,1)S(1)}, u32[]{:S(2)}, u32[]{:S(2)}) %all-to-all-start.1) | async-done | bytes 2097184 | tf_op jit(solution)/shard_map/all_to_all | solution.py:133
  52.3 6.7 %all-to-all-start.2 = ((bf16[64,64,256]{2,1,0:T(8,128)(2,1)}), bf16[64,64,256]{2,1,0:T(8,128)(2,1)}, u32[]{:S(2)}, u32[]{:S(2)}) async-start(bf16[64,64,256]{2,1,0:T(8,128)(2,1)} %gather_fusion.1), calls=%async_computation.2 | async-start | bytes 4194304 | tf_op jit(solution)/shard_map/all_to_all | solution.py:133
  59.1 0.0 copy-start.1
  59.1 0.0 copy-start.2
  59.2 1.8 %constant_dynamic-slice_fusion.3 = (bf16[256,256]{1,0:T(8,128)(2,1)}, bf16[256,256]{1,0:T(8,128)(2,1)}, bf16[256,256]{1,0:T(8,128)(2,1)}) fusion(bf16[256,1024]{1,0:T(8,128)(2,1)} %param.9, s32[]{:T(128)S(6)} %select_n.91, s32[]{:T(128)S(6)} %select_n.95, s32[]{:T(128)S(6)} %select_n.93), kind=kLoop, calls=%fused_computation.68 | loop fusion | bytes 786444 | tf_op jit(solution)/shard_map/dynamic_slice | solution.py:115
  60.9 4.0 %collective-permute-start.5 = (bf16[256,256]{1,0:T(8,128)(2,1)}, bf16[256,256]{1,0:T(8,128)(2,1)}, u32[]{:S(2)}, u32[]{:S(2)}) collective-permute-start(bf16[256,256]{1,0:T(8,128)(2,1)} %get-tuple-element.12), channel_id=1, source_target_pairs={{0,3},{1,0},{2,1},{3,2},{4,7},{5,4},{6,5},{7,6},{8,11},{9,8},{10,9... | collective-permute-start | bytes 393224 | tf_op jit(solution)/shard_map/ppermute | solution.py:117
  65.0 0.0 collective-permute-start.4
  65.0 1.3 collective-permute-start.3
  66.2 0.0 copy-done.7
  66.3 0.1 eq.61
  66.3 0.1 select_reduce_fusion
  66.4 0.7 reshape.57
  67.1 1.5 %convolution_convert_fusion.2 = bf16[512,256]{1,0:T(8,128)(2,1)S(1)} fusion(bf16[512,1024]{1,0:T(8,128)(2,1)S(1)} %copy-done, bf16[3,1024,256]{2,1,0:T(8,128)(2,1)} %param.8), kind=kOutput, calls=%fused_computation.6 | convolution fusion | flops 268566528 | bytes 1835008 | tf_op jit(solution)/shard_map/dot_general | solution.py:109
  68.6 0.0 copy-done.8
  68.6 1.5 %constant_dynamic-slice_fusion = (bf16[128,256]{1,0:T(8,128)(2,1)}, bf16[128,256]{1,0:T(8,128)(2,1)}) fusion(bf16[256,1024]{1,0:T(8,128)(2,1)} %param.9, s32[]{:T(128)S(6)} %select_n.89, s32[]{:T(128)S(6)} %add.60), kind=kLoop, calls=%fused_computation.65 | loop fusion | bytes 262152 | tf_op jit(solution)/shard_map/slice | solution.py:137
  70.2 1.0 collective-permute-done.5
  71.1 1.5 %fusion.46 = (bf16[128,256]{1,0:T(8,128)(2,1)}, bf16[128,256]{1,0:T(8,128)(2,1)}) fusion(bf16[256,256]{1,0:T(8,128)(2,1)} %collective-permute-done.5), kind=kLoop, calls=%fused_computation.75 | loop fusion | bytes 262144 | tf_op jit(solution)/shard_map/slice | solution.py:141
  72.7 14.5 %all-to-all-done.2.kv_ref = bf16[64,64,256]{2,1,0:T(8,128)(2,1)} async-done(((bf16[64,64,256]{2,1,0:T(8,128)(2,1)}), bf16[64,64,256]{2,1,0:T(8,128)(2,1)}, u32[]{:S(2)}, u32[]{:S(2)}) %all-to-all-start.2) | async-done | bytes 2097184 | tf_op jit(solution)/shard_map/all_to_all | solution.py:133
  87.2 0.0 copy-done.1
  87.2 0.0 copy-done.2
  87.2 14.0 %shard_map.74 = bf16[8,64,128]{2,1,0:T(8,128)(2,1)S(1)} custom-call(s32[8,64]{1,0:T(8,128)S(1)} %convert_add_fusion.nbr_ref, s32[8]{0:T(128)S(1)} %copy-done.1, f32[4]{0:T(128)S(1)} %copy-done.2, bf16[8,64,256]{2,1,0:T(8,128)(2,1)S(1)} %bitcast.25, bf16[8,64,4096]{2,1,0:T(8,128)(2,1)} %bias_ref.3, bf16[64,64,256]{2,1,0:T(8,128)(2,1)} %all-to-all-done.2.kv_ref), custom_call_target="tpu_custom_call" | custom-call | tf_op jit(solution)/shard_map/pallas_call | solution.py:70
  101.2 4.1 %collective-permute-start.8 = (bf16[512,128]{1,0:T(8,128)(2,1)S(1)}, bf16[512,128]{1,0:T(8,128)(2,1)S(1)}, u32[]{:S(2)}, u32[]{:S(2)}) collective-permute-start(bf16[512,128]{1,0:T(8,128)(2,1)S(1)} %bitcast.31), channel_id=1, source_target_pairs={{0,3},{1,0},{2,1},{3,2},{4,7},{5,4},{6,5},{7,6},{8,11},{9,8},{10,9... | collective-permute-start | bytes 393224 | tf_op jit(solution)/shard_map/ppermute | solution.py:140
  105.3 0.0 collective-permute-done.4
  105.3 0.9 fusion.45
  106.2 0.0 copy-start.5
  106.2 0.0 copy-start.6
  106.2 13.3 %shard_map.73 = bf16[8,64,128]{2,1,0:T(8,128)(2,1)S(1)} custom-call(s32[8,64]{1,0:T(8,128)S(1)} %convert_add_fusion.nbr_ref, s32[8]{0:T(128)S(1)} %copy-done.1, f32[4]{0:T(128)S(1)} %copy-done.2, bf16[8,64,256]{2,1,0:T(8,128)(2,1)S(1)} %bitcast.26, bf16[8,64,4096]{2,1,0:T(8,128)(2,1)} %bias_ref.3, bf16[64,64,256]{2,1,0:T(8,128)(2,1)S(1)} %all-to-all-done.1.kv_ref), custom_call_target="tpu_custom_call" | custom-call | tf_op jit(solution)/shard_map/pallas_call | solution.py:70
  119.5 0.0 copy-start.3
  119.5 0.0 copy-start.4
  119.5 0.5 collective-permute-start.2
  120.0 0.0 collective-permute-start.1
  120.0 1.6 %collective-permute-start = (bf16[512,128]{1,0:T(8,128)(2,1)S(1)}, bf16[512,128]{1,0:T(8,128)(2,1)S(1)}, u32[]{:S(2)}, u32[]{:S(2)}) collective-permute-start(bf16[512,128]{1,0:T(8,128)(2,1)S(1)} %bitcast.29), channel_id=1, source_target_pairs={{0,1},{1,2},{2,3},{3,0},{4,5},{5,6},{6,7},{7,4},{8,9},{9,10},{10,1... | collective-permute-start | bytes 393224 | tf_op jit(solution)/shard_map/ppermute | solution.py:140
  121.6 0.0 collective-permute-done.3
  121.7 4.1 %collective-permute-start.7 = (bf16[512,128]{1,0:T(8,128)(2,1)S(1)}, bf16[512,128]{1,0:T(8,128)(2,1)S(1)}, u32[]{:S(2)}, u32[]{:S(2)}) collective-permute-start(bf16[512,128]{1,0:T(8,128)(2,1)S(1)} %bitcast.32), channel_id=1, source_target_pairs={{0,2},{1,3},{2,0},{3,1},{4,6},{5,7},{6,4},{7,5},{8,10},{9,11},{10,... | collective-permute-start | bytes 393224 | tf_op jit(solution)/shard_map/ppermute | solution.py:140
  125.8 0.0 collective-permute-done.8
  125.8 0.0 collective-permute-start.6
  125.8 7.6 %collective-permute-done.7 = bf16[512,128]{1,0:T(8,128)(2,1)S(1)} collective-permute-done((bf16[512,128]{1,0:T(8,128)(2,1)S(1)}, bf16[512,128]{1,0:T(8,128)(2,1)S(1)}, u32[]{:S(2)}, u32[]{:S(2)}) %collective-permute-start.7) | collective-permute-done | bytes 131104 | tf_op jit(solution)/shard_map/ppermute | solution.py:140
  133.4 0.8 collective-permute-done.6
  134.3 0.0 copy-done.6
  134.3 0.3 fusion.8
  134.6 0.0 collective-permute-done.2
  134.6 0.0 collective-permute-done.1
  134.6 0.0 collective-permute-done
  134.7 1.0 fusion
  (14 shorter events, 0.1 us)
Async XLA Ops:
  0.0 9.6 %copy-start = (bf16[512,1024]{1,0:T(8,128)(2,1)S(1)}, bf16[512,1024]{1,0:T(8,128)(2,1)}, u32[]{:S(2)}) copy-start(bf16[512,1024]{1,0:T(8,128)(2,1)} %param.7) | copy-start | bytes 3145732
  1.9 13.8 %all-to-all-start = ((s32[32,1,2]{2,1,0:T(1,128)}), s32[32,1,2]{2,1,0:T(1,128)S(1)}, u32[]{:S(2)}, u32[]{:S(2)}) async-start(s32[32,1,2]{2,1,0:T(1,128)} %copy.16), calls=%async_computation | async-start | bytes 32768 | tf_op jit(solution)/shard_map/all_to_all | solution.py:108
  19.2 33.2 %all-to-all-start.1 = ((bf16[64,64,256]{2,1,0:T(8,128)(2,1)}), bf16[64,64,256]{2,1,0:T(8,128)(2,1)S(1)}, u32[]{:S(2)}, u32[]{:S(2)}) async-start(bf16[64,64,256]{2,1,0:T(8,128)(2,1)} %gather_fusion), calls=%async_computation.1 | async-start | bytes 4194304 | tf_op jit(solution)/shard_map/all_to_all | solution.py:133
  27.5 38.7 %copy-start.7 = (s32[8,64]{1,0:T(8,128)S(1)}, s32[8,64]{1,0:T(8,128)}, u32[]{:S(2)}) copy-start(s32[8,64]{1,0:T(8,128)} %param.12) | copy-start | bytes 6148
  52.3 34.8 %all-to-all-start.2 = ((bf16[64,64,256]{2,1,0:T(8,128)(2,1)}), bf16[64,64,256]{2,1,0:T(8,128)(2,1)}, u32[]{:S(2)}, u32[]{:S(2)}) async-start(bf16[64,64,256]{2,1,0:T(8,128)(2,1)} %gather_fusion.1), calls=%async_computation.2 | async-start | bytes 4194304 | tf_op jit(solution)/shard_map/all_to_all | solution.py:133
  59.1 28.1 %copy-start.1 = (s32[8]{0:T(128)S(1)}, s32[8]{0:T(128)}, u32[]{:S(2)}) copy-start(s32[8]{0:T(128)} %cnt_ref.3) | copy-start | bytes 100
  59.1 28.1 %copy-start.2 = (f32[4]{0:T(128)S(1)}, f32[4]{0:T(128)}, u32[]{:S(2)}) copy-start(f32[4]{0:T(128)} %gain_ref.3) | copy-start | bytes 52
  60.9 10.2 %collective-permute-start.5 = (bf16[256,256]{1,0:T(8,128)(2,1)}, bf16[256,256]{1,0:T(8,128)(2,1)}, u32[]{:S(2)}, u32[]{:S(2)}) collective-permute-start(bf16[256,256]{1,0:T(8,128)(2,1)} %get-tuple-element.12), channel_id=1, source_target_pairs={{0,3},{1,0},{2,1},{3,2},{4,7},{5,4},{6,5},{7,6},{8,11},{9,8},{10,9... | collective-permute-start | bytes 393224 | tf_op jit(solution)/shard_map/ppermute | solution.py:117
  65.0 40.3 %collective-permute-start.4 = (bf16[256,256]{1,0:T(8,128)(2,1)}, bf16[256,256]{1,0:T(8,128)(2,1)}, u32[]{:S(2)}, u32[]{:S(2)}) collective-permute-start(bf16[256,256]{1,0:T(8,128)(2,1)} %get-tuple-element.13), channel_id=1, source_target_pairs={{0,2},{1,3},{2,0},{3,1},{4,6},{5,7},{6,4},{7,5},{8,10},{9,11},{10,... | collective-permute-start | bytes 393224 | tf_op jit(solution)/shard_map/ppermute | solution.py:117
  65.0 56.7 %collective-permute-start.3 = (bf16[256,256]{1,0:T(8,128)(2,1)}, bf16[256,256]{1,0:T(8,128)(2,1)S(1)}, u32[]{:S(2)}, u32[]{:S(2)}) collective-permute-start(bf16[256,256]{1,0:T(8,128)(2,1)} %get-tuple-element.11), channel_id=1, source_target_pairs={{0,1},{1,2},{2,3},{3,0},{4,5},{5,6},{6,7},{7,4},{8,9},{9,10},{10,1... | collective-permute-start | bytes 393224 | tf_op jit(solution)/shard_map/ppermute | solution.py:117
  67.1 1.5 %copy-start.8 = (s32[8,64]{1,0:T(8,128)S(1)}, s32[8,64]{1,0:T(8,128)}, u32[]{:S(2)}) copy-start(s32[8,64]{1,0:T(8,128)} %reshape.57) | copy-start | bytes 6148
  101.2 24.6 %collective-permute-start.8 = (bf16[512,128]{1,0:T(8,128)(2,1)S(1)}, bf16[512,128]{1,0:T(8,128)(2,1)S(1)}, u32[]{:S(2)}, u32[]{:S(2)}) collective-permute-start(bf16[512,128]{1,0:T(8,128)(2,1)S(1)} %bitcast.31), channel_id=1, source_target_pairs={{0,3},{1,0},{2,1},{3,2},{4,7},{5,4},{6,5},{7,6},{8,11},{9,8},{10,9... | collective-permute-start | bytes 393224 | tf_op jit(solution)/shard_map/ppermute | solution.py:140
  106.2 28.1 %copy-start.5 = (bf16[128,256]{1,0:T(8,128)(2,1)S(1)}, bf16[128,256]{1,0:T(8,128)(2,1)}, u32[]{:S(2)}) copy-start(bf16[128,256]{1,0:T(8,128)(2,1)} %get-tuple-element.10) | copy-start | bytes 196612
  106.2 28.1 %copy-start.6 = (bf16[128,256]{1,0:T(8,128)(2,1)S(1)}, bf16[128,256]{1,0:T(8,128)(2,1)}, u32[]{:S(2)}) copy-start(bf16[128,256]{1,0:T(8,128)(2,1)} %get-tuple-element.23) | copy-start | bytes 196612
  119.5 15.1 %copy-start.3 = (bf16[128,256]{1,0:T(8,128)(2,1)S(1)}, bf16[128,256]{1,0:T(8,128)(2,1)}, u32[]{:S(2)}) copy-start(bf16[128,256]{1,0:T(8,128)(2,1)} %get-tuple-element.9) | copy-start | bytes 196612
  119.5 15.1 %copy-start.4 = (bf16[128,256]{1,0:T(8,128)(2,1)S(1)}, bf16[128,256]{1,0:T(8,128)(2,1)}, u32[]{:S(2)}) copy-start(bf16[128,256]{1,0:T(8,128)(2,1)} %get-tuple-element.22) | copy-start | bytes 196612
  119.5 15.1 %collective-permute-start.2 = (bf16[512,128]{1,0:T(8,128)(2,1)S(1)}, bf16[512,128]{1,0:T(8,128)(2,1)S(1)}, u32[]{:S(2)}, u32[]{:S(2)}) collective-permute-start(bf16[512,128]{1,0:T(8,128)(2,1)S(1)} %bitcast.27), channel_id=1, source_target_pairs={{0,3},{1,0},{2,1},{3,2},{4,7},{5,4},{6,5},{7,6},{8,11},{9,8},{10,9... | collective-permute-start | bytes 393224 | tf_op jit(solution)/shard_map/ppermute | solution.py:140
  120.0 14.6 %collective-permute-start.1 = (bf16[512,128]{1,0:T(8,128)(2,1)S(1)}, bf16[512,128]{1,0:T(8,128)(2,1)S(1)}, u32[]{:S(2)}, u32[]{:S(2)}) collective-permute-start(bf16[512,128]{1,0:T(8,128)(2,1)S(1)} %bitcast.28), channel_id=1, source_target_pairs={{0,2},{1,3},{2,0},{3,1},{4,6},{5,7},{6,4},{7,5},{8,10},{9,11},{10,... | collective-permute-start | bytes 393224 | tf_op jit(solution)/shard_map/ppermute | solution.py:140
  120.0 14.6 %collective-permute-start = (bf16[512,128]{1,0:T(8,128)(2,1)S(1)}, bf16[512,128]{1,0:T(8,128)(2,1)S(1)}, u32[]{:S(2)}, u32[]{:S(2)}) collective-permute-start(bf16[512,128]{1,0:T(8,128)(2,1)S(1)} %bitcast.29), channel_id=1, source_target_pairs={{0,1},{1,2},{2,3},{3,0},{4,5},{5,6},{6,7},{7,4},{8,9},{9,10},{10,1... | collective-permute-start | bytes 393224 | tf_op jit(solution)/shard_map/ppermute | solution.py:140
  121.7 11.8 %collective-permute-start.7 = (bf16[512,128]{1,0:T(8,128)(2,1)S(1)}, bf16[512,128]{1,0:T(8,128)(2,1)S(1)}, u32[]{:S(2)}, u32[]{:S(2)}) collective-permute-start(bf16[512,128]{1,0:T(8,128)(2,1)S(1)} %bitcast.32), channel_id=1, source_target_pairs={{0,2},{1,3},{2,0},{3,1},{4,6},{5,7},{6,4},{7,5},{8,10},{9,11},{10,... | collective-permute-start | bytes 393224 | tf_op jit(solution)/shard_map/ppermute | solution.py:140
  125.8 8.5 %collective-permute-start.6 = (bf16[512,128]{1,0:T(8,128)(2,1)S(1)}, bf16[512,128]{1,0:T(8,128)(2,1)S(1)}, u32[]{:S(2)}, u32[]{:S(2)}) collective-permute-start(bf16[512,128]{1,0:T(8,128)(2,1)S(1)} %bitcast.33), channel_id=1, source_target_pairs={{0,1},{1,2},{2,3},{3,0},{4,5},{5,6},{6,7},{7,4},{8,9},{9,10},{10,1... | collective-permute-start | bytes 393224 | tf_op jit(solution)/shard_map/ppermute | solution.py:140

commit v11 on v9

--- a/solution.py
+++ b/solution.py
@@ -7,13 +7,14 @@
 from jax.experimental.pallas import tpu as pltpu
 from jax.sharding import PartitionSpec as P
 
+
 HD = 64
 BLK = 64
 NB = 64
 
 
-def _attend_kernel(p0, nbr_ref, cnt_ref, gain_ref, q_ref, bias_ref, kv_ref, o_ref):
-    g = pl.program_id(0)
+def _attend_kernel(p0, g0, nbr_ref, cnt_ref, gain_ref, q_ref, bias_ref, kv_ref, o_ref):
+    g = g0 + pl.program_id(0)
     width = kv_ref.shape[-1]
     half_w = width // 2
     pairs = half_w // 128
@@ -40,35 +41,36 @@
             q2, kp, (((1,), (1,)), ((), ())), preferred_element_type=jnp.float32
         )
         ws = []
+        sums = []
         for half in range(2):
             h = (p0 + pair) * 2 + half
             s = s2[half * BLK:(half + 1) * BLK] + gain_ref[h] * bias
             top = jnp.max(s, axis=1, keepdims=True)
             expo = jnp.exp(s - top)
-            total = jnp.sum(expo, axis=1, keepdims=True)
-            ws.append((expo * (1.0 / total)).astype(jnp.bfloat16))
+            sums.append(jnp.sum(expo, axis=1, keepdims=True))
+            ws.append(expo.astype(jnp.bfloat16))
         o2 = jnp.dot(jnp.concatenate(ws, axis=0), vp, preferred_element_type=jnp.float32)
+        o2 = o2 * (1.0 / jnp.concatenate(sums, axis=0))
         res = jnp.where(lane < HD, o2[:BLK], o2[BLK:])
         outs.append(res.astype(jnp.bfloat16))
     o_ref[0] = outs[0] if len(outs) == 1 else jnp.concatenate(outs, axis=1)
 
 
-def attend(nbr, cnt, gain, q_blocks, bias, kv_table, p0, width_q):
-    steps = q_blocks.shape[0]
+def attend(nbr, cnt, gain, q_blocks, bias, kv_table, p0, width_q, g0, steps):
     span = NB * BLK
     grid_spec = pltpu.PrefetchScalarGridSpec(
         num_scalar_prefetch=2,
         grid=(steps,),
         in_specs=[
             pl.BlockSpec(memory_space=pltpu.SMEM),
-            pl.BlockSpec((1, BLK, width_q), lambda g, n, c: (g, 0, p0)),
-            pl.BlockSpec((1, BLK, span), lambda g, n, c: (g, 0, 0)),
+            pl.BlockSpec((1, BLK, width_q), lambda g, n, c: (g + g0, 0, p0)),
+            pl.BlockSpec((1, BLK, span), lambda g, n, c: (g + g0, 0, 0)),
             pl.BlockSpec(kv_table.shape, lambda g, n, c: (0, 0, 0)),
         ],
         out_specs=pl.BlockSpec((1, BLK, width_q), lambda g, n, c: (g, 0, 0)),
     )
     return pl.pallas_call(
-        functools.partial(_attend_kernel, p0),
+        functools.partial(_attend_kernel, p0, g0),
         grid_spec=grid_spec,
         out_shape=jax.ShapeDtypeStruct((steps, BLK, width_q), jnp.bfloat16),
         compiler_params=pltpu.CompilerParams(
@@ -89,11 +91,13 @@
     second = jnp.max(jnp.where(present, lidx, -1), axis=1)
     second = jnp.where(second < 0, first, second)
     req = jnp.stack([first, second], axis=1).astype(jnp.int32)
-    pos = owner * 2 + (local != first[owner]).astype(jnp.int32)
+    hit = owner.reshape(-1)[:, None] == jnp.arange(owners, dtype=jnp.int32)[None, :]
+    first_of = jnp.sum(jnp.where(hit, first[None, :], 0), axis=1).reshape(owner.shape)
+    pos = owner * 2 + (local != first_of).astype(jnp.int32)
     return req, pos.astype(jnp.int32)
 
 
-def body(features, w_qkv, w_out, bias_gain, edge_bias, neighbours, counts):
+def _body(features, w_qkv, w_out, bias_gain, edge_bias, neighbours, counts):
     rows = features.shape[0]
     width_heads = w_qkv.shape[2]
     blocks_dev = rows // BLK
@@ -129,14 +133,28 @@
         if table is not None:
             table, send = lax.optimization_barrier((table, send))
         table = lax.all_to_all(send, "row", 0, 0, tiled=True)
-        att = attend(pos, counts, bias_gain, q_blocks, edge_bias, table, c, chunk)
-        att = att.reshape(rows, chunk)
-        part = jnp.dot(att, w_own[cols], preferred_element_type=jnp.float32)
-        total = part if total is None else total + part
-        for s in range(1, head_devs):
-            perm = [(i, (i + s) % head_devs) for i in range(head_devs)]
-            att_s = lax.ppermute(att, "head", perm)
-            total = total + jnp.dot(att_s, w_parts[s - 1][cols], preferred_element_type=jnp.float32)
+        splits = 1 if c == 0 else 2
+        steps = blocks_dev // splits
+        for half in range(splits):
+            rs = slice(half * steps * BLK, (half + 1) * steps * BLK)
+            att = attend(
+                pos, counts, bias_gain, q_blocks, edge_bias, table, c, chunk, half * steps, steps
+            ).reshape(steps * BLK, chunk)
+            att_all = [att]
+            w_all = [w_own[cols]]
+            for s in range(1, head_devs):
+                perm = [(i, (i + s) % head_devs) for i in range(head_devs)]
+                att_all.append(lax.ppermute(att, "head", perm))
+                w_all.append(w_parts[s - 1][cols])
+            part = jnp.dot(
+                jnp.concatenate(att_all, axis=1),
+                jnp.concatenate(w_all, axis=0),
+                preferred_element_type=jnp.float32,
+            )
+            if total is None:
+                total = part
+            else:
+                total = total.at[rs].add(part)
     return total.astype(jnp.bfloat16)
 
 
@@ -151,4 +169,4 @@
         P("row"),
     )
     out_specs = P("row", "head")
-    return jax.shard_map(body, mesh=mesh, in_specs=in_specs, out_specs=out_specs, check_vma=False)
+    return jax.shard_map(_body, mesh=mesh, in_specs=in_specs, out_specs=out_specs, check_vma=False)

time: 124 us -> 124 us (level)
  matrix products: 15.4 us -> 6.34 us
  starting transfers between devices: 33.3 us -> 37.6 us
  local copies, waits for them, and re-layouts: 14.2 us -> 18.3 us
    dot_general x11 -> x6, matrix products: 15.4 us -> 6.34 us  [the longest x3 1.81 us: _body(): jnp.dot(jnp.concatenate(att_all, axis=1), jnp.concatenate(w_all, axis=0),...]
    slice x2 -> x6, local copies, waits for them, and re-layouts: 0.04 us -> 5.28 us  [the longest x3 3.71 us: _body(): w_all.append(w_parts[s - 1][cols])]
    ppermute x9 -> x12, starting transfers between devices: 14.4 us -> 18.7 us  [the longest x9 12.2 us: _body(): att_all.append(lax.ppermute(att, 'head', perm))]
    gather x4 -> x2, local copies, waits for them, and re-layouts: 7.45 us -> 4.01 us  [_body(): outgoing.append(jnp.take(kv, wanted, axis=0, mode='clip'))]
    unnamed x16 -> x30, local copies, waits for them, and re-layouts: 1.43 us -> 2.96 us
    pallas_call x2 -> x3, Pallas kernels: 26.6 us -> 26.3 us  [attend(): pl.pallas_call(functools.partial(_attend_kernel, p0, g0), grid_spec=grid_...]
    ppermute x9 -> x12, waiting for transfers between devices: 4.59 us -> 4.58 us  [the longest x9 4.51 us: _body(): att_all.append(lax.ppermute(att, 'head', perm))]
  transfers between devices with their start and end apart: 12 -> 15, of which waited for: 4 -> 5; matrix products, arithmetic and copies ran while one was open for 19% -> 15% of each run, Pallas kernels for 22% -> 21%
where the time goes in v11:
time: 124 us; the launch traced here: 123 us
  starting transfers between devices  37.6 us (30%)
  waiting for transfers between devices  31.6 us (25%)
  Pallas kernels  26.3 us (21%)
  local copies, waits for them, and re-layouts  18.3 us (15%)
  matrix products  6.34 us (5%)
  other arithmetic  2.61 us (2%)
    pallas_call x3, Pallas kernels, attend(): pl.pallas_call(functools.partial(_attend_kernel, p0, g0), grid_spec=grid_...  26.3 us
    all_to_all x2, waiting for transfers between devices, _body(): table = lax.all_to_all(send, 'row', 0, 0, tiled=True)  24.8 us
    ppermute x9, starting transfers between devices, _body(): att_all.append(lax.ppermute(att, 'head', perm))  12.2 us
    all_to_all x2, starting transfers between devices, _body(): table = lax.all_to_all(send, 'row', 0, 0, tiled=True)  11.3 us
    all_to_all x1, starting transfers between devices, _body(): wanted = lax.all_to_all(req, 'row', 0, 0, tiled=True).reshape(-1)  7.62 us
    ppermute x3, starting transfers between devices, _body(): w_parts.append(lax.ppermute(piece, 'head', perm))  6.5 us
    ppermute x9, waiting for transfers between devices, _body(): att_all.append(lax.ppermute(att, 'head', perm))  4.51 us
    gather x2, local copies, waits for them, and re-layouts, _body(): outgoing.append(jnp.take(kv, wanted, axis=0, mode='clip'))  4.01 us
  transfers between devices with their start and end apart: 15, of which 5 were waited for; matrix products, arithmetic and copies ran while one was open for 15% of the time, Pallas kernels for 21%

profile of v11, /device:TPU:2, one launch (start us, length us, event | category | flops | bytes accessed | tf_op | source)
XLA Modules:
  0.0 123.2 jit_solution(3873987326390578292)
XLA Ops:
  0.0 0.8 eq.65
  0.9 0.2 fusion.14
  1.0 0.1 reshape.108
  1.1 0.1 select_reduce_fusion.1
  1.3 0.7 copy.16
  1.9 7.6 %all-to-all-start = ((s32[32,1,2]{2,1,0:T(1,128)}), s32[32,1,2]{2,1,0:T(1,128)S(1)}, u32[]{:S(2)}, u32[]{:S(2)}) async-start(s32[32,1,2]{2,1,0:T(1,128)} %copy.16), calls=%async_computation | async-start | bytes 32768 | tf_op jit(solution)/shard_map/all_to_all | solution.py:110
  9.6 1.5 %convolution_convert_fusion.1 = bf16[512,256]{0,1:T(8,128)(2,1)S(1)} fusion(bf16[512,1024]{1,0:T(8,128)(2,1)S(1)} %copy-done, bf16[3,1024,256]{2,1,0:T(8,128)(2,1)} %param.12), kind=kOutput, calls=%fused_computation.3 | convolution fusion | flops 268566528 | bytes 1835008 | tf_op jit(solution)/shard_map/dot_general | solution.py:112
  11.1 1.5 %convolution_convert_fusion = bf16[512,256]{0,1:T(8,128)(2,1)S(1)} fusion(bf16[512,1024]{1,0:T(8,128)(2,1)S(1)} %copy-done, bf16[3,1024,256]{2,1,0:T(8,128)(2,1)} %param.12), kind=kOutput, calls=%fused_computation.2 | convolution fusion | flops 268566528 | bytes 1835008 | tf_op jit(solution)/shard_map/dot_general | solution.py:113
  12.7 0.7 pad_maximum_fusion
  13.4 0.1 copy.15
  13.6 2.2 %all-to-all-done = s32[32,1,2]{2,1,0:T(1,128)S(1)} async-done(((s32[32,1,2]{2,1,0:T(1,128)}), s32[32,1,2]{2,1,0:T(1,128)S(1)}, u32[]{:S(2)}, u32[]{:S(2)}) %all-to-all-start) | async-done | bytes 288 | tf_op jit(solution)/shard_map/all_to_all | solution.py:110
  15.7 0.6 broadcast.97
  16.3 0.7 reduce.7
  17.1 0.1 reshape.118
  17.2 2.0 %gather_fusion = bf16[64,64,256]{2,1,0:T(8,128)(2,1)} fusion(bf16[8,64,256]{2,1,0:T(8,128)(2,1)S(1)} %bitcast.41, s32[1024]{0:T(1024)S(1)} %pad_clamp_fusion), kind=kCustom, calls=%fused_computation | custom fusion | bytes 4194560 | tf_op jit(solution)/shard_map/jit(_take)/gather | solution.py:127
  19.2 5.2 %all-to-all-start.1 = ((bf16[64,64,256]{2,1,0:T(8,128)(2,1)}), bf16[64,64,256]{2,1,0:T(8,128)(2,1)S(1)}, u32[]{:S(2)}, u32[]{:S(2)}) async-start(bf16[64,64,256]{2,1,0:T(8,128)(2,1)} %gather_fusion), calls=%async_computation.1 | async-start | bytes 4194304 | tf_op jit(solution)/shard_map/all_to_all | solution.py:135
  24.4 1.1 copy.17
  25.5 2.0 %gather_fusion.1 = bf16[64,64,256]{2,1,0:T(8,128)(2,1)} fusion(bf16[8,64,256]{2,1,0:T(8,128)(2,1)S(1)} %bitcast.42, s32[1024]{0:T(1024)S(1)} %pad_clamp_fusion), kind=kCustom, calls=%fused_computation.1 | custom fusion | bytes 4194560 | tf_op jit(solution)/shard_map/jit(_take)/gather | solution.py:127
  27.5 24.8 %all-to-all-done.1.kv_ref = bf16[64,64,256]{2,1,0:T(8,128)(2,1)S(1)} async-done(((bf16[64,64,256]{2,1,0:T(8,128)(2,1)}), bf16[64,64,256]{2,1,0:T(8,128)(2,1)S(1)}, u32[]{:S(2)}, u32[]{:S(2)}) %all-to-all-start.1) | async-done | bytes 2097184 | tf_op jit(solution)/shard_map/all_to_all | solution.py:135
  52.3 1.3 %copy-done.1 = bf16[64,64,256]{2,1,0:T(8,128)(2,1)} copy-done((bf16[64,64,256]{2,1,0:T(8,128)(2,1)}, bf16[64,64,256]{2,1,0:T(8,128)(2,1)S(1)}, u32[]{:S(2)}) %copy-start.1) | copy-done | bytes 2097176
  53.6 6.0 %all-to-all-start.2 = ((bf16[64,64,256]{2,1,0:T(8,128)(2,1)}), bf16[64,64,256]{2,1,0:T(8,128)(2,1)S(1)}, u32[]{:S(2)}, u32[]{:S(2)}) async-start(bf16[64,64,256]{2,1,0:T(8,128)(2,1)} %gather_fusion.1), calls=%async_computation.2 | async-start | bytes 4194304 | tf_op jit(solution)/shard_map/all_to_all | solution.py:135
  59.7 0.0 copy-start.3
  59.7 0.0 copy-start.4
  59.8 1.8 %constant_dynamic-slice_fusion.3 = (bf16[256,256]{1,0:T(8,128)(2,1)}, bf16[256,256]{1,0:T(8,128)(2,1)}, bf16[256,256]{1,0:T(8,128)(2,1)}) fusion(bf16[256,1024]{1,0:T(8,128)(2,1)} %param.13, s32[]{:T(128)S(6)} %select_n.91, s32[]{:T(128)S(6)} %select_n.95, s32[]{:T(128)S(6)} %select_n.93), kind=kLoop, calls=%fused_computation.72 | loop fusion | bytes 786444 | tf_op jit(solution)/shard_map/dynamic_slice | solution.py:117
  61.6 1.9 %collective-permute-start.3 = (bf16[256,256]{1,0:T(8,128)(2,1)}, bf16[256,256]{1,0:T(8,128)(2,1)}, u32[]{:S(2)}, u32[]{:S(2)}) collective-permute-start(bf16[256,256]{1,0:T(8,128)(2,1)} %get-tuple-element.35), channel_id=1, source_target_pairs={{0,1},{1,2},{2,3},{3,0},{4,5},{5,6},{6,7},{7,4},{8,9},{9,10},{10,1... | collective-permute-start | bytes 393224 | tf_op jit(solution)/shard_map/ppermute | solution.py:119
  63.5 3.6 %collective-permute-start.4 = (bf16[256,256]{1,0:T(8,128)(2,1)}, bf16[256,256]{1,0:T(8,128)(2,1)S(1)}, u32[]{:S(2)}, u32[]{:S(2)}) collective-permute-start(bf16[256,256]{1,0:T(8,128)(2,1)} %get-tuple-element.37), channel_id=1, source_target_pairs={{0,2},{1,3},{2,0},{3,1},{4,6},{5,7},{6,4},{7,5},{8,10},{9,11},{10,... | collective-permute-start | bytes 393224 | tf_op jit(solution)/shard_map/ppermute | solution.py:119
  67.1 1.0 collective-permute-start.5
  68.1 0.1 eq.61
  68.2 0.1 select_reduce_fusion
  68.3 0.7 reshape.109
  68.9 1.5 %convolution_convert_fusion.2 = bf16[512,256]{1,0:T(8,128)(2,1)S(1)} fusion(bf16[512,1024]{1,0:T(8,128)(2,1)S(1)} %copy-done, bf16[3,1024,256]{2,1,0:T(8,128)(2,1)} %param.12), kind=kOutput, calls=%fused_computation.4 | convolution fusion | flops 268566528 | bytes 1835008 | tf_op jit(solution)/shard_map/dot_general | solution.py:111
  70.5 1.5 %fusion.50 = (bf16[128,256]{1,0:T(8,128)(2,1)}, bf16[128,256]{1,0:T(8,128)(2,1)}) fusion(bf16[256,1024]{1,0:T(8,128)(2,1)} %param.13, s32[]{:T(128)S(6)} %add.72, s32[]{:T(128)S(6)} %select_n.89), kind=kLoop, calls=%fused_computation.77 | loop fusion | bytes 262152 | tf_op jit(solution)/shard_map/slice | solution.py:144
  72.0 0.0 collective-permute-done.3
  72.0 1.5 %fusion.53 = (bf16[128,256]{1,0:T(8,128)(2,1)}, bf16[128,256]{1,0:T(8,128)(2,1)}) fusion(bf16[256,256]{1,0:T(8,128)(2,1)} %collective-permute-done.3), kind=kLoop, calls=%fused_computation.80 | loop fusion | bytes 262144 | tf_op jit(solution)/shard_map/slice | solution.py:148
  73.5 0.1 collective-permute-done.4
  73.6 0.7 fusion.54
  74.3 1.6 %copy-done.2 = bf16[64,64,256]{2,1,0:T(8,128)(2,1)S(1)} copy-done((bf16[64,64,256]{2,1,0:T(8,128)(2,1)S(1)}, bf16[64,64,256]{2,1,0:T(8,128)(2,1)}, u32[]{:S(2)}) %copy-start.2) | copy-done | bytes 2097176
  75.9 12.6 %shard_map.73 = bf16[8,64,128]{2,1,0:T(8,128)(2,1)S(1)} custom-call(s32[8,64]{1,0:T(8,128)S(1)} %convert_add_fusion.nbr_ref, s32[8]{0:T(128)S(1)} %copy-done.3, f32[4]{0:T(128)S(1)} %copy-done.4, bf16[8,64,256]{2,1,0:T(8,128)(2,1)S(1)} %bitcast.26, bf16[8,64,4096]{2,1,0:T(8,128)(2,1)} %bias_ref.5, bf16[64,64,256]{2,1,0:T(8,128)(2,1)S(1)} %copy-done.2), custom_call_target="tpu_custom_call" | custom-call | tf_op jit(solution)/shard_map/pallas_call | solution.py:72
  88.5 1.1 collective-permute-start
  89.6 0.7 collective-permute-start.1
  90.3 2.0 %collective-permute-start.2 = (bf16[512,128]{1,0:T(8,128)(2,1)S(1)}, bf16[512,128]{1,0:T(8,128)(2,1)}, u32[]{:S(2)}, u32[]{:S(2)}) collective-permute-start(bf16[512,128]{1,0:T(8,128)(2,1)S(1)} %bitcast.31), channel_id=1, source_target_pairs={{0,3},{1,0},{2,1},{3,2},{4,7},{5,4},{6,5},{7,6},{8,11},{9,8},{10,9... | collective-permute-start | bytes 393224 | tf_op jit(solution)/shard_map/ppermute | solution.py:147
  92.4 0.0 collective-permute-done.5
  92.4 1.5 %fusion.55 = (bf16[128,256]{1,0:T(8,128)(2,1)}, bf16[128,256]{1,0:T(8,128)(2,1)}) fusion(bf16[256,256]{1,0:T(8,128)(2,1)} %collective-permute-done.5), kind=kLoop, calls=%fused_computation.82 | loop fusion | bytes 262144 | tf_op jit(solution)/shard_map/slice | solution.py:148
  93.9 0.0 all-to-all-done.2.kv_ref
  93.9 6.8 %shard_map.74 = bf16[4,64,128]{2,1,0:T(8,128)(2,1)S(1)} custom-call(s32[8,64]{1,0:T(8,128)S(1)} %convert_add_fusion.nbr_ref, s32[8]{0:T(128)S(1)} %copy-done.3, f32[4]{0:T(128)S(1)} %copy-done.4, bf16[8,64,256]{2,1,0:T(8,128)(2,1)S(1)} %bitcast.27, bf16[8,64,4096]{2,1,0:T(8,128)(2,1)} %bias_ref.5, bf16[64,64,256]{2,1,0:T(8,128)(2,1)S(1)} %all-to-all-done.2.kv_ref), custom_call_target="tpu_custom_call" | custom-call | tf_op jit(solution)/shard_map/pallas_call | solution.py:72
  100.8 0.4 collective-permute-start.6
  101.1 2.5 %collective-permute-start.7 = (bf16[256,128]{1,0:T(8,128)(2,1)S(1)}, bf16[256,128]{1,0:T(8,128)(2,1)S(1)}, u32[]{:S(2)}, u32[]{:S(2)}) collective-permute-start(bf16[256,128]{1,0:T(8,128)(2,1)S(1)} %bitcast.34), channel_id=1, source_target_pairs={{0,2},{1,3},{2,0},{3,1},{4,6},{5,7},{6,4},{7,5},{8,10},{9,11},{10,... | collective-permute-start | bytes 196616 | tf_op jit(solution)/shard_map/ppermute | solution.py:147
  103.6 0.0 collective-permute-done
  103.6 2.2 %collective-permute-start.8 = (bf16[256,128]{1,0:T(8,128)(2,1)S(1)}, bf16[256,128]{1,0:T(8,128)(2,1)S(1)}, u32[]{:S(2)}, u32[]{:S(2)}) collective-permute-start(bf16[256,128]{1,0:T(8,128)(2,1)S(1)} %bitcast.35), channel_id=1, source_target_pairs={{0,3},{1,0},{2,1},{3,2},{4,7},{5,4},{6,5},{7,6},{8,11},{9,8},{10,9... | collective-permute-start | bytes 196616 | tf_op jit(solution)/shard_map/ppermute | solution.py:147
  105.8 0.0 collective-permute-done.1
  105.9 0.0 collective-permute-done.2
  105.9 1.3 %fusion = f32[512,256]{1,0:T(8,128)S(1)} fusion(bf16[512,128]{1,0:T(8,128)(2,1)} %collective-permute-done.2, bf16[512,128]{1,0:T(8,128)(2,1)} %collective-permute-done.1, bf16[512,128]{1,0:T(8,128)(2,1)} %collective-permute-done, bf16[512,128]{1,0:T(8,128)(2,1)S(1)} %bitcast.32, bf16[128,256]{1,0:T(8,128)(2,1)S(1)} %copy-done.12, ...), kind=kOutput, calls=%fused_computation.5 | convolution fusion | flops 137363456 | bytes 1310720 | tf_op jit(solution)/shard_map/dot_general | solution.py:149
  107.3 0.0 copy-start.8
  107.3 6.9 %shard_map.75 = bf16[4,64,128]{2,1,0:T(8,128)(2,1)S(1)} custom-call(s32[8,64]{1,0:T(8,128)S(1)} %convert_add_fusion.nbr_ref, s32[8]{0:T(128)S(1)} %copy-done.3, f32[4]{0:T(128)S(1)} %copy-done.4, bf16[8,64,256]{2,1,0:T(8,128)(2,1)S(1)} %bitcast.28, bf16[8,64,4096]{2,1,0:T(8,128)(2,1)} %bias_ref.5, bf16[64,64,256]{2,1,0:T(8,128)(2,1)S(1)} %all-to-all-done.2.kv_ref), custom_call_target="tpu_custom_call" | custom-call | tf_op jit(solution)/shard_map/pallas_call | solution.py:72
  114.1 1.2 collective-permute-start.10
  115.4 1.3 %collective-permute-start.11 = (bf16[256,128]{1,0:T(8,128)(2,1)S(1)}, bf16[256,128]{1,0:T(8,128)(2,1)S(1)}, u32[]{:S(2)}, u32[]{:S(2)}) collective-permute-start(bf16[256,128]{1,0:T(8,128)(2,1)S(1)} %bitcast.38), channel_id=1, source_target_pairs={{0,3},{1,0},{2,1},{3,2},{4,7},{5,4},{6,5},{7,6},{8,11},{9,8},{10,9... | collective-permute-start | bytes 196616 | tf_op jit(solution)/shard_map/ppermute | solution.py:147
  116.7 0.0 collective-permute-done.6
  116.7 0.7 collective-permute-start.9
  117.4 0.0 collective-permute-done.8
  117.4 0.2 fusion.16
  117.7 2.3 %collective-permute-done.10 = bf16[256,128]{1,0:T(8,128)(2,1)S(1)} collective-permute-done((bf16[256,128]{1,0:T(8,128)(2,1)S(1)}, bf16[256,128]{1,0:T(8,128)(2,1)S(1)}, u32[]{:S(2)}, u32[]{:S(2)}) %collective-permute-start.10) | collective-permute-done | bytes 65568 | tf_op jit(solution)/shard_map/ppermute | solution.py:147
  120.0 2.2 %collective-permute-done.9 = bf16[256,128]{1,0:T(8,128)(2,1)S(1)} collective-permute-done((bf16[256,128]{1,0:T(8,128)(2,1)S(1)}, bf16[256,128]{1,0:T(8,128)(2,1)S(1)}, u32[]{:S(2)}, u32[]{:S(2)}) %collective-permute-start.9) | collective-permute-done | bytes 65568 | tf_op jit(solution)/shard_map/ppermute | solution.py:147
  122.2 0.2 fusion.15
  122.4 0.7 convert_element_type.19
  (35 shorter events, 0.1 us)
Async XLA Ops:
  0.0 9.6 %copy-start = (bf16[512,1024]{1,0:T(8,128)(2,1)S(1)}, bf16[512,1024]{1,0:T(8,128)(2,1)}, u32[]{:S(2)}) copy-start(bf16[512,1024]{1,0:T(8,128)(2,1)} %param.11) | copy-start | bytes 3145732
  1.9 13.8 %all-to-all-start = ((s32[32,1,2]{2,1,0:T(1,128)}), s32[32,1,2]{2,1,0:T(1,128)S(1)}, u32[]{:S(2)}, u32[]{:S(2)}) async-start(s32[32,1,2]{2,1,0:T(1,128)} %copy.16), calls=%async_computation | async-start | bytes 32768 | tf_op jit(solution)/shard_map/all_to_all | solution.py:110
  19.2 33.2 %all-to-all-start.1 = ((bf16[64,64,256]{2,1,0:T(8,128)(2,1)}), bf16[64,64,256]{2,1,0:T(8,128)(2,1)S(1)}, u32[]{:S(2)}, u32[]{:S(2)}) async-start(bf16[64,64,256]{2,1,0:T(8,128)(2,1)} %gather_fusion), calls=%async_computation.1 | async-start | bytes 4194304 | tf_op jit(solution)/shard_map/all_to_all | solution.py:135
  27.5 40.5 %copy-start.13 = (s32[8,64]{1,0:T(8,128)S(1)}, s32[8,64]{1,0:T(8,128)}, u32[]{:S(2)}) copy-start(s32[8,64]{1,0:T(8,128)} %param.16) | copy-start | bytes 6148
  52.3 1.3 %copy-start.1 = (bf16[64,64,256]{2,1,0:T(8,128)(2,1)}, bf16[64,64,256]{2,1,0:T(8,128)(2,1)S(1)}, u32[]{:S(2)}) copy-start(bf16[64,64,256]{2,1,0:T(8,128)(2,1)S(1)} %all-to-all-done.1.kv_ref) | copy-start | bytes 6291460
  53.6 40.2 %all-to-all-start.2 = ((bf16[64,64,256]{2,1,0:T(8,128)(2,1)}), bf16[64,64,256]{2,1,0:T(8,128)(2,1)S(1)}, u32[]{:S(2)}, u32[]{:S(2)}) async-start(bf16[64,64,256]{2,1,0:T(8,128)(2,1)} %gather_fusion.1), calls=%async_computation.2 | async-start | bytes 4194304 | tf_op jit(solution)/shard_map/all_to_all | solution.py:135
  59.7 14.6 %copy-start.3 = (s32[8]{0:T(128)S(1)}, s32[8]{0:T(128)}, u32[]{:S(2)}) copy-start(s32[8]{0:T(128)} %cnt_ref.5) | copy-start | bytes 100
  59.7 14.6 %copy-start.4 = (f32[4]{0:T(128)S(1)}, f32[4]{0:T(128)}, u32[]{:S(2)}) copy-start(f32[4]{0:T(128)} %gain_ref.5) | copy-start | bytes 52
  61.6 10.4 %collective-permute-start.3 = (bf16[256,256]{1,0:T(8,128)(2,1)}, bf16[256,256]{1,0:T(8,128)(2,1)}, u32[]{:S(2)}, u32[]{:S(2)}) collective-permute-start(bf16[256,256]{1,0:T(8,128)(2,1)} %get-tuple-element.35), channel_id=1, source_target_pairs={{0,1},{1,2},{2,3},{3,0},{4,5},{5,6},{6,7},{7,4},{8,9},{9,10},{10,1... | collective-permute-start | bytes 393224 | tf_op jit(solution)/shard_map/ppermute | solution.py:119
  63.5 10.1 %collective-permute-start.4 = (bf16[256,256]{1,0:T(8,128)(2,1)}, bf16[256,256]{1,0:T(8,128)(2,1)S(1)}, u32[]{:S(2)}, u32[]{:S(2)}) collective-permute-start(bf16[256,256]{1,0:T(8,128)(2,1)} %get-tuple-element.37), channel_id=1, source_target_pairs={{0,2},{1,3},{2,0},{3,1},{4,6},{5,7},{6,4},{7,5},{8,10},{9,11},{10,... | collective-permute-start | bytes 393224 | tf_op jit(solution)/shard_map/ppermute | solution.py:119
  67.1 25.3 %collective-permute-start.5 = (bf16[256,256]{1,0:T(8,128)(2,1)}, bf16[256,256]{1,0:T(8,128)(2,1)}, u32[]{:S(2)}, u32[]{:S(2)}) collective-permute-start(bf16[256,256]{1,0:T(8,128)(2,1)} %get-tuple-element.36), channel_id=1, source_target_pairs={{0,3},{1,0},{2,1},{3,2},{4,7},{5,4},{6,5},{7,6},{8,11},{9,8},{10,9... | collective-permute-start | bytes 393224 | tf_op jit(solution)/shard_map/ppermute | solution.py:119
  68.9 1.5 %copy-start.14 = (s32[8,64]{1,0:T(8,128)S(1)}, s32[8,64]{1,0:T(8,128)}, u32[]{:S(2)}) copy-start(s32[8,64]{1,0:T(8,128)} %reshape.109) | copy-start | bytes 6148
  74.3 1.6 %copy-start.2 = (bf16[64,64,256]{2,1,0:T(8,128)(2,1)S(1)}, bf16[64,64,256]{2,1,0:T(8,128)(2,1)}, u32[]{:S(2)}) copy-start(bf16[64,64,256]{2,1,0:T(8,128)(2,1)} %copy-done.1) | copy-start | bytes 6291460
  88.5 15.1 %collective-permute-start = (bf16[512,128]{1,0:T(8,128)(2,1)S(1)}, bf16[512,128]{1,0:T(8,128)(2,1)}, u32[]{:S(2)}, u32[]{:S(2)}) collective-permute-start(bf16[512,128]{1,0:T(8,128)(2,1)S(1)} %bitcast.29), channel_id=1, source_target_pairs={{0,1},{1,2},{2,3},{3,0},{4,5},{5,6},{6,7},{7,4},{8,9},{9,10},{10,1... | collective-permute-start | bytes 393224 | tf_op jit(solution)/shard_map/ppermute | solution.py:147
  89.6 16.3 %collective-permute-start.1 = (bf16[512,128]{1,0:T(8,128)(2,1)S(1)}, bf16[512,128]{1,0:T(8,128)(2,1)}, u32[]{:S(2)}, u32[]{:S(2)}) collective-permute-start(bf16[512,128]{1,0:T(8,128)(2,1)S(1)} %bitcast.30), channel_id=1, source_target_pairs={{0,2},{1,3},{2,0},{3,1},{4,6},{5,7},{6,4},{7,5},{8,10},{9,11},{10,... | collective-permute-start | bytes 393224 | tf_op jit(solution)/shard_map/ppermute | solution.py:147
  90.3 15.5 %collective-permute-start.2 = (bf16[512,128]{1,0:T(8,128)(2,1)S(1)}, bf16[512,128]{1,0:T(8,128)(2,1)}, u32[]{:S(2)}, u32[]{:S(2)}) collective-permute-start(bf16[512,128]{1,0:T(8,128)(2,1)S(1)} %bitcast.31), channel_id=1, source_target_pairs={{0,3},{1,0},{2,1},{3,2},{4,7},{5,4},{6,5},{7,6},{8,11},{9,8},{10,9... | collective-permute-start | bytes 393224 | tf_op jit(solution)/shard_map/ppermute | solution.py:147
  93.9 12.0 %copy-start.9 = (bf16[128,256]{1,0:T(8,128)(2,1)S(1)}, bf16[128,256]{1,0:T(8,128)(2,1)}, u32[]{:S(2)}) copy-start(bf16[128,256]{1,0:T(8,128)(2,1)} %get-tuple-element.34) | copy-start | bytes 196612
  93.9 12.0 %copy-start.10 = (bf16[128,256]{1,0:T(8,128)(2,1)S(1)}, bf16[128,256]{1,0:T(8,128)(2,1)}, u32[]{:S(2)}) copy-start(bf16[128,256]{1,0:T(8,128)(2,1)} %get-tuple-element.43) | copy-start | bytes 196612
  93.9 12.0 %copy-start.11 = (bf16[128,256]{1,0:T(8,128)(2,1)S(1)}, bf16[128,256]{1,0:T(8,128)(2,1)}, u32[]{:S(2)}) copy-start(bf16[128,256]{1,0:T(8,128)(2,1)} %get-tuple-element.45) | copy-start | bytes 196612
  93.9 12.0 %copy-start.12 = (bf16[128,256]{1,0:T(8,128)(2,1)S(1)}, bf16[128,256]{1,0:T(8,128)(2,1)}, u32[]{:S(2)}) copy-start(bf16[128,256]{1,0:T(8,128)(2,1)} %get-tuple-element.47) | copy-start | bytes 196612
  100.8 15.9 %collective-permute-start.6 = (bf16[256,128]{1,0:T(8,128)(2,1)S(1)}, bf16[256,128]{1,0:T(8,128)(2,1)S(1)}, u32[]{:S(2)}, u32[]{:S(2)}) collective-permute-start(bf16[256,128]{1,0:T(8,128)(2,1)S(1)} %bitcast.33), channel_id=1, source_target_pairs={{0,1},{1,2},{2,3},{3,0},{4,5},{5,6},{6,7},{7,4},{8,9},{9,10},{10,1... | collective-permute-start | bytes 196616 | tf_op jit(solution)/shard_map/ppermute | solution.py:147
  101.1 16.3 %collective-permute-start.7 = (bf16[256,128]{1,0:T(8,128)(2,1)S(1)}, bf16[256,128]{1,0:T(8,128)(2,1)S(1)}, u32[]{:S(2)}, u32[]{:S(2)}) collective-permute-start(bf16[256,128]{1,0:T(8,128)(2,1)S(1)} %bitcast.34), channel_id=1, source_target_pairs={{0,2},{1,3},{2,0},{3,1},{4,6},{5,7},{6,4},{7,5},{8,10},{9,11},{10,... | collective-permute-start | bytes 196616 | tf_op jit(solution)/shard_map/ppermute | solution.py:147
  103.6 13.8 %collective-permute-start.8 = (bf16[256,128]{1,0:T(8,128)(2,1)S(1)}, bf16[256,128]{1,0:T(8,128)(2,1)S(1)}, u32[]{:S(2)}, u32[]{:S(2)}) collective-permute-start(bf16[256,128]{1,0:T(8,128)(2,1)S(1)} %bitcast.35), channel_id=1, source_target_pairs={{0,3},{1,0},{2,1},{3,2},{4,7},{5,4},{6,5},{7,6},{8,11},{9,8},{10,9... | collective-permute-start | bytes 196616 | tf_op jit(solution)/shard_map/ppermute | solution.py:147
  107.2 10.2 %copy-start.5 = (bf16[128,256]{1,0:T(8,128)(2,1)S(1)}, bf16[128,256]{1,0:T(8,128)(2,1)}, u32[]{:S(2)}) copy-start(bf16[128,256]{1,0:T(8,128)(2,1)} %get-tuple-element.33) | copy-start | bytes 196612
  107.2 10.2 %copy-start.6 = (bf16[128,256]{1,0:T(8,128)(2,1)S(1)}, bf16[128,256]{1,0:T(8,128)(2,1)}, u32[]{:S(2)}) copy-start(bf16[128,256]{1,0:T(8,128)(2,1)} %get-tuple-element.42) | copy-start | bytes 196612
  107.2 10.2 %copy-start.7 = (bf16[128,256]{1,0:T(8,128)(2,1)S(1)}, bf16[128,256]{1,0:T(8,128)(2,1)}, u32[]{:S(2)}) copy-start(bf16[128,256]{1,0:T(8,128)(2,1)} %get-tuple-element.44) | copy-start | bytes 196612
  107.3 10.2 %copy-start.8 = (bf16[128,256]{1,0:T(8,128)(2,1)S(1)}, bf16[128,256]{1,0:T(8,128)(2,1)}, u32[]{:S(2)}) copy-start(bf16[128,256]{1,0:T(8,128)(2,1)} %get-tuple-element.46) | copy-start | bytes 196612
  114.1 5.8 %collective-permute-start.10 = (bf16[256,128]{1,0:T(8,128)(2,1)S(1)}, bf16[256,128]{1,0:T(8,128)(2,1)S(1)}, u32[]{:S(2)}, u32[]{:S(2)}) collective-permute-start(bf16[256,128]{1,0:T(8,128)(2,1)S(1)} %bitcast.37), channel_id=1, source_target_pairs={{0,2},{1,3},{2,0},{3,1},{4,6},{5,7},{6,4},{7,5},{8,10},{9,11},{10,... | collective-permute-start | bytes 196616 | tf_op jit(solution)/shard_map/ppermute | solution.py:147
  115.4 4.6 %collective-permute-start.11 = (bf16[256,128]{1,0:T(8,128)(2,1)S(1)}, bf16[256,128]{1,0:T(8,128)(2,1)S(1)}, u32[]{:S(2)}, u32[]{:S(2)}) collective-permute-start(bf16[256,128]{1,0:T(8,128)(2,1)S(1)} %bitcast.38), channel_id=1, source_target_pairs={{0,3},{1,0},{2,1},{3,2},{4,7},{5,4},{6,5},{7,6},{8,11},{9,8},{10,9... | collective-permute-start | bytes 196616 | tf_op jit(solution)/shard_map/ppermute | solution.py:147
  116.7 5.5 %collective-permute-start.9 = (bf16[256,128]{1,0:T(8,128)(2,1)S(1)}, bf16[256,128]{1,0:T(8,128)(2,1)S(1)}, u32[]{:S(2)}, u32[]{:S(2)}) collective-permute-start(bf16[256,128]{1,0:T(8,128)(2,1)S(1)} %bitcast.39), channel_id=1, source_target_pairs={{0,1},{1,2},{2,3},{3,0},{4,5},{5,6},{6,7},{7,4},{8,9},{9,10},{10,1... | collective-permute-start | bytes 196616 | tf_op jit(solution)/shard_map/ppermute | solution.py:147

commit v12 on v10

--- a/solution.py
+++ b/solution.py
@@ -6,6 +6,7 @@
 from jax.experimental import pallas as pl
 from jax.experimental.pallas import tpu as pltpu
 from jax.sharding import PartitionSpec as P
+
 
 HD = 64
 BLK = 64
@@ -40,14 +41,16 @@
             q2, kp, (((1,), (1,)), ((), ())), preferred_element_type=jnp.float32
         )
         ws = []
+        sums = []
         for half in range(2):
             h = (p0 + pair) * 2 + half
             s = s2[half * BLK:(half + 1) * BLK] + gain_ref[h] * bias
             top = jnp.max(s, axis=1, keepdims=True)
             expo = jnp.exp(s - top)
-            total = jnp.sum(expo, axis=1, keepdims=True)
-            ws.append((expo * (1.0 / total)).astype(jnp.bfloat16))
+            sums.append(jnp.sum(expo, axis=1, keepdims=True))
+            ws.append(expo.astype(jnp.bfloat16))
         o2 = jnp.dot(jnp.concatenate(ws, axis=0), vp, preferred_element_type=jnp.float32)
+        o2 = o2 * (1.0 / jnp.concatenate(sums, axis=0))
         res = jnp.where(lane < HD, o2[:BLK], o2[BLK:])
         outs.append(res.astype(jnp.bfloat16))
     o_ref[0] = outs[0] if len(outs) == 1 else jnp.concatenate(outs, axis=1)
@@ -95,7 +98,7 @@
     return req, pos.astype(jnp.int32)
 
 
-def body(features, w_qkv, w_out, bias_gain, edge_bias, neighbours, counts):
+def _body(features, w_qkv, w_out, bias_gain, edge_bias, neighbours, counts):
     rows = features.shape[0]
     width_heads = w_qkv.shape[2]
     blocks_dev = rows // BLK
@@ -159,4 +162,4 @@
         P("row"),
     )
     out_specs = P("row", "head")
-    return jax.shard_map(body, mesh=mesh, in_specs=in_specs, out_specs=out_specs, check_vma=False)
+    return jax.shard_map(_body, mesh=mesh, in_specs=in_specs, out_specs=out_specs, check_vma=False)

time: 138 us -> 135 us (0.978)
  Pallas kernels: 27.3 us -> 24.9 us
    pallas_call x2, Pallas kernels: 27.3 us -> 24.9 us  [attend(): pl.pallas_call(functools.partial(_attend_kernel, p0), grid_spec=grid_spec...]
  transfers between devices with their start and end apart: 12 -> 12, of which waited for: 6 -> 6; matrix products, arithmetic and copies ran while one was open for 11% -> 12% of each run, Pallas kernels for 20% -> 19%
where the time goes in v12:
time: 135 us; the launch traced here: 133 us
  waiting for transfers between devices  51 us (38%)
  starting transfers between devices  35.2 us (26%)
  Pallas kernels  24.9 us (18%)
  local copies, waits for them, and re-layouts  14.1 us (10%)
  matrix products  5.82 us (4%)
  other arithmetic  1.88 us (1%)
    all_to_all x2, waiting for transfers between devices, _body(): table = lax.all_to_all(send, 'row', 0, 0, tiled=True)  39.3 us
    pallas_call x2, Pallas kernels, attend(): pl.pallas_call(functools.partial(_attend_kernel, p0), grid_spec=grid_spec...  24.9 us
    all_to_all x2, starting transfers between devices, _body(): table = lax.all_to_all(send, 'row', 0, 0, tiled=True)  12 us
    ppermute x6, starting transfers between devices, _body(): att_all.append(lax.ppermute(att, 'head', perm))  10.3 us
    ppermute x6, waiting for transfers between devices, _body(): att_all.append(lax.ppermute(att, 'head', perm))  8.5 us
    all_to_all x1, starting transfers between devices, _body(): wanted = lax.all_to_all(req, 'row', 0, 0, tiled=True).reshape(-1)  7.62 us
    ppermute x3, starting transfers between devices, _body(): w_parts.append(lax.ppermute(piece, 'head', perm))  5.3 us
    gather x2, local copies, waits for them, and re-layouts, _body(): outgoing.append(jnp.take(kv, wanted, axis=0, mode='clip'))  4.02 us
  transfers between devices with their start and end apart: 12, of which 6 were waited for; matrix products, arithmetic and copies ran while one was open for 12% of the time, Pallas kernels for 19%

profile of v12, /device:TPU:2, one launch (start us, length us, event | category | flops | bytes accessed | tf_op | source)
XLA Modules:
  0.0 133.3 jit_solution(4003654648088583040)
XLA Ops:
  0.0 0.0 copy-start
  0.0 0.8 eq.65
  0.9 0.2 fusion.22
  1.0 0.1 reshape.56
  1.1 0.1 select_reduce_fusion.1
  1.3 0.7 copy.16
  1.9 7.6 %all-to-all-start = ((s32[32,1,2]{2,1,0:T(1,128)}), s32[32,1,2]{2,1,0:T(1,128)S(1)}, u32[]{:S(2)}, u32[]{:S(2)}) async-start(s32[32,1,2]{2,1,0:T(1,128)} %copy.16), calls=%async_computation | async-start | bytes 32768 | tf_op jit(solution)/shard_map/all_to_all | solution.py:111
  9.6 0.0 copy-done
  9.6 1.5 %convolution_convert_fusion = bf16[512,256]{0,1:T(8,128)(2,1)S(1)} fusion(bf16[512,1024]{1,0:T(8,128)(2,1)S(1)} %copy-done, bf16[3,1024,256]{2,1,0:T(8,128)(2,1)} %param.8), kind=kOutput, calls=%fused_computation.4 | convolution fusion | flops 268566528 | bytes 1835008 | tf_op jit(solution)/shard_map/dot_general | solution.py:114
  11.1 1.5 %convolution_convert_fusion.1 = bf16[512,256]{0,1:T(8,128)(2,1)S(1)} fusion(bf16[512,1024]{1,0:T(8,128)(2,1)S(1)} %copy-done, bf16[3,1024,256]{2,1,0:T(8,128)(2,1)} %param.8), kind=kOutput, calls=%fused_computation.5 | convolution fusion | flops 268566528 | bytes 1835008 | tf_op jit(solution)/shard_map/dot_general | solution.py:113
  12.7 0.7 pad_maximum_fusion
  13.4 0.1 copy.15
  13.6 2.2 %all-to-all-done = s32[32,1,2]{2,1,0:T(1,128)S(1)} async-done(((s32[32,1,2]{2,1,0:T(1,128)}), s32[32,1,2]{2,1,0:T(1,128)S(1)}, u32[]{:S(2)}, u32[]{:S(2)}) %all-to-all-start) | async-done | bytes 288 | tf_op jit(solution)/shard_map/all_to_all | solution.py:111
  15.7 0.6 broadcast.71
  16.3 0.7 reduce.3
  17.1 0.1 reshape.65
  17.2 2.0 %gather_fusion = bf16[64,64,256]{2,1,0:T(8,128)(2,1)} fusion(bf16[8,64,256]{2,1,0:T(8,128)(2,1)S(1)} %bitcast.35, s32[1024]{0:T(1024)S(1)} %pad_clamp_fusion), kind=kCustom, calls=%fused_computation | custom fusion | bytes 4194560 | tf_op jit(solution)/shard_map/jit(_take)/gather | solution.py:128
  19.2 5.2 %all-to-all-start.1 = ((bf16[64,64,256]{2,1,0:T(8,128)(2,1)}), bf16[64,64,256]{2,1,0:T(8,128)(2,1)S(1)}, u32[]{:S(2)}, u32[]{:S(2)}) async-start(bf16[64,64,256]{2,1,0:T(8,128)(2,1)} %gather_fusion), calls=%async_computation.1 | async-start | bytes 4194304 | tf_op jit(solution)/shard_map/all_to_all | solution.py:136
  24.4 1.1 copy.17
  25.5 2.0 %gather_fusion.1 = bf16[64,64,256]{2,1,0:T(8,128)(2,1)} fusion(bf16[8,64,256]{2,1,0:T(8,128)(2,1)S(1)} %bitcast.36, s32[1024]{0:T(1024)S(1)} %pad_clamp_fusion), kind=kCustom, calls=%fused_computation.1 | custom fusion | bytes 4194560 | tf_op jit(solution)/shard_map/jit(_take)/gather | solution.py:128
  27.5 24.8 %all-to-all-done.1.kv_ref = bf16[64,64,256]{2,1,0:T(8,128)(2,1)S(1)} async-done(((bf16[64,64,256]{2,1,0:T(8,128)(2,1)}), bf16[64,64,256]{2,1,0:T(8,128)(2,1)S(1)}, u32[]{:S(2)}, u32[]{:S(2)}) %all-to-all-start.1) | async-done | bytes 2097184 | tf_op jit(solution)/shard_map/all_to_all | solution.py:136
  52.3 6.7 %all-to-all-start.2 = ((bf16[64,64,256]{2,1,0:T(8,128)(2,1)}), bf16[64,64,256]{2,1,0:T(8,128)(2,1)}, u32[]{:S(2)}, u32[]{:S(2)}) async-start(bf16[64,64,256]{2,1,0:T(8,128)(2,1)} %gather_fusion.1), calls=%async_computation.2 | async-start | bytes 4194304 | tf_op jit(solution)/shard_map/all_to_all | solution.py:136
  59.1 0.0 copy-start.1
  59.1 0.0 copy-start.2
  59.2 1.8 %constant_dynamic-slice_fusion.3 = (bf16[256,256]{1,0:T(8,128)(2,1)}, bf16[256,256]{1,0:T(8,128)(2,1)}, bf16[256,256]{1,0:T(8,128)(2,1)}) fusion(bf16[256,1024]{1,0:T(8,128)(2,1)} %param.9, s32[]{:T(128)S(6)} %select_n.91, s32[]{:T(128)S(6)} %select_n.95, s32[]{:T(128)S(6)} %select_n.93), kind=kLoop, calls=%fused_computation.68 | loop fusion | bytes 786444 | tf_op jit(solution)/shard_map/dynamic_slice | solution.py:118
  60.9 4.0 %collective-permute-start.5 = (bf16[256,256]{1,0:T(8,128)(2,1)}, bf16[256,256]{1,0:T(8,128)(2,1)}, u32[]{:S(2)}, u32[]{:S(2)}) collective-permute-start(bf16[256,256]{1,0:T(8,128)(2,1)} %get-tuple-element.12), channel_id=1, source_target_pairs={{0,3},{1,0},{2,1},{3,2},{4,7},{5,4},{6,5},{7,6},{8,11},{9,8},{10,9... | collective-permute-start | bytes 393224 | tf_op jit(solution)/shard_map/ppermute | solution.py:120
  65.0 0.0 collective-permute-start.4
  65.0 1.3 collective-permute-start.3
  66.2 0.0 copy-done.7
  66.3 0.1 eq.61
  66.3 0.1 select_reduce_fusion
  66.4 0.7 reshape.57
  67.1 1.5 %convolution_convert_fusion.2 = bf16[512,256]{1,0:T(8,128)(2,1)S(1)} fusion(bf16[512,1024]{1,0:T(8,128)(2,1)S(1)} %copy-done, bf16[3,1024,256]{2,1,0:T(8,128)(2,1)} %param.8), kind=kOutput, calls=%fused_computation.6 | convolution fusion | flops 268566528 | bytes 1835008 | tf_op jit(solution)/shard_map/dot_general | solution.py:112
  68.6 0.0 copy-done.8
  68.6 1.5 %constant_dynamic-slice_fusion = (bf16[128,256]{1,0:T(8,128)(2,1)}, bf16[128,256]{1,0:T(8,128)(2,1)}) fusion(bf16[256,1024]{1,0:T(8,128)(2,1)} %param.9, s32[]{:T(128)S(6)} %select_n.89, s32[]{:T(128)S(6)} %add.60), kind=kLoop, calls=%fused_computation.65 | loop fusion | bytes 262152 | tf_op jit(solution)/shard_map/slice | solution.py:140
  70.2 1.0 collective-permute-done.5
  71.1 1.5 %fusion.46 = (bf16[128,256]{1,0:T(8,128)(2,1)}, bf16[128,256]{1,0:T(8,128)(2,1)}) fusion(bf16[256,256]{1,0:T(8,128)(2,1)} %collective-permute-done.5), kind=kLoop, calls=%fused_computation.75 | loop fusion | bytes 262144 | tf_op jit(solution)/shard_map/slice | solution.py:144
  72.7 14.5 %all-to-all-done.2.kv_ref = bf16[64,64,256]{2,1,0:T(8,128)(2,1)} async-done(((bf16[64,64,256]{2,1,0:T(8,128)(2,1)}), bf16[64,64,256]{2,1,0:T(8,128)(2,1)}, u32[]{:S(2)}, u32[]{:S(2)}) %all-to-all-start.2) | async-done | bytes 2097184 | tf_op jit(solution)/shard_map/all_to_all | solution.py:136
  87.2 0.0 copy-done.1
  87.2 0.0 copy-done.2
  87.2 12.9 %shard_map.74 = bf16[8,64,128]{2,1,0:T(8,128)(2,1)S(1)} custom-call(s32[8,64]{1,0:T(8,128)S(1)} %convert_add_fusion.nbr_ref, s32[8]{0:T(128)S(1)} %copy-done.1, f32[4]{0:T(128)S(1)} %copy-done.2, bf16[8,64,256]{2,1,0:T(8,128)(2,1)S(1)} %bitcast.25, bf16[8,64,4096]{2,1,0:T(8,128)(2,1)} %bias_ref.3, bf16[64,64,256]{2,1,0:T(8,128)(2,1)} %all-to-all-done.2.kv_ref), custom_call_target="tpu_custom_call" | custom-call | tf_op jit(solution)/shard_map/pallas_call | solution.py:73
  100.1 4.1 %collective-permute-start.8 = (bf16[512,128]{1,0:T(8,128)(2,1)S(1)}, bf16[512,128]{1,0:T(8,128)(2,1)S(1)}, u32[]{:S(2)}, u32[]{:S(2)}) collective-permute-start(bf16[512,128]{1,0:T(8,128)(2,1)S(1)} %bitcast.31), channel_id=1, source_target_pairs={{0,3},{1,0},{2,1},{3,2},{4,7},{5,4},{6,5},{7,6},{8,11},{9,8},{10,9... | collective-permute-start | bytes 393224 | tf_op jit(solution)/shard_map/ppermute | solution.py:143
  104.2 0.0 collective-permute-done.4
  104.2 0.9 fusion.45
  105.1 0.0 copy-start.5
  105.1 0.0 copy-start.6
  105.1 12.1 %shard_map.73 = bf16[8,64,128]{2,1,0:T(8,128)(2,1)S(1)} custom-call(s32[8,64]{1,0:T(8,128)S(1)} %convert_add_fusion.nbr_ref, s32[8]{0:T(128)S(1)} %copy-done.1, f32[4]{0:T(128)S(1)} %copy-done.2, bf16[8,64,256]{2,1,0:T(8,128)(2,1)S(1)} %bitcast.26, bf16[8,64,4096]{2,1,0:T(8,128)(2,1)} %bias_ref.3, bf16[64,64,256]{2,1,0:T(8,128)(2,1)S(1)} %all-to-all-done.1.kv_ref), custom_call_target="tpu_custom_call" | custom-call | tf_op jit(solution)/shard_map/pallas_call | solution.py:73
  117.1 0.0 copy-start.3
  117.1 0.0 copy-start.4
  117.2 0.5 collective-permute-start.2
  117.6 0.0 collective-permute-start.1
  117.6 1.6 %collective-permute-start = (bf16[512,128]{1,0:T(8,128)(2,1)S(1)}, bf16[512,128]{1,0:T(8,128)(2,1)S(1)}, u32[]{:S(2)}, u32[]{:S(2)}) collective-permute-start(bf16[512,128]{1,0:T(8,128)(2,1)S(1)} %bitcast.29), channel_id=1, source_target_pairs={{0,1},{1,2},{2,3},{3,0},{4,5},{5,6},{6,7},{7,4},{8,9},{9,10},{10,1... | collective-permute-start | bytes 393224 | tf_op jit(solution)/shard_map/ppermute | solution.py:143
  119.3 0.0 collective-permute-done.3
  119.3 4.1 %collective-permute-start.7 = (bf16[512,128]{1,0:T(8,128)(2,1)S(1)}, bf16[512,128]{1,0:T(8,128)(2,1)S(1)}, u32[]{:S(2)}, u32[]{:S(2)}) collective-permute-start(bf16[512,128]{1,0:T(8,128)(2,1)S(1)} %bitcast.32), channel_id=1, source_target_pairs={{0,2},{1,3},{2,0},{3,1},{4,6},{5,7},{6,4},{7,5},{8,10},{9,11},{10,... | collective-permute-start | bytes 393224 | tf_op jit(solution)/shard_map/ppermute | solution.py:143
  123.4 0.0 collective-permute-done.8
  123.4 0.0 collective-permute-start.6
  123.4 7.6 %collective-permute-done.7 = bf16[512,128]{1,0:T(8,128)(2,1)S(1)} collective-permute-done((bf16[512,128]{1,0:T(8,128)(2,1)S(1)}, bf16[512,128]{1,0:T(8,128)(2,1)S(1)}, u32[]{:S(2)}, u32[]{:S(2)}) %collective-permute-start.7) | collective-permute-done | bytes 131104 | tf_op jit(solution)/shard_map/ppermute | solution.py:143
  131.0 0.9 collective-permute-done.6
  131.9 0.0 copy-done.5
  131.9 0.3 fusion.8
  132.2 0.0 collective-permute-done.2
  132.2 0.0 collective-permute-done.1
  132.2 0.0 collective-permute-done
  132.3 1.0 fusion
  (14 shorter events, 0.1 us)
Async XLA Ops:
  0.0 9.6 %copy-start = (bf16[512,1024]{1,0:T(8,128)(2,1)S(1)}, bf16[512,1024]{1,0:T(8,128)(2,1)}, u32[]{:S(2)}) copy-start(bf16[512,1024]{1,0:T(8,128)(2,1)} %param.7) | copy-start | bytes 3145732
  1.9 13.8 %all-to-all-start = ((s32[32,1,2]{2,1,0:T(1,128)}), s32[32,1,2]{2,1,0:T(1,128)S(1)}, u32[]{:S(2)}, u32[]{:S(2)}) async-start(s32[32,1,2]{2,1,0:T(1,128)} %copy.16), calls=%async_computation | async-start | bytes 32768 | tf_op jit(solution)/shard_map/all_to_all | solution.py:111
  19.2 33.2 %all-to-all-start.1 = ((bf16[64,64,256]{2,1,0:T(8,128)(2,1)}), bf16[64,64,256]{2,1,0:T(8,128)(2,1)S(1)}, u32[]{:S(2)}, u32[]{:S(2)}) async-start(bf16[64,64,256]{2,1,0:T(8,128)(2,1)} %gather_fusion), calls=%async_computation.1 | async-start | bytes 4194304 | tf_op jit(solution)/shard_map/all_to_all | solution.py:136
  27.5 38.7 %copy-start.7 = (s32[8,64]{1,0:T(8,128)S(1)}, s32[8,64]{1,0:T(8,128)}, u32[]{:S(2)}) copy-start(s32[8,64]{1,0:T(8,128)} %param.12) | copy-start | bytes 6148
  52.3 34.8 %all-to-all-start.2 = ((bf16[64,64,256]{2,1,0:T(8,128)(2,1)}), bf16[64,64,256]{2,1,0:T(8,128)(2,1)}, u32[]{:S(2)}, u32[]{:S(2)}) async-start(bf16[64,64,256]{2,1,0:T(8,128)(2,1)} %gather_fusion.1), calls=%async_computation.2 | async-start | bytes 4194304 | tf_op jit(solution)/shard_map/all_to_all | solution.py:136
  59.1 28.1 %copy-start.1 = (s32[8]{0:T(128)S(1)}, s32[8]{0:T(128)}, u32[]{:S(2)}) copy-start(s32[8]{0:T(128)} %cnt_ref.3) | copy-start | bytes 100
  59.1 28.1 %copy-start.2 = (f32[4]{0:T(128)S(1)}, f32[4]{0:T(128)}, u32[]{:S(2)}) copy-start(f32[4]{0:T(128)} %gain_ref.3) | copy-start | bytes 52
  60.9 10.2 %collective-permute-start.5 = (bf16[256,256]{1,0:T(8,128)(2,1)}, bf16[256,256]{1,0:T(8,128)(2,1)}, u32[]{:S(2)}, u32[]{:S(2)}) collective-permute-start(bf16[256,256]{1,0:T(8,128)(2,1)} %get-tuple-element.12), channel_id=1, source_target_pairs={{0,3},{1,0},{2,1},{3,2},{4,7},{5,4},{6,5},{7,6},{8,11},{9,8},{10,9... | collective-permute-start | bytes 393224 | tf_op jit(solution)/shard_map/ppermute | solution.py:120
  65.0 39.2 %collective-permute-start.4 = (bf16[256,256]{1,0:T(8,128)(2,1)}, bf16[256,256]{1,0:T(8,128)(2,1)}, u32[]{:S(2)}, u32[]{:S(2)}) collective-permute-start(bf16[256,256]{1,0:T(8,128)(2,1)} %get-tuple-element.13), channel_id=1, source_target_pairs={{0,2},{1,3},{2,0},{3,1},{4,6},{5,7},{6,4},{7,5},{8,10},{9,11},{10,... | collective-permute-start | bytes 393224 | tf_op jit(solution)/shard_map/ppermute | solution.py:120
  65.0 54.3 %collective-permute-start.3 = (bf16[256,256]{1,0:T(8,128)(2,1)}, bf16[256,256]{1,0:T(8,128)(2,1)S(1)}, u32[]{:S(2)}, u32[]{:S(2)}) collective-permute-start(bf16[256,256]{1,0:T(8,128)(2,1)} %get-tuple-element.11), channel_id=1, source_target_pairs={{0,1},{1,2},{2,3},{3,0},{4,5},{5,6},{6,7},{7,4},{8,9},{9,10},{10,1... | collective-permute-start | bytes 393224 | tf_op jit(solution)/shard_map/ppermute | solution.py:120
  67.1 1.5 %copy-start.8 = (s32[8,64]{1,0:T(8,128)S(1)}, s32[8,64]{1,0:T(8,128)}, u32[]{:S(2)}) copy-start(s32[8,64]{1,0:T(8,128)} %reshape.57) | copy-start | bytes 6148
  100.1 23.3 %collective-permute-start.8 = (bf16[512,128]{1,0:T(8,128)(2,1)S(1)}, bf16[512,128]{1,0:T(8,128)(2,1)S(1)}, u32[]{:S(2)}, u32[]{:S(2)}) collective-permute-start(bf16[512,128]{1,0:T(8,128)(2,1)S(1)} %bitcast.31), channel_id=1, source_target_pairs={{0,3},{1,0},{2,1},{3,2},{4,7},{5,4},{6,5},{7,6},{8,11},{9,8},{10,9... | collective-permute-start | bytes 393224 | tf_op jit(solution)/shard_map/ppermute | solution.py:143
  105.1 26.8 %copy-start.5 = (bf16[128,256]{1,0:T(8,128)(2,1)S(1)}, bf16[128,256]{1,0:T(8,128)(2,1)}, u32[]{:S(2)}) copy-start(bf16[128,256]{1,0:T(8,128)(2,1)} %get-tuple-element.10) | copy-start | bytes 196612
  105.1 26.8 %copy-start.6 = (bf16[128,256]{1,0:T(8,128)(2,1)S(1)}, bf16[128,256]{1,0:T(8,128)(2,1)}, u32[]{:S(2)}) copy-start(bf16[128,256]{1,0:T(8,128)(2,1)} %get-tuple-element.23) | copy-start | bytes 196612
  117.1 15.1 %copy-start.3 = (bf16[128,256]{1,0:T(8,128)(2,1)S(1)}, bf16[128,256]{1,0:T(8,128)(2,1)}, u32[]{:S(2)}) copy-start(bf16[128,256]{1,0:T(8,128)(2,1)} %get-tuple-element.9) | copy-start | bytes 196612
  117.1 15.1 %copy-start.4 = (bf16[128,256]{1,0:T(8,128)(2,1)S(1)}, bf16[128,256]{1,0:T(8,128)(2,1)}, u32[]{:S(2)}) copy-start(bf16[128,256]{1,0:T(8,128)(2,1)} %get-tuple-element.22) | copy-start | bytes 196612
  117.2 15.1 %collective-permute-start.2 = (bf16[512,128]{1,0:T(8,128)(2,1)S(1)}, bf16[512,128]{1,0:T(8,128)(2,1)S(1)}, u32[]{:S(2)}, u32[]{:S(2)}) collective-permute-start(bf16[512,128]{1,0:T(8,128)(2,1)S(1)} %bitcast.27), channel_id=1, source_target_pairs={{0,3},{1,0},{2,1},{3,2},{4,7},{5,4},{6,5},{7,6},{8,11},{9,8},{10,9... | collective-permute-start | bytes 393224 | tf_op jit(solution)/shard_map/ppermute | solution.py:143
  117.6 14.6 %collective-permute-start.1 = (bf16[512,128]{1,0:T(8,128)(2,1)S(1)}, bf16[512,128]{1,0:T(8,128)(2,1)S(1)}, u32[]{:S(2)}, u32[]{:S(2)}) collective-permute-start(bf16[512,128]{1,0:T(8,128)(2,1)S(1)} %bitcast.28), channel_id=1, source_target_pairs={{0,2},{1,3},{2,0},{3,1},{4,6},{5,7},{6,4},{7,5},{8,10},{9,11},{10,... | collective-permute-start | bytes 393224 | tf_op jit(solution)/shard_map/ppermute | solution.py:143
  117.6 14.6 %collective-permute-start = (bf16[512,128]{1,0:T(8,128)(2,1)S(1)}, bf16[512,128]{1,0:T(8,128)(2,1)S(1)}, u32[]{:S(2)}, u32[]{:S(2)}) collective-permute-start(bf16[512,128]{1,0:T(8,128)(2,1)S(1)} %bitcast.29), channel_id=1, source_target_pairs={{0,1},{1,2},{2,3},{3,0},{4,5},{5,6},{6,7},{7,4},{8,9},{9,10},{10,1... | collective-permute-start | bytes 393224 | tf_op jit(solution)/shard_map/ppermute | solution.py:143
  119.3 11.8 %collective-permute-start.7 = (bf16[512,128]{1,0:T(8,128)(2,1)S(1)}, bf16[512,128]{1,0:T(8,128)(2,1)S(1)}, u32[]{:S(2)}, u32[]{:S(2)}) collective-permute-start(bf16[512,128]{1,0:T(8,128)(2,1)S(1)} %bitcast.32), channel_id=1, source_target_pairs={{0,2},{1,3},{2,0},{3,1},{4,6},{5,7},{6,4},{7,5},{8,10},{9,11},{10,... | collective-permute-start | bytes 393224 | tf_op jit(solution)/shard_map/ppermute | solution.py:143
  123.4 8.5 %collective-permute-start.6 = (bf16[512,128]{1,0:T(8,128)(2,1)S(1)}, bf16[512,128]{1,0:T(8,128)(2,1)S(1)}, u32[]{:S(2)}, u32[]{:S(2)}) collective-permute-start(bf16[512,128]{1,0:T(8,128)(2,1)S(1)} %bitcast.33), channel_id=1, source_target_pairs={{0,1},{1,2},{2,3},{3,0},{4,5},{5,6},{6,7},{7,4},{8,9},{9,10},{10,1... | collective-permute-start | bytes 393224 | tf_op jit(solution)/shard_map/ppermute | solution.py:143

commit v13 on v12

--- a/solution.py
+++ b/solution.py
@@ -136,17 +136,28 @@
         table = lax.all_to_all(send, "row", 0, 0, tiled=True)
         att = attend(pos, counts, bias_gain, q_blocks, edge_bias, table, c, chunk)
         att = att.reshape(rows, chunk)
-        att_all = [att]
-        w_all = [w_own[cols]]
-        for s in range(1, head_devs):
-            perm = [(i, (i + s) % head_devs) for i in range(head_devs)]
-            att_all.append(lax.ppermute(att, "head", perm))
-            w_all.append(w_parts[s - 1][cols])
-        part = jnp.dot(
-            jnp.concatenate(att_all, axis=1),
-            jnp.concatenate(w_all, axis=0),
-            preferred_element_type=jnp.float32,
-        )
+        if c + 1 < chunks:
+            att_all = [att]
+            w_all = [w_own[cols]]
+            for s in range(1, head_devs):
+                perm = [(i, (i + s) % head_devs) for i in range(head_devs)]
+                att_all.append(lax.ppermute(att, "head", perm))
+                w_all.append(w_parts[s - 1][cols])
+            part = jnp.dot(
+                jnp.concatenate(att_all, axis=1),
+                jnp.concatenate(w_all, axis=0),
+                preferred_element_type=jnp.float32,
+            )
+        else:
+            by_shift = jnp.stack([w_own[cols]] + [w[cols] for w in w_parts])
+            order = (me - jnp.arange(head_devs, dtype=jnp.int32)) % head_devs
+            by_device = jnp.take(by_shift, order, axis=0, mode="clip")
+            rep = jnp.broadcast_to(att[None], (head_devs,) + att.shape)
+            recv = lax.all_to_all(rep, "head", 0, 0, tiled=True)
+            part = lax.dot_general(
+                recv, by_device, (((0, 2), (0, 1)), ((), ())),
+                preferred_element_type=jnp.float32,
+            )
         total = part if total is None else total + part
     return total.astype(jnp.bfloat16)
 

time: 135 us -> 141 us (1.044)
  local copies, waits for them, and re-layouts: 14.1 us -> 18.5 us
  waiting for transfers between devices: 51 us -> 48.5 us
  matrix products: 5.82 us -> 7.88 us
    ppermute x6 -> x3, starting transfers between devices: 10.3 us -> 5.02 us  [_body(): att_all.append(lax.ppermute(att, 'head', perm))]
    all_to_all x0 -> x1, starting transfers between devices: none -> 5.3 us  [_body(): recv = lax.all_to_all(rep, 'head', 0, 0, tiled=True)]
    ppermute x6 -> x3, waiting for transfers between devices: 8.5 us -> 5.44 us  [_body(): att_all.append(lax.ppermute(att, 'head', perm))]
    gather x0 -> x1, local copies, waits for them, and re-layouts: none -> 2.23 us  [_body(): by_device = jnp.take(by_shift, order, axis=0, mode='clip')]
    slice x3, local copies, waits for them, and re-layouts: 2.42 us -> 4.49 us  [_body(): w_all.append(w_parts[s - 1][cols])]
  transfers between devices with their start and end apart: 12 -> 10, of which waited for: 6 -> 7; matrix products, arithmetic and copies ran while one was open for 12% -> 16% of each run, Pallas kernels for 19% -> 18%
where the time goes in v13:
time: 141 us; the launch traced here: 138 us
  waiting for transfers between devices  48.5 us (34%)
  starting transfers between devices  35.2 us (25%)
  Pallas kernels  25.5 us (18%)
  local copies, waits for them, and re-layouts  18.5 us (13%)
  matrix products  7.88 us (6%)
  other arithmetic  2.51 us (2%)
    all_to_all x2, waiting for transfers between devices, _body(): table = lax.all_to_all(send, 'row', 0, 0, tiled=True)  39.3 us
    pallas_call x2, Pallas kernels, attend(): pl.pallas_call(functools.partial(_attend_kernel, p0), grid_spec=grid_spec...  25.5 us
    all_to_all x2, starting transfers between devices, _body(): table = lax.all_to_all(send, 'row', 0, 0, tiled=True)  12 us
    all_to_all x1, starting transfers between devices, _body(): wanted = lax.all_to_all(req, 'row', 0, 0, tiled=True).reshape(-1)  7.62 us
    ppermute x3, waiting for transfers between devices, _body(): att_all.append(lax.ppermute(att, 'head', perm))  5.44 us
    all_to_all x1, starting transfers between devices, _body(): recv = lax.all_to_all(rep, 'head', 0, 0, tiled=True)  5.3 us
    ppermute x3, starting transfers between devices, _body(): w_parts.append(lax.ppermute(piece, 'head', perm))  5.3 us
    ppermute x3, starting transfers between devices, _body(): att_all.append(lax.ppermute(att, 'head', perm))  5.02 us
  transfers between devices with their start and end apart: 10, of which 7 were waited for; matrix products, arithmetic and copies ran while one was open for 16% of the time, Pallas kernels for 18%

profile of v13, /device:TPU:2, one launch (start us, length us, event | category | flops | bytes accessed | tf_op | source)
XLA Modules:
  0.0 138.5 jit_solution(7695830395403256344)
XLA Ops:
  0.0 0.0 copy-start
  0.0 0.8 eq.67
  0.9 0.2 fusion.14
  1.0 0.1 reshape.94
  1.1 0.1 select_reduce_fusion.1
  1.3 0.7 copy.16
  2.0 7.6 %all-to-all-start = ((s32[32,1,2]{2,1,0:T(1,128)}), s32[32,1,2]{2,1,0:T(1,128)S(1)}, u32[]{:S(2)}, u32[]{:S(2)}) async-start(s32[32,1,2]{2,1,0:T(1,128)} %copy.16), calls=%async_computation | async-start | bytes 32768 | tf_op jit(solution)/shard_map/all_to_all | solution.py:111
  9.6 0.0 copy-done
  9.6 1.5 %convolution_convert_fusion = bf16[512,256]{0,1:T(8,128)(2,1)S(1)} fusion(bf16[512,1024]{1,0:T(8,128)(2,1)S(1)} %copy-done, bf16[3,1024,256]{2,1,0:T(8,128)(2,1)} %param.8), kind=kOutput, calls=%fused_computation.6 | convolution fusion | flops 268566528 | bytes 1835008 | tf_op jit(solution)/shard_map/dot_general | solution.py:114
  11.1 1.5 %convolution_convert_fusion.1 = bf16[512,256]{0,1:T(8,128)(2,1)S(1)} fusion(bf16[512,1024]{1,0:T(8,128)(2,1)S(1)} %copy-done, bf16[3,1024,256]{2,1,0:T(8,128)(2,1)} %param.8), kind=kOutput, calls=%fused_computation.7 | convolution fusion | flops 268566528 | bytes 1835008 | tf_op jit(solution)/shard_map/dot_general | solution.py:113
  12.7 0.7 pad_maximum_fusion
  13.5 0.1 copy.15
  13.6 2.2 %all-to-all-done = s32[32,1,2]{2,1,0:T(1,128)S(1)} async-done(((s32[32,1,2]{2,1,0:T(1,128)}), s32[32,1,2]{2,1,0:T(1,128)S(1)}, u32[]{:S(2)}, u32[]{:S(2)}) %all-to-all-start) | async-done | bytes 288 | tf_op jit(solution)/shard_map/all_to_all | solution.py:111
  15.7 0.5 broadcast.124
  16.3 0.6 reduce.3
  16.9 0.1 reshape.102
  17.0 2.0 %gather_fusion = bf16[64,64,256]{2,1,0:T(8,128)(2,1)} fusion(bf16[8,64,256]{2,1,0:T(8,128)(2,1)S(1)} %bitcast.46, s32[1024]{0:T(1024)S(1)} %pad_clamp_fusion.1), kind=kCustom, calls=%fused_computation | custom fusion | bytes 4194560 | tf_op jit(solution)/shard_map/jit(_take)/gather | solution.py:128
  19.0 5.2 %all-to-all-start.1 = ((bf16[64,64,256]{2,1,0:T(8,128)(2,1)}), bf16[64,64,256]{2,1,0:T(8,128)(2,1)S(1)}, u32[]{:S(2)}, u32[]{:S(2)}) async-start(bf16[64,64,256]{2,1,0:T(8,128)(2,1)} %gather_fusion), calls=%async_computation.1 | async-start | bytes 4194304 | tf_op jit(solution)/shard_map/all_to_all | solution.py:136
  24.2 1.1 copy.17
  25.3 2.0 %gather_fusion.1 = bf16[64,64,256]{2,1,0:T(8,128)(2,1)} fusion(bf16[8,64,256]{2,1,0:T(8,128)(2,1)S(1)} %bitcast.47, s32[1024]{0:T(1024)S(1)} %pad_clamp_fusion.1), kind=kCustom, calls=%fused_computation.1 | custom fusion | bytes 4194560 | tf_op jit(solution)/shard_map/jit(_take)/gather | solution.py:128
  27.3 0.0 copy-start.3
  27.3 24.8 %all-to-all-done.1.kv_ref = bf16[64,64,256]{2,1,0:T(8,128)(2,1)S(1)} async-done(((bf16[64,64,256]{2,1,0:T(8,128)(2,1)}), bf16[64,64,256]{2,1,0:T(8,128)(2,1)S(1)}, u32[]{:S(2)}, u32[]{:S(2)}) %all-to-all-start.1) | async-done | bytes 2097184 | tf_op jit(solution)/shard_map/all_to_all | solution.py:136
  52.1 6.7 %all-to-all-start.2 = ((bf16[64,64,256]{2,1,0:T(8,128)(2,1)}), bf16[64,64,256]{2,1,0:T(8,128)(2,1)}, u32[]{:S(2)}, u32[]{:S(2)}) async-start(bf16[64,64,256]{2,1,0:T(8,128)(2,1)} %gather_fusion.1), calls=%async_computation.2 | async-start | bytes 4194304 | tf_op jit(solution)/shard_map/all_to_all | solution.py:136
  58.9 0.0 copy-start.1
  58.9 0.0 copy-start.2
  59.0 1.8 %constant_dynamic-slice_fusion.3 = (bf16[256,256]{1,0:T(8,128)(2,1)}, bf16[256,256]{1,0:T(8,128)(2,1)}, bf16[256,256]{1,0:T(8,128)(2,1)}) fusion(bf16[256,1024]{1,0:T(8,128)(2,1)} %param.9, s32[]{:T(128)S(6)} %select_n.104, s32[]{:T(128)S(6)} %select_n.108, s32[]{:T(128)S(6)} %select_n.106), kind=kLoop, calls=%fused_computation.64 | loop fusion | bytes 786444 | tf_op jit(solution)/shard_map/dynamic_slice | solution.py:118
  60.7 4.0 %collective-permute-start.5 = (bf16[256,256]{1,0:T(8,128)(2,1)}, bf16[256,256]{1,0:T(8,128)(2,1)}, u32[]{:S(2)}, u32[]{:S(2)}) collective-permute-start(bf16[256,256]{1,0:T(8,128)(2,1)} %get-tuple-element.12), channel_id=1, source_target_pairs={{0,3},{1,0},{2,1},{3,2},{4,7},{5,4},{6,5},{7,6},{8,11},{9,8},{10,9... | collective-permute-start | bytes 393224 | tf_op jit(solution)/shard_map/ppermute | solution.py:120
  64.8 0.0 collective-permute-start.4
  64.8 1.3 collective-permute-start.3
  66.0 0.0 copy-done.3
  66.1 0.1 eq.63
  66.1 0.1 select_reduce_fusion
  66.2 0.1 reshape.95
  66.3 1.5 %convolution_convert_fusion.2 = bf16[512,256]{1,0:T(8,128)(2,1)S(1)} fusion(bf16[512,1024]{1,0:T(8,128)(2,1)S(1)} %copy-done, bf16[3,1024,256]{2,1,0:T(8,128)(2,1)} %param.8), kind=kOutput, calls=%fused_computation.8 | convolution fusion | flops 268566528 | bytes 1835008 | tf_op jit(solution)/shard_map/dot_general | solution.py:112
  67.8 1.5 %constant_dynamic-slice_fusion = (bf16[128,256]{1,0:T(8,128)(2,1)}, bf16[1,128,256]{2,1,0:T(8,128)(2,1)S(1)}) fusion(bf16[256,1024]{1,0:T(8,128)(2,1)} %param.9, s32[]{:T(128)S(6)} %select_n.102, s32[]{:T(128)S(6)} %add.74), kind=kLoop, calls=%fused_computation.61 | loop fusion | bytes 262152 | tf_op jit(solution)/shard_map/slice | solution.py:141
  69.3 1.6 %collective-permute-done.5 = bf16[256,256]{1,0:T(8,128)(2,1)} collective-permute-done((bf16[256,256]{1,0:T(8,128)(2,1)}, bf16[256,256]{1,0:T(8,128)(2,1)}, u32[]{:S(2)}, u32[]{:S(2)}) %collective-permute-start.5) | collective-permute-done | bytes 131104 | tf_op jit(solution)/shard_map/ppermute | solution.py:120
  70.9 1.5 %fusion.32 = (bf16[128,256]{1,0:T(8,128)(2,1)}, bf16[1,128,256]{2,1,0:T(8,128)(2,1)S(1)}) fusion(bf16[256,256]{1,0:T(8,128)(2,1)} %collective-permute-done.5), kind=kLoop, calls=%fused_computation.72 | loop fusion | bytes 262144 | tf_op jit(solution)/shard_map/slice | solution.py:145
  72.4 14.5 %all-to-all-done.2.kv_ref = bf16[64,64,256]{2,1,0:T(8,128)(2,1)} async-done(((bf16[64,64,256]{2,1,0:T(8,128)(2,1)}), bf16[64,64,256]{2,1,0:T(8,128)(2,1)}, u32[]{:S(2)}, u32[]{:S(2)}) %all-to-all-start.2) | async-done | bytes 2097184 | tf_op jit(solution)/shard_map/all_to_all | solution.py:136
  87.0 0.0 copy-done.1
  87.0 0.0 copy-done.2
  87.0 13.5 %shard_map.74 = bf16[8,64,128]{2,1,0:T(8,128)(2,1)S(1)} custom-call(s32[8,64]{1,0:T(8,128)S(1)} %convert_add_fusion.nbr_ref, s32[8]{0:T(128)S(1)} %copy-done.1, f32[4]{0:T(128)S(1)} %copy-done.2, bf16[8,64,256]{2,1,0:T(8,128)(2,1)S(1)} %bitcast.39, bf16[8,64,4096]{2,1,0:T(8,128)(2,1)} %bias_ref.3, bf16[64,64,256]{2,1,0:T(8,128)(2,1)} %all-to-all-done.2.kv_ref), custom_call_target="tpu_custom_call" | custom-call | tf_op jit(solution)/shard_map/pallas_call | solution.py:73
  100.5 0.9 broadcast_in_dim.66
  101.3 5.3 %all-to-all-start.3 = ((bf16[4,512,128]{2,1,0:T(8,128)(2,1)}), bf16[4,512,128]{2,1,0:T(8,128)(2,1)}, u32[]{:S(2)}, u32[]{:S(2)}) async-start(bf16[4,512,128]{2,1,0:T(8,128)(2,1)} %broadcast_in_dim.66), calls=%async_computation.3 | async-start | bytes 1048576 | tf_op jit(solution)/shard_map/all_to_all | solution.py:156
  106.6 0.0 collective-permute-done.4
  106.6 1.5 %fusion.31 = (bf16[128,256]{1,0:T(8,128)(2,1)}, bf16[1,128,256]{2,1,0:T(8,128)(2,1)S(1)}) fusion(bf16[256,256]{1,0:T(8,128)(2,1)} %collective-permute-done.4), kind=kLoop, calls=%fused_computation.71 | loop fusion | bytes 262144 | tf_op jit(solution)/shard_map/slice | solution.py:145
  108.1 0.0 collective-permute-done.3
  108.1 1.5 %fusion.30 = (bf16[128,256]{1,0:T(8,128)(2,1)}, bf16[1,128,256]{2,1,0:T(8,128)(2,1)S(1)}) fusion(bf16[256,256]{1,0:T(8,128)(2,1)} %collective-permute-done.3), kind=kLoop, calls=%fused_computation.70 | loop fusion | bytes 262144 | tf_op jit(solution)/shard_map/slice | solution.py:145
  109.6 0.7 pad_maximum_fusion.2
  110.4 2.2 %gather_fusion.2 = bf16[4,128,256]{2,1,0:T(8,128)(2,1)} fusion(bf16[4,128,256]{2,1,0:T(8,128)(2,1)} %pad_maximum_fusion.2, s32[1024]{0:T(1024)S(1)} %pad_clamp_fusion), kind=kCustom, calls=%fused_computation.2 | custom fusion | bytes 524304 | tf_op jit(solution)/shard_map/jit(_take)/gather | solution.py:154
  112.6 12.0 %shard_map.73 = bf16[8,64,128]{2,1,0:T(8,128)(2,1)S(1)} custom-call(s32[8,64]{1,0:T(8,128)S(1)} %convert_add_fusion.nbr_ref, s32[8]{0:T(128)S(1)} %copy-done.1, f32[4]{0:T(128)S(1)} %copy-done.2, bf16[8,64,256]{2,1,0:T(8,128)(2,1)S(1)} %bitcast.40, bf16[8,64,4096]{2,1,0:T(8,128)(2,1)} %bias_ref.3, bf16[64,64,256]{2,1,0:T(8,128)(2,1)S(1)} %all-to-all-done.1.kv_ref), custom_call_target="tpu_custom_call" | custom-call | tf_op jit(solution)/shard_map/pallas_call | solution.py:73
  124.6 3.3 %collective-permute-start.2 = (bf16[512,128]{1,0:T(8,128)(2,1)S(1)}, bf16[512,128]{1,0:T(8,128)(2,1)S(1)}, u32[]{:S(2)}, u32[]{:S(2)}) collective-permute-start(bf16[512,128]{1,0:T(8,128)(2,1)S(1)} %bitcast.42), channel_id=1, source_target_pairs={{0,3},{1,0},{2,1},{3,2},{4,7},{5,4},{6,5},{7,6},{8,11},{9,8},{10,9... | collective-permute-start | bytes 393224 | tf_op jit(solution)/shard_map/ppermute | solution.py:144
  127.9 0.9 collective-permute-start.1
  128.8 0.9 collective-permute-start
  129.7 0.0 all-to-all-done.3
  129.7 1.4 %convolution_bitcast_fusion = f32[512,256]{1,0:T(8,128)S(1)} fusion(bf16[4,512,128]{2,1,0:T(8,128)(2,1)} %all-to-all-done.3, bf16[4,128,256]{2,1,0:T(8,128)(2,1)} %gather_fusion.2), kind=kOutput, calls=%fused_computation.3 | convolution fusion | flops 134217728 | bytes 1310720 | tf_op jit(solution)/shard_map/dot_general | solution.py:157
  131.1 1.8 %collective-permute-done.2 = bf16[512,128]{1,0:T(8,128)(2,1)S(1)} collective-permute-done((bf16[512,128]{1,0:T(8,128)(2,1)S(1)}, bf16[512,128]{1,0:T(8,128)(2,1)S(1)}, u32[]{:S(2)}, u32[]{:S(2)}) %collective-permute-start.2) | collective-permute-done | bytes 131104 | tf_op jit(solution)/shard_map/ppermute | solution.py:144
  132.8 2.3 %collective-permute-done.1 = bf16[512,128]{1,0:T(8,128)(2,1)S(1)} collective-permute-done((bf16[512,128]{1,0:T(8,128)(2,1)S(1)}, bf16[512,128]{1,0:T(8,128)(2,1)S(1)}, u32[]{:S(2)}, u32[]{:S(2)}) %collective-permute-start.1) | collective-permute-done | bytes 131104 | tf_op jit(solution)/shard_map/ppermute | solution.py:144
  135.1 1.4 %collective-permute-done = bf16[512,128]{1,0:T(8,128)(2,1)S(1)} collective-permute-done((bf16[512,128]{1,0:T(8,128)(2,1)S(1)}, bf16[512,128]{1,0:T(8,128)(2,1)S(1)}, u32[]{:S(2)}, u32[]{:S(2)}) %collective-permute-start) | collective-permute-done | bytes 131104 | tf_op jit(solution)/shard_map/ppermute | solution.py:144
  136.5 1.9 %fusion = bf16[512,256]{1,0:T(8,128)(2,1)} fusion(f32[512,256]{1,0:T(8,128)S(1)} %convolution_bitcast_fusion, bf16[512,128]{1,0:T(8,128)(2,1)S(1)} %collective-permute-done.2, bf16[512,128]{1,0:T(8,128)(2,1)S(1)} %collective-permute-done.1, bf16[512,128]{1,0:T(8,128)(2,1)S(1)} %collective-permute-done, bf16[512,128]{1,0:T(8,128)(2,1)S(1)} %bitcast.45, ...), kind=kOutput, calls=%fused_computation.5 | convolution fusion | flops 137625600 | bytes 1572864 | tf_op jit(solution)/shard_map/dot_general | solution.py:146
  (10 shorter events, 0.1 us)
Async XLA Ops:
  0.0 9.6 %copy-start = (bf16[512,1024]{1,0:T(8,128)(2,1)S(1)}, bf16[512,1024]{1,0:T(8,128)(2,1)}, u32[]{:S(2)}) copy-start(bf16[512,1024]{1,0:T(8,128)(2,1)} %param.7) | copy-start | bytes 3145732
  2.0 13.8 %all-to-all-start = ((s32[32,1,2]{2,1,0:T(1,128)}), s32[32,1,2]{2,1,0:T(1,128)S(1)}, u32[]{:S(2)}, u32[]{:S(2)}) async-start(s32[32,1,2]{2,1,0:T(1,128)} %copy.16), calls=%async_computation | async-start | bytes 32768 | tf_op jit(solution)/shard_map/all_to_all | solution.py:111
  19.0 33.2 %all-to-all-start.1 = ((bf16[64,64,256]{2,1,0:T(8,128)(2,1)}), bf16[64,64,256]{2,1,0:T(8,128)(2,1)S(1)}, u32[]{:S(2)}, u32[]{:S(2)}) async-start(bf16[64,64,256]{2,1,0:T(8,128)(2,1)} %gather_fusion), calls=%async_computation.1 | async-start | bytes 4194304 | tf_op jit(solution)/shard_map/all_to_all | solution.py:136
  27.3 38.7 %copy-start.3 = (s32[8,64]{1,0:T(8,128)S(1)}, s32[8,64]{1,0:T(8,128)}, u32[]{:S(2)}) copy-start(s32[8,64]{1,0:T(8,128)} %param.12) | copy-start | bytes 6148
  52.1 34.8 %all-to-all-start.2 = ((bf16[64,64,256]{2,1,0:T(8,128)(2,1)}), bf16[64,64,256]{2,1,0:T(8,128)(2,1)}, u32[]{:S(2)}, u32[]{:S(2)}) async-start(bf16[64,64,256]{2,1,0:T(8,128)(2,1)} %gather_fusion.1), calls=%async_computation.2 | async-start | bytes 4194304 | tf_op jit(solution)/shard_map/all_to_all | solution.py:136
  58.9 28.1 %copy-start.1 = (s32[8]{0:T(128)S(1)}, s32[8]{0:T(128)}, u32[]{:S(2)}) copy-start(s32[8]{0:T(128)} %cnt_ref.3) | copy-start | bytes 100
  58.9 28.1 %copy-start.2 = (f32[4]{0:T(128)S(1)}, f32[4]{0:T(128)}, u32[]{:S(2)}) copy-start(f32[4]{0:T(128)} %gain_ref.3) | copy-start | bytes 52
  60.7 10.2 %collective-permute-start.5 = (bf16[256,256]{1,0:T(8,128)(2,1)}, bf16[256,256]{1,0:T(8,128)(2,1)}, u32[]{:S(2)}, u32[]{:S(2)}) collective-permute-start(bf16[256,256]{1,0:T(8,128)(2,1)} %get-tuple-element.12), channel_id=1, source_target_pairs={{0,3},{1,0},{2,1},{3,2},{4,7},{5,4},{6,5},{7,6},{8,11},{9,8},{10,9... | collective-permute-start | bytes 393224 | tf_op jit(solution)/shard_map/ppermute | solution.py:120
  64.8 41.9 %collective-permute-start.4 = (bf16[256,256]{1,0:T(8,128)(2,1)}, bf16[256,256]{1,0:T(8,128)(2,1)}, u32[]{:S(2)}, u32[]{:S(2)}) collective-permute-start(bf16[256,256]{1,0:T(8,128)(2,1)} %get-tuple-element.13), channel_id=1, source_target_pairs={{0,2},{1,3},{2,0},{3,1},{4,6},{5,7},{6,4},{7,5},{8,10},{9,11},{10,... | collective-permute-start | bytes 393224 | tf_op jit(solution)/shard_map/ppermute | solution.py:120
  64.8 43.4 %collective-permute-start.3 = (bf16[256,256]{1,0:T(8,128)(2,1)}, bf16[256,256]{1,0:T(8,128)(2,1)}, u32[]{:S(2)}, u32[]{:S(2)}) collective-permute-start(bf16[256,256]{1,0:T(8,128)(2,1)} %get-tuple-element.11), channel_id=1, source_target_pairs={{0,1},{1,2},{2,3},{3,0},{4,5},{5,6},{6,7},{7,4},{8,9},{9,10},{10,1... | collective-permute-start | bytes 393224 | tf_op jit(solution)/shard_map/ppermute | solution.py:120
  101.3 28.3 %all-to-all-start.3 = ((bf16[4,512,128]{2,1,0:T(8,128)(2,1)}), bf16[4,512,128]{2,1,0:T(8,128)(2,1)}, u32[]{:S(2)}, u32[]{:S(2)}) async-start(bf16[4,512,128]{2,1,0:T(8,128)(2,1)} %broadcast_in_dim.66), calls=%async_computation.3 | async-start | bytes 1048576 | tf_op jit(solution)/shard_map/all_to_all | solution.py:156
  124.6 8.2 %collective-permute-start.2 = (bf16[512,128]{1,0:T(8,128)(2,1)S(1)}, bf16[512,128]{1,0:T(8,128)(2,1)S(1)}, u32[]{:S(2)}, u32[]{:S(2)}) collective-permute-start(bf16[512,128]{1,0:T(8,128)(2,1)S(1)} %bitcast.42), channel_id=1, source_target_pairs={{0,3},{1,0},{2,1},{3,2},{4,7},{5,4},{6,5},{7,6},{8,11},{9,8},{10,9... | collective-permute-start | bytes 393224 | tf_op jit(solution)/shard_map/ppermute | solution.py:144
  127.9 7.2 %collective-permute-start.1 = (bf16[512,128]{1,0:T(8,128)(2,1)S(1)}, bf16[512,128]{1,0:T(8,128)(2,1)S(1)}, u32[]{:S(2)}, u32[]{:S(2)}) collective-permute-start(bf16[512,128]{1,0:T(8,128)(2,1)S(1)} %bitcast.43), channel_id=1, source_target_pairs={{0,2},{1,3},{2,0},{3,1},{4,6},{5,7},{6,4},{7,5},{8,10},{9,11},{10,... | collective-permute-start | bytes 393224 | tf_op jit(solution)/shard_map/ppermute | solution.py:144
  128.8 7.7 %collective-permute-start = (bf16[512,128]{1,0:T(8,128)(2,1)S(1)}, bf16[512,128]{1,0:T(8,128)(2,1)S(1)}, u32[]{:S(2)}, u32[]{:S(2)}) collective-permute-start(bf16[512,128]{1,0:T(8,128)(2,1)S(1)} %bitcast.44), channel_id=1, source_target_pairs={{0,1},{1,2},{2,3},{3,0},{4,5},{5,6},{6,7},{7,4},{8,9},{9,10},{10,1... | collective-permute-start | bytes 393224 | tf_op jit(solution)/shard_map/ppermute | solution.py:144

commit v14 on v13

--- a/solution.py
+++ b/solution.py
@@ -125,7 +125,12 @@
         cols = slice(c * chunk, (c + 1) * chunk)
         kv = jnp.concatenate([keys[:, cols], values[:, cols]], axis=1)
         kv = kv.reshape(blocks_dev, BLK, 2 * chunk)
-        outgoing.append(jnp.take(kv, wanted, axis=0, mode="clip"))
+        pick = (wanted[:, None] == jnp.arange(blocks_dev, dtype=jnp.int32)[None, :])
+        picked = jnp.dot(
+            pick.astype(jnp.bfloat16), kv.reshape(blocks_dev, -1),
+            preferred_element_type=jnp.float32,
+        )
+        outgoing.append(picked.astype(jnp.bfloat16).reshape((-1,) + kv.shape[1:]))
     total = None
     table = None
     for c in range(chunks):

time: 141 us -> 142 us (level)
  waiting for transfers between devices: 48.5 us -> 46.9 us
  matrix products: 7.88 us -> 9.36 us
    gather x2 -> x0, local copies, waits for them, and re-layouts: 4 us -> none  [_body(): outgoing.append(jnp.take(kv, wanted, axis=0, mode='clip'))]
    unnamed x8 -> x12, local copies, waits for them, and re-layouts: 0.02 us -> 3.76 us
    dot_general x0 -> x2, matrix products: none -> 1.49 us  [_body(): jnp.dot(pick.astype(jnp.bfloat16), kv.reshape(blocks_dev, -1), preferred_...]
    all_to_all x2, waiting for transfers between devices: 39.3 us -> 37.9 us  [_body(): table = lax.all_to_all(send, 'row', 0, 0, tiled=True)]
  transfers between devices with their start and end apart: 10 -> 10, of which waited for: 7 -> 7; matrix products, arithmetic and copies ran while one was open for 16% -> 17% of each run, Pallas kernels for 18% -> 18%
where the time goes in v14:
time: 142 us; the launch traced here: 140 us
  waiting for transfers between devices  46.9 us (33%)
  starting transfers between devices  35.6 us (25%)
  Pallas kernels  25.5 us (18%)
  local copies, waits for them, and re-layouts  19.4 us (14%)
  matrix products  9.36 us (7%)
  other arithmetic  2.57 us (2%)
    all_to_all x2, waiting for transfers between devices, _body(): table = lax.all_to_all(send, 'row', 0, 0, tiled=True)  37.9 us
    pallas_call x2, Pallas kernels, attend(): pl.pallas_call(functools.partial(_attend_kernel, p0), grid_spec=grid_spec...  25.5 us
    all_to_all x2, starting transfers between devices, _body(): table = lax.all_to_all(send, 'row', 0, 0, tiled=True)  12.4 us
    all_to_all x1, starting transfers between devices, _body(): wanted = lax.all_to_all(req, 'row', 0, 0, tiled=True).reshape(-1)  7.62 us
    ppermute x3, waiting for transfers between devices, _body(): att_all.append(lax.ppermute(att, 'head', perm))  5.44 us
    all_to_all x1, starting transfers between devices, _body(): recv = lax.all_to_all(rep, 'head', 0, 0, tiled=True)  5.3 us
    ppermute x3, starting transfers between devices, _body(): w_parts.append(lax.ppermute(piece, 'head', perm))  5.3 us
    ppermute x3, starting transfers between devices, _body(): att_all.append(lax.ppermute(att, 'head', perm))  5.02 us
  transfers between devices with their start and end apart: 10, of which 7 were waited for; matrix products, arithmetic and copies ran while one was open for 17% of the time, Pallas kernels for 18%

profile of v14, /device:TPU:2, one launch (start us, length us, event | category | flops | bytes accessed | tf_op | source)
XLA Modules:
  0.0 139.6 jit_solution(14293010703025224234)
XLA Ops:
  0.0 0.0 copy-start
  0.0 0.8 eq.89
  0.9 0.2 fusion.14
  1.0 0.1 reshape.93
  1.1 0.1 select_reduce_fusion.1
  1.3 0.7 copy.15
  1.9 7.6 %all-to-all-start = ((s32[32,1,2]{2,1,0:T(1,128)}), s32[32,1,2]{2,1,0:T(1,128)S(1)}, u32[]{:S(2)}, u32[]{:S(2)}) async-start(s32[32,1,2]{2,1,0:T(1,128)} %copy.15), calls=%async_computation | async-start | bytes 32768 | tf_op jit(solution)/shard_map/all_to_all | solution.py:111
  9.6 0.0 copy-done
  9.6 1.5 %convolution_convert_fusion.2 = bf16[512,256]{0,1:T(8,128)(2,1)S(1)} fusion(bf16[512,1024]{1,0:T(8,128)(2,1)S(1)} %copy-done, bf16[3,1024,256]{2,1,0:T(8,128)(2,1)} %param.8), kind=kOutput, calls=%fused_computation.6 | convolution fusion | flops 268566528 | bytes 1835008 | tf_op jit(solution)/shard_map/dot_general | solution.py:114
  11.1 1.5 %convolution_convert_fusion.3 = bf16[512,256]{0,1:T(8,128)(2,1)S(1)} fusion(bf16[512,1024]{1,0:T(8,128)(2,1)S(1)} %copy-done, bf16[3,1024,256]{2,1,0:T(8,128)(2,1)} %param.8), kind=kOutput, calls=%fused_computation.7 | convolution fusion | flops 268566528 | bytes 1835008 | tf_op jit(solution)/shard_map/dot_general | solution.py:113
  12.7 0.7 pad_maximum_fusion
  13.4 0.1 copy.16
  13.6 0.1 reshape_reshape.6
  13.7 2.0 %all-to-all-done = s32[32,1,2]{2,1,0:T(1,128)S(1)} async-done(((s32[32,1,2]{2,1,0:T(1,128)}), s32[32,1,2]{2,1,0:T(1,128)S(1)}, u32[]{:S(2)}, u32[]{:S(2)}) %all-to-all-start) | async-done | bytes 288 | tf_op jit(solution)/shard_map/all_to_all | solution.py:111
  15.7 0.5 broadcast.118
  16.3 0.7 reduce.3
  17.0 0.1 eq.97
  17.1 0.7 convolution_convert_fusion.1
  17.8 1.9 %copy.18 = bf16[8,8,64,256]{3,2,1,0:T(8,128)(2,1)} copy(bf16[8,8,64,256]{3,1,2,0:T(8,128)(2,1)S(1)} %bitcast.51) | data formatting | bytes 4194304
  19.7 0.0 copy-start.3
  19.7 5.5 %all-to-all-start.1 = ((bf16[64,64,256]{2,1,0:T(8,128)(2,1)}), bf16[64,64,256]{2,1,0:T(8,128)(2,1)S(1)}, u32[]{:S(2)}, u32[]{:S(2)}) async-start(bf16[64,64,256]{2,1,0:T(8,128)(2,1)} %bitcast.53), calls=%async_computation.1 | async-start | bytes 4194304 | tf_op jit(solution)/shard_map/all_to_all | solution.py:141
  25.2 0.0 copy-done.3
  25.2 0.8 copy.17
  26.0 1.1 reshape_reshape.7
  27.1 0.7 convolution_convert_fusion
  27.9 1.9 %copy.19 = bf16[8,8,64,256]{3,2,1,0:T(8,128)(2,1)} copy(bf16[8,8,64,256]{3,1,2,0:T(8,128)(2,1)S(1)} %bitcast.50) | data formatting | bytes 4194304
  29.7 23.4 %all-to-all-done.1.kv_ref = bf16[64,64,256]{2,1,0:T(8,128)(2,1)S(1)} async-done(((bf16[64,64,256]{2,1,0:T(8,128)(2,1)}), bf16[64,64,256]{2,1,0:T(8,128)(2,1)S(1)}, u32[]{:S(2)}, u32[]{:S(2)}) %all-to-all-start.1) | async-done | bytes 2097184 | tf_op jit(solution)/shard_map/all_to_all | solution.py:141
  53.1 6.9 %all-to-all-start.2 = ((bf16[64,64,256]{2,1,0:T(8,128)(2,1)}), bf16[64,64,256]{2,1,0:T(8,128)(2,1)}, u32[]{:S(2)}, u32[]{:S(2)}) async-start(bf16[64,64,256]{2,1,0:T(8,128)(2,1)} %bitcast.52), calls=%async_computation.2 | async-start | bytes 4194304 | tf_op jit(solution)/shard_map/all_to_all | solution.py:141
  60.0 0.0 copy-start.1
  60.0 0.0 copy-start.2
  60.1 1.8 %constant_dynamic-slice_fusion.3 = (bf16[256,256]{1,0:T(8,128)(2,1)}, bf16[256,256]{1,0:T(8,128)(2,1)}, bf16[256,256]{1,0:T(8,128)(2,1)}) fusion(bf16[256,1024]{1,0:T(8,128)(2,1)} %param.9, s32[]{:T(128)S(6)} %select_n.104, s32[]{:T(128)S(6)} %select_n.108, s32[]{:T(128)S(6)} %select_n.106), kind=kLoop, calls=%fused_computation.66 | loop fusion | bytes 786444 | tf_op jit(solution)/shard_map/dynamic_slice | solution.py:118
  61.9 4.0 %collective-permute-start.5 = (bf16[256,256]{1,0:T(8,128)(2,1)}, bf16[256,256]{1,0:T(8,128)(2,1)}, u32[]{:S(2)}, u32[]{:S(2)}) collective-permute-start(bf16[256,256]{1,0:T(8,128)(2,1)} %get-tuple-element.12), channel_id=1, source_target_pairs={{0,3},{1,0},{2,1},{3,2},{4,7},{5,4},{6,5},{7,6},{8,11},{9,8},{10,9... | collective-permute-start | bytes 393224 | tf_op jit(solution)/shard_map/ppermute | solution.py:120
  65.9 0.0 collective-permute-start.4
  65.9 1.3 collective-permute-start.3
  67.2 0.0 copy-done.4
  67.2 0.1 eq.85
  67.3 0.1 select_reduce_fusion
  67.4 0.1 reshape.94
  67.5 1.5 %convolution_convert_fusion.4 = bf16[512,256]{1,0:T(8,128)(2,1)S(1)} fusion(bf16[512,1024]{1,0:T(8,128)(2,1)S(1)} %copy-done, bf16[3,1024,256]{2,1,0:T(8,128)(2,1)} %param.8), kind=kOutput, calls=%fused_computation.8 | convolution fusion | flops 268566528 | bytes 1835008 | tf_op jit(solution)/shard_map/dot_general | solution.py:112
  69.0 1.5 %constant_dynamic-slice_fusion = (bf16[128,256]{1,0:T(8,128)(2,1)}, bf16[1,128,256]{2,1,0:T(8,128)(2,1)S(1)}) fusion(bf16[256,1024]{1,0:T(8,128)(2,1)} %param.9, s32[]{:T(128)S(6)} %select_n.102, s32[]{:T(128)S(6)} %add.74), kind=kLoop, calls=%fused_computation.63 | loop fusion | bytes 262152 | tf_op jit(solution)/shard_map/slice | solution.py:146
  70.5 1.6 %collective-permute-done.5 = bf16[256,256]{1,0:T(8,128)(2,1)} collective-permute-done((bf16[256,256]{1,0:T(8,128)(2,1)}, bf16[256,256]{1,0:T(8,128)(2,1)}, u32[]{:S(2)}, u32[]{:S(2)}) %collective-permute-start.5) | collective-permute-done | bytes 131104 | tf_op jit(solution)/shard_map/ppermute | solution.py:120
  72.1 1.5 %fusion.34 = (bf16[128,256]{1,0:T(8,128)(2,1)}, bf16[1,128,256]{2,1,0:T(8,128)(2,1)S(1)}) fusion(bf16[256,256]{1,0:T(8,128)(2,1)} %collective-permute-done.5), kind=kLoop, calls=%fused_computation.74 | loop fusion | bytes 262144 | tf_op jit(solution)/shard_map/slice | solution.py:150
  73.6 14.5 %all-to-all-done.2.kv_ref = bf16[64,64,256]{2,1,0:T(8,128)(2,1)} async-done(((bf16[64,64,256]{2,1,0:T(8,128)(2,1)}), bf16[64,64,256]{2,1,0:T(8,128)(2,1)}, u32[]{:S(2)}, u32[]{:S(2)}) %all-to-all-start.2) | async-done | bytes 2097184 | tf_op jit(solution)/shard_map/all_to_all | solution.py:141
  88.1 0.0 copy-done.1
  88.1 0.0 copy-done.2
  88.1 13.5 %shard_map.74 = bf16[8,64,128]{2,1,0:T(8,128)(2,1)S(1)} custom-call(s32[8,64]{1,0:T(8,128)S(1)} %convert_add_fusion.nbr_ref, s32[8]{0:T(128)S(1)} %copy-done.1, f32[4]{0:T(128)S(1)} %copy-done.2, bf16[8,64,256]{2,1,0:T(8,128)(2,1)S(1)} %bitcast.43, bf16[8,64,4096]{2,1,0:T(8,128)(2,1)} %bias_ref.3, bf16[64,64,256]{2,1,0:T(8,128)(2,1)} %all-to-all-done.2.kv_ref), custom_call_target="tpu_custom_call" | custom-call | tf_op jit(solution)/shard_map/pallas_call | solution.py:73
  101.6 0.9 broadcast_in_dim.62
  102.4 5.3 %all-to-all-start.3 = ((bf16[4,512,128]{2,1,0:T(8,128)(2,1)}), bf16[4,512,128]{2,1,0:T(8,128)(2,1)}, u32[]{:S(2)}, u32[]{:S(2)}) async-start(bf16[4,512,128]{2,1,0:T(8,128)(2,1)} %broadcast_in_dim.62), calls=%async_computation.3 | async-start | bytes 1048576 | tf_op jit(solution)/shard_map/all_to_all | solution.py:161
  107.8 0.0 collective-permute-done.4
  107.8 1.5 %fusion.33 = (bf16[128,256]{1,0:T(8,128)(2,1)}, bf16[1,128,256]{2,1,0:T(8,128)(2,1)S(1)}) fusion(bf16[256,256]{1,0:T(8,128)(2,1)} %collective-permute-done.4), kind=kLoop, calls=%fused_computation.73 | loop fusion | bytes 262144 | tf_op jit(solution)/shard_map/slice | solution.py:150
  109.3 0.0 collective-permute-done.3
  109.3 1.5 %fusion.32 = (bf16[128,256]{1,0:T(8,128)(2,1)}, bf16[1,128,256]{2,1,0:T(8,128)(2,1)S(1)}) fusion(bf16[256,256]{1,0:T(8,128)(2,1)} %collective-permute-done.3), kind=kLoop, calls=%fused_computation.72 | loop fusion | bytes 262144 | tf_op jit(solution)/shard_map/slice | solution.py:150
  110.8 0.7 pad_maximum_fusion.2
  111.5 2.2 %gather_fusion = bf16[4,128,256]{2,1,0:T(8,128)(2,1)} fusion(bf16[4,128,256]{2,1,0:T(8,128)(2,1)} %pad_maximum_fusion.2, s32[1024]{0:T(1024)S(1)} %pad_clamp_fusion), kind=kCustom, calls=%fused_computation | custom fusion | bytes 524304 | tf_op jit(solution)/shard_map/jit(_take)/gather | solution.py:159
  113.8 12.0 %shard_map.73 = bf16[8,64,128]{2,1,0:T(8,128)(2,1)S(1)} custom-call(s32[8,64]{1,0:T(8,128)S(1)} %convert_add_fusion.nbr_ref, s32[8]{0:T(128)S(1)} %copy-done.1, f32[4]{0:T(128)S(1)} %copy-done.2, bf16[8,64,256]{2,1,0:T(8,128)(2,1)S(1)} %bitcast.44, bf16[8,64,4096]{2,1,0:T(8,128)(2,1)} %bias_ref.3, bf16[64,64,256]{2,1,0:T(8,128)(2,1)S(1)} %all-to-all-done.1.kv_ref), custom_call_target="tpu_custom_call" | custom-call | tf_op jit(solution)/shard_map/pallas_call | solution.py:73
  125.8 3.3 %collective-permute-start.2 = (bf16[512,128]{1,0:T(8,128)(2,1)S(1)}, bf16[512,128]{1,0:T(8,128)(2,1)S(1)}, u32[]{:S(2)}, u32[]{:S(2)}) collective-permute-start(bf16[512,128]{1,0:T(8,128)(2,1)S(1)} %bitcast.46), channel_id=1, source_target_pairs={{0,3},{1,0},{2,1},{3,2},{4,7},{5,4},{6,5},{7,6},{8,11},{9,8},{10,9... | collective-permute-start | bytes 393224 | tf_op jit(solution)/shard_map/ppermute | solution.py:149
  129.1 0.9 collective-permute-start.1
  130.0 0.9 collective-permute-start
  130.8 0.0 all-to-all-done.3
  130.8 1.4 %convolution_bitcast_fusion = f32[512,256]{1,0:T(8,128)S(1)} fusion(bf16[4,512,128]{2,1,0:T(8,128)(2,1)} %all-to-all-done.3, bf16[4,128,256]{2,1,0:T(8,128)(2,1)} %gather_fusion), kind=kOutput, calls=%fused_computation.3 | convolution fusion | flops 134217728 | bytes 1310720 | tf_op jit(solution)/shard_map/dot_general | solution.py:162
  132.2 1.8 %collective-permute-done.2 = bf16[512,128]{1,0:T(8,128)(2,1)S(1)} collective-permute-done((bf16[512,128]{1,0:T(8,128)(2,1)S(1)}, bf16[512,128]{1,0:T(8,128)(2,1)S(1)}, u32[]{:S(2)}, u32[]{:S(2)}) %collective-permute-start.2) | collective-permute-done | bytes 131104 | tf_op jit(solution)/shard_map/ppermute | solution.py:149
  134.0 2.3 %collective-permute-done.1 = bf16[512,128]{1,0:T(8,128)(2,1)S(1)} collective-permute-done((bf16[512,128]{1,0:T(8,128)(2,1)S(1)}, bf16[512,128]{1,0:T(8,128)(2,1)S(1)}, u32[]{:S(2)}, u32[]{:S(2)}) %collective-permute-start.1) | collective-permute-done | bytes 131104 | tf_op jit(solution)/shard_map/ppermute | solution.py:149
  136.3 1.4 %collective-permute-done = bf16[512,128]{1,0:T(8,128)(2,1)S(1)} collective-permute-done((bf16[512,128]{1,0:T(8,128)(2,1)S(1)}, bf16[512,128]{1,0:T(8,128)(2,1)S(1)}, u32[]{:S(2)}, u32[]{:S(2)}) %collective-permute-start) | collective-permute-done | bytes 131104 | tf_op jit(solution)/shard_map/ppermute | solution.py:149
  137.7 1.9 %fusion = bf16[512,256]{1,0:T(8,128)(2,1)} fusion(f32[512,256]{1,0:T(8,128)S(1)} %convolution_bitcast_fusion, bf16[512,128]{1,0:T(8,128)(2,1)S(1)} %collective-permute-done.2, bf16[512,128]{1,0:T(8,128)(2,1)S(1)} %collective-permute-done.1, bf16[512,128]{1,0:T(8,128)(2,1)S(1)} %collective-permute-done, bf16[512,128]{1,0:T(8,128)(2,1)S(1)} %bitcast.49, ...), kind=kOutput, calls=%fused_computation.5 | convolution fusion | flops 137625600 | bytes 1572864 | tf_op jit(solution)/shard_map/dot_general | solution.py:151
  (10 shorter events, 0.1 us)
Async XLA Ops:
  0.0 9.6 %copy-start = (bf16[512,1024]{1,0:T(8,128)(2,1)S(1)}, bf16[512,1024]{1,0:T(8,128)(2,1)}, u32[]{:S(2)}) copy-start(bf16[512,1024]{1,0:T(8,128)(2,1)} %param.7) | copy-start | bytes 3145732
  1.9 13.8 %all-to-all-start = ((s32[32,1,2]{2,1,0:T(1,128)}), s32[32,1,2]{2,1,0:T(1,128)S(1)}, u32[]{:S(2)}, u32[]{:S(2)}) async-start(s32[32,1,2]{2,1,0:T(1,128)} %copy.15), calls=%async_computation | async-start | bytes 32768 | tf_op jit(solution)/shard_map/all_to_all | solution.py:111
  19.7 5.5 %copy-start.3 = (bf16[512,256]{0,1:T(8,128)(2,1)S(1)}, bf16[512,256]{0,1:T(8,128)(2,1)}, u32[]{:S(2)}) copy-start(bf16[512,256]{0,1:T(8,128)(2,1)} %get-tuple-element.27) | copy-start | bytes 786436
  19.7 33.4 %all-to-all-start.1 = ((bf16[64,64,256]{2,1,0:T(8,128)(2,1)}), bf16[64,64,256]{2,1,0:T(8,128)(2,1)S(1)}, u32[]{:S(2)}, u32[]{:S(2)}) async-start(bf16[64,64,256]{2,1,0:T(8,128)(2,1)} %bitcast.53), calls=%async_computation.1 | async-start | bytes 4194304 | tf_op jit(solution)/shard_map/all_to_all | solution.py:141
  53.1 14.1 %copy-start.4 = (s32[8,64]{1,0:T(8,128)S(1)}, s32[8,64]{1,0:T(8,128)}, u32[]{:S(2)}) copy-start(s32[8,64]{1,0:T(8,128)} %param.12) | copy-start | bytes 6148
  53.1 35.0 %all-to-all-start.2 = ((bf16[64,64,256]{2,1,0:T(8,128)(2,1)}), bf16[64,64,256]{2,1,0:T(8,128)(2,1)}, u32[]{:S(2)}, u32[]{:S(2)}) async-start(bf16[64,64,256]{2,1,0:T(8,128)(2,1)} %bitcast.52), calls=%async_computation.2 | async-start | bytes 4194304 | tf_op jit(solution)/shard_map/all_to_all | solution.py:141
  60.0 28.1 %copy-start.1 = (s32[8]{0:T(128)S(1)}, s32[8]{0:T(128)}, u32[]{:S(2)}) copy-start(s32[8]{0:T(128)} %cnt_ref.3) | copy-start | bytes 100
  60.0 28.1 %copy-start.2 = (f32[4]{0:T(128)S(1)}, f32[4]{0:T(128)}, u32[]{:S(2)}) copy-start(f32[4]{0:T(128)} %gain_ref.3) | copy-start | bytes 52
  61.9 10.2 %collective-permute-start.5 = (bf16[256,256]{1,0:T(8,128)(2,1)}, bf16[256,256]{1,0:T(8,128)(2,1)}, u32[]{:S(2)}, u32[]{:S(2)}) collective-permute-start(bf16[256,256]{1,0:T(8,128)(2,1)} %get-tuple-element.12), channel_id=1, source_target_pairs={{0,3},{1,0},{2,1},{3,2},{4,7},{5,4},{6,5},{7,6},{8,11},{9,8},{10,9... | collective-permute-start | bytes 393224 | tf_op jit(solution)/shard_map/ppermute | solution.py:120
  65.9 41.9 %collective-permute-start.4 = (bf16[256,256]{1,0:T(8,128)(2,1)}, bf16[256,256]{1,0:T(8,128)(2,1)}, u32[]{:S(2)}, u32[]{:S(2)}) collective-permute-start(bf16[256,256]{1,0:T(8,128)(2,1)} %get-tuple-element.13), channel_id=1, source_target_pairs={{0,2},{1,3},{2,0},{3,1},{4,6},{5,7},{6,4},{7,5},{8,10},{9,11},{10,... | collective-permute-start | bytes 393224 | tf_op jit(solution)/shard_map/ppermute | solution.py:120
  65.9 43.4 %collective-permute-start.3 = (bf16[256,256]{1,0:T(8,128)(2,1)}, bf16[256,256]{1,0:T(8,128)(2,1)}, u32[]{:S(2)}, u32[]{:S(2)}) collective-permute-start(bf16[256,256]{1,0:T(8,128)(2,1)} %get-tuple-element.11), channel_id=1, source_target_pairs={{0,1},{1,2},{2,3},{3,0},{4,5},{5,6},{6,7},{7,4},{8,9},{9,10},{10,1... | collective-permute-start | bytes 393224 | tf_op jit(solution)/shard_map/ppermute | solution.py:120
  102.4 28.4 %all-to-all-start.3 = ((bf16[4,512,128]{2,1,0:T(8,128)(2,1)}), bf16[4,512,128]{2,1,0:T(8,128)(2,1)}, u32[]{:S(2)}, u32[]{:S(2)}) async-start(bf16[4,512,128]{2,1,0:T(8,128)(2,1)} %broadcast_in_dim.62), calls=%async_computation.3 | async-start | bytes 1048576 | tf_op jit(solution)/shard_map/all_to_all | solution.py:161
  125.8 8.2 %collective-permute-start.2 = (bf16[512,128]{1,0:T(8,128)(2,1)S(1)}, bf16[512,128]{1,0:T(8,128)(2,1)S(1)}, u32[]{:S(2)}, u32[]{:S(2)}) collective-permute-start(bf16[512,128]{1,0:T(8,128)(2,1)S(1)} %bitcast.46), channel_id=1, source_target_pairs={{0,3},{1,0},{2,1},{3,2},{4,7},{5,4},{6,5},{7,6},{8,11},{9,8},{10,9... | collective-permute-start | bytes 393224 | tf_op jit(solution)/shard_map/ppermute | solution.py:149
  129.1 7.2 %collective-permute-start.1 = (bf16[512,128]{1,0:T(8,128)(2,1)S(1)}, bf16[512,128]{1,0:T(8,128)(2,1)S(1)}, u32[]{:S(2)}, u32[]{:S(2)}) collective-permute-start(bf16[512,128]{1,0:T(8,128)(2,1)S(1)} %bitcast.47), channel_id=1, source_target_pairs={{0,2},{1,3},{2,0},{3,1},{4,6},{5,7},{6,4},{7,5},{8,10},{9,11},{10,... | collective-permute-start | bytes 393224 | tf_op jit(solution)/shard_map/ppermute | solution.py:149
  130.0 7.7 %collective-permute-start = (bf16[512,128]{1,0:T(8,128)(2,1)S(1)}, bf16[512,128]{1,0:T(8,128)(2,1)S(1)}, u32[]{:S(2)}, u32[]{:S(2)}) collective-permute-start(bf16[512,128]{1,0:T(8,128)(2,1)S(1)} %bitcast.48), channel_id=1, source_target_pairs={{0,1},{1,2},{2,3},{3,0},{4,5},{5,6},{6,7},{7,4},{8,9},{9,10},{10,1... | collective-permute-start | bytes 393224 | tf_op jit(solution)/shard_map/ppermute | solution.py:149

commit v15 on v13

--- a/solution.py
+++ b/solution.py
@@ -13,7 +13,7 @@
 NB = 64
 
 
-def _attend_kernel(p0, nbr_ref, cnt_ref, gain_ref, q_ref, bias_ref, kv_ref, o_ref):
+def _attend_kernel(p0, masked, nbr_ref, cnt_ref, gain_ref, q_ref, bias_ref, kv_ref, o_ref, *extra):
     g = pl.program_id(0)
     width = kv_ref.shape[-1]
     half_w = width // 2
@@ -21,7 +21,12 @@
     span = NB * BLK
     live_cols = cnt_ref[g] * BLK
     col = lax.broadcasted_iota(jnp.int32, (BLK, span), 1)
-    bias = jnp.where(col < live_cols, bias_ref[0].astype(jnp.float32), -jnp.inf)
+    if masked:
+        bias = bias_ref[0].astype(jnp.float32)
+    else:
+        bias_m = jnp.where(col < live_cols, bias_ref[0], jnp.asarray(-jnp.inf, bias_ref.dtype))
+        extra[0][0] = bias_m
+        bias = bias_m.astype(jnp.float32)
     q = q_ref[0]
     lane = lax.broadcasted_iota(jnp.int32, (BLK, 128), 1)
     scale = HD ** (-0.5)
@@ -56,7 +61,7 @@
     o_ref[0] = outs[0] if len(outs) == 1 else jnp.concatenate(outs, axis=1)
 
 
-def attend(nbr, cnt, gain, q_blocks, bias, kv_table, p0, width_q):
+def attend(nbr, cnt, gain, q_blocks, bias, kv_table, p0, width_q, masked):
     steps = q_blocks.shape[0]
     span = NB * BLK
     grid_spec = pltpu.PrefetchScalarGridSpec(
@@ -68,12 +73,14 @@
             pl.BlockSpec((1, BLK, span), lambda g, n, c: (g, 0, 0)),
             pl.BlockSpec(kv_table.shape, lambda g, n, c: (0, 0, 0)),
         ],
-        out_specs=pl.BlockSpec((1, BLK, width_q), lambda g, n, c: (g, 0, 0)),
+        out_specs=[pl.BlockSpec((1, BLK, width_q), lambda g, n, c: (g, 0, 0))]
+        + ([] if masked else [pl.BlockSpec((1, BLK, span), lambda g, n, c: (g, 0, 0))]),
     )
     return pl.pallas_call(
-        functools.partial(_attend_kernel, p0),
+        functools.partial(_attend_kernel, p0, masked),
         grid_spec=grid_spec,
-        out_shape=jax.ShapeDtypeStruct((steps, BLK, width_q), jnp.bfloat16),
+        out_shape=[jax.ShapeDtypeStruct((steps, BLK, width_q), jnp.bfloat16)]
+        + ([] if masked else [jax.ShapeDtypeStruct(bias.shape, bias.dtype)]),
         compiler_params=pltpu.CompilerParams(
             dimension_semantics=("arbitrary",), vmem_limit_bytes=48 * 1024 * 1024
         ),
@@ -128,13 +135,17 @@
         outgoing.append(jnp.take(kv, wanted, axis=0, mode="clip"))
     total = None
     table = None
+    bias_in = edge_bias
     for c in range(chunks):
         cols = slice(c * chunk, (c + 1) * chunk)
         send = outgoing[c]
         if table is not None:
             table, send = lax.optimization_barrier((table, send))
         table = lax.all_to_all(send, "row", 0, 0, tiled=True)
-        att = attend(pos, counts, bias_gain, q_blocks, edge_bias, table, c, chunk)
+        outs = attend(pos, counts, bias_gain, q_blocks, bias_in, table, c, chunk, c > 0)
+        att = outs[0]
+        if c == 0:
+            bias_in = outs[1]
         att = att.reshape(rows, chunk)
         if c + 1 < chunks:
             att_all = [att]

time: 141 us -> 124 us (0.88)
  waiting for transfers between devices: 48.5 us -> 39.2 us
  local copies, waits for them, and re-layouts: 18.5 us -> 15 us
  matrix products: 7.88 us -> 5.84 us
    all_to_all x2, waiting for transfers between devices: 39.3 us -> 28.4 us  [_body(): table = lax.all_to_all(send, 'row', 0, 0, tiled=True)]
    all_to_all x1, waiting for transfers between devices: 0.01 us -> 2.36 us  [_body(): recv = lax.all_to_all(rep, 'head', 0, 0, tiled=True)]
    slice x3, local copies, waits for them, and re-layouts: 4.49 us -> 2.43 us  [_body(): w_all.append(w_parts[s - 1][cols])]
    gather x1, local copies, waits for them, and re-layouts: 2.23 us -> 0.56 us  [_body(): by_device = jnp.take(by_shift, order, axis=0, mode='clip')]
  transfers between devices with their start and end apart: 10 -> 10, of which waited for: 7 -> 8; matrix products, arithmetic and copies ran while one was open for 16% -> 13% of each run, Pallas kernels for 18% -> 20%
where the time goes in v15:
time: 124 us; the launch traced here: 122 us
  waiting for transfers between devices  39.2 us (32%)
  starting transfers between devices  35.3 us (28%)
  Pallas kernels  24.8 us (20%)
  local copies, waits for them, and re-layouts  15 us (12%)
  matrix products  5.84 us (5%)
  other arithmetic  1.93 us (2%)
    all_to_all x2, waiting for transfers between devices, _body(): table = lax.all_to_all(send, 'row', 0, 0, tiled=True)  28.4 us
    pallas_call x2, Pallas kernels, attend(): pl.pallas_call(functools.partial(_attend_kernel, p0, masked), grid_spec=g...  24.8 us
    all_to_all x2, starting transfers between devices, _body(): table = lax.all_to_all(send, 'row', 0, 0, tiled=True)  12 us
    all_to_all x1, starting transfers between devices, _body(): wanted = lax.all_to_all(req, 'row', 0, 0, tiled=True).reshape(-1)  7.62 us
    all_to_all x1, starting transfers between devices, _body(): recv = lax.all_to_all(rep, 'head', 0, 0, tiled=True)  5.44 us
    ppermute x3, starting transfers between devices, _body(): w_parts.append(lax.ppermute(piece, 'head', perm))  5.3 us
    ppermute x3, starting transfers between devices, _body(): att_all.append(lax.ppermute(att, 'head', perm))  5.02 us
    ppermute x3, waiting for transfers between devices, _body(): att_all.append(lax.ppermute(att, 'head', perm))  4.65 us
  transfers between devices with their start and end apart: 10, of which 8 were waited for; matrix products, arithmetic and copies ran while one was open for 13% of the time, Pallas kernels for 20%

profile of v15, /device:TPU:2, one launch (start us, length us, event | category | flops | bytes accessed | tf_op | source)
XLA Modules:
  0.0 122.4 jit_solution(4296457571511349227)
XLA Ops:
  0.0 0.0 copy-start
  0.0 0.8 eq.67
  0.9 0.2 fusion.14
  1.0 0.1 reshape.94
  1.1 0.1 select_reduce_fusion.1
  1.3 0.7 copy.16
  1.9 7.6 %all-to-all-start = ((s32[32,1,2]{2,1,0:T(1,128)}), s32[32,1,2]{2,1,0:T(1,128)S(1)}, u32[]{:S(2)}, u32[]{:S(2)}) async-start(s32[32,1,2]{2,1,0:T(1,128)} %copy.16), calls=%async_computation | async-start | bytes 32768 | tf_op jit(solution)/shard_map/all_to_all | solution.py:118
  9.6 0.0 copy-done
  9.6 1.5 %convolution_convert_fusion = bf16[512,256]{0,1:T(8,128)(2,1)S(1)} fusion(bf16[512,1024]{1,0:T(8,128)(2,1)S(1)} %copy-done, bf16[3,1024,256]{2,1,0:T(8,128)(2,1)} %param.8), kind=kOutput, calls=%fused_computation.6 | convolution fusion | flops 268566528 | bytes 1835008 | tf_op jit(solution)/shard_map/dot_general | solution.py:121
  11.1 1.5 %convolution_convert_fusion.1 = bf16[512,256]{0,1:T(8,128)(2,1)S(1)} fusion(bf16[512,1024]{1,0:T(8,128)(2,1)S(1)} %copy-done, bf16[3,1024,256]{2,1,0:T(8,128)(2,1)} %param.8), kind=kOutput, calls=%fused_computation.7 | convolution fusion | flops 268566528 | bytes 1835008 | tf_op jit(solution)/shard_map/dot_general | solution.py:120
  12.7 0.7 pad_maximum_fusion
  13.5 0.1 copy.15
  13.6 2.2 %all-to-all-done = s32[32,1,2]{2,1,0:T(1,128)S(1)} async-done(((s32[32,1,2]{2,1,0:T(1,128)}), s32[32,1,2]{2,1,0:T(1,128)S(1)}, u32[]{:S(2)}, u32[]{:S(2)}) %all-to-all-start) | async-done | bytes 288 | tf_op jit(solution)/shard_map/all_to_all | solution.py:118
  15.8 0.6 broadcast.124
  16.3 0.7 reduce.3
  17.1 0.1 reshape.102
  17.2 2.0 %gather_fusion = bf16[64,64,256]{2,1,0:T(8,128)(2,1)} fusion(bf16[8,64,256]{2,1,0:T(8,128)(2,1)S(1)} %bitcast.46, s32[1024]{0:T(1024)S(1)} %pad_clamp_fusion.1), kind=kCustom, calls=%fused_computation | custom fusion | bytes 4194560 | tf_op jit(solution)/shard_map/jit(_take)/gather | solution.py:135
  19.2 5.2 %all-to-all-start.1 = ((bf16[64,64,256]{2,1,0:T(8,128)(2,1)}), bf16[64,64,256]{2,1,0:T(8,128)(2,1)S(1)}, u32[]{:S(2)}, u32[]{:S(2)}) async-start(bf16[64,64,256]{2,1,0:T(8,128)(2,1)} %gather_fusion), calls=%async_computation.1 | async-start | bytes 4194304 | tf_op jit(solution)/shard_map/all_to_all | solution.py:144
  24.4 1.1 copy.17
  25.5 2.0 %gather_fusion.1 = bf16[64,64,256]{2,1,0:T(8,128)(2,1)} fusion(bf16[8,64,256]{2,1,0:T(8,128)(2,1)S(1)} %bitcast.47, s32[1024]{0:T(1024)S(1)} %pad_clamp_fusion.1), kind=kCustom, calls=%fused_computation.1 | custom fusion | bytes 4194560 | tf_op jit(solution)/shard_map/jit(_take)/gather | solution.py:135
  27.6 0.0 copy-start.7
  27.6 24.8 %all-to-all-done.1.kv_ref = bf16[64,64,256]{2,1,0:T(8,128)(2,1)S(1)} async-done(((bf16[64,64,256]{2,1,0:T(8,128)(2,1)}), bf16[64,64,256]{2,1,0:T(8,128)(2,1)S(1)}, u32[]{:S(2)}, u32[]{:S(2)}) %all-to-all-start.1) | async-done | bytes 2097184 | tf_op jit(solution)/shard_map/all_to_all | solution.py:144
  52.4 6.7 %all-to-all-start.2 = ((bf16[64,64,256]{2,1,0:T(8,128)(2,1)}), bf16[64,64,256]{2,1,0:T(8,128)(2,1)}, u32[]{:S(2)}, u32[]{:S(2)}) async-start(bf16[64,64,256]{2,1,0:T(8,128)(2,1)} %gather_fusion.1), calls=%async_computation.2 | async-start | bytes 4194304 | tf_op jit(solution)/shard_map/all_to_all | solution.py:144
  59.1 0.0 copy-start.1
  59.1 0.0 copy-start.2
  59.2 1.8 %constant_dynamic-slice_fusion.3 = (bf16[256,256]{1,0:T(8,128)(2,1)}, bf16[256,256]{1,0:T(8,128)(2,1)}, bf16[256,256]{1,0:T(8,128)(2,1)}) fusion(bf16[256,1024]{1,0:T(8,128)(2,1)} %param.9, s32[]{:T(128)S(6)} %select_n.104, s32[]{:T(128)S(6)} %select_n.108, s32[]{:T(128)S(6)} %select_n.106), kind=kLoop, calls=%fused_computation.64 | loop fusion | bytes 786444 | tf_op jit(solution)/shard_map/dynamic_slice | solution.py:125
  61.0 4.0 %collective-permute-start.5 = (bf16[256,256]{1,0:T(8,128)(2,1)}, bf16[256,256]{1,0:T(8,128)(2,1)S(1)}, u32[]{:S(2)}, u32[]{:S(2)}) collective-permute-start(bf16[256,256]{1,0:T(8,128)(2,1)} %get-tuple-element.16), channel_id=1, source_target_pairs={{0,3},{1,0},{2,1},{3,2},{4,7},{5,4},{6,5},{7,6},{8,11},{9,8},{10,9... | collective-permute-start | bytes 393224 | tf_op jit(solution)/shard_map/ppermute | solution.py:127
  65.0 0.0 collective-permute-start.4
  65.0 1.3 %collective-permute-start.3 = (bf16[256,256]{1,0:T(8,128)(2,1)}, bf16[256,256]{1,0:T(8,128)(2,1)}, u32[]{:S(2)}, u32[]{:S(2)}) collective-permute-start(bf16[256,256]{1,0:T(8,128)(2,1)} %get-tuple-element.15), channel_id=1, source_target_pairs={{0,1},{1,2},{2,3},{3,0},{4,5},{5,6},{6,7},{7,4},{8,9},{9,10},{10,1... | collective-permute-start | bytes 393224 | tf_op jit(solution)/shard_map/ppermute | solution.py:127
  66.3 0.0 copy-done.7
  66.3 0.1 eq.63
  66.4 0.1 select_reduce_fusion
  66.5 0.1 reshape.95
  66.6 1.5 %convolution_convert_fusion.2 = bf16[512,256]{1,0:T(8,128)(2,1)S(1)} fusion(bf16[512,1024]{1,0:T(8,128)(2,1)S(1)} %copy-done, bf16[3,1024,256]{2,1,0:T(8,128)(2,1)} %param.8), kind=kOutput, calls=%fused_computation.8 | convolution fusion | flops 268566528 | bytes 1835008 | tf_op jit(solution)/shard_map/dot_general | solution.py:119
  68.1 1.6 %constant_dynamic-slice_fusion = (bf16[128,256]{1,0:T(8,128)(2,1)}, bf16[1,128,256]{2,1,0:T(8,128)(2,1)}) fusion(bf16[256,1024]{1,0:T(8,128)(2,1)} %param.9, s32[]{:T(128)S(6)} %select_n.102, s32[]{:T(128)S(6)} %add.74), kind=kLoop, calls=%fused_computation.61 | loop fusion | bytes 262152 | tf_op jit(solution)/shard_map/slice | solution.py:152
  69.6 1.6 %collective-permute-done.5 = bf16[256,256]{1,0:T(8,128)(2,1)S(1)} collective-permute-done((bf16[256,256]{1,0:T(8,128)(2,1)}, bf16[256,256]{1,0:T(8,128)(2,1)S(1)}, u32[]{:S(2)}, u32[]{:S(2)}) %collective-permute-start.5) | collective-permute-done | bytes 131104 | tf_op jit(solution)/shard_map/ppermute | solution.py:127
  71.2 0.7 fusion.32
  71.8 0.0 copy-done.1
  71.8 0.0 copy-done.2
  71.8 11.7 %shard_map.73 = (bf16[8,64,128]{2,1,0:T(8,128)(2,1)S(1)}, bf16[8,64,4096]{2,1,0:T(8,128)(2,1)}) custom-call(s32[8,64]{1,0:T(8,128)S(1)} %convert_add_fusion.nbr_ref, s32[8]{0:T(128)S(1)} %copy-done.1, f32[4]{0:T(128)S(1)} %copy-done.2, bf16[8,64,256]{2,1,0:T(8,128)(2,1)S(1)} %bitcast.39, bf16[8,64,4096]{2,1,0:T(8,128)(2,1)} %bias_ref.1, ...), custom_call_target="tpu_custom_call" | custom-call | tf_op jit(solution)/shard_map/pallas_call | solution.py:79
  83.5 3.6 %all-to-all-done.2.kv_ref = bf16[64,64,256]{2,1,0:T(8,128)(2,1)} async-done(((bf16[64,64,256]{2,1,0:T(8,128)(2,1)}), bf16[64,64,256]{2,1,0:T(8,128)(2,1)}, u32[]{:S(2)}, u32[]{:S(2)}) %all-to-all-start.2) | async-done | bytes 2097184 | tf_op jit(solution)/shard_map/all_to_all | solution.py:144
  87.2 13.1 %shard_map.74 = bf16[8,64,128]{2,1,0:T(8,128)(2,1)S(1)} custom-call(s32[8,64]{1,0:T(8,128)S(1)} %convert_add_fusion.nbr_ref, s32[8]{0:T(128)S(1)} %copy-done.1, f32[4]{0:T(128)S(1)} %copy-done.2, bf16[8,64,256]{2,1,0:T(8,128)(2,1)S(1)} %bitcast.40, bf16[8,64,4096]{2,1,0:T(8,128)(2,1)} %get-tuple-element.9.bias_ref, bf16[64,64,256]{2,1,0:T(8,128)(2,1)} %all-to-all-done.2.kv_ref), custom_call_target="tpu_custom_call" | custom-call | tf_op jit(solution)/shard_map/pallas_call | solution.py:79
  100.3 0.0 copy-start.3
  100.3 0.0 copy-start.4
  100.3 0.9 broadcast_in_dim.66
  101.2 5.4 %all-to-all-start.3 = ((bf16[4,512,128]{2,1,0:T(8,128)(2,1)}), bf16[4,512,128]{2,1,0:T(8,128)(2,1)S(1)}, u32[]{:S(2)}, u32[]{:S(2)}) async-start(bf16[4,512,128]{2,1,0:T(8,128)(2,1)} %broadcast_in_dim.66), calls=%async_computation.3 | async-start | bytes 1048576 | tf_op jit(solution)/shard_map/all_to_all | solution.py:167
  106.6 0.0 collective-permute-done.4
  106.6 0.9 fusion.31
  107.5 0.0 collective-permute-done.3
  107.5 0.9 fusion.30
  108.4 0.0 copy-done.3
  108.4 0.0 copy-done.4
  108.5 0.6 gather_fusion.2
  109.0 3.3 %collective-permute-start.2 = (bf16[512,128]{1,0:T(8,128)(2,1)S(1)}, bf16[512,128]{1,0:T(8,128)(2,1)S(1)}, u32[]{:S(2)}, u32[]{:S(2)}) collective-permute-start(bf16[512,128]{1,0:T(8,128)(2,1)S(1)} %bitcast.42), channel_id=1, source_target_pairs={{0,3},{1,0},{2,1},{3,2},{4,7},{5,4},{6,5},{7,6},{8,11},{9,8},{10,9... | collective-permute-start | bytes 393224 | tf_op jit(solution)/shard_map/ppermute | solution.py:155
  112.3 0.9 collective-permute-start.1
  113.2 0.9 collective-permute-start
  114.1 2.4 %all-to-all-done.3 = bf16[4,512,128]{2,1,0:T(8,128)(2,1)S(1)} async-done(((bf16[4,512,128]{2,1,0:T(8,128)(2,1)}), bf16[4,512,128]{2,1,0:T(8,128)(2,1)S(1)}, u32[]{:S(2)}, u32[]{:S(2)}) %all-to-all-start.3) | async-done | bytes 524320 | tf_op jit(solution)/shard_map/all_to_all | solution.py:167
  116.4 0.3 convolution_bitcast_fusion
  116.7 1.7 %collective-permute-done.2 = bf16[512,128]{1,0:T(8,128)(2,1)S(1)} collective-permute-done((bf16[512,128]{1,0:T(8,128)(2,1)S(1)}, bf16[512,128]{1,0:T(8,128)(2,1)S(1)}, u32[]{:S(2)}, u32[]{:S(2)}) %collective-permute-start.2) | collective-permute-done | bytes 131104 | tf_op jit(solution)/shard_map/ppermute | solution.py:155
  118.5 1.5 %collective-permute-done.1 = bf16[512,128]{1,0:T(8,128)(2,1)S(1)} collective-permute-done((bf16[512,128]{1,0:T(8,128)(2,1)S(1)}, bf16[512,128]{1,0:T(8,128)(2,1)S(1)}, u32[]{:S(2)}, u32[]{:S(2)}) %collective-permute-start.1) | collective-permute-done | bytes 131104 | tf_op jit(solution)/shard_map/ppermute | solution.py:155
  120.0 1.4 %collective-permute-done = bf16[512,128]{1,0:T(8,128)(2,1)S(1)} collective-permute-done((bf16[512,128]{1,0:T(8,128)(2,1)S(1)}, bf16[512,128]{1,0:T(8,128)(2,1)S(1)}, u32[]{:S(2)}, u32[]{:S(2)}) %collective-permute-start) | collective-permute-done | bytes 131104 | tf_op jit(solution)/shard_map/ppermute | solution.py:155
  121.4 0.0 copy-done.5
  121.4 0.0 copy-done.6
  121.4 1.0 fusion
  (13 shorter events, 0.1 us)
Async XLA Ops:
  0.0 9.6 %copy-start = (bf16[512,1024]{1,0:T(8,128)(2,1)S(1)}, bf16[512,1024]{1,0:T(8,128)(2,1)}, u32[]{:S(2)}) copy-start(bf16[512,1024]{1,0:T(8,128)(2,1)} %param.7) | copy-start | bytes 3145732
  1.9 13.8 %all-to-all-start = ((s32[32,1,2]{2,1,0:T(1,128)}), s32[32,1,2]{2,1,0:T(1,128)S(1)}, u32[]{:S(2)}, u32[]{:S(2)}) async-start(s32[32,1,2]{2,1,0:T(1,128)} %copy.16), calls=%async_computation | async-start | bytes 32768 | tf_op jit(solution)/shard_map/all_to_all | solution.py:118
  19.2 33.2 %all-to-all-start.1 = ((bf16[64,64,256]{2,1,0:T(8,128)(2,1)}), bf16[64,64,256]{2,1,0:T(8,128)(2,1)S(1)}, u32[]{:S(2)}, u32[]{:S(2)}) async-start(bf16[64,64,256]{2,1,0:T(8,128)(2,1)} %gather_fusion), calls=%async_computation.1 | async-start | bytes 4194304 | tf_op jit(solution)/shard_map/all_to_all | solution.py:144
  27.6 38.7 %copy-start.7 = (s32[8,64]{1,0:T(8,128)S(1)}, s32[8,64]{1,0:T(8,128)}, u32[]{:S(2)}) copy-start(s32[8,64]{1,0:T(8,128)} %param.12) | copy-start | bytes 6148
  52.4 34.8 %all-to-all-start.2 = ((bf16[64,64,256]{2,1,0:T(8,128)(2,1)}), bf16[64,64,256]{2,1,0:T(8,128)(2,1)}, u32[]{:S(2)}, u32[]{:S(2)}) async-start(bf16[64,64,256]{2,1,0:T(8,128)(2,1)} %gather_fusion.1), calls=%async_computation.2 | async-start | bytes 4194304 | tf_op jit(solution)/shard_map/all_to_all | solution.py:144
  59.1 12.7 %copy-start.1 = (s32[8]{0:T(128)S(1)}, s32[8]{0:T(128)}, u32[]{:S(2)}) copy-start(s32[8]{0:T(128)} %cnt_ref.3) | copy-start | bytes 100
  59.1 12.7 %copy-start.2 = (f32[4]{0:T(128)S(1)}, f32[4]{0:T(128)}, u32[]{:S(2)}) copy-start(f32[4]{0:T(128)} %gain_ref.3) | copy-start | bytes 52
  61.0 10.2 %collective-permute-start.5 = (bf16[256,256]{1,0:T(8,128)(2,1)}, bf16[256,256]{1,0:T(8,128)(2,1)S(1)}, u32[]{:S(2)}, u32[]{:S(2)}) collective-permute-start(bf16[256,256]{1,0:T(8,128)(2,1)} %get-tuple-element.16), channel_id=1, source_target_pairs={{0,3},{1,0},{2,1},{3,2},{4,7},{5,4},{6,5},{7,6},{8,11},{9,8},{10,9... | collective-permute-start | bytes 393224 | tf_op jit(solution)/shard_map/ppermute | solution.py:127
  65.0 41.6 %collective-permute-start.4 = (bf16[256,256]{1,0:T(8,128)(2,1)}, bf16[256,256]{1,0:T(8,128)(2,1)}, u32[]{:S(2)}, u32[]{:S(2)}) collective-permute-start(bf16[256,256]{1,0:T(8,128)(2,1)} %get-tuple-element.17), channel_id=1, source_target_pairs={{0,2},{1,3},{2,0},{3,1},{4,6},{5,7},{6,4},{7,5},{8,10},{9,11},{10,... | collective-permute-start | bytes 393224 | tf_op jit(solution)/shard_map/ppermute | solution.py:127
  65.0 42.5 %collective-permute-start.3 = (bf16[256,256]{1,0:T(8,128)(2,1)}, bf16[256,256]{1,0:T(8,128)(2,1)}, u32[]{:S(2)}, u32[]{:S(2)}) collective-permute-start(bf16[256,256]{1,0:T(8,128)(2,1)} %get-tuple-element.15), channel_id=1, source_target_pairs={{0,1},{1,2},{2,3},{3,0},{4,5},{5,6},{6,7},{7,4},{8,9},{9,10},{10,1... | collective-permute-start | bytes 393224 | tf_op jit(solution)/shard_map/ppermute | solution.py:127
  100.3 8.1 %copy-start.3 = (bf16[1,128,256]{2,1,0:T(8,128)(2,1)S(1)}, bf16[1,128,256]{2,1,0:T(8,128)(2,1)}, u32[]{:S(2)}) copy-start(bf16[1,128,256]{2,1,0:T(8,128)(2,1)} %get-tuple-element.14) | copy-start | bytes 196612
  100.3 8.1 %copy-start.4 = (bf16[1,128,256]{2,1,0:T(8,128)(2,1)S(1)}, bf16[1,128,256]{2,1,0:T(8,128)(2,1)}, u32[]{:S(2)}) copy-start(bf16[1,128,256]{2,1,0:T(8,128)(2,1)} %get-tuple-element.27) | copy-start | bytes 196612
  101.2 20.2 %copy-start.5 = (bf16[128,256]{1,0:T(8,128)(2,1)S(1)}, bf16[128,256]{1,0:T(8,128)(2,1)}, u32[]{:S(2)}) copy-start(bf16[128,256]{1,0:T(8,128)(2,1)} %get-tuple-element.13) | copy-start | bytes 196612
  101.2 20.2 %copy-start.6 = (bf16[128,256]{1,0:T(8,128)(2,1)S(1)}, bf16[128,256]{1,0:T(8,128)(2,1)}, u32[]{:S(2)}) copy-start(bf16[128,256]{1,0:T(8,128)(2,1)} %get-tuple-element.26) | copy-start | bytes 196612
  101.2 15.2 %all-to-all-start.3 = ((bf16[4,512,128]{2,1,0:T(8,128)(2,1)}), bf16[4,512,128]{2,1,0:T(8,128)(2,1)S(1)}, u32[]{:S(2)}, u32[]{:S(2)}) async-start(bf16[4,512,128]{2,1,0:T(8,128)(2,1)} %broadcast_in_dim.66), calls=%async_computation.3 | async-start | bytes 1048576 | tf_op jit(solution)/shard_map/all_to_all | solution.py:167
  109.0 9.4 %collective-permute-start.2 = (bf16[512,128]{1,0:T(8,128)(2,1)S(1)}, bf16[512,128]{1,0:T(8,128)(2,1)S(1)}, u32[]{:S(2)}, u32[]{:S(2)}) collective-permute-start(bf16[512,128]{1,0:T(8,128)(2,1)S(1)} %bitcast.42), channel_id=1, source_target_pairs={{0,3},{1,0},{2,1},{3,2},{4,7},{5,4},{6,5},{7,6},{8,11},{9,8},{10,9... | collective-permute-start | bytes 393224 | tf_op jit(solution)/shard_map/ppermute | solution.py:155
  112.3 7.6 %collective-permute-start.1 = (bf16[512,128]{1,0:T(8,128)(2,1)S(1)}, bf16[512,128]{1,0:T(8,128)(2,1)S(1)}, u32[]{:S(2)}, u32[]{:S(2)}) collective-permute-start(bf16[512,128]{1,0:T(8,128)(2,1)S(1)} %bitcast.43), channel_id=1, source_target_pairs={{0,2},{1,3},{2,0},{3,1},{4,6},{5,7},{6,4},{7,5},{8,10},{9,11},{10,... | collective-permute-start | bytes 393224 | tf_op jit(solution)/shard_map/ppermute | solution.py:155
  113.2 8.2 %collective-permute-start = (bf16[512,128]{1,0:T(8,128)(2,1)S(1)}, bf16[512,128]{1,0:T(8,128)(2,1)S(1)}, u32[]{:S(2)}, u32[]{:S(2)}) collective-permute-start(bf16[512,128]{1,0:T(8,128)(2,1)S(1)} %bitcast.44), channel_id=1, source_target_pairs={{0,1},{1,2},{2,3},{3,0},{4,5},{5,6},{6,7},{7,4},{8,9},{9,10},{10,1... | collective-permute-start | bytes 393224 | tf_op jit(solution)/shard_map/ppermute | solution.py:155

commit v16 on v13

--- a/solution.py
+++ b/solution.py
@@ -53,10 +53,12 @@
         o2 = o2 * (1.0 / jnp.concatenate(sums, axis=0))
         res = jnp.where(lane < HD, o2[:BLK], o2[BLK:])
         outs.append(res.astype(jnp.bfloat16))
-    o_ref[0] = outs[0] if len(outs) == 1 else jnp.concatenate(outs, axis=1)
+    result = outs[0] if len(outs) == 1 else jnp.concatenate(outs, axis=1)
+    for r in range(o_ref.shape[0]):
+        o_ref[r, 0] = result
 
 
-def attend(nbr, cnt, gain, q_blocks, bias, kv_table, p0, width_q):
+def attend(nbr, cnt, gain, q_blocks, bias, kv_table, p0, width_q, reps=1):
     steps = q_blocks.shape[0]
     span = NB * BLK
     grid_spec = pltpu.PrefetchScalarGridSpec(
@@ -68,12 +70,12 @@
             pl.BlockSpec((1, BLK, span), lambda g, n, c: (g, 0, 0)),
             pl.BlockSpec(kv_table.shape, lambda g, n, c: (0, 0, 0)),
         ],
-        out_specs=pl.BlockSpec((1, BLK, width_q), lambda g, n, c: (g, 0, 0)),
+        out_specs=pl.BlockSpec((reps, 1, BLK, width_q), lambda g, n, c: (0, g, 0, 0)),
     )
     return pl.pallas_call(
         functools.partial(_attend_kernel, p0),
         grid_spec=grid_spec,
-        out_shape=jax.ShapeDtypeStruct((steps, BLK, width_q), jnp.bfloat16),
+        out_shape=jax.ShapeDtypeStruct((reps, steps, BLK, width_q), jnp.bfloat16),
         compiler_params=pltpu.CompilerParams(
             dimension_semantics=("arbitrary",), vmem_limit_bytes=48 * 1024 * 1024
         ),
@@ -134,8 +136,10 @@
         if table is not None:
             table, send = lax.optimization_barrier((table, send))
         table = lax.all_to_all(send, "row", 0, 0, tiled=True)
-        att = attend(pos, counts, bias_gain, q_blocks, edge_bias, table, c, chunk)
-        att = att.reshape(rows, chunk)
+        reps = 1 if c + 1 < chunks else head_devs
+        att_rep = attend(pos, counts, bias_gain, q_blocks, edge_bias, table, c, chunk, reps)
+        att_rep = att_rep.reshape(reps, rows, chunk)
+        att = att_rep[0]
         if c + 1 < chunks:
             att_all = [att]
             w_all = [w_own[cols]]
@@ -152,8 +156,7 @@
             by_shift = jnp.stack([w_own[cols]] + [w[cols] for w in w_parts])
             order = (me - jnp.arange(head_devs, dtype=jnp.int32)) % head_devs
             by_device = jnp.take(by_shift, order, axis=0, mode="clip")
-            rep = jnp.broadcast_to(att[None], (head_devs,) + att.shape)
-            recv = lax.all_to_all(rep, "head", 0, 0, tiled=True)
+            recv = lax.all_to_all(att_rep, "head", 0, 0, tiled=True)
             part = lax.dot_general(
                 recv, by_device, (((0, 2), (0, 1)), ((), ())),
                 preferred_element_type=jnp.float32,

time: 141 us -> 141 us (level)
  transfers between devices with their start and end apart: 10 -> 10, of which waited for: 7 -> 7; matrix products, arithmetic and copies ran while one was open for 16% -> 15% of each run, Pallas kernels for 18% -> 18%
where the time goes in v16:
time: 141 us; the launch traced here: 139 us
  waiting for transfers between devices  48.5 us (34%)
  starting transfers between devices  35.2 us (25%)
  Pallas kernels  25.6 us (18%)
  local copies, waits for them, and re-layouts  18.6 us (13%)
  matrix products  7.88 us (6%)
  other arithmetic  2.57 us (2%)
    all_to_all x2, waiting for transfers between devices, _body(): table = lax.all_to_all(send, 'row', 0, 0, tiled=True)  39.3 us
    pallas_call x2, Pallas kernels, attend(): pl.pallas_call(functools.partial(_attend_kernel, p0), grid_spec=grid_spec...  25.6 us
    all_to_all x2, starting transfers between devices, _body(): table = lax.all_to_all(send, 'row', 0, 0, tiled=True)  12 us
    all_to_all x1, starting transfers between devices, _body(): wanted = lax.all_to_all(req, 'row', 0, 0, tiled=True).reshape(-1)  7.62 us
    ppermute x3, waiting for transfers between devices, _body(): att_all.append(lax.ppermute(att, 'head', perm))  5.45 us
    all_to_all x1, starting transfers between devices, _body(): recv = lax.all_to_all(att_rep, 'head', 0, 0, tiled=True)  5.3 us
    ppermute x3, starting transfers between devices, _body(): w_parts.append(lax.ppermute(piece, 'head', perm))  5.3 us
    ppermute x3, starting transfers between devices, _body(): att_all.append(lax.ppermute(att, 'head', perm))  5.02 us
  transfers between devices with their start and end apart: 10, of which 7 were waited for; matrix products, arithmetic and copies ran while one was open for 15% of the time, Pallas kernels for 18%

profile of v16, /device:TPU:2, one launch (start us, length us, event | category | flops | bytes accessed | tf_op | source)
XLA Modules:
  0.0 138.6 jit_solution(2158165677550805802)
XLA Ops:
  0.0 0.0 copy-start
  0.0 0.8 eq.67
  0.9 0.2 fusion.14
  1.0 0.1 reshape.93
  1.1 0.1 select_reduce_fusion.1
  1.3 0.7 copy.16
  1.9 7.6 %all-to-all-start = ((s32[32,1,2]{2,1,0:T(1,128)}), s32[32,1,2]{2,1,0:T(1,128)S(1)}, u32[]{:S(2)}, u32[]{:S(2)}) async-start(s32[32,1,2]{2,1,0:T(1,128)} %copy.16), calls=%async_computation | async-start | bytes 32768 | tf_op jit(solution)/shard_map/all_to_all | solution.py:113
  9.6 0.0 copy-done
  9.6 1.5 %convolution_convert_fusion = bf16[512,256]{0,1:T(8,128)(2,1)S(1)} fusion(bf16[512,1024]{1,0:T(8,128)(2,1)S(1)} %copy-done, bf16[3,1024,256]{2,1,0:T(8,128)(2,1)} %param.8), kind=kOutput, calls=%fused_computation.6 | convolution fusion | flops 268566528 | bytes 1835008 | tf_op jit(solution)/shard_map/dot_general | solution.py:116
  11.1 1.5 %convolution_convert_fusion.1 = bf16[512,256]{0,1:T(8,128)(2,1)S(1)} fusion(bf16[512,1024]{1,0:T(8,128)(2,1)S(1)} %copy-done, bf16[3,1024,256]{2,1,0:T(8,128)(2,1)} %param.8), kind=kOutput, calls=%fused_computation.7 | convolution fusion | flops 268566528 | bytes 1835008 | tf_op jit(solution)/shard_map/dot_general | solution.py:115
  12.7 0.7 pad_maximum_fusion
  13.4 0.1 copy.15
  13.6 2.2 %all-to-all-done = s32[32,1,2]{2,1,0:T(1,128)S(1)} async-done(((s32[32,1,2]{2,1,0:T(1,128)}), s32[32,1,2]{2,1,0:T(1,128)S(1)}, u32[]{:S(2)}, u32[]{:S(2)}) %all-to-all-start) | async-done | bytes 288 | tf_op jit(solution)/shard_map/all_to_all | solution.py:113
  15.7 0.5 broadcast.124
  16.3 0.7 reduce.3
  17.0 0.1 reshape.101
  17.1 2.0 %gather_fusion = bf16[64,64,256]{2,1,0:T(8,128)(2,1)} fusion(bf16[8,64,256]{2,1,0:T(8,128)(2,1)S(1)} %bitcast.46, s32[1024]{0:T(1024)S(1)} %pad_clamp_fusion.1), kind=kCustom, calls=%fused_computation | custom fusion | bytes 4194560 | tf_op jit(solution)/shard_map/jit(_take)/gather | solution.py:130
  19.1 5.2 %all-to-all-start.1 = ((bf16[64,64,256]{2,1,0:T(8,128)(2,1)}), bf16[64,64,256]{2,1,0:T(8,128)(2,1)S(1)}, u32[]{:S(2)}, u32[]{:S(2)}) async-start(bf16[64,64,256]{2,1,0:T(8,128)(2,1)} %gather_fusion), calls=%async_computation.1 | async-start | bytes 4194304 | tf_op jit(solution)/shard_map/all_to_all | solution.py:138
  24.3 1.1 copy.17
  25.4 2.0 %gather_fusion.1 = bf16[64,64,256]{2,1,0:T(8,128)(2,1)} fusion(bf16[8,64,256]{2,1,0:T(8,128)(2,1)S(1)} %bitcast.47, s32[1024]{0:T(1024)S(1)} %pad_clamp_fusion.1), kind=kCustom, calls=%fused_computation.1 | custom fusion | bytes 4194560 | tf_op jit(solution)/shard_map/jit(_take)/gather | solution.py:130
  27.4 0.0 copy-start.4
  27.4 24.8 %all-to-all-done.1.kv_ref = bf16[64,64,256]{2,1,0:T(8,128)(2,1)S(1)} async-done(((bf16[64,64,256]{2,1,0:T(8,128)(2,1)}), bf16[64,64,256]{2,1,0:T(8,128)(2,1)S(1)}, u32[]{:S(2)}, u32[]{:S(2)}) %all-to-all-start.1) | async-done | bytes 2097184 | tf_op jit(solution)/shard_map/all_to_all | solution.py:138
  52.2 6.7 %all-to-all-start.2 = ((bf16[64,64,256]{2,1,0:T(8,128)(2,1)}), bf16[64,64,256]{2,1,0:T(8,128)(2,1)}, u32[]{:S(2)}, u32[]{:S(2)}) async-start(bf16[64,64,256]{2,1,0:T(8,128)(2,1)} %gather_fusion.1), calls=%async_computation.2 | async-start | bytes 4194304 | tf_op jit(solution)/shard_map/all_to_all | solution.py:138
  59.0 0.0 copy-start.2
  59.0 0.0 copy-start.3
  59.1 1.8 %constant_dynamic-slice_fusion.3 = (bf16[256,256]{1,0:T(8,128)(2,1)}, bf16[256,256]{1,0:T(8,128)(2,1)}, bf16[256,256]{1,0:T(8,128)(2,1)}) fusion(bf16[256,1024]{1,0:T(8,128)(2,1)} %param.9, s32[]{:T(128)S(6)} %select_n.104, s32[]{:T(128)S(6)} %select_n.108, s32[]{:T(128)S(6)} %select_n.106), kind=kLoop, calls=%fused_computation.64 | loop fusion | bytes 786444 | tf_op jit(solution)/shard_map/dynamic_slice | solution.py:120
  60.9 4.0 %collective-permute-start.5 = (bf16[256,256]{1,0:T(8,128)(2,1)}, bf16[256,256]{1,0:T(8,128)(2,1)}, u32[]{:S(2)}, u32[]{:S(2)}) collective-permute-start(bf16[256,256]{1,0:T(8,128)(2,1)} %get-tuple-element.12), channel_id=1, source_target_pairs={{0,3},{1,0},{2,1},{3,2},{4,7},{5,4},{6,5},{7,6},{8,11},{9,8},{10,9... | collective-permute-start | bytes 393224 | tf_op jit(solution)/shard_map/ppermute | solution.py:122
  64.9 0.0 collective-permute-start.4
  64.9 1.3 collective-permute-start.3
  66.2 0.0 copy-done.4
  66.2 0.1 eq.63
  66.3 0.1 select_reduce_fusion
  66.4 0.1 reshape.94
  66.5 1.5 %convolution_convert_fusion.2 = bf16[512,256]{1,0:T(8,128)(2,1)S(1)} fusion(bf16[512,1024]{1,0:T(8,128)(2,1)S(1)} %copy-done, bf16[3,1024,256]{2,1,0:T(8,128)(2,1)} %param.8), kind=kOutput, calls=%fused_computation.8 | convolution fusion | flops 268566528 | bytes 1835008 | tf_op jit(solution)/shard_map/dot_general | solution.py:114
  68.0 1.5 %constant_dynamic-slice_fusion = (bf16[128,256]{1,0:T(8,128)(2,1)}, bf16[1,128,256]{2,1,0:T(8,128)(2,1)S(1)}) fusion(bf16[256,1024]{1,0:T(8,128)(2,1)} %param.9, s32[]{:T(128)S(6)} %select_n.102, s32[]{:T(128)S(6)} %add.74), kind=kLoop, calls=%fused_computation.61 | loop fusion | bytes 262152 | tf_op jit(solution)/shard_map/slice | solution.py:145
  69.5 1.6 %collective-permute-done.5 = bf16[256,256]{1,0:T(8,128)(2,1)} collective-permute-done((bf16[256,256]{1,0:T(8,128)(2,1)}, bf16[256,256]{1,0:T(8,128)(2,1)}, u32[]{:S(2)}, u32[]{:S(2)}) %collective-permute-start.5) | collective-permute-done | bytes 131104 | tf_op jit(solution)/shard_map/ppermute | solution.py:122
  71.1 1.5 %fusion.32 = (bf16[128,256]{1,0:T(8,128)(2,1)}, bf16[1,128,256]{2,1,0:T(8,128)(2,1)S(1)}) fusion(bf16[256,256]{1,0:T(8,128)(2,1)} %collective-permute-done.5), kind=kLoop, calls=%fused_computation.72 | loop fusion | bytes 262144 | tf_op jit(solution)/shard_map/slice | solution.py:149
  72.6 14.5 %all-to-all-done.2.kv_ref = bf16[64,64,256]{2,1,0:T(8,128)(2,1)} async-done(((bf16[64,64,256]{2,1,0:T(8,128)(2,1)}), bf16[64,64,256]{2,1,0:T(8,128)(2,1)}, u32[]{:S(2)}, u32[]{:S(2)}) %all-to-all-start.2) | async-done | bytes 2097184 | tf_op jit(solution)/shard_map/all_to_all | solution.py:138
  87.1 0.0 copy-done.2
  87.1 0.0 copy-done.3
  87.1 13.6 %shard_map.74 = bf16[4,8,64,128]{3,2,1,0:T(8,128)(2,1)S(1)} custom-call(s32[8,64]{1,0:T(8,128)S(1)} %convert_add_fusion.nbr_ref, s32[8]{0:T(128)S(1)} %copy-done.2, f32[4]{0:T(128)S(1)} %copy-done.3, bf16[8,64,256]{2,1,0:T(8,128)(2,1)S(1)} %bitcast.40, bf16[8,64,4096]{2,1,0:T(8,128)(2,1)} %bias_ref.3, bf16[64,64,256]{2,1,0:T(8,128)(2,1)} %all-to-all-done.2.kv_ref), custom_call_target="tpu_custom_call" | custom-call | tf_op jit(solution)/shard_map/pallas_call | solution.py:75
  100.6 0.0 copy-start.1
  100.7 0.8 copy-done.1
  101.4 5.3 %all-to-all-start.3 = ((bf16[4,512,128]{2,1,0:T(8,128)(2,1)}), bf16[4,512,128]{2,1,0:T(8,128)(2,1)}, u32[]{:S(2)}, u32[]{:S(2)}) async-start(bf16[4,512,128]{2,1,0:T(8,128)(2,1)} %bitcast.39), calls=%async_computation.3 | async-start | bytes 1048576 | tf_op jit(solution)/shard_map/all_to_all | solution.py:159
  106.8 0.0 collective-permute-done.4
  106.8 1.5 %fusion.31 = (bf16[128,256]{1,0:T(8,128)(2,1)}, bf16[1,128,256]{2,1,0:T(8,128)(2,1)S(1)}) fusion(bf16[256,256]{1,0:T(8,128)(2,1)} %collective-permute-done.4), kind=kLoop, calls=%fused_computation.71 | loop fusion | bytes 262144 | tf_op jit(solution)/shard_map/slice | solution.py:149
  108.3 0.0 collective-permute-done.3
  108.3 1.5 %fusion.30 = (bf16[128,256]{1,0:T(8,128)(2,1)}, bf16[1,128,256]{2,1,0:T(8,128)(2,1)S(1)}) fusion(bf16[256,256]{1,0:T(8,128)(2,1)} %collective-permute-done.3), kind=kLoop, calls=%fused_computation.70 | loop fusion | bytes 262144 | tf_op jit(solution)/shard_map/slice | solution.py:149
  109.8 0.7 pad_maximum_fusion.2
  110.5 2.2 %gather_fusion.2 = bf16[4,128,256]{2,1,0:T(8,128)(2,1)} fusion(bf16[4,128,256]{2,1,0:T(8,128)(2,1)} %pad_maximum_fusion.2, s32[1024]{0:T(1024)S(1)} %pad_clamp_fusion), kind=kCustom, calls=%fused_computation.2 | custom fusion | bytes 524304 | tf_op jit(solution)/shard_map/jit(_take)/gather | solution.py:158
  112.8 12.0 %shard_map.73 = bf16[1,8,64,128]{3,2,1,0:T(8,128)(2,1)S(1)} custom-call(s32[8,64]{1,0:T(8,128)S(1)} %convert_add_fusion.nbr_ref, s32[8]{0:T(128)S(1)} %copy-done.2, f32[4]{0:T(128)S(1)} %copy-done.3, bf16[8,64,256]{2,1,0:T(8,128)(2,1)S(1)} %bitcast.41, bf16[8,64,4096]{2,1,0:T(8,128)(2,1)} %bias_ref.3, bf16[64,64,256]{2,1,0:T(8,128)(2,1)S(1)} %all-to-all-done.1.kv_ref), custom_call_target="tpu_custom_call" | custom-call | tf_op jit(solution)/shard_map/pallas_call | solution.py:75
  124.8 3.3 %collective-permute-start.2 = (bf16[512,128]{1,0:T(8,128)(2,1)S(1)}, bf16[512,128]{1,0:T(8,128)(2,1)S(1)}, u32[]{:S(2)}, u32[]{:S(2)}) collective-permute-start(bf16[512,128]{1,0:T(8,128)(2,1)S(1)} %bitcast.42), channel_id=1, source_target_pairs={{0,3},{1,0},{2,1},{3,2},{4,7},{5,4},{6,5},{7,6},{8,11},{9,8},{10,9... | collective-permute-start | bytes 393224 | tf_op jit(solution)/shard_map/ppermute | solution.py:148
  128.1 0.9 collective-permute-start.1
  128.9 0.9 collective-permute-start
  129.8 0.0 all-to-all-done.3
  129.8 1.4 %convolution_bitcast_fusion = f32[512,256]{1,0:T(8,128)S(1)} fusion(bf16[4,512,128]{2,1,0:T(8,128)(2,1)} %all-to-all-done.3, bf16[4,128,256]{2,1,0:T(8,128)(2,1)} %gather_fusion.2), kind=kOutput, calls=%fused_computation.3 | convolution fusion | flops 134217728 | bytes 1310720 | tf_op jit(solution)/shard_map/dot_general | solution.py:160
  131.2 1.7 %collective-permute-done.2 = bf16[512,128]{1,0:T(8,128)(2,1)S(1)} collective-permute-done((bf16[512,128]{1,0:T(8,128)(2,1)S(1)}, bf16[512,128]{1,0:T(8,128)(2,1)S(1)}, u32[]{:S(2)}, u32[]{:S(2)}) %collective-permute-start.2) | collective-permute-done | bytes 131104 | tf_op jit(solution)/shard_map/ppermute | solution.py:148
  133.0 2.3 %collective-permute-done.1 = bf16[512,128]{1,0:T(8,128)(2,1)S(1)} collective-permute-done((bf16[512,128]{1,0:T(8,128)(2,1)S(1)}, bf16[512,128]{1,0:T(8,128)(2,1)S(1)}, u32[]{:S(2)}, u32[]{:S(2)}) %collective-permute-start.1) | collective-permute-done | bytes 131104 | tf_op jit(solution)/shard_map/ppermute | solution.py:148
  135.3 1.4 %collective-permute-done = bf16[512,128]{1,0:T(8,128)(2,1)S(1)} collective-permute-done((bf16[512,128]{1,0:T(8,128)(2,1)S(1)}, bf16[512,128]{1,0:T(8,128)(2,1)S(1)}, u32[]{:S(2)}, u32[]{:S(2)}) %collective-permute-start) | collective-permute-done | bytes 131104 | tf_op jit(solution)/shard_map/ppermute | solution.py:148
  136.7 1.9 %fusion = bf16[512,256]{1,0:T(8,128)(2,1)} fusion(f32[512,256]{1,0:T(8,128)S(1)} %convolution_bitcast_fusion, bf16[512,128]{1,0:T(8,128)(2,1)S(1)} %collective-permute-done.2, bf16[512,128]{1,0:T(8,128)(2,1)S(1)} %collective-permute-done.1, bf16[512,128]{1,0:T(8,128)(2,1)S(1)} %collective-permute-done, bf16[512,128]{1,0:T(8,128)(2,1)S(1)} %bitcast.45, ...), kind=kOutput, calls=%fused_computation.5 | convolution fusion | flops 137625600 | bytes 1572864 | tf_op jit(solution)/shard_map/dot_general | solution.py:150
  (10 shorter events, 0.1 us)
Async XLA Ops:
  0.0 9.6 %copy-start = (bf16[512,1024]{1,0:T(8,128)(2,1)S(1)}, bf16[512,1024]{1,0:T(8,128)(2,1)}, u32[]{:S(2)}) copy-start(bf16[512,1024]{1,0:T(8,128)(2,1)} %param.7) | copy-start | bytes 3145732
  1.9 13.8 %all-to-all-start = ((s32[32,1,2]{2,1,0:T(1,128)}), s32[32,1,2]{2,1,0:T(1,128)S(1)}, u32[]{:S(2)}, u32[]{:S(2)}) async-start(s32[32,1,2]{2,1,0:T(1,128)} %copy.16), calls=%async_computation | async-start | bytes 32768 | tf_op jit(solution)/shard_map/all_to_all | solution.py:113
  19.1 33.2 %all-to-all-start.1 = ((bf16[64,64,256]{2,1,0:T(8,128)(2,1)}), bf16[64,64,256]{2,1,0:T(8,128)(2,1)S(1)}, u32[]{:S(2)}, u32[]{:S(2)}) async-start(bf16[64,64,256]{2,1,0:T(8,128)(2,1)} %gather_fusion), calls=%async_computation.1 | async-start | bytes 4194304 | tf_op jit(solution)/shard_map/all_to_all | solution.py:138
  27.4 38.7 %copy-start.4 = (s32[8,64]{1,0:T(8,128)S(1)}, s32[8,64]{1,0:T(8,128)}, u32[]{:S(2)}) copy-start(s32[8,64]{1,0:T(8,128)} %param.12) | copy-start | bytes 6148
  52.2 34.8 %all-to-all-start.2 = ((bf16[64,64,256]{2,1,0:T(8,128)(2,1)}), bf16[64,64,256]{2,1,0:T(8,128)(2,1)}, u32[]{:S(2)}, u32[]{:S(2)}) async-start(bf16[64,64,256]{2,1,0:T(8,128)(2,1)} %gather_fusion.1), calls=%async_computation.2 | async-start | bytes 4194304 | tf_op jit(solution)/shard_map/all_to_all | solution.py:138
  59.0 28.1 %copy-start.2 = (s32[8]{0:T(128)S(1)}, s32[8]{0:T(128)}, u32[]{:S(2)}) copy-start(s32[8]{0:T(128)} %cnt_ref.3) | copy-start | bytes 100
  59.0 28.1 %copy-start.3 = (f32[4]{0:T(128)S(1)}, f32[4]{0:T(128)}, u32[]{:S(2)}) copy-start(f32[4]{0:T(128)} %gain_ref.3) | copy-start | bytes 52
  60.9 10.2 %collective-permute-start.5 = (bf16[256,256]{1,0:T(8,128)(2,1)}, bf16[256,256]{1,0:T(8,128)(2,1)}, u32[]{:S(2)}, u32[]{:S(2)}) collective-permute-start(bf16[256,256]{1,0:T(8,128)(2,1)} %get-tuple-element.12), channel_id=1, source_target_pairs={{0,3},{1,0},{2,1},{3,2},{4,7},{5,4},{6,5},{7,6},{8,11},{9,8},{10,9... | collective-permute-start | bytes 393224 | tf_op jit(solution)/shard_map/ppermute | solution.py:122
  64.9 41.9 %collective-permute-start.4 = (bf16[256,256]{1,0:T(8,128)(2,1)}, bf16[256,256]{1,0:T(8,128)(2,1)}, u32[]{:S(2)}, u32[]{:S(2)}) collective-permute-start(bf16[256,256]{1,0:T(8,128)(2,1)} %get-tuple-element.13), channel_id=1, source_target_pairs={{0,2},{1,3},{2,0},{3,1},{4,6},{5,7},{6,4},{7,5},{8,10},{9,11},{10,... | collective-permute-start | bytes 393224 | tf_op jit(solution)/shard_map/ppermute | solution.py:122
  64.9 43.4 %collective-permute-start.3 = (bf16[256,256]{1,0:T(8,128)(2,1)}, bf16[256,256]{1,0:T(8,128)(2,1)}, u32[]{:S(2)}, u32[]{:S(2)}) collective-permute-start(bf16[256,256]{1,0:T(8,128)(2,1)} %get-tuple-element.11), channel_id=1, source_target_pairs={{0,1},{1,2},{2,3},{3,0},{4,5},{5,6},{6,7},{7,4},{8,9},{9,10},{10,1... | collective-permute-start | bytes 393224 | tf_op jit(solution)/shard_map/ppermute | solution.py:122
  100.6 0.8 copy-start.1
  101.4 28.4 %all-to-all-start.3 = ((bf16[4,512,128]{2,1,0:T(8,128)(2,1)}), bf16[4,512,128]{2,1,0:T(8,128)(2,1)}, u32[]{:S(2)}, u32[]{:S(2)}) async-start(bf16[4,512,128]{2,1,0:T(8,128)(2,1)} %bitcast.39), calls=%async_computation.3 | async-start | bytes 1048576 | tf_op jit(solution)/shard_map/all_to_all | solution.py:159
  124.8 8.2 %collective-permute-start.2 = (bf16[512,128]{1,0:T(8,128)(2,1)S(1)}, bf16[512,128]{1,0:T(8,128)(2,1)S(1)}, u32[]{:S(2)}, u32[]{:S(2)}) collective-permute-start(bf16[512,128]{1,0:T(8,128)(2,1)S(1)} %bitcast.42), channel_id=1, source_target_pairs={{0,3},{1,0},{2,1},{3,2},{4,7},{5,4},{6,5},{7,6},{8,11},{9,8},{10,9... | collective-permute-start | bytes 393224 | tf_op jit(solution)/shard_map/ppermute | solution.py:148
  128.1 7.2 %collective-permute-start.1 = (bf16[512,128]{1,0:T(8,128)(2,1)S(1)}, bf16[512,128]{1,0:T(8,128)(2,1)S(1)}, u32[]{:S(2)}, u32[]{:S(2)}) collective-permute-start(bf16[512,128]{1,0:T(8,128)(2,1)S(1)} %bitcast.43), channel_id=1, source_target_pairs={{0,2},{1,3},{2,0},{3,1},{4,6},{5,7},{6,4},{7,5},{8,10},{9,11},{10,... | collective-permute-start | bytes 393224 | tf_op jit(solution)/shard_map/ppermute | solution.py:148
  128.9 7.7 %collective-permute-start = (bf16[512,128]{1,0:T(8,128)(2,1)S(1)}, bf16[512,128]{1,0:T(8,128)(2,1)S(1)}, u32[]{:S(2)}, u32[]{:S(2)}) collective-permute-start(bf16[512,128]{1,0:T(8,128)(2,1)S(1)} %bitcast.44), channel_id=1, source_target_pairs={{0,1},{1,2},{2,3},{3,0},{4,5},{5,6},{6,7},{7,4},{8,9},{9,10},{10,1... | collective-permute-start | bytes 393224 | tf_op jit(solution)/shard_map/ppermute | solution.py:148
